TPU v7x, 512 devices: a whole 4x4x16 slice. The times are simulated.
512 devices in a mesh: group: 32 (over y, z_lo, core), expert: 16 (over x, z_hi).
Axes of the slice: x: 4, y: 4, z: 16 (z_hi: 4, z_lo: 4; z = z_hi * 4 + z_lo), core: 2. Of those that a mesh axis runs over, the one named last changes fastest.
Arguments:
- tokens: bfloat16 [65536, 1536], P(('group', 'expert')), may hold values from -6 to 6
- gate_train: float32 [32, 1536, 512], P('expert', 'group'), may hold values from -0.15625 to 0.15625
- up_train: float32 [32, 1536, 512], P('expert', 'group'), may hold values from -0.15625 to 0.15625
- down_train: float32 [32, 512, 1536], P('expert', None, 'group'), may hold values from -0.25 to 0.25
- routes: int32 [65536, 6], P(('group', 'expert')), may hold values from 0 to 31, as said below
- route_scores: float32 [65536, 6], P(('group', 'expert')), may hold values from 0.05 to 1
- live: int32 [65536], P(('group', 'expert')), may hold values from 0 to 1
Outputs:
- moe_out: bfloat16 [65536, 1536], P(('group', 'expert'))
Inputs may be any that keep to these rules, and one draw needn't show every extreme that they name: `routes`: each row names 6 different experts; one expert, the same on every device, is named by at least 24 live rows among each device's 128 rows.
All inputs are finite; a program needn't handle non-finite values.
Results may differ from a plain program's by a relative error of at most 0.0075.
Values may be sent and summed in bfloat16 or wider, within the bound.
No kernel may reach another device: no remote copies, remote signals or barrier semaphores. Data moves between devices by JAX's collectives and lax.ppermute only.
A program may use at most 64 MiB of HBM per device.

v0:
```python
import jax
import jax.numpy as jnp
from jax import lax
from jax.sharding import PartitionSpec as P


def local(tokens, gate_train, up_train, down_train, routes, route_scores, live):
    local_experts = gate_train.shape[0]
    hidden_width = gate_train.shape[2]
    holders = lax.axis_size("expert")
    experts = local_experts * holders
    tok_dev, model_width = tokens.shape
    top_count = routes.shape[1]
    capacity = tok_dev * top_count // experts
    total_slots = experts * capacity
    route_share = route_scores / jnp.sum(route_scores, axis=1, keepdims=True)
    flat_route = routes.reshape(-1)
    flat_live = jnp.repeat(live, top_count)
    expert_ids = jnp.arange(experts, dtype=jnp.int32)
    onehot = ((flat_route[:, None] == expert_ids[None, :]) & (flat_live[:, None] > 0)).astype(
        jnp.int32
    )
    earlier = jnp.cumsum(onehot, axis=0) - onehot
    slot_index = jnp.sum(earlier * onehot, axis=1)
    kept_mask = (flat_live > 0) & (slot_index < capacity)
    target = jnp.where(kept_mask, flat_route * capacity + slot_index, total_slots)
    anchor = jnp.arange(tok_dev * top_count, dtype=jnp.int32) // top_count
    source_row = jnp.zeros((total_slots,), jnp.int32).at[target].set(anchor, mode="drop")
    filled = jnp.zeros((total_slots,), jnp.int32).at[target].set(1, mode="drop")
    outgoing = jnp.where(filled[:, None] > 0, tokens[source_row], jnp.zeros((), jnp.bfloat16))
    outgoing = outgoing.reshape(holders, local_experts * capacity, model_width)
    incoming = lax.all_to_all(outgoing, "expert", split_axis=0, concat_axis=0, tiled=True)
    incoming = incoming.reshape(holders, local_experts, capacity, model_width)
    gate_up_local = jnp.concatenate([gate_train, up_train], axis=2).astype(jnp.bfloat16)
    down_local = down_train.astype(jnp.bfloat16)
    gate_up_w, down_w = (
        lax.all_gather(gate_up_local, "group", axis=1, tiled=True),
        lax.all_gather(down_local, "group", axis=2, tiled=True),
    )
    gate_up = jnp.einsum("sjcd,jdf->sjcf", incoming, gate_up_w, preferred_element_type=jnp.float32)
    hidden = (jax.nn.silu(gate_up[..., :hidden_width]) * gate_up[..., hidden_width:]).astype(
        jnp.bfloat16
    )
    expert_out = jnp.einsum("sjcf,jfd->sjcd", hidden, down_w, preferred_element_type=jnp.float32)
    expert_rows = expert_out.astype(jnp.bfloat16).reshape(
        holders, local_experts * capacity, model_width
    )
    returned = lax.all_to_all(
        expert_rows, "expert", split_axis=0, concat_axis=0, tiled=True
    ).reshape(total_slots, model_width)
    picked = returned[jnp.minimum(target, total_slots - 1)]
    weight = jnp.where(kept_mask, route_share.reshape(-1), 0.0)
    combined = jnp.sum(
        picked.reshape(tok_dev, top_count, model_width).astype(jnp.float32)
        * weight.reshape(tok_dev, top_count, 1),
        axis=1,
    )
    return combined.astype(jnp.bfloat16)


def solution(mesh):
    in_specs = (
        P(("group", "expert"), None),
        P("expert", "group", None),
        P("expert", "group", None),
        P("expert", None, "group"),
        P(("group", "expert"), None),
        P(("group", "expert"), None),
        P(("group", "expert")),
    )
    out_specs = P(("group", "expert"), None)
    return jax.shard_map(local, mesh=mesh, in_specs=in_specs, out_specs=out_specs, check_vma=False)
```

profile of v0, /device:TPU:1, one launch (start us, length us, event | category | flops | bytes accessed | tf_op | source)
XLA Modules:
  0.0 402.3 jit_solution(16092670859250466878)
XLA Ops:
  6.5 0.0 copy-start
  6.5 0.0 all-gather.3.cloned.1.call-start
  6.5 1.0 convert.7
  7.5 0.9 convert.8
  8.5 0.7 pad_maximum_fusion
  9.2 0.0 all-gather.3.cloned.1.call-update
  9.2 0.7 broadcast_compare_fusion.2
  9.9 0.1 broadcast_in_dim.37.clone
  10.0 0.2 gt.41
  10.1 0.1 gt.40
  10.3 0.8 copy.18
  11.1 0.1 eq.29
  11.2 0.1 eq.25
  11.3 0.1 gt.39
  11.5 1.7 reduce-window.6
  13.2 0.3 slice_reduce_fusion
  13.5 0.7 broadcast_multiply_fusion
  14.2 0.1 copy.23
  14.3 0.1 mul.37
  14.5 0.1 fusion.17
  14.7 3.4 scatter_custom_fusion.1
  18.0 3.4 scatter_custom_fusion
  21.4 0.1 broadcast_in_dim.40
  21.6 0.0 copy-done
  21.6 2.9 gather_fusion
  24.5 1.6 broadcast_select_fusion
  26.1 0.0 copy-start.1
  26.1 18.3 %all-to-all-start = ((bf16[16,48,1536]{2,1,0:T(8,128)(2,1)}), bf16[16,48,1536]{2,1,0:T(8,128)(2,1)S(1)}, u32[]{:S(2)}, u32[]{:S(2)}) async-start(bf16[16,48,1536]{2,1,0:T(8,128)(2,1)} %broadcast_select_fusion), calls=%async_computation | async-start | bytes 4718592 | tf_op jit(solution)/shard_map/all_to_all | solution.py:32
  44.5 0.0 all-gather.5.cloned.1.call-start
  44.5 0.0 copy-done.1
  44.5 0.7 convert_element_type.32
  45.2 0.0 all-gather.5.cloned.1.call-update
  45.2 115.2 %all-to-all-done = bf16[16,48,1536]{2,1,0:T(8,128)(2,1)S(1)} async-done(((bf16[16,48,1536]{2,1,0:T(8,128)(2,1)}), bf16[16,48,1536]{2,1,0:T(8,128)(2,1)S(1)}, u32[]{:S(2)}, u32[]{:S(2)}) %all-to-all-start) | async-done | bytes 2359328 | tf_op jit(solution)/shard_map/all_to_all | solution.py:32
  160.4 23.6 %all-gather.3.cloned.1.call-done = bf16[2,1536,1024]{2,1,0:T(8,128)(2,1)} async-done(((bf16[2,48,1024]{2,1,0:T(8,128)(2,1)}), bf16[2,1536,1024]{2,1,0:T(8,128)(2,1)}) %all-gather.3.cloned.1.call-update) | async-done | bytes 6291472 | tf_op jit(solution)/shard_map/all_gather | solution.py:37
  184.1 7.0 %fusion.7 = f32[16,2,24,1024]{3,2,0,1:T(8,128)} fusion(bf16[16,2,24,1536]{3,2,1,0:T(8,128)(2,1)S(1)} %bitcast.45, bf16[2,1536,1024]{2,1,0:T(8,128)(2,1)} %all-gather.3.cloned.1.call-done), kind=kOutput, calls=%fused_computation.12 | convolution fusion | flops 2415919104 | bytes 11796480 | tf_op jit(solution)/shard_map/sjcd,jdf->sjcf/dot_general | solution.py:40
  191.1 61.9 %all-gather.5.cloned.1.call-done = bf16[2,512,1536]{1,2,0:T(8,128)(2,1)} async-done(((bf16[2,512,48]{1,2,0:T(8,128)(2,1)}), bf16[2,512,1536]{1,2,0:T(8,128)(2,1)}) %all-gather.5.cloned.1.call-update) | async-done | bytes 3145744 | tf_op jit(solution)/shard_map/all_gather | solution.py:38
  253.0 4.3 %fusion.3 = bf16[16,2,24,1536]{3,2,0,1:T(8,128)(2,1)S(1)} fusion(bf16[2,512,1536]{1,2,0:T(8,128)(2,1)} %all-gather.5.cloned.1.call-done, f32[16,2,24,1024]{3,2,0,1:T(8,128)} %fusion.7), kind=kOutput, calls=%fused_computation.9 | convolution fusion | flops 1211498496 | bytes 8650752 | tf_op jit(solution)/shard_map/sjcf,jfd->sjcd/dot_general | solution.py:44
  257.3 1.7 copy.25
  259.0 0.0 copy-start.2
  259.0 13.2 %all-to-all-start.1 = ((bf16[16,48,1536]{2,1,0:T(8,128)(2,1)}), bf16[16,48,1536]{2,1,0:T(8,128)(2,1)S(1)}, u32[]{:S(2)}, u32[]{:S(2)}) async-start(bf16[16,48,1536]{2,1,0:T(8,128)(2,1)} %bitcast.43), calls=%async_computation.1 | async-start | bytes 4718592 | tf_op jit(solution)/shard_map/all_to_all | solution.py:48
  272.2 0.2 lt.50
  272.4 0.1 copy.26
  272.5 0.0 copy-done.2
  272.5 0.1 copy.27
  272.7 108.1 %all-to-all-done.1 = bf16[16,48,1536]{2,1,0:T(8,128)(2,1)S(1)} async-done(((bf16[16,48,1536]{2,1,0:T(8,128)(2,1)}), bf16[16,48,1536]{2,1,0:T(8,128)(2,1)S(1)}, u32[]{:S(2)}, u32[]{:S(2)}) %all-to-all-start.1) | async-done | bytes 2359328 | tf_op jit(solution)/shard_map/all_to_all | solution.py:48
  380.7 3.9 gather_fusion.1
  384.6 5.0 %reshape.148 = f32[128,6,1536]{2,1,0:T(8,128)} reshape(bf16[768,1536]{1,0:T(8,128)(2,1)} %gather_fusion.1) | data formatting | bytes 7077888 | tf_op jit(solution)/shard_map/convert_element_type | solution.py:54
  389.6 5.9 %multiply_reduce_fusion = bf16[128,1536]{1,0:T(8,128)(2,1)} fusion(f32[128,6,1536]{2,1,0:T(8,128)} %reshape.148, f32[128,6]{1,0:T(8,128)S(1)} %copy.27), kind=kLoop, calls=%fused_computation.6 | loop fusion | flops 2162688 | bytes 5114880 | tf_op jit(solution)/shard_map/reduce_sum | solution.py:53
  (12 shorter events, 0.2 us)
Async XLA Ops:
  6.5 15.0 %copy-start = (bf16[128,1536]{1,0:T(8,128)(2,1)S(1)}, bf16[128,1536]{1,0:T(8,128)(2,1)}, u32[]{:S(2)}) copy-start(bf16[128,1536]{1,0:T(8,128)(2,1)} %param.7) | copy-start | bytes 1179652
  6.5 177.5 %all-gather.3.cloned.1.call-start = ((), (), s32[]{:S(2)}) async-start(), calls=%async_computation.2 | async-start | bytes 6488064 | tf_op jit(solution)/shard_map/all_gather | solution.py:37
  26.1 18.4 %copy-start.1 = (f32[2,512,48]{1,2,0:T(8,128)S(1)}, f32[2,512,48]{1,2,0:T(8,128)}, u32[]{:S(2)}) copy-start(f32[2,512,48]{1,2,0:T(8,128)} %param.10) | copy-start | bytes 589828
  26.1 134.3 %all-to-all-start = ((bf16[16,48,1536]{2,1,0:T(8,128)(2,1)}), bf16[16,48,1536]{2,1,0:T(8,128)(2,1)S(1)}, u32[]{:S(2)}, u32[]{:S(2)}) async-start(bf16[16,48,1536]{2,1,0:T(8,128)(2,1)} %broadcast_select_fusion), calls=%async_computation | async-start | bytes 4718592 | tf_op jit(solution)/shard_map/all_to_all | solution.py:32
  44.5 208.6 %all-gather.5.cloned.1.call-start = ((), (), s32[]{:S(2)}) async-start(), calls=%async_computation.3 | async-start | bytes 3244032 | tf_op jit(solution)/shard_map/all_gather | solution.py:38
  259.0 13.4 %copy-start.2 = (f32[128,6]{0,1:T(8,128)S(1)}, f32[128,6]{0,1:T(8,128)}, u32[]{:S(2)}) copy-start(f32[128,6]{0,1:T(8,128)} %param.12) | copy-start | bytes 9220
  259.0 121.7 %all-to-all-start.1 = ((bf16[16,48,1536]{2,1,0:T(8,128)(2,1)}), bf16[16,48,1536]{2,1,0:T(8,128)(2,1)S(1)}, u32[]{:S(2)}, u32[]{:S(2)}) async-start(bf16[16,48,1536]{2,1,0:T(8,128)(2,1)} %bitcast.43), calls=%async_computation.1 | async-start | bytes 4718592 | tf_op jit(solution)/shard_map/all_to_all | solution.py:48
Sparse Core Ops, SparseCore 0:
  9.4 174.5 all-gather.2
  186.1 66.8 all-gather.4
where the time goes:
time: 405 us; the launch traced here: 402 us
  waiting for transfers between devices  309 us (76%)
  starting transfers between devices  31.6 us (8%)
  local copies, waits for them, and re-layouts  22.8 us (6%)
  other arithmetic  14.2 us (4%)
  between operations  13.6 us (3%)
  matrix products  11.4 us (3%)
    all_to_all x1, waiting for transfers between devices, local(): lax.all_to_all(outgoing, 'expert', split_axis=0, concat_axis=0, tiled=True)  115 us
    all_to_all x1, waiting for transfers between devices, local(): lax.all_to_all(expert_rows, 'expert', split_axis=0, concat_axis=0, tiled=...  108 us
    all_gather x1, waiting for transfers between devices, local(): lax.all_gather(down_local, 'group', axis=2, tiled=True)  61.9 us
    all_gather x1, waiting for transfers between devices, local(): lax.all_gather(gate_up_local, 'group', axis=1, tiled=True)  23.6 us
    all_to_all x1, starting transfers between devices, local(): lax.all_to_all(outgoing, 'expert', split_axis=0, concat_axis=0, tiled=True)  18.3 us
    all_to_all x1, starting transfers between devices, local(): lax.all_to_all(expert_rows, 'expert', split_axis=0, concat_axis=0, tiled=...  13.2 us
  transfers between devices with their start and end apart: 4, of which 4 were waited for; matrix products, arithmetic and copies ran while one was open for 6% of the time, Pallas kernels for 0%

commit v1 on v0

v1 whole, which is shorter than its diff:
```python
import jax
import jax.numpy as jnp
from jax import lax
from jax.sharding import Mesh
from jax.sharding import PartitionSpec as P

AXES = ("y", "zl", "c", "x", "zh")
ROWS = ("y", "zl", "c", "x", "zh")
TOKEN_GROUP = ("x", "zl", "c")


def local(tokens, gate_train, up_train, down_train, routes, route_scores, live):
    hidden_width = gate_train.shape[2]
    tok_dev, model_width = tokens.shape
    top_count = routes.shape[1]
    experts = lax.axis_size(TOKEN_GROUP)
    capacity = tok_dev * top_count // experts
    total_slots = experts * capacity

    slab = jnp.concatenate(
        [gate_train, up_train, jnp.swapaxes(down_train, 1, 2)], axis=2
    ).astype(jnp.bfloat16)
    slab = lax.all_gather(slab, "zh", axis=0, tiled=False)
    n_pairs, local_experts, rows, width = slab.shape
    slab = slab.reshape(n_pairs * local_experts, rows, width)
    slab = lax.all_to_all(slab, ("zl", "c"), split_axis=0, concat_axis=0, tiled=True)
    slab = lax.all_gather(slab, "y", axis=0, tiled=True)
    weights = slab.reshape(model_width, width)
    gate_up_w = weights[:, : 2 * hidden_width]
    down_t = weights[:, 2 * hidden_width :]

    route_share = route_scores / jnp.sum(route_scores, axis=1, keepdims=True)
    flat_route = routes.reshape(-1)
    flat_live = jnp.repeat(live, top_count)
    expert_ids = jnp.arange(experts, dtype=jnp.int32)
    onehot = ((flat_route[:, None] == expert_ids[None, :]) & (flat_live[:, None] > 0)).astype(
        jnp.int32
    )
    earlier = jnp.cumsum(onehot, axis=0) - onehot
    slot_index = jnp.sum(earlier * onehot, axis=1)
    kept_mask = (flat_live > 0) & (slot_index < capacity)
    target = jnp.where(kept_mask, flat_route * capacity + slot_index, total_slots)
    anchor = jnp.arange(tok_dev * top_count, dtype=jnp.int32) // top_count
    source_row = jnp.zeros((total_slots,), jnp.int32).at[target].set(anchor, mode="drop")
    filled = jnp.zeros((total_slots,), jnp.int32).at[target].set(1, mode="drop")
    outgoing = jnp.where(filled[:, None] > 0, tokens[source_row], jnp.zeros((), jnp.bfloat16))
    incoming = lax.all_to_all(outgoing, TOKEN_GROUP, split_axis=0, concat_axis=0, tiled=True)

    gate_up = jnp.dot(incoming, gate_up_w, preferred_element_type=jnp.float32)
    hidden = (jax.nn.silu(gate_up[:, :hidden_width]) * gate_up[:, hidden_width:]).astype(
        jnp.bfloat16
    )
    expert_out = lax.dot_general(
        hidden, down_t, (((1,), (1,)), ((), ())), preferred_element_type=jnp.float32
    )
    expert_rows = expert_out.astype(jnp.bfloat16)
    returned = lax.all_to_all(expert_rows, TOKEN_GROUP, split_axis=0, concat_axis=0, tiled=True)
    picked = returned[jnp.minimum(target, total_slots - 1)]
    weight = jnp.where(kept_mask, route_share.reshape(-1), 0.0)
    combined = jnp.sum(
        picked.reshape(tok_dev, top_count, model_width).astype(jnp.float32)
        * weight.reshape(tok_dev, top_count, 1),
        axis=1,
    )
    return combined.astype(jnp.bfloat16)


def solution(mesh):
    fine = Mesh(mesh.devices.reshape(4, 4, 2, 4, 4), AXES)
    in_specs = (
        P(ROWS, None),
        P(("x", "zh"), ("y", "zl", "c"), None),
        P(("x", "zh"), ("y", "zl", "c"), None),
        P(("x", "zh"), None, ("y", "zl", "c")),
        P(ROWS, None),
        P(ROWS, None),
        P(ROWS),
    )
    out_specs = P(ROWS, None)
    return jax.shard_map(local, mesh=fine, in_specs=in_specs, out_specs=out_specs, check_vma=False)
```

time: 405 us -> 275 us (0.68)
  waiting for transfers between devices: 309 us -> 199 us
  starting transfers between devices: 31.6 us -> 20.6 us
    all_to_all x2 -> x3, waiting for transfers between devices: 223 us -> 123 us  [the longest x1 54.8 us: local(): lax.all_to_all(expert_rows, TOKEN_GROUP, split_axis=0, concat_axis=0, til...]
    all_to_all x2 -> x3, starting transfers between devices: 31.5 us -> 20.6 us  [the longest x1 8.35 us: local(): lax.all_to_all(expert_rows, TOKEN_GROUP, split_axis=0, concat_axis=0, til...]
    all_gather x2, waiting for transfers between devices: 85.5 us -> 74.9 us  [the longest x1 71.4 us: local(): slab = lax.all_gather(slab, 'zh', axis=0, tiled=False)]
  transfers between devices with their start and end apart: 4 -> 5, of which waited for: 4 -> 5; matrix products, arithmetic and copies ran while one was open for 6% -> 6% of each run, Pallas kernels for 0% -> 0%
where the time goes in v1:
time: 275 us; the launch traced here: 274 us
  waiting for transfers between devices  199 us (72%)
  starting transfers between devices  20.6 us (7%)
  local copies, waits for them, and re-layouts  20.4 us (7%)
  between operations  13.6 us (5%)
  other arithmetic  12.4 us (5%)
  matrix products  8.8 us (3%)
    all_gather x1, waiting for transfers between devices, local(): slab = lax.all_gather(slab, 'zh', axis=0, tiled=False)  71.4 us
    all_to_all x1, waiting for transfers between devices, local(): lax.all_to_all(expert_rows, TOKEN_GROUP, split_axis=0, concat_axis=0, til...  54.8 us
    all_to_all x1, waiting for transfers between devices, local(): lax.all_to_all(outgoing, TOKEN_GROUP, split_axis=0, concat_axis=0, tiled=...  54.5 us
    all_to_all x1, waiting for transfers between devices, local(): lax.all_to_all(slab, ('zl', 'c'), split_axis=0, concat_axis=0, tiled=True)  13.6 us
    all_to_all x1, starting transfers between devices, local(): lax.all_to_all(expert_rows, TOKEN_GROUP, split_axis=0, concat_axis=0, til...  8.35 us
    all_to_all x1, starting transfers between devices, local(): lax.all_to_all(slab, ('zl', 'c'), split_axis=0, concat_axis=0, tiled=True)  6.12 us
    all_to_all x1, starting transfers between devices, local(): lax.all_to_all(outgoing, TOKEN_GROUP, split_axis=0, concat_axis=0, tiled=...  6.11 us
    reduce_sum x1, other arithmetic, local(): jnp.sum(picked.reshape(tok_dev, top_count, model_width).astype(jnp.float3...  5.92 us
  transfers between devices with their start and end apart: 5, of which 5 were waited for; matrix products, arithmetic and copies ran while one was open for 6% of the time, Pallas kernels for 0%

profile of v1, /device:TPU:1, one launch (start us, length us, event | category | flops | bytes accessed | tf_op | source)
XLA Modules:
  0.0 274.3 jit_solution(7686041357641155009)
XLA Ops:
  6.5 0.0 copy-start
  6.5 0.0 copy-start.3
  6.5 0.0 copy-start.1
  6.5 0.0 all-gather.3.cloned.1.call-start
  6.5 1.0 convert_bitcast_fusion
  7.5 1.0 convert_bitcast_fusion.1
  8.6 0.7 pad_maximum_fusion
  9.3 0.0 all-gather.3.cloned.1.call-update
  9.4 71.4 %all-gather.3.cloned.1.call-done = bf16[4,2,48,1536]{3,2,1,0:T(8,128)(2,1)} async-done(((bf16[1,2,48,1536]{3,2,1,0:T(8,128)(2,1)}), bf16[4,2,48,1536]{3,2,1,0:T(8,128)(2,1)}) %all-gather.3.cloned.1.call-update) | async-done | bytes 1179664 | tf_op jit(solution)/shard_map/all_gather | solution.py:23
  80.8 6.1 %all-to-all-start.1 = ((bf16[8,48,1536]{2,1,0:T(8,128)(2,1)}), bf16[8,48,1536]{2,1,0:T(8,128)(2,1)}, u32[]{:S(2)}, u32[]{:S(2)}) async-start(bf16[8,48,1536]{2,1,0:T(8,128)(2,1)} %bitcast.39), calls=%async_computation.1 | async-start | bytes 2359296 | tf_op jit(solution)/shard_map/all_to_all | solution.py:26
  86.9 0.0 copy-done.3
  86.9 0.1 broadcast_in_dim.37.clone
  87.0 0.2 gt.41
  87.1 0.1 gt.40
  87.3 0.0 copy-done.1
  87.3 0.1 copy.22
  87.4 0.1 eq.29
  87.5 0.1 eq.25
  87.7 0.1 gt.39
  87.8 1.7 reduce-window.6
  89.6 0.3 slice_reduce_fusion
  89.9 0.1 copy.27
  90.0 0.1 mul.37
  90.2 0.1 fusion.8
  90.3 3.4 %scatter_custom_fusion.1 = s32[768]{0:T(1024)S(1)} fusion(s32[768]{0:T(1024)S(1)} %get-tuple-element.6, s32[768]{0:T(1024)S(1)} %add_select_fusion, s32[]{:T(128)} %constant.11.clone.1), kind=kCustom, calls=%fused_computation.46 | custom fusion | bytes 3076 | tf_op jit(solution)/shard_map/scatter | solution.py:44
  93.7 3.4 %scatter_custom_fusion = s32[768]{0:T(1024)S(1)} fusion(s32[768]{0:T(1024)S(1)} %get-tuple-element.6, s32[768]{0:T(1024)S(1)} %broadcast.166, s32[]{:T(128)} %constant.11.clone.1), kind=kCustom, calls=%fused_computation.49 | custom fusion | bytes 3076 | tf_op jit(solution)/shard_map/scatter | solution.py:45
  97.1 0.1 broadcast_in_dim.40
  97.2 0.0 copy-done
  97.2 2.9 %gather_fusion = bf16[768,1536]{1,0:T(8,128)(2,1)S(1)} fusion(bf16[128,1536]{1,0:T(8,128)(2,1)S(1)} %copy-done, s32[1024]{0:T(1024)S(1)} %pad_clamp_fusion.1), kind=kCustom, calls=%fused_computation | custom fusion | bytes 4721664 | tf_op jit(solution)/shard_map/gather | solution.py:46
  100.2 1.7 broadcast_select_fusion
  101.9 13.6 %all-to-all-done.1 = bf16[8,48,1536]{2,1,0:T(8,128)(2,1)} async-done(((bf16[8,48,1536]{2,1,0:T(8,128)(2,1)}), bf16[8,48,1536]{2,1,0:T(8,128)(2,1)}, u32[]{:S(2)}, u32[]{:S(2)}) %all-to-all-start.1) | async-done | bytes 1179680 | tf_op jit(solution)/shard_map/all_to_all | solution.py:26
  115.4 6.1 %all-to-all-start = ((bf16[32,24,1536]{2,1,0:T(8,128)(2,1)}), bf16[32,24,1536]{2,1,0:T(8,128)(2,1)S(1)}, u32[]{:S(2)}, u32[]{:S(2)}) async-start(bf16[32,24,1536]{2,1,0:T(8,128)(2,1)} %broadcast_select_fusion), calls=%async_computation | async-start | bytes 4718592 | tf_op jit(solution)/shard_map/all_to_all | solution.py:47
  121.5 0.0 all-gather.5.cloned.1.call-start
  121.6 0.7 all-gather.5.cloned.1.call-update
  122.3 54.5 %all-to-all-done = bf16[32,24,1536]{2,1,0:T(8,128)(2,1)S(1)} async-done(((bf16[32,24,1536]{2,1,0:T(8,128)(2,1)}), bf16[32,24,1536]{2,1,0:T(8,128)(2,1)S(1)}, u32[]{:S(2)}, u32[]{:S(2)}) %all-to-all-start) | async-done | bytes 2359328 | tf_op jit(solution)/shard_map/all_to_all | solution.py:47
  176.8 3.5 %all-gather.5.cloned.1.call-done = bf16[32,48,1536]{2,1,0:T(8,128)(2,1)} async-done(((bf16[8,48,1536]{2,1,0:T(8,128)(2,1)}), bf16[32,48,1536]{2,1,0:T(8,128)(2,1)}) %all-gather.5.cloned.1.call-update) | async-done | bytes 4718608 | tf_op jit(solution)/shard_map/all_gather | solution.py:27
  180.3 4.5 %fusion = f32[768,1024]{1,0:T(8,128)S(1)} fusion(bf16[768,1536]{1,0:T(8,128)(2,1)S(1)} %bitcast.38, bf16[1536,1536]{1,0:T(8,128)(2,1)} %bitcast.41), kind=kOutput, calls=%fused_computation.6 | convolution fusion | flops 2415919104 | bytes 8650752 | tf_op jit(solution)/shard_map/dot_general | solution.py:49
  184.8 4.3 %convolution_convert_fusion = bf16[768,1536]{1,0:T(8,128)(2,1)} fusion(bf16[1536,1536]{1,0:T(8,128)(2,1)} %bitcast.42, f32[768,1024]{1,0:T(8,128)S(1)} %fusion), kind=kOutput, calls=%fused_computation.5 | convolution fusion | flops 1211498496 | bytes 7077888 | tf_op jit(solution)/shard_map/dot_general | solution.py:53
  189.1 0.0 copy-start.2
  189.1 8.4 %all-to-all-start.2 = ((bf16[32,24,1536]{2,1,0:T(8,128)(2,1)}), bf16[32,24,1536]{2,1,0:T(8,128)(2,1)S(1)}, u32[]{:S(2)}, u32[]{:S(2)}) async-start(bf16[32,24,1536]{2,1,0:T(8,128)(2,1)} %bitcast.37), calls=%async_computation.2 | async-start | bytes 4718592 | tf_op jit(solution)/shard_map/all_to_all | solution.py:57
  197.5 0.2 lt.50
  197.6 0.1 copy.28
  197.7 0.0 copy-done.2
  197.8 0.1 copy.29
  197.9 54.8 %all-to-all-done.2 = bf16[32,24,1536]{2,1,0:T(8,128)(2,1)S(1)} async-done(((bf16[32,24,1536]{2,1,0:T(8,128)(2,1)}), bf16[32,24,1536]{2,1,0:T(8,128)(2,1)S(1)}, u32[]{:S(2)}, u32[]{:S(2)}) %all-to-all-start.2) | async-done | bytes 2359328 | tf_op jit(solution)/shard_map/all_to_all | solution.py:57
  252.7 3.9 %gather_fusion.1 = bf16[768,1536]{1,0:T(8,128)(2,1)} fusion(bf16[768,1536]{1,0:T(8,128)(2,1)S(1)} %bitcast.35, s32[1024]{0:T(1024)S(1)} %pad_clamp_fusion), kind=kCustom, calls=%fused_computation.1 | custom fusion | bytes 4721664 | tf_op jit(solution)/shard_map/gather | solution.py:58
  256.6 5.0 %reshape.192 = f32[128,6,1536]{2,1,0:T(8,128)} reshape(bf16[768,1536]{1,0:T(8,128)(2,1)} %gather_fusion.1) | data formatting | bytes 7077888 | tf_op jit(solution)/shard_map/convert_element_type | solution.py:61
  261.6 5.9 %multiply_reduce_fusion = bf16[128,1536]{1,0:T(8,128)(2,1)} fusion(f32[128,6,1536]{2,1,0:T(8,128)} %reshape.192, f32[128,6]{1,0:T(8,128)S(1)} %copy.29), kind=kLoop, calls=%fused_computation.4 | loop fusion | flops 2162688 | bytes 5114880 | tf_op jit(solution)/shard_map/reduce_sum | solution.py:60
  (14 shorter events, 0.2 us)
Async XLA Ops:
  6.5 90.7 %copy-start = (bf16[128,1536]{1,0:T(8,128)(2,1)S(1)}, bf16[128,1536]{1,0:T(8,128)(2,1)}, u32[]{:S(2)}) copy-start(bf16[128,1536]{1,0:T(8,128)(2,1)} %param.7) | copy-start | bytes 1179652
  6.5 80.3 %copy-start.3 = (s32[128]{0:T(128)S(1)}, s32[128]{0:T(128)}, u32[]{:S(2)}) copy-start(s32[128]{0:T(128)} %param.13) | copy-start | bytes 1540
  6.5 80.7 %copy-start.1 = (s32[128,6]{0,1:T(8,128)S(1)}, s32[128,6]{0,1:T(8,128)}, u32[]{:S(2)}) copy-start(s32[128,6]{0,1:T(8,128)} %param.11) | copy-start | bytes 9220
  6.5 74.2 %all-gather.3.cloned.1.call-start = ((), (), s32[]{:S(2)}) async-start(), calls=%async_computation.3 | async-start | bytes 1474560 | tf_op jit(solution)/shard_map/all_gather | solution.py:23
  80.8 34.7 %all-to-all-start.1 = ((bf16[8,48,1536]{2,1,0:T(8,128)(2,1)}), bf16[8,48,1536]{2,1,0:T(8,128)(2,1)}, u32[]{:S(2)}, u32[]{:S(2)}) async-start(bf16[8,48,1536]{2,1,0:T(8,128)(2,1)} %bitcast.39), calls=%async_computation.1 | async-start | bytes 2359296 | tf_op jit(solution)/shard_map/all_to_all | solution.py:26
  115.4 61.4 %all-to-all-start = ((bf16[32,24,1536]{2,1,0:T(8,128)(2,1)}), bf16[32,24,1536]{2,1,0:T(8,128)(2,1)S(1)}, u32[]{:S(2)}, u32[]{:S(2)}) async-start(bf16[32,24,1536]{2,1,0:T(8,128)(2,1)} %broadcast_select_fusion), calls=%async_computation | async-start | bytes 4718592 | tf_op jit(solution)/shard_map/all_to_all | solution.py:47
  121.5 58.8 %all-gather.5.cloned.1.call-start = ((), (), s32[]{:S(2)}) async-start(), calls=%async_computation.4 | async-start | bytes 5898240 | tf_op jit(solution)/shard_map/all_gather | solution.py:27
  189.1 8.6 %copy-start.2 = (f32[128,6]{0,1:T(8,128)S(1)}, f32[128,6]{0,1:T(8,128)}, u32[]{:S(2)}) copy-start(f32[128,6]{0,1:T(8,128)} %param.12) | copy-start | bytes 9220
  189.1 63.6 %all-to-all-start.2 = ((bf16[32,24,1536]{2,1,0:T(8,128)(2,1)}), bf16[32,24,1536]{2,1,0:T(8,128)(2,1)S(1)}, u32[]{:S(2)}, u32[]{:S(2)}) async-start(bf16[32,24,1536]{2,1,0:T(8,128)(2,1)} %bitcast.37), calls=%async_computation.2 | async-start | bytes 4718592 | tf_op jit(solution)/shard_map/all_to_all | solution.py:57
Sparse Core Ops, SparseCore 0:
  9.5 71.2 all-gather.2
  124.5 55.7 all-gather.4

commit v2 on v1

--- a/solution.py
+++ b/solution.py
@@ -20,15 +20,11 @@
     slab = jnp.concatenate(
         [gate_train, up_train, jnp.swapaxes(down_train, 1, 2)], axis=2
     ).astype(jnp.bfloat16)
+    slab, tokens, routes, route_scores, live = lax.optimization_barrier(
+        (slab, tokens, routes, route_scores, live)
+    )
     slab = lax.all_gather(slab, "zh", axis=0, tiled=False)
     n_pairs, local_experts, rows, width = slab.shape
-    slab = slab.reshape(n_pairs * local_experts, rows, width)
-    slab = lax.all_to_all(slab, ("zl", "c"), split_axis=0, concat_axis=0, tiled=True)
-    slab = lax.all_gather(slab, "y", axis=0, tiled=True)
-    weights = slab.reshape(model_width, width)
-    gate_up_w = weights[:, : 2 * hidden_width]
-    down_t = weights[:, 2 * hidden_width :]
-
     route_share = route_scores / jnp.sum(route_scores, axis=1, keepdims=True)
     flat_route = routes.reshape(-1)
     flat_live = jnp.repeat(live, top_count)
@@ -45,6 +41,13 @@
     filled = jnp.zeros((total_slots,), jnp.int32).at[target].set(1, mode="drop")
     outgoing = jnp.where(filled[:, None] > 0, tokens[source_row], jnp.zeros((), jnp.bfloat16))
     incoming = lax.all_to_all(outgoing, TOKEN_GROUP, split_axis=0, concat_axis=0, tiled=True)
+    incoming, slab = lax.optimization_barrier((incoming, slab))
+    slab = slab.reshape(n_pairs * local_experts, rows, width)
+    slab = lax.all_to_all(slab, ("zl", "c"), split_axis=0, concat_axis=0, tiled=True)
+    slab = lax.all_gather(slab, "y", axis=0, tiled=True)
+    weights = slab.reshape(model_width, width)
+    gate_up_w = weights[:, : 2 * hidden_width]
+    down_t = weights[:, 2 * hidden_width :]
 
     gate_up = jnp.dot(incoming, gate_up_w, preferred_element_type=jnp.float32)
     hidden = (jax.nn.silu(gate_up[:, :hidden_width]) * gate_up[:, hidden_width:]).astype(

time: 275 us -> 319 us (1.16)
  blocking collectives: 0 us -> 33.7 us
  waiting for transfers between devices: 199 us -> 207 us
    all_gather x1, waiting for transfers between devices: 3.48 us -> 59.3 us  [local(): slab = lax.all_gather(slab, 'y', axis=0, tiled=True)]
    all_to_all x0 -> x1, blocking collectives: none -> 33.7 us  [local(): lax.all_to_all(slab, ('zl', 'c'), split_axis=0, concat_axis=0, tiled=True)]
    all_to_all x1, waiting for transfers between devices: 54.5 us -> 26.4 us  [local(): lax.all_to_all(outgoing, TOKEN_GROUP, split_axis=0, concat_axis=0, tiled=...]
    all_to_all x1 -> x0, waiting for transfers between devices: 13.6 us -> none  [local(): lax.all_to_all(slab, ('zl', 'c'), split_axis=0, concat_axis=0, tiled=True)]
    all_to_all x1 -> x0, starting transfers between devices: 6.12 us -> none  [local(): lax.all_to_all(slab, ('zl', 'c'), split_axis=0, concat_axis=0, tiled=True)]
    all_gather x1, waiting for transfers between devices: 71.4 us -> 66.2 us  [local(): slab = lax.all_gather(slab, 'zh', axis=0, tiled=False)]
    all_to_all x1, starting transfers between devices: 6.11 us -> 10.5 us  [local(): lax.all_to_all(outgoing, TOKEN_GROUP, split_axis=0, concat_axis=0, tiled=...]
  transfers between devices with their start and end apart: 5 -> 4, of which waited for: 5 -> 4; matrix products, arithmetic and copies ran while one was open for 6% -> 0% of each run, Pallas kernels for 0% -> 0%
where the time goes in v2:
time: 319 us; the launch traced here: 318 us
  waiting for transfers between devices  207 us (65%)
  blocking collectives  33.7 us (11%)
  local copies, waits for them, and re-layouts  21.1 us (7%)
  starting transfers between devices  19 us (6%)
  other arithmetic  14.5 us (5%)
  between operations  13.6 us (4%)
  matrix products  8.79 us (3%)
    all_gather x1, waiting for transfers between devices, local(): slab = lax.all_gather(slab, 'zh', axis=0, tiled=False)  66.2 us
    all_gather x1, waiting for transfers between devices, local(): slab = lax.all_gather(slab, 'y', axis=0, tiled=True)  59.3 us
    all_to_all x1, waiting for transfers between devices, local(): lax.all_to_all(expert_rows, TOKEN_GROUP, split_axis=0, concat_axis=0, til...  54.8 us
    all_to_all x1, blocking collectives, local(): lax.all_to_all(slab, ('zl', 'c'), split_axis=0, concat_axis=0, tiled=True)  33.7 us
    all_to_all x1, waiting for transfers between devices, local(): lax.all_to_all(outgoing, TOKEN_GROUP, split_axis=0, concat_axis=0, tiled=...  26.4 us
    all_to_all x1, starting transfers between devices, local(): lax.all_to_all(outgoing, TOKEN_GROUP, split_axis=0, concat_axis=0, tiled=...  10.5 us
    all_to_all x1, starting transfers between devices, local(): lax.all_to_all(expert_rows, TOKEN_GROUP, split_axis=0, concat_axis=0, til...  8.37 us
  transfers between devices with their start and end apart: 4, of which 4 were waited for; matrix products, arithmetic and copies ran while one was open for 0% of the time, Pallas kernels for 0%

profile of v2, /device:TPU:1, one launch (start us, length us, event | category | flops | bytes accessed | tf_op | source)
XLA Modules:
  0.0 318.1 jit_solution(8654054208560849699)
XLA Ops:
  6.5 0.0 copy-start
  6.5 1.0 convert.11
  7.5 0.9 convert.12
  8.5 0.9 convert_bitcast_fusion
  9.4 0.7 pad_maximum_fusion
  10.2 0.7 broadcast_compare_fusion.2
  10.8 0.1 broadcast_in_dim.37.clone
  10.9 0.2 gt.41
  11.1 0.1 gt.40
  11.2 0.8 copy.22
  12.0 0.1 eq.29
  12.1 0.1 eq.25
  12.3 0.1 gt.39
  12.4 0.7 broadcast_multiply_fusion
  13.2 1.7 reduce-window.6
  14.9 0.3 slice_reduce_fusion
  15.2 0.1 copy.27
  15.3 0.1 mul.37
  15.5 0.1 fusion.8
  15.6 3.4 %scatter_custom_fusion.1 = s32[768]{0:T(1024)S(1)} fusion(s32[768]{0:T(1024)S(1)} %get-tuple-element.20, s32[768]{0:T(1024)S(1)} %add_select_fusion, s32[]{:T(128)} %constant.11.clone.1), kind=kCustom, calls=%fused_computation.44 | custom fusion | bytes 3076 | tf_op jit(solution)/shard_map/scatter | solution.py:40
  19.0 3.4 %scatter_custom_fusion = s32[768]{0:T(1024)S(1)} fusion(s32[768]{0:T(1024)S(1)} %get-tuple-element.20, s32[768]{0:T(1024)S(1)} %broadcast.166, s32[]{:T(128)} %constant.11.clone.1), kind=kCustom, calls=%fused_computation.47 | custom fusion | bytes 3076 | tf_op jit(solution)/shard_map/scatter | solution.py:41
  22.4 0.1 broadcast_in_dim.40
  22.5 0.0 copy-done
  22.5 2.9 gather_fusion
  25.5 1.6 broadcast_select_fusion
  27.1 10.5 %all-to-all-start = ((bf16[32,24,1536]{2,1,0:T(8,128)(2,1)}), bf16[32,24,1536]{2,1,0:T(8,128)(2,1)S(1)}, u32[]{:S(2)}, u32[]{:S(2)}) async-start(bf16[32,24,1536]{2,1,0:T(8,128)(2,1)} %broadcast_select_fusion), calls=%async_computation | async-start | bytes 4718592 | tf_op jit(solution)/shard_map/all_to_all | solution.py:43
  37.7 0.0 all-gather.6.cloned.1.call-start
  37.7 0.7 all-gather.6.cloned.1.call-update
  38.4 0.0 all-gather.4.cloned.1.call-start
  38.5 66.2 %all-gather.6.cloned.1.call-done = bf16[8,48,1536]{2,1,0:T(8,128)(2,1)} async-done(((bf16[2,48,1536]{2,1,0:T(8,128)(2,1)}), bf16[8,48,1536]{2,1,0:T(8,128)(2,1)}) %all-gather.6.cloned.1.call-update) | async-done | bytes 1179664 | tf_op jit(solution)/shard_map/all_gather | solution.py:26
  104.6 26.4 %all-to-all-done = bf16[32,24,1536]{2,1,0:T(8,128)(2,1)S(1)} async-done(((bf16[32,24,1536]{2,1,0:T(8,128)(2,1)}), bf16[32,24,1536]{2,1,0:T(8,128)(2,1)S(1)}, u32[]{:S(2)}, u32[]{:S(2)}) %all-to-all-start) | async-done | bytes 2359328 | tf_op jit(solution)/shard_map/all_to_all | solution.py:43
  131.0 33.7 %all_to_all.26 = bf16[8,48,1536]{2,1,0:T(8,128)(2,1)} all-to-all(bf16[8,48,1536]{2,1,0:T(8,128)(2,1)} %all-gather.6.cloned.1.call-done), channel_id=1, replica_groups=mesh['y'=4,'zl'=4,'c'=2,'x'=4,'zh'=4] {'zl','c'}, dimensions={0} | all-to-all | bytes 2359296 | tf_op jit(solution)/shard_map/all_to_all | solution.py:46
  164.7 0.0 all-gather.4.cloned.1.call-update
  164.7 59.3 %all-gather.4.cloned.1.call-done = bf16[32,48,1536]{2,1,0:T(8,128)(2,1)} async-done(((bf16[8,48,1536]{2,1,0:T(8,128)(2,1)}), bf16[32,48,1536]{2,1,0:T(8,128)(2,1)}) %all-gather.4.cloned.1.call-update) | async-done | bytes 4718608 | tf_op jit(solution)/shard_map/all_gather | solution.py:47
  224.0 4.5 %fusion = f32[768,1024]{1,0:T(8,128)S(1)} fusion(bf16[768,1536]{1,0:T(8,128)(2,1)S(1)} %bitcast.32, bf16[1536,1536]{1,0:T(8,128)(2,1)} %bitcast.35), kind=kOutput, calls=%fused_computation.6 | convolution fusion | flops 2415919104 | bytes 8650752 | tf_op jit(solution)/shard_map/dot_general | solution.py:52
  228.5 4.3 %convolution_convert_fusion = bf16[768,1536]{1,0:T(8,128)(2,1)} fusion(bf16[1536,1536]{1,0:T(8,128)(2,1)} %bitcast.36, f32[768,1024]{1,0:T(8,128)S(1)} %fusion), kind=kOutput, calls=%fused_computation.5 | convolution fusion | flops 1211498496 | bytes 7077888 | tf_op jit(solution)/shard_map/dot_general | solution.py:56
  232.8 0.0 copy-start.1
  232.8 8.4 %all-to-all-start.2 = ((bf16[32,24,1536]{2,1,0:T(8,128)(2,1)}), bf16[32,24,1536]{2,1,0:T(8,128)(2,1)S(1)}, u32[]{:S(2)}, u32[]{:S(2)}) async-start(bf16[32,24,1536]{2,1,0:T(8,128)(2,1)} %bitcast.33), calls=%async_computation.2 | async-start | bytes 4718592 | tf_op jit(solution)/shard_map/all_to_all | solution.py:60
  241.2 0.2 lt.50
  241.4 0.1 copy.28
  241.4 0.0 copy-done.1
  241.5 0.1 copy.29
  241.6 54.8 %all-to-all-done.2 = bf16[32,24,1536]{2,1,0:T(8,128)(2,1)S(1)} async-done(((bf16[32,24,1536]{2,1,0:T(8,128)(2,1)}), bf16[32,24,1536]{2,1,0:T(8,128)(2,1)S(1)}, u32[]{:S(2)}, u32[]{:S(2)}) %all-to-all-start.2) | async-done | bytes 2359328 | tf_op jit(solution)/shard_map/all_to_all | solution.py:60
  296.5 3.9 %gather_fusion.1 = bf16[768,1536]{1,0:T(8,128)(2,1)} fusion(bf16[768,1536]{1,0:T(8,128)(2,1)S(1)} %bitcast.30, s32[1024]{0:T(1024)S(1)} %pad_clamp_fusion), kind=kCustom, calls=%fused_computation.1 | custom fusion | bytes 4721664 | tf_op jit(solution)/shard_map/gather | solution.py:61
  300.3 5.0 %reshape.147 = f32[128,6,1536]{2,1,0:T(8,128)} reshape(bf16[768,1536]{1,0:T(8,128)(2,1)} %gather_fusion.1) | data formatting | bytes 7077888 | tf_op jit(solution)/shard_map/convert_element_type | solution.py:64
  305.3 5.9 %multiply_reduce_fusion = bf16[128,1536]{1,0:T(8,128)(2,1)} fusion(f32[128,6,1536]{2,1,0:T(8,128)} %reshape.147, f32[128,6]{1,0:T(8,128)S(1)} %copy.29), kind=kLoop, calls=%fused_computation.4 | loop fusion | flops 2162688 | bytes 5114880 | tf_op jit(solution)/shard_map/reduce_sum | solution.py:63
  (12 shorter events, 0.2 us)
Async XLA Ops:
  6.5 16.0 %copy-start = (bf16[128,1536]{1,0:T(8,128)(2,1)S(1)}, bf16[128,1536]{1,0:T(8,128)(2,1)}, u32[]{:S(2)}) copy-start(bf16[128,1536]{1,0:T(8,128)(2,1)} %param.7) | copy-start | bytes 1179652
  27.1 103.9 %all-to-all-start = ((bf16[32,24,1536]{2,1,0:T(8,128)(2,1)}), bf16[32,24,1536]{2,1,0:T(8,128)(2,1)S(1)}, u32[]{:S(2)}, u32[]{:S(2)}) async-start(bf16[32,24,1536]{2,1,0:T(8,128)(2,1)} %broadcast_select_fusion), calls=%async_computation | async-start | bytes 4718592 | tf_op jit(solution)/shard_map/all_to_all | solution.py:43
  37.7 67.0 %all-gather.6.cloned.1.call-start = ((), (), s32[]{:S(2)}) async-start(), calls=%async_computation.4 | async-start | bytes 1474560 | tf_op jit(solution)/shard_map/all_gather | solution.py:26
  38.4 185.6 %all-gather.4.cloned.1.call-start = ((), (), s32[]{:S(2)}) async-start(), calls=%async_computation.3 | async-start | bytes 5898240 | tf_op jit(solution)/shard_map/all_gather | solution.py:47
  232.8 8.6 %copy-start.1 = (f32[128,6]{0,1:T(8,128)S(1)}, f32[128,6]{0,1:T(8,128)}, u32[]{:S(2)}) copy-start(f32[128,6]{0,1:T(8,128)} %param.12) | copy-start | bytes 9220
  232.8 63.6 %all-to-all-start.2 = ((bf16[32,24,1536]{2,1,0:T(8,128)(2,1)}), bf16[32,24,1536]{2,1,0:T(8,128)(2,1)S(1)}, u32[]{:S(2)}, u32[]{:S(2)}) async-start(bf16[32,24,1536]{2,1,0:T(8,128)(2,1)} %bitcast.33), calls=%async_computation.2 | async-start | bytes 4718592 | tf_op jit(solution)/shard_map/all_to_all | solution.py:60
Sparse Core Ops, SparseCore 0:
  40.6 64.0 all-gather.5
  164.9 59.0 all-gather.3

commit v3 on v2

--- a/solution.py
+++ b/solution.py
@@ -6,7 +6,7 @@
 
 AXES = ("y", "zl", "c", "x", "zh")
 ROWS = ("y", "zl", "c", "x", "zh")
-TOKEN_GROUP = ("x", "zl", "c")
+TOKEN_GROUP = ("x", "y", "c")
 
 
 def local(tokens, gate_train, up_train, down_train, routes, route_scores, live):
@@ -43,9 +43,11 @@
     incoming = lax.all_to_all(outgoing, TOKEN_GROUP, split_axis=0, concat_axis=0, tiled=True)
     incoming, slab = lax.optimization_barrier((incoming, slab))
     slab = slab.reshape(n_pairs * local_experts, rows, width)
-    slab = lax.all_to_all(slab, ("zl", "c"), split_axis=0, concat_axis=0, tiled=True)
-    slab = lax.all_gather(slab, "y", axis=0, tiled=True)
-    weights = slab.reshape(model_width, width)
+    slab = lax.all_to_all(slab, ("y", "c"), split_axis=0, concat_axis=0, tiled=True)
+    slab = lax.all_gather(slab, "zl", axis=0, tiled=False)
+    zl_size, y_size = slab.shape[0], slab.shape[1] // local_experts
+    slab = slab.reshape(zl_size, y_size, local_experts, rows, width)
+    weights = jnp.swapaxes(slab, 0, 1).reshape(model_width, width)
     gate_up_w = weights[:, : 2 * hidden_width]
     down_t = weights[:, 2 * hidden_width :]
 

time: 319 us -> 293 us (0.918)
  waiting for transfers between devices: 207 us -> 194 us
  blocking collectives: 33.7 us -> 22.9 us
  matrix products: 8.79 us -> 5.44 us
    all_gather x1, waiting for transfers between devices: 59.3 us -> 91.8 us  [local(): slab = lax.all_gather(slab, 'zl', axis=0, tiled=False)]
    all_to_all x1, waiting for transfers between devices: 26.4 us -> 0.01 us  [local(): lax.all_to_all(outgoing, TOKEN_GROUP, split_axis=0, concat_axis=0, tiled=...]
    all_to_all x1, waiting for transfers between devices: 54.8 us -> 30.7 us  [local(): lax.all_to_all(expert_rows, TOKEN_GROUP, split_axis=0, concat_axis=0, til...]
    all_to_all x1, blocking collectives: 33.7 us -> 22.9 us  [local(): lax.all_to_all(slab, ('y', 'c'), split_axis=0, concat_axis=0, tiled=True)]
    all_gather x1, waiting for transfers between devices: 66.2 us -> 70.2 us  [local(): slab = lax.all_gather(slab, 'zh', axis=0, tiled=False)]
  transfers between devices with their start and end apart: 4 -> 4, of which waited for: 4 -> 3; matrix products, arithmetic and copies ran while one was open for 0% -> 0% of each run, Pallas kernels for 0% -> 0%
where the time goes in v3:
time: 293 us; the launch traced here: 292 us
  waiting for transfers between devices  194 us (66%)
  local copies, waits for them, and re-layouts  23.7 us (8%)
  blocking collectives  22.9 us (8%)
  starting transfers between devices  18.5 us (6%)
  other arithmetic  14.5 us (5%)
  between operations  13.6 us (5%)
  matrix products  5.44 us (2%)
    all_gather x1, waiting for transfers between devices, local(): slab = lax.all_gather(slab, 'zl', axis=0, tiled=False)  91.8 us
    all_gather x1, waiting for transfers between devices, local(): slab = lax.all_gather(slab, 'zh', axis=0, tiled=False)  70.2 us
    all_to_all x1, waiting for transfers between devices, local(): lax.all_to_all(expert_rows, TOKEN_GROUP, split_axis=0, concat_axis=0, til...  30.7 us
    all_to_all x1, blocking collectives, local(): lax.all_to_all(slab, ('y', 'c'), split_axis=0, concat_axis=0, tiled=True)  22.9 us
    all_to_all x1, starting transfers between devices, local(): lax.all_to_all(outgoing, TOKEN_GROUP, split_axis=0, concat_axis=0, tiled=...  10.5 us
    all_to_all x1, starting transfers between devices, local(): lax.all_to_all(expert_rows, TOKEN_GROUP, split_axis=0, concat_axis=0, til...  7.84 us
    reduce_sum x1, other arithmetic, local(): jnp.sum(picked.reshape(tok_dev, top_count, model_width).astype(jnp.float3...  5.92 us
  transfers between devices with their start and end apart: 4, of which 3 were waited for; matrix products, arithmetic and copies ran while one was open for 0% of the time, Pallas kernels for 0%

profile of v3, /device:TPU:1, one launch (start us, length us, event | category | flops | bytes accessed | tf_op | source)
XLA Modules:
  0.0 292.2 jit_solution(10145307854425433517)
XLA Ops:
  6.5 0.0 copy-start
  6.5 1.0 convert.11
  7.5 0.9 convert.12
  8.5 0.9 convert_bitcast_fusion
  9.4 0.7 pad_maximum_fusion
  10.2 0.7 broadcast_compare_fusion.2
  10.8 0.1 broadcast_in_dim.37.clone
  10.9 0.2 gt.41
  11.1 0.1 gt.40
  11.2 0.8 copy.30
  12.0 0.1 eq.29
  12.1 0.1 eq.25
  12.3 0.1 gt.39
  12.4 0.7 broadcast_multiply_fusion
  13.2 1.7 reduce-window.6
  14.9 0.3 slice_reduce_fusion
  15.2 0.1 copy.35
  15.3 0.1 mul.37
  15.5 0.1 fusion.8
  15.6 3.4 %scatter_custom_fusion.1 = s32[768]{0:T(1024)S(1)} fusion(s32[768]{0:T(1024)S(1)} %get-tuple-element.20, s32[768]{0:T(1024)S(1)} %add_select_fusion, s32[]{:T(128)} %constant.11.clone.1), kind=kCustom, calls=%fused_computation.44 | custom fusion | bytes 3076 | tf_op jit(solution)/shard_map/scatter | solution.py:40
  19.0 3.4 %scatter_custom_fusion = s32[768]{0:T(1024)S(1)} fusion(s32[768]{0:T(1024)S(1)} %get-tuple-element.20, s32[768]{0:T(1024)S(1)} %broadcast.166, s32[]{:T(128)} %constant.11.clone.1), kind=kCustom, calls=%fused_computation.47 | custom fusion | bytes 3076 | tf_op jit(solution)/shard_map/scatter | solution.py:41
  22.4 0.1 broadcast_in_dim.40
  22.5 0.0 copy-done
  22.5 2.9 %gather_fusion = bf16[768,1536]{1,0:T(8,128)(2,1)S(1)} fusion(bf16[128,1536]{1,0:T(8,128)(2,1)S(1)} %copy-done, s32[1024]{0:T(1024)S(1)} %pad_clamp_fusion.1), kind=kCustom, calls=%fused_computation | custom fusion | bytes 4721664 | tf_op jit(solution)/shard_map/gather | solution.py:42
  25.5 1.6 broadcast_select_fusion
  27.1 10.5 %all-to-all-start = ((bf16[32,24,1536]{2,1,0:T(8,128)(2,1)}), bf16[32,24,1536]{2,1,0:T(8,128)(2,1)S(1)}, u32[]{:S(2)}, u32[]{:S(2)}) async-start(bf16[32,24,1536]{2,1,0:T(8,128)(2,1)} %broadcast_select_fusion), calls=%async_computation | async-start | bytes 4718592 | tf_op jit(solution)/shard_map/all_to_all | solution.py:43
  37.7 0.0 all-gather.5.cloned.1.call-start
  37.7 0.7 all-gather.5.cloned.1.call-update
  38.4 0.0 all-gather.7.cloned.1.call-start
  38.5 70.2 %all-gather.5.cloned.1.call-done = bf16[8,48,1536]{2,1,0:T(8,128)(2,1)} async-done(((bf16[2,48,1536]{2,1,0:T(8,128)(2,1)}), bf16[8,48,1536]{2,1,0:T(8,128)(2,1)}) %all-gather.5.cloned.1.call-update) | async-done | bytes 1179664 | tf_op jit(solution)/shard_map/all_gather | solution.py:26
  108.7 0.0 all-to-all-done
  108.7 22.9 %all_to_all.26 = bf16[8,48,1536]{2,1,0:T(8,128)(2,1)} all-to-all(bf16[8,48,1536]{2,1,0:T(8,128)(2,1)} %all-gather.5.cloned.1.call-done), channel_id=1, replica_groups=mesh['y'=4,'zl'=4,'c'=2,'x'=4,'zh'=4] {'y','c'}, dimensions={0} | all-to-all | bytes 2359296 | tf_op jit(solution)/shard_map/all_to_all | solution.py:46
  131.6 0.0 all-gather.7.cloned.1.call-update
  131.6 91.8 %all-gather.7.cloned.1.call-done = bf16[32,48,1536]{2,1,0:T(8,128)(2,1)} async-done(((bf16[8,48,1536]{2,1,0:T(8,128)(2,1)}), bf16[32,48,1536]{2,1,0:T(8,128)(2,1)}) %all-gather.7.cloned.1.call-update) | async-done | bytes 4718608 | tf_op jit(solution)/shard_map/all_gather | solution.py:47
  223.5 2.6 copy.36
  226.1 2.6 fusion
  228.7 2.9 convolution_convert_fusion
  231.5 0.0 copy-start.1
  231.5 7.8 %all-to-all-start.2 = ((bf16[32,24,1536]{2,1,0:T(8,128)(2,1)}), bf16[32,24,1536]{2,1,0:T(8,128)(2,1)S(1)}, u32[]{:S(2)}, u32[]{:S(2)}) async-start(bf16[32,24,1536]{2,1,0:T(8,128)(2,1)} %bitcast.39), calls=%async_computation.2 | async-start | bytes 4718592 | tf_op jit(solution)/shard_map/all_to_all | solution.py:62
  239.4 0.2 lt.50
  239.6 0.1 copy.37
  239.6 0.0 copy-done.1
  239.7 0.1 copy.38
  239.8 30.7 %all-to-all-done.2 = bf16[32,24,1536]{2,1,0:T(8,128)(2,1)S(1)} async-done(((bf16[32,24,1536]{2,1,0:T(8,128)(2,1)}), bf16[32,24,1536]{2,1,0:T(8,128)(2,1)S(1)}, u32[]{:S(2)}, u32[]{:S(2)}) %all-to-all-start.2) | async-done | bytes 2359328 | tf_op jit(solution)/shard_map/all_to_all | solution.py:62
  270.6 3.9 %gather_fusion.1 = bf16[768,1536]{1,0:T(8,128)(2,1)} fusion(bf16[768,1536]{1,0:T(8,128)(2,1)S(1)} %bitcast.33, s32[1024]{0:T(1024)S(1)} %pad_clamp_fusion), kind=kCustom, calls=%fused_computation.1 | custom fusion | bytes 4721664 | tf_op jit(solution)/shard_map/gather | solution.py:63
  274.4 5.0 %reshape.151 = f32[128,6,1536]{2,1,0:T(8,128)} reshape(bf16[768,1536]{1,0:T(8,128)(2,1)} %gather_fusion.1) | data formatting | bytes 7077888 | tf_op jit(solution)/shard_map/convert_element_type | solution.py:66
  279.4 5.9 %multiply_reduce_fusion = bf16[128,1536]{1,0:T(8,128)(2,1)} fusion(f32[128,6,1536]{2,1,0:T(8,128)} %reshape.151, f32[128,6]{1,0:T(8,128)S(1)} %copy.38), kind=kLoop, calls=%fused_computation.4 | loop fusion | flops 2162688 | bytes 5114880 | tf_op jit(solution)/shard_map/reduce_sum | solution.py:65
  (12 shorter events, 0.2 us)
Async XLA Ops:
  6.5 16.0 %copy-start = (bf16[128,1536]{1,0:T(8,128)(2,1)S(1)}, bf16[128,1536]{1,0:T(8,128)(2,1)}, u32[]{:S(2)}) copy-start(bf16[128,1536]{1,0:T(8,128)(2,1)} %param.7) | copy-start | bytes 1179652
  27.1 81.6 %all-to-all-start = ((bf16[32,24,1536]{2,1,0:T(8,128)(2,1)}), bf16[32,24,1536]{2,1,0:T(8,128)(2,1)S(1)}, u32[]{:S(2)}, u32[]{:S(2)}) async-start(bf16[32,24,1536]{2,1,0:T(8,128)(2,1)} %broadcast_select_fusion), calls=%async_computation | async-start | bytes 4718592 | tf_op jit(solution)/shard_map/all_to_all | solution.py:43
  37.7 71.0 %all-gather.5.cloned.1.call-start = ((), (), s32[]{:S(2)}) async-start(), calls=%async_computation.3 | async-start | bytes 1474560 | tf_op jit(solution)/shard_map/all_gather | solution.py:26
  38.4 185.0 %all-gather.7.cloned.1.call-start = ((), (), s32[]{:S(2)}) async-start(), calls=%async_computation.4 | async-start | bytes 5898240 | tf_op jit(solution)/shard_map/all_gather | solution.py:47
  231.5 8.1 %copy-start.1 = (f32[128,6]{0,1:T(8,128)S(1)}, f32[128,6]{0,1:T(8,128)}, u32[]{:S(2)}) copy-start(f32[128,6]{0,1:T(8,128)} %param.12) | copy-start | bytes 9220
  231.5 39.0 %all-to-all-start.2 = ((bf16[32,24,1536]{2,1,0:T(8,128)(2,1)}), bf16[32,24,1536]{2,1,0:T(8,128)(2,1)S(1)}, u32[]{:S(2)}, u32[]{:S(2)}) async-start(bf16[32,24,1536]{2,1,0:T(8,128)(2,1)} %bitcast.39), calls=%async_computation.2 | async-start | bytes 4718592 | tf_op jit(solution)/shard_map/all_to_all | solution.py:62
Sparse Core Ops, SparseCore 0:
  40.6 68.0 all-gather.4
  131.7 91.6 all-gather.6

commit v4 on v1

--- a/solution.py
+++ b/solution.py
@@ -40,10 +40,10 @@
     slot_index = jnp.sum(earlier * onehot, axis=1)
     kept_mask = (flat_live > 0) & (slot_index < capacity)
     target = jnp.where(kept_mask, flat_route * capacity + slot_index, total_slots)
-    anchor = jnp.arange(tok_dev * top_count, dtype=jnp.int32) // top_count
-    source_row = jnp.zeros((total_slots,), jnp.int32).at[target].set(anchor, mode="drop")
-    filled = jnp.zeros((total_slots,), jnp.int32).at[target].set(1, mode="drop")
-    outgoing = jnp.where(filled[:, None] > 0, tokens[source_row], jnp.zeros((), jnp.bfloat16))
+    slot_ids = jnp.arange(total_slots, dtype=jnp.int32)
+    picks = target.reshape(tok_dev, top_count)[None, :, :] == slot_ids[:, None, None]
+    dispatch = jnp.any(picks, axis=2).astype(jnp.bfloat16)
+    outgoing = jnp.dot(dispatch, tokens, preferred_element_type=jnp.float32).astype(jnp.bfloat16)
     incoming = lax.all_to_all(outgoing, TOKEN_GROUP, split_axis=0, concat_axis=0, tiled=True)
 
     gate_up = jnp.dot(incoming, gate_up_w, preferred_element_type=jnp.float32)
@@ -55,12 +55,12 @@
     )
     expert_rows = expert_out.astype(jnp.bfloat16)
     returned = lax.all_to_all(expert_rows, TOKEN_GROUP, split_axis=0, concat_axis=0, tiled=True)
-    picked = returned[jnp.minimum(target, total_slots - 1)]
-    weight = jnp.where(kept_mask, route_share.reshape(-1), 0.0)
-    combined = jnp.sum(
-        picked.reshape(tok_dev, top_count, model_width).astype(jnp.float32)
-        * weight.reshape(tok_dev, top_count, 1),
-        axis=1,
+    weight = jnp.where(kept_mask, route_share.reshape(-1), 0.0).reshape(tok_dev, top_count)
+    combine = jnp.sum(jnp.where(jnp.swapaxes(picks, 0, 1), weight[:, None, :], 0.0), axis=2)
+    combine_hi = combine.astype(jnp.bfloat16)
+    combine_lo = (combine - combine_hi.astype(jnp.float32)).astype(jnp.bfloat16)
+    combined = jnp.dot(combine_hi, returned, preferred_element_type=jnp.float32) + jnp.dot(
+        combine_lo, returned, preferred_element_type=jnp.float32
     )
     return combined.astype(jnp.bfloat16)
 

time: 275 us -> 263 us (0.956)
  local copies, waits for them, and re-layouts: 20.4 us -> 2.22 us
  waiting for transfers between devices: 199 us -> 208 us
  other arithmetic: 12.4 us -> 5.42 us
  matrix products: 8.8 us -> 13.4 us
    all_to_all x1, waiting for transfers between devices: 13.6 us -> 22.6 us  [local(): lax.all_to_all(slab, ('zl', 'c'), split_axis=0, concat_axis=0, tiled=True)]
    gather x2 -> x0, local copies, waits for them, and re-layouts: 6.79 us -> none  [the longest x1 3.86 us: local(): picked = returned[jnp.minimum(target, total_slots - 1)]]
    scatter x2 -> x0, local copies, waits for them, and re-layouts: 6.76 us -> none  [the longest x1 3.38 us: local(): jnp.zeros((total_slots,), jnp.int32).at[target].set(anchor, mode='drop')]
    reduce_sum x1, other arithmetic: 5.92 us -> 0.29 us  [local(): jnp.sum(jnp.where(jnp.swapaxes(picks, 0, 1), weight[:, None, :], 0.0), ax...]
    convert_element_type x1 -> x0, local copies, waits for them, and re-layouts: 4.98 us -> none  [local(): picked.reshape(tok_dev, top_count, model_width).astype(jnp.float32)]
    dot_general x0 -> x3, matrix products: none -> 3.95 us  [the longest x1 2.21 us: local(): jnp.dot(dispatch, tokens, preferred_element_type=jnp.float32)]
  transfers between devices with their start and end apart: 5 -> 5, of which waited for: 5 -> 5; matrix products, arithmetic and copies ran while one was open for 6% -> 2% of each run, Pallas kernels for 0% -> 0%
where the time goes in v4:
time: 263 us; the launch traced here: 262 us
  waiting for transfers between devices  208 us (79%)
  starting transfers between devices  20 us (8%)
  between operations  13.6 us (5%)
  matrix products  13.4 us (5%)
  other arithmetic  5.42 us (2%)
    all_gather x1, waiting for transfers between devices, local(): slab = lax.all_gather(slab, 'zh', axis=0, tiled=False)  71.4 us
    all_to_all x1, waiting for transfers between devices, local(): lax.all_to_all(expert_rows, TOKEN_GROUP, split_axis=0, concat_axis=0, til...  54.9 us
    all_to_all x1, waiting for transfers between devices, local(): lax.all_to_all(outgoing, TOKEN_GROUP, split_axis=0, concat_axis=0, tiled=...  54.6 us
    all_to_all x1, waiting for transfers between devices, local(): lax.all_to_all(slab, ('zl', 'c'), split_axis=0, concat_axis=0, tiled=True)  22.6 us
    all_to_all x1, starting transfers between devices, local(): lax.all_to_all(expert_rows, TOKEN_GROUP, split_axis=0, concat_axis=0, til...  8.36 us
    all_to_all x1, starting transfers between devices, local(): lax.all_to_all(outgoing, TOKEN_GROUP, split_axis=0, concat_axis=0, tiled=...  6.16 us
    all_to_all x1, starting transfers between devices, local(): lax.all_to_all(slab, ('zl', 'c'), split_axis=0, concat_axis=0, tiled=True)  5.45 us
  transfers between devices with their start and end apart: 5, of which 5 were waited for; matrix products, arithmetic and copies ran while one was open for 2% of the time, Pallas kernels for 0%

profile of v4, /device:TPU:1, one launch (start us, length us, event | category | flops | bytes accessed | tf_op | source)
XLA Modules:
  0.0 262.3 jit_solution(163866045161609495)
XLA Ops:
  6.5 0.0 copy-start
  6.5 0.0 copy-start.2
  6.5 0.0 copy-start.4
  6.5 0.0 all-gather.3.cloned.1.call-start
  6.5 1.0 convert_bitcast_fusion
  7.5 1.0 convert_bitcast_fusion.1
  8.6 0.7 pad_maximum_fusion
  9.3 0.0 all-gather.3.cloned.1.call-update
  9.4 71.4 %all-gather.3.cloned.1.call-done = bf16[4,2,48,1536]{3,2,1,0:T(8,128)(2,1)} async-done(((bf16[1,2,48,1536]{3,2,1,0:T(8,128)(2,1)}), bf16[4,2,48,1536]{3,2,1,0:T(8,128)(2,1)}) %all-gather.3.cloned.1.call-update) | async-done | bytes 1179664 | tf_op jit(solution)/shard_map/all_gather | solution.py:23
  80.8 5.5 %all-to-all-start.1 = ((bf16[8,48,1536]{2,1,0:T(8,128)(2,1)}), bf16[8,48,1536]{2,1,0:T(8,128)(2,1)S(1)}, u32[]{:S(2)}, u32[]{:S(2)}) async-start(bf16[8,48,1536]{2,1,0:T(8,128)(2,1)} %bitcast.42), calls=%async_computation.1 | async-start | bytes 2359296 | tf_op jit(solution)/shard_map/all_to_all | solution.py:26
  86.2 0.0 copy-done.2
  86.2 0.1 copy.35
  86.3 0.1 eq.45
  86.5 0.1 eq.49
  86.6 0.0 copy-done.4
  86.6 0.1 broadcast_in_dim.26.clone
  86.7 0.2 gt.28
  86.9 0.1 gt.29
  87.0 1.7 reduce-window.6
  88.8 0.3 slice_reduce_fusion
  89.1 0.1 fusion.10
  89.2 0.1 reduce_sum.30
  89.3 0.1 copy.40
  89.4 0.4 fusion.3
  89.8 0.0 copy-done
  89.8 2.2 convolution_convert_fusion.1
  92.0 22.6 %all-to-all-done.1 = bf16[8,48,1536]{2,1,0:T(8,128)(2,1)S(1)} async-done(((bf16[8,48,1536]{2,1,0:T(8,128)(2,1)}), bf16[8,48,1536]{2,1,0:T(8,128)(2,1)S(1)}, u32[]{:S(2)}, u32[]{:S(2)}) %all-to-all-start.1) | async-done | bytes 1179680 | tf_op jit(solution)/shard_map/all_to_all | solution.py:26
  114.6 0.0 copy-start.1
  114.6 1.0 copy-done.1
  115.6 6.2 %all-to-all-start = ((bf16[32,24,1536]{2,1,0:T(8,128)(2,1)}), bf16[32,24,1536]{2,1,0:T(8,128)(2,1)}, u32[]{:S(2)}, u32[]{:S(2)}) async-start(bf16[32,24,1536]{2,1,0:T(8,128)(2,1)} %bitcast.1), calls=%async_computation | async-start | bytes 4718592 | tf_op jit(solution)/shard_map/all_to_all | solution.py:47
  121.8 0.0 all-gather.5.cloned.1.call-start
  121.9 0.7 all-gather.5.cloned.1.call-update
  122.6 54.6 %all-to-all-done = bf16[32,24,1536]{2,1,0:T(8,128)(2,1)} async-done(((bf16[32,24,1536]{2,1,0:T(8,128)(2,1)}), bf16[32,24,1536]{2,1,0:T(8,128)(2,1)}, u32[]{:S(2)}, u32[]{:S(2)}) %all-to-all-start) | async-done | bytes 2359328 | tf_op jit(solution)/shard_map/all_to_all | solution.py:47
  177.1 3.4 %all-gather.5.cloned.1.call-done = bf16[32,48,1536]{2,1,0:T(8,128)(2,1)} async-done(((bf16[8,48,1536]{2,1,0:T(8,128)(2,1)}), bf16[32,48,1536]{2,1,0:T(8,128)(2,1)}) %all-gather.5.cloned.1.call-update) | async-done | bytes 4718608 | tf_op jit(solution)/shard_map/all_gather | solution.py:27
  180.6 5.2 %fusion = f32[768,1024]{1,0:T(8,128)S(1)} fusion(bf16[768,1536]{1,0:T(8,128)(2,1)} %bitcast.2, bf16[1536,1536]{1,0:T(8,128)(2,1)} %bitcast.44), kind=kOutput, calls=%fused_computation.2 | convolution fusion | flops 2415919104 | bytes 8650752 | tf_op jit(solution)/shard_map/dot_general | solution.py:49
  185.8 4.3 %convolution_convert_fusion = bf16[768,1536]{1,0:T(8,128)(2,1)} fusion(bf16[1536,1536]{1,0:T(8,128)(2,1)} %bitcast.45, f32[768,1024]{1,0:T(8,128)S(1)} %fusion), kind=kOutput, calls=%fused_computation | convolution fusion | flops 1211498496 | bytes 7077888 | tf_op jit(solution)/shard_map/dot_general | solution.py:53
  190.0 0.0 copy-start.3
  190.1 8.4 %all-to-all-start.2 = ((bf16[32,24,1536]{2,1,0:T(8,128)(2,1)}), bf16[32,24,1536]{2,1,0:T(8,128)(2,1)S(1)}, u32[]{:S(2)}, u32[]{:S(2)}) async-start(bf16[32,24,1536]{2,1,0:T(8,128)(2,1)} %bitcast.41), calls=%async_computation.2 | async-start | bytes 4718592 | tf_op jit(solution)/shard_map/all_to_all | solution.py:57
  198.4 0.0 copy-done.3
  198.5 0.3 select_reduce_fusion
  198.8 54.9 %all-to-all-done.2 = bf16[32,24,1536]{2,1,0:T(8,128)(2,1)S(1)} async-done(((bf16[32,24,1536]{2,1,0:T(8,128)(2,1)}), bf16[32,24,1536]{2,1,0:T(8,128)(2,1)S(1)}, u32[]{:S(2)}, u32[]{:S(2)}) %all-to-all-start.2) | async-done | bytes 2359328 | tf_op jit(solution)/shard_map/all_to_all | solution.py:57
  253.7 0.5 fusion.12
  254.2 1.3 fusion.2
  (6 shorter events, 0.1 us)
Async XLA Ops:
  6.5 83.3 %copy-start = (bf16[128,1536]{1,0:T(8,128)(2,1)S(1)}, bf16[128,1536]{1,0:T(8,128)(2,1)}, u32[]{:S(2)}) copy-start(bf16[128,1536]{1,0:T(8,128)(2,1)} %param.7) | copy-start | bytes 1179652
  6.5 79.7 %copy-start.2 = (s32[128,6]{0,1:T(8,128)S(1)}, s32[128,6]{0,1:T(8,128)}, u32[]{:S(2)}) copy-start(s32[128,6]{0,1:T(8,128)} %param.11) | copy-start | bytes 9220
  6.5 80.1 %copy-start.4 = (s32[128]{0:T(128)S(1)}, s32[128]{0:T(128)}, u32[]{:S(2)}) copy-start(s32[128]{0:T(128)} %param.13) | copy-start | bytes 1540
  6.5 74.2 %all-gather.3.cloned.1.call-start = ((), (), s32[]{:S(2)}) async-start(), calls=%async_computation.3 | async-start | bytes 1474560 | tf_op jit(solution)/shard_map/all_gather | solution.py:23
  80.8 33.9 %all-to-all-start.1 = ((bf16[8,48,1536]{2,1,0:T(8,128)(2,1)}), bf16[8,48,1536]{2,1,0:T(8,128)(2,1)S(1)}, u32[]{:S(2)}, u32[]{:S(2)}) async-start(bf16[8,48,1536]{2,1,0:T(8,128)(2,1)} %bitcast.42), calls=%async_computation.1 | async-start | bytes 2359296 | tf_op jit(solution)/shard_map/all_to_all | solution.py:26
  114.6 1.0 copy-start.1
  115.6 61.5 %all-to-all-start = ((bf16[32,24,1536]{2,1,0:T(8,128)(2,1)}), bf16[32,24,1536]{2,1,0:T(8,128)(2,1)}, u32[]{:S(2)}, u32[]{:S(2)}) async-start(bf16[32,24,1536]{2,1,0:T(8,128)(2,1)} %bitcast.1), calls=%async_computation | async-start | bytes 4718592 | tf_op jit(solution)/shard_map/all_to_all | solution.py:47
  121.8 58.8 %all-gather.5.cloned.1.call-start = ((), (), s32[]{:S(2)}) async-start(), calls=%async_computation.4 | async-start | bytes 5898240 | tf_op jit(solution)/shard_map/all_gather | solution.py:27
  190.0 8.4 %copy-start.3 = (f32[128,6]{0,1:T(8,128)S(1)}, f32[128,6]{0,1:T(8,128)}, u32[]{:S(2)}) copy-start(f32[128,6]{0,1:T(8,128)} %param.12) | copy-start | bytes 9220
  190.1 63.6 %all-to-all-start.2 = ((bf16[32,24,1536]{2,1,0:T(8,128)(2,1)}), bf16[32,24,1536]{2,1,0:T(8,128)(2,1)S(1)}, u32[]{:S(2)}, u32[]{:S(2)}) async-start(bf16[32,24,1536]{2,1,0:T(8,128)(2,1)} %bitcast.41), calls=%async_computation.2 | async-start | bytes 4718592 | tf_op jit(solution)/shard_map/all_to_all | solution.py:57
Sparse Core Ops, SparseCore 0:
  9.5 71.2 all-gather.2
  124.7 55.7 all-gather.4

commit v5 on v4

--- a/solution.py
+++ b/solution.py
@@ -20,10 +20,25 @@
     slab = jnp.concatenate(
         [gate_train, up_train, jnp.swapaxes(down_train, 1, 2)], axis=2
     ).astype(jnp.bfloat16)
-    slab = lax.all_gather(slab, "zh", axis=0, tiled=False)
-    n_pairs, local_experts, rows, width = slab.shape
-    slab = slab.reshape(n_pairs * local_experts, rows, width)
-    slab = lax.all_to_all(slab, ("zl", "c"), split_axis=0, concat_axis=0, tiled=True)
+    width = slab.shape[-1]
+    zl_size, core_size, zh_size = (lax.axis_size(n) for n in ("zl", "c", "zh"))
+    zl_at, core_at, zh_at = (lax.axis_index(n) for n in ("zl", "c", "zh"))
+    flat = lambda zl, c, zh: (zl * core_size + c) * zh_size + zh
+    received, places = [], []
+    for p in range(zl_size):
+        for q in range(core_size):
+            perm = [
+                (flat(j, c, a), flat(a, c ^ q, (j + p) % zh_size))
+                for j in range(zl_size)
+                for c in range(core_size)
+                for a in range(zh_size)
+            ]
+            piece = jnp.where(core_at == 0, slab[q], slab[1 - q]) if core_size == 2 else slab[q]
+            received.append(lax.ppermute(piece, ("zl", "c", "zh"), perm))
+            places.append(((zh_at - p) % zl_size) * core_size + (core_at ^ q))
+    received = jnp.stack(received)
+    order = jnp.argsort(jnp.stack(places))
+    slab = jnp.take(received, order, axis=0)
     slab = lax.all_gather(slab, "y", axis=0, tiled=True)
     weights = slab.reshape(model_width, width)
     gate_up_w = weights[:, : 2 * hidden_width]
@@ -57,8 +72,9 @@
     returned = lax.all_to_all(expert_rows, TOKEN_GROUP, split_axis=0, concat_axis=0, tiled=True)
     weight = jnp.where(kept_mask, route_share.reshape(-1), 0.0).reshape(tok_dev, top_count)
     combine = jnp.sum(jnp.where(jnp.swapaxes(picks, 0, 1), weight[:, None, :], 0.0), axis=2)
-    combine_hi = combine.astype(jnp.bfloat16)
-    combine_lo = (combine - combine_hi.astype(jnp.float32)).astype(jnp.bfloat16)
+    combine_hi = lax.reduce_precision(combine, exponent_bits=8, mantissa_bits=7)
+    combine_lo = (combine - combine_hi).astype(jnp.bfloat16)
+    combine_hi = combine_hi.astype(jnp.bfloat16)
     combined = jnp.dot(combine_hi, returned, preferred_element_type=jnp.float32) + jnp.dot(
         combine_lo, returned, preferred_element_type=jnp.float32
     )

time: 263 us -> 290 us (1.10)
  starting transfers between devices: 20 us -> 69.1 us
  waiting for transfers between devices: 208 us -> 183 us
    all_gather x1 -> x0, waiting for transfers between devices: 71.4 us -> none  [local(): slab = lax.all_gather(slab, 'zh', axis=0, tiled=False)]
    all_gather x1, waiting for transfers between devices: 3.43 us -> 67.3 us  [local(): slab = lax.all_gather(slab, 'y', axis=0, tiled=True)]
    ppermute x0 -> x8, waiting for transfers between devices: none -> 60.7 us  [local(): received.append(lax.ppermute(piece, ('zl', 'c', 'zh'), perm))]
    ppermute x0 -> x8, starting transfers between devices: none -> 54.8 us  [local(): received.append(lax.ppermute(piece, ('zl', 'c', 'zh'), perm))]
    all_to_all x1, waiting for transfers between devices: 54.6 us -> 0.01 us  [local(): lax.all_to_all(outgoing, TOKEN_GROUP, split_axis=0, concat_axis=0, tiled=...]
    all_to_all x1 -> x0, waiting for transfers between devices: 22.6 us -> none  [local(): lax.all_to_all(slab, ('zl', 'c'), split_axis=0, concat_axis=0, tiled=True)]
    all_to_all x1 -> x0, starting transfers between devices: 5.45 us -> none  [local(): lax.all_to_all(slab, ('zl', 'c'), split_axis=0, concat_axis=0, tiled=True)]
  transfers between devices with their start and end apart: 5 -> 11, of which waited for: 5 -> 3; matrix products, arithmetic and copies ran while one was open for 2% -> 3% of each run, Pallas kernels for 0% -> 0%
where the time goes in v5:
time: 290 us; the launch traced here: 289 us
  waiting for transfers between devices  183 us (63%)
  starting transfers between devices  69.1 us (24%)
  between operations  13.8 us (5%)
  matrix products  13.5 us (5%)
  other arithmetic  7.73 us (3%)
    all_gather x1, waiting for transfers between devices, local(): slab = lax.all_gather(slab, 'y', axis=0, tiled=True)  67.3 us
    ppermute x8, waiting for transfers between devices, local(): received.append(lax.ppermute(piece, ('zl', 'c', 'zh'), perm))  60.7 us
    all_to_all x1, waiting for transfers between devices, local(): lax.all_to_all(expert_rows, TOKEN_GROUP, split_axis=0, concat_axis=0, til...  54.9 us
    ppermute x8, starting transfers between devices, local(): received.append(lax.ppermute(piece, ('zl', 'c', 'zh'), perm))  54.8 us
    all_to_all x1, starting transfers between devices, local(): lax.all_to_all(expert_rows, TOKEN_GROUP, split_axis=0, concat_axis=0, til...  8.36 us
    all_to_all x1, starting transfers between devices, local(): lax.all_to_all(outgoing, TOKEN_GROUP, split_axis=0, concat_axis=0, tiled=...  5.93 us
  transfers between devices with their start and end apart: 11, of which 3 were waited for; matrix products, arithmetic and copies ran while one was open for 3% of the time, Pallas kernels for 0%

profile of v5, /device:TPU:1, one launch (start us, length us, event | category | flops | bytes accessed | tf_op | source)
XLA Modules:
  0.0 289.1 jit_solution(10798443850770452981)
XLA Ops:
  6.5 0.0 copy-start
  6.5 0.0 copy-start.3
  6.5 0.0 copy-start.1
  6.5 1.0 convert.10
  7.5 0.9 convert.11
  8.5 0.9 convert_bitcast_fusion
  9.5 0.7 collective-permute-start
  10.2 10.9 %collective-permute-start.2 = (bf16[48,1536]{1,0:T(8,128)(2,1)S(1)}, bf16[48,1536]{1,0:T(8,128)(2,1)S(1)}, u32[]{:S(2)}, u32[]{:S(2)}) collective-permute-start(bf16[48,1536]{1,0:T(8,128)(2,1)S(1)} %get-tuple-element.8), channel_id=1, source_target_pairs={{0,1},{1,33},{2,65},{3,97},{16,17},{17,49},{18,81},{19,113},{32,2}... | collective-permute-start | bytes 442376 | tf_op jit(solution)/shard_map/ppermute | solution.py:37
  21.1 2.9 collective-permute-start.1
  23.9 12.3 %collective-permute-start.3 = (bf16[48,1536]{1,0:T(8,128)(2,1)S(1)}, bf16[48,1536]{1,0:T(8,128)(2,1)S(1)}, u32[]{:S(2)}, u32[]{:S(2)}) collective-permute-start(bf16[48,1536]{1,0:T(8,128)(2,1)S(1)} %get-tuple-element.7), channel_id=1, source_target_pairs={{0,17},{1,49},{2,81},{3,113},{16,1},{17,33},{18,65},{19,97},{32,18... | collective-permute-start | bytes 442376 | tf_op jit(solution)/shard_map/ppermute | solution.py:37
  36.3 7.4 %collective-permute-start.4 = (bf16[48,1536]{1,0:T(8,128)(2,1)S(1)}, bf16[48,1536]{1,0:T(8,128)(2,1)S(1)}, u32[]{:S(2)}, u32[]{:S(2)}) collective-permute-start(bf16[48,1536]{1,0:T(8,128)(2,1)S(1)} %get-tuple-element.8), channel_id=1, source_target_pairs={{0,2},{1,34},{2,66},{3,98},{16,18},{17,50},{18,82},{19,114},{32,3}... | collective-permute-start | bytes 442376 | tf_op jit(solution)/shard_map/ppermute | solution.py:37
  43.7 0.0 copy-done.3
  43.7 0.1 broadcast_in_dim.38.clone
  43.8 0.2 gt.29
  43.9 0.1 gt.28
  44.1 0.0 copy-done.1
  44.1 0.1 copy.35
  44.2 0.1 eq.68
  44.4 0.1 eq.64
  44.5 1.7 reduce-window.6
  46.3 0.3 slice_reduce_fusion
  46.5 0.1 fusion.13
  46.7 0.1 reduce_sum.30
  46.8 0.1 copy.40
  46.9 0.4 fusion.3
  47.3 0.0 copy-done
  47.3 2.2 convolution_convert_fusion.1
  49.5 5.9 %all-to-all-start = ((bf16[32,24,1536]{2,1,0:T(8,128)(2,1)}), bf16[32,24,1536]{2,1,0:T(8,128)(2,1)}, u32[]{:S(2)}, u32[]{:S(2)}) async-start(bf16[32,24,1536]{2,1,0:T(8,128)(2,1)} %bitcast.1), calls=%async_computation | async-start | bytes 4718592 | tf_op jit(solution)/shard_map/all_to_all | solution.py:62
  55.5 0.0 all-gather.2.cloned.1.call-start
  55.6 0.1 stack.62
  55.7 1.0 sort.17
  56.7 0.0 collective-permute-done
  56.7 9.0 %collective-permute-start.5 = (bf16[48,1536]{1,0:T(8,128)(2,1)S(1)}, bf16[48,1536]{1,0:T(8,128)(2,1)S(1)}, u32[]{:S(2)}, u32[]{:S(2)}) collective-permute-start(bf16[48,1536]{1,0:T(8,128)(2,1)S(1)} %get-tuple-element.7), channel_id=1, source_target_pairs={{0,18},{1,50},{2,82},{3,114},{16,2},{17,34},{18,66},{19,98},{32,19... | collective-permute-start | bytes 442376 | tf_op jit(solution)/shard_map/ppermute | solution.py:37
  65.7 0.0 collective-permute-done.1
  65.7 2.5 collective-permute-start.6
  68.2 0.0 collective-permute-done.2
  68.2 9.2 %collective-permute-start.7 = (bf16[48,1536]{1,0:T(8,128)(2,1)S(1)}, bf16[48,1536]{1,0:T(8,128)(2,1)S(1)}, u32[]{:S(2)}, u32[]{:S(2)}) collective-permute-start(bf16[48,1536]{1,0:T(8,128)(2,1)S(1)} %get-tuple-element.7), channel_id=1, source_target_pairs={{0,19},{1,51},{2,83},{3,115},{16,3},{17,35},{18,67},{19,99},{32,16... | collective-permute-start | bytes 442376 | tf_op jit(solution)/shard_map/ppermute | solution.py:37
  77.5 0.0 collective-permute-done.3
  77.5 0.0 collective-permute-done.4
  77.5 60.7 %collective-permute-done.5 = bf16[48,1536]{1,0:T(8,128)(2,1)S(1)} collective-permute-done((bf16[48,1536]{1,0:T(8,128)(2,1)S(1)}, bf16[48,1536]{1,0:T(8,128)(2,1)S(1)}, u32[]{:S(2)}, u32[]{:S(2)}) %collective-permute-start.5) | collective-permute-done | bytes 147488 | tf_op jit(solution)/shard_map/ppermute | solution.py:37
  138.2 0.0 collective-permute-done.6
  138.2 0.0 collective-permute-done.7
  138.3 0.6 gather_fusion
  138.9 1.2 broadcast_select_fusion
  140.1 0.0 all-gather.2.cloned.1.call-update
  140.1 67.3 %all-gather.2.cloned.1.call-done = bf16[32,48,1536]{2,1,0:T(8,128)(2,1)} async-done(((bf16[8,48,1536]{2,1,0:T(8,128)(2,1)}), bf16[32,48,1536]{2,1,0:T(8,128)(2,1)}) %all-gather.2.cloned.1.call-update) | async-done | bytes 4718608 | tf_op jit(solution)/shard_map/all_gather | solution.py:42
  207.4 0.0 all-to-all-done
  207.4 5.2 %fusion = f32[768,1024]{1,0:T(8,128)S(1)} fusion(bf16[768,1536]{1,0:T(8,128)(2,1)} %bitcast.2, bf16[1536,1536]{1,0:T(8,128)(2,1)} %bitcast.64), kind=kOutput, calls=%fused_computation.3 | convolution fusion | flops 2415919104 | bytes 8650752 | tf_op jit(solution)/shard_map/dot_general | solution.py:64
  212.6 4.3 %convolution_convert_fusion = bf16[768,1536]{1,0:T(8,128)(2,1)} fusion(bf16[1536,1536]{1,0:T(8,128)(2,1)} %bitcast.65, f32[768,1024]{1,0:T(8,128)S(1)} %fusion), kind=kOutput, calls=%fused_computation.1 | convolution fusion | flops 1211498496 | bytes 7077888 | tf_op jit(solution)/shard_map/dot_general | solution.py:68
  216.9 0.0 copy-start.2
  216.9 8.4 %all-to-all-start.1 = ((bf16[32,24,1536]{2,1,0:T(8,128)(2,1)}), bf16[32,24,1536]{2,1,0:T(8,128)(2,1)S(1)}, u32[]{:S(2)}, u32[]{:S(2)}) async-start(bf16[32,24,1536]{2,1,0:T(8,128)(2,1)} %bitcast.62), calls=%async_computation.1 | async-start | bytes 4718592 | tf_op jit(solution)/shard_map/all_to_all | solution.py:72
  225.3 0.0 copy-done.2
  225.3 0.3 select_reduce_fusion
  225.6 54.9 %all-to-all-done.1 = bf16[32,24,1536]{2,1,0:T(8,128)(2,1)S(1)} async-done(((bf16[32,24,1536]{2,1,0:T(8,128)(2,1)}), bf16[32,24,1536]{2,1,0:T(8,128)(2,1)S(1)}, u32[]{:S(2)}, u32[]{:S(2)}) %all-to-all-start.1) | async-done | bytes 2359328 | tf_op jit(solution)/shard_map/all_to_all | solution.py:72
  280.6 0.5 fusion.10
  281.0 1.2 fusion.2
  (20 shorter events, 0.2 us)
Async XLA Ops:
  6.5 40.8 %copy-start = (bf16[128,1536]{1,0:T(8,128)(2,1)S(1)}, bf16[128,1536]{1,0:T(8,128)(2,1)}, u32[]{:S(2)}) copy-start(bf16[128,1536]{1,0:T(8,128)(2,1)} %param.7) | copy-start | bytes 1179652
  6.5 37.1 %copy-start.3 = (s32[128]{0:T(128)S(1)}, s32[128]{0:T(128)}, u32[]{:S(2)}) copy-start(s32[128]{0:T(128)} %param.13) | copy-start | bytes 1540
  6.5 37.5 %copy-start.1 = (s32[128,6]{0,1:T(8,128)S(1)}, s32[128,6]{0,1:T(8,128)}, u32[]{:S(2)}) copy-start(s32[128,6]{0,1:T(8,128)} %param.11) | copy-start | bytes 9220
  9.5 47.2 %collective-permute-start = (bf16[48,1536]{1,0:T(8,128)(2,1)S(1)}, bf16[48,1536]{1,0:T(8,128)(2,1)S(1)}, u32[]{:S(2)}, u32[]{:S(2)}) collective-permute-start(bf16[48,1536]{1,0:T(8,128)(2,1)S(1)} %get-tuple-element.8), channel_id=1, source_target_pairs={{0,0},{1,32},{2,64},{3,96},{16,16},{17,48},{18,80},{19,112},{32,1}... | collective-permute-start | bytes 442376 | tf_op jit(solution)/shard_map/ppermute | solution.py:37
  10.2 58.0 %collective-permute-start.2 = (bf16[48,1536]{1,0:T(8,128)(2,1)S(1)}, bf16[48,1536]{1,0:T(8,128)(2,1)S(1)}, u32[]{:S(2)}, u32[]{:S(2)}) collective-permute-start(bf16[48,1536]{1,0:T(8,128)(2,1)S(1)} %get-tuple-element.8), channel_id=1, source_target_pairs={{0,1},{1,33},{2,65},{3,97},{16,17},{17,49},{18,81},{19,113},{32,2}... | collective-permute-start | bytes 442376 | tf_op jit(solution)/shard_map/ppermute | solution.py:37
  21.1 44.6 %collective-permute-start.1 = (bf16[48,1536]{1,0:T(8,128)(2,1)S(1)}, bf16[48,1536]{1,0:T(8,128)(2,1)S(1)}, u32[]{:S(2)}, u32[]{:S(2)}) collective-permute-start(bf16[48,1536]{1,0:T(8,128)(2,1)S(1)} %get-tuple-element.7), channel_id=1, source_target_pairs={{0,16},{1,48},{2,80},{3,112},{16,0},{17,32},{18,64},{19,96},{32,17... | collective-permute-start | bytes 442376 | tf_op jit(solution)/shard_map/ppermute | solution.py:37
  23.9 53.5 %collective-permute-start.3 = (bf16[48,1536]{1,0:T(8,128)(2,1)S(1)}, bf16[48,1536]{1,0:T(8,128)(2,1)S(1)}, u32[]{:S(2)}, u32[]{:S(2)}) collective-permute-start(bf16[48,1536]{1,0:T(8,128)(2,1)S(1)} %get-tuple-element.7), channel_id=1, source_target_pairs={{0,17},{1,49},{2,81},{3,113},{16,1},{17,33},{18,65},{19,97},{32,18... | collective-permute-start | bytes 442376 | tf_op jit(solution)/shard_map/ppermute | solution.py:37
  36.3 41.2 %collective-permute-start.4 = (bf16[48,1536]{1,0:T(8,128)(2,1)S(1)}, bf16[48,1536]{1,0:T(8,128)(2,1)S(1)}, u32[]{:S(2)}, u32[]{:S(2)}) collective-permute-start(bf16[48,1536]{1,0:T(8,128)(2,1)S(1)} %get-tuple-element.8), channel_id=1, source_target_pairs={{0,2},{1,34},{2,66},{3,98},{16,18},{17,50},{18,82},{19,114},{32,3}... | collective-permute-start | bytes 442376 | tf_op jit(solution)/shard_map/ppermute | solution.py:37
  49.5 157.9 %all-to-all-start = ((bf16[32,24,1536]{2,1,0:T(8,128)(2,1)}), bf16[32,24,1536]{2,1,0:T(8,128)(2,1)}, u32[]{:S(2)}, u32[]{:S(2)}) async-start(bf16[32,24,1536]{2,1,0:T(8,128)(2,1)} %bitcast.1), calls=%async_computation | async-start | bytes 4718592 | tf_op jit(solution)/shard_map/all_to_all | solution.py:62
  55.5 151.9 %all-gather.2.cloned.1.call-start = ((), (), s32[]{:S(2)}) async-start(), calls=%async_computation.2 | async-start | bytes 5898240 | tf_op jit(solution)/shard_map/all_gather | solution.py:42
  56.7 81.5 %collective-permute-start.5 = (bf16[48,1536]{1,0:T(8,128)(2,1)S(1)}, bf16[48,1536]{1,0:T(8,128)(2,1)S(1)}, u32[]{:S(2)}, u32[]{:S(2)}) collective-permute-start(bf16[48,1536]{1,0:T(8,128)(2,1)S(1)} %get-tuple-element.7), channel_id=1, source_target_pairs={{0,18},{1,50},{2,82},{3,114},{16,2},{17,34},{18,66},{19,98},{32,19... | collective-permute-start | bytes 442376 | tf_op jit(solution)/shard_map/ppermute | solution.py:37
  65.7 72.5 %collective-permute-start.6 = (bf16[48,1536]{1,0:T(8,128)(2,1)S(1)}, bf16[48,1536]{1,0:T(8,128)(2,1)S(1)}, u32[]{:S(2)}, u32[]{:S(2)}) collective-permute-start(bf16[48,1536]{1,0:T(8,128)(2,1)S(1)} %get-tuple-element.8), channel_id=1, source_target_pairs={{0,3},{1,35},{2,67},{3,99},{16,19},{17,51},{18,83},{19,115},{32,0}... | collective-permute-start | bytes 442376 | tf_op jit(solution)/shard_map/ppermute | solution.py:37
  68.2 70.0 %collective-permute-start.7 = (bf16[48,1536]{1,0:T(8,128)(2,1)S(1)}, bf16[48,1536]{1,0:T(8,128)(2,1)S(1)}, u32[]{:S(2)}, u32[]{:S(2)}) collective-permute-start(bf16[48,1536]{1,0:T(8,128)(2,1)S(1)} %get-tuple-element.7), channel_id=1, source_target_pairs={{0,19},{1,51},{2,83},{3,115},{16,3},{17,35},{18,67},{19,99},{32,16... | collective-permute-start | bytes 442376 | tf_op jit(solution)/shard_map/ppermute | solution.py:37
  216.9 8.4 %copy-start.2 = (f32[128,6]{0,1:T(8,128)S(1)}, f32[128,6]{0,1:T(8,128)}, u32[]{:S(2)}) copy-start(f32[128,6]{0,1:T(8,128)} %param.12) | copy-start | bytes 9220
  216.9 63.6 %all-to-all-start.1 = ((bf16[32,24,1536]{2,1,0:T(8,128)(2,1)}), bf16[32,24,1536]{2,1,0:T(8,128)(2,1)S(1)}, u32[]{:S(2)}, u32[]{:S(2)}) async-start(bf16[32,24,1536]{2,1,0:T(8,128)(2,1)} %bitcast.62), calls=%async_computation.1 | async-start | bytes 4718592 | tf_op jit(solution)/shard_map/all_to_all | solution.py:72
Sparse Core Ops, SparseCore 0:
  140.2 67.1 all-gather.1

commit v6 on v4

--- a/solution.py
+++ b/solution.py
@@ -6,7 +6,7 @@
 
 AXES = ("y", "zl", "c", "x", "zh")
 ROWS = ("y", "zl", "c", "x", "zh")
-TOKEN_GROUP = ("x", "zl", "c")
+TOKEN_GROUP = ("x", "y", "c")
 
 
 def local(tokens, gate_train, up_train, down_train, routes, route_scores, live):
@@ -20,15 +20,11 @@
     slab = jnp.concatenate(
         [gate_train, up_train, jnp.swapaxes(down_train, 1, 2)], axis=2
     ).astype(jnp.bfloat16)
+    slab, tokens, routes, route_scores, live = lax.optimization_barrier(
+        (slab, tokens, routes, route_scores, live)
+    )
     slab = lax.all_gather(slab, "zh", axis=0, tiled=False)
     n_pairs, local_experts, rows, width = slab.shape
-    slab = slab.reshape(n_pairs * local_experts, rows, width)
-    slab = lax.all_to_all(slab, ("zl", "c"), split_axis=0, concat_axis=0, tiled=True)
-    slab = lax.all_gather(slab, "y", axis=0, tiled=True)
-    weights = slab.reshape(model_width, width)
-    gate_up_w = weights[:, : 2 * hidden_width]
-    down_t = weights[:, 2 * hidden_width :]
-
     route_share = route_scores / jnp.sum(route_scores, axis=1, keepdims=True)
     flat_route = routes.reshape(-1)
     flat_live = jnp.repeat(live, top_count)
@@ -45,6 +41,29 @@
     dispatch = jnp.any(picks, axis=2).astype(jnp.bfloat16)
     outgoing = jnp.dot(dispatch, tokens, preferred_element_type=jnp.float32).astype(jnp.bfloat16)
     incoming = lax.all_to_all(outgoing, TOKEN_GROUP, split_axis=0, concat_axis=0, tiled=True)
+    incoming, slab = lax.optimization_barrier((incoming, slab))
+    slab = slab.reshape(n_pairs * local_experts, rows, width)
+    slab = lax.all_to_all(slab, ("y", "c"), split_axis=0, concat_axis=0, tiled=True)
+    zl_size, zh_size = lax.axis_size("zl"), lax.axis_size("zh")
+    ring = zl_size * zh_size
+    index = lambda z: (z % zl_size) * zh_size + z // zl_size
+    pairs = lambda k: [(index(z), index((z + k) % ring)) for z in range(ring)]
+    shift = lambda v, k: lax.ppermute(v, ("zl", "zh"), pairs(k))
+    half = slab.shape[0] // 2
+    quarters = [
+        slab,
+        shift(slab, 1),
+        shift(slab, -1),
+        jnp.concatenate([shift(slab[:half], 2), shift(slab[half:], -2)]),
+    ]
+    zl_at = lax.axis_index("zl")
+    places = jnp.stack([zl_at, zl_at - 1, zl_at + 1, zl_at + 2]) % zl_size
+    slab = jnp.take(jnp.stack(quarters), jnp.argsort(places), axis=0)
+    y_size = slab.shape[1] // local_experts
+    slab = slab.reshape(zl_size, y_size, local_experts, rows, width)
+    weights = jnp.swapaxes(slab, 0, 1).reshape(model_width, width)
+    gate_up_w = weights[:, : 2 * hidden_width]
+    down_t = weights[:, 2 * hidden_width :]
 
     gate_up = jnp.dot(incoming, gate_up_w, preferred_element_type=jnp.float32)
     hidden = (jax.nn.silu(gate_up[:, :hidden_width]) * gate_up[:, hidden_width:]).astype(
@@ -57,8 +76,9 @@
     returned = lax.all_to_all(expert_rows, TOKEN_GROUP, split_axis=0, concat_axis=0, tiled=True)
     weight = jnp.where(kept_mask, route_share.reshape(-1), 0.0).reshape(tok_dev, top_count)
     combine = jnp.sum(jnp.where(jnp.swapaxes(picks, 0, 1), weight[:, None, :], 0.0), axis=2)
-    combine_hi = combine.astype(jnp.bfloat16)
-    combine_lo = (combine - combine_hi.astype(jnp.float32)).astype(jnp.bfloat16)
+    combine_hi = lax.reduce_precision(combine, exponent_bits=8, mantissa_bits=7)
+    combine_lo = (combine - combine_hi).astype(jnp.bfloat16)
+    combine_hi = combine_hi.astype(jnp.bfloat16)
     combined = jnp.dot(combine_hi, returned, preferred_element_type=jnp.float32) + jnp.dot(
         combine_lo, returned, preferred_element_type=jnp.float32
     )

time: 263 us -> 247 us (0.939)
  waiting for transfers between devices: 208 us -> 153 us
  starting transfers between devices: 20 us -> 43.3 us
  other arithmetic: 5.42 us -> 15.3 us
  local copies, waits for them, and re-layouts: 2.22 us -> 11.4 us
  matrix products: 13.4 us -> 9.33 us
    all_to_all x1, waiting for transfers between devices: 54.6 us -> 0.01 us  [local(): lax.all_to_all(outgoing, TOKEN_GROUP, split_axis=0, concat_axis=0, tiled=...]
    ppermute x0 -> x4, waiting for transfers between devices: none -> 34.7 us  [local(): shift = lambda v, k: lax.ppermute(v, ('zl', 'zh'), pairs(k))]
    all_to_all x1, waiting for transfers between devices: 54.9 us -> 30.8 us  [local(): lax.all_to_all(expert_rows, TOKEN_GROUP, split_axis=0, concat_axis=0, til...]
    ppermute x0 -> x4, starting transfers between devices: none -> 13.9 us  [local(): shift = lambda v, k: lax.ppermute(v, ('zl', 'zh'), pairs(k))]
    another operation x2 -> x6, other arithmetic: 1.77 us -> 8.37 us  [the longest x2 4.65 us: local(): slab = jnp.take(jnp.stack(quarters), jnp.argsort(places), axis=0)]
    all_to_all x1, waiting for transfers between devices: 22.6 us -> 16.4 us  [local(): lax.all_to_all(slab, ('y', 'c'), split_axis=0, concat_axis=0, tiled=True)]
    gather x0 -> x1, local copies, waits for them, and re-layouts: none -> 5.35 us  [local(): slab = jnp.take(jnp.stack(quarters), jnp.argsort(places), axis=0)]
    all_to_all x1, starting transfers between devices: 6.16 us -> 10.5 us  [local(): lax.all_to_all(outgoing, TOKEN_GROUP, split_axis=0, concat_axis=0, tiled=...]
  transfers between devices with their start and end apart: 5 -> 8, of which waited for: 5 -> 4; matrix products, arithmetic and copies ran while one was open for 2% -> 1% of each run, Pallas kernels for 0% -> 0%
where the time goes in v6:
time: 247 us; the launch traced here: 246 us
  waiting for transfers between devices  153 us (62%)
  starting transfers between devices  43.3 us (18%)
  other arithmetic  15.3 us (6%)
  between operations  13.6 us (6%)
  local copies, waits for them, and re-layouts  11.4 us (5%)
  matrix products  9.33 us (4%)
    all_gather x1, waiting for transfers between devices, local(): slab = lax.all_gather(slab, 'zh', axis=0, tiled=False)  70.3 us
    ppermute x4, waiting for transfers between devices, local(): shift = lambda v, k: lax.ppermute(v, ('zl', 'zh'), pairs(k))  34.7 us
    all_to_all x1, waiting for transfers between devices, local(): lax.all_to_all(expert_rows, TOKEN_GROUP, split_axis=0, concat_axis=0, til...  30.8 us
    all_to_all x1, waiting for transfers between devices, local(): lax.all_to_all(slab, ('y', 'c'), split_axis=0, concat_axis=0, tiled=True)  16.4 us
    ppermute x4, starting transfers between devices, local(): shift = lambda v, k: lax.ppermute(v, ('zl', 'zh'), pairs(k))  13.9 us
    all_to_all x1, starting transfers between devices, local(): lax.all_to_all(expert_rows, TOKEN_GROUP, split_axis=0, concat_axis=0, til...  12.6 us
    all_to_all x1, starting transfers between devices, local(): lax.all_to_all(outgoing, TOKEN_GROUP, split_axis=0, concat_axis=0, tiled=...  10.5 us
    all_to_all x1, starting transfers between devices, local(): lax.all_to_all(slab, ('y', 'c'), split_axis=0, concat_axis=0, tiled=True)  6.27 us
  transfers between devices with their start and end apart: 8, of which 4 were waited for; matrix products, arithmetic and copies ran while one was open for 1% of the time, Pallas kernels for 0%

profile of v6, /device:TPU:1, one launch (start us, length us, event | category | flops | bytes accessed | tf_op | source)
XLA Modules:
  0.0 245.9 jit_solution(13409074018316531386)
XLA Ops:
  6.5 0.0 copy-start
  6.5 0.0 copy-start.3
  6.5 1.0 convert.10
  7.5 0.9 convert.11
  8.5 0.9 convert_bitcast_fusion
  9.4 0.7 pad_maximum_fusion.1
  10.2 0.7 broadcast_compare_fusion
  10.8 0.1 broadcast_in_dim.38.clone
  10.9 0.2 gt.29
  11.1 0.1 gt.28
  11.2 0.8 copy.45
  12.0 0.1 eq.51
  12.2 0.1 eq.47
  12.3 1.7 reduce-window.6
  14.1 0.3 slice_reduce_fusion
  14.4 0.1 fusion.13
  14.5 0.1 reduce_sum.30
  14.6 0.1 copy.50
  14.7 0.0 copy-done.3
  14.7 0.4 fusion.3
  15.1 0.0 copy-done
  15.1 2.2 convolution_convert_fusion.1
  17.3 10.5 %all-to-all-start = ((bf16[32,24,1536]{2,1,0:T(8,128)(2,1)}), bf16[32,24,1536]{2,1,0:T(8,128)(2,1)S(1)}, u32[]{:S(2)}, u32[]{:S(2)}) async-start(bf16[32,24,1536]{2,1,0:T(8,128)(2,1)} %bitcast.2), calls=%async_computation | async-start | bytes 4718592 | tf_op jit(solution)/shard_map/all_to_all | solution.py:43
  27.9 0.0 all-gather.3.cloned.1.call-start
  27.9 0.7 all-gather.3.cloned.1.call-update
  28.6 70.3 %all-gather.3.cloned.1.call-done = bf16[8,48,1536]{2,1,0:T(8,128)(2,1)} async-done(((bf16[2,48,1536]{2,1,0:T(8,128)(2,1)}), bf16[8,48,1536]{2,1,0:T(8,128)(2,1)}) %all-gather.3.cloned.1.call-update) | async-done | bytes 1179664 | tf_op jit(solution)/shard_map/all_gather | solution.py:26
  98.9 0.0 all-to-all-done
  98.9 0.0 copy-start.1
  98.9 1.4 copy-done.1
  100.3 6.3 %all-to-all-start.1 = ((bf16[8,48,1536]{2,1,0:T(8,128)(2,1)}), bf16[8,48,1536]{2,1,0:T(8,128)(2,1)S(1)}, u32[]{:S(2)}, u32[]{:S(2)}) async-start(bf16[8,48,1536]{2,1,0:T(8,128)(2,1)} %all-gather.3.cloned.1.call-done), calls=%async_computation.1 | async-start | bytes 2359296 | tf_op jit(solution)/shard_map/all_to_all | solution.py:46
  106.5 16.4 %all-to-all-done.1 = bf16[8,48,1536]{2,1,0:T(8,128)(2,1)S(1)} async-done(((bf16[8,48,1536]{2,1,0:T(8,128)(2,1)}), bf16[8,48,1536]{2,1,0:T(8,128)(2,1)S(1)}, u32[]{:S(2)}, u32[]{:S(2)}) %all-to-all-start.1) | async-done | bytes 1179680 | tf_op jit(solution)/shard_map/all_to_all | solution.py:46
  122.9 1.9 collective-permute-start
  124.8 4.6 %collective-permute-start.1 = (bf16[8,48,1536]{2,1,0:T(8,128)(2,1)S(1)}, bf16[8,48,1536]{2,1,0:T(8,128)(2,1)}, u32[]{:S(2)}, u32[]{:S(2)}) collective-permute-start(bf16[8,48,1536]{2,1,0:T(8,128)(2,1)S(1)} %all-to-all-done.1), channel_id=1, source_target_pairs={{0,99},{32,0},{64,32},{96,64},{1,96},{33,1},{65,33},{97,65},{2,97}... | collective-permute-start | bytes 3538952 | tf_op jit(solution)/shard_map/ppermute | solution.py:51
  129.4 1.1 fusion.19
  130.5 1.9 collective-permute-start.2
  132.4 5.5 %collective-permute-start.3 = (bf16[4,48,1536]{2,1,0:T(8,128)(2,1)}, bf16[4,48,1536]{2,1,0:T(8,128)(2,1)}, u32[]{:S(2)}, u32[]{:S(2)}) collective-permute-start(bf16[4,48,1536]{2,1,0:T(8,128)(2,1)} %get-tuple-element.22), channel_id=1, source_target_pairs={{0,67},{32,99},{64,0},{96,32},{1,64},{33,96},{65,1},{97,33},{2,65}... | collective-permute-start | bytes 1769480 | tf_op jit(solution)/shard_map/ppermute | solution.py:51
  137.9 0.1 and_select_fusion
  138.0 0.7 sort.17
  138.8 34.7 %collective-permute-done.2 = bf16[4,48,1536]{2,1,0:T(8,128)(2,1)S(1)} collective-permute-done((bf16[4,48,1536]{2,1,0:T(8,128)(2,1)}, bf16[4,48,1536]{2,1,0:T(8,128)(2,1)S(1)}, u32[]{:S(2)}, u32[]{:S(2)}) %collective-permute-start.2) | collective-permute-done | bytes 589856 | tf_op jit(solution)/shard_map/ppermute | solution.py:51
  173.5 0.0 collective-permute-done.3
  173.5 1.2 maximum_bitcast_fusion
  174.7 0.0 collective-permute-done
  174.7 0.0 collective-permute-done.1
  174.7 3.5 %pad_maximum_fusion = bf16[4,8,48,1536]{3,2,1,0:T(8,128)(2,1)} fusion(bf16[1,8,48,1536]{3,2,1,0:T(8,128)(2,1)S(1)} %maximum_bitcast_fusion, bf16[1,8,48,1536]{3,2,1,0:T(8,128)(2,1)} %bitcast.12, bf16[1,8,48,1536]{3,2,1,0:T(8,128)(2,1)S(1)} %bitcast.54, bf16[1,8,48,1536]{3,2,1,0:T(8,128)(2,1)S(1)} %bitcast.49), kind=kLoop, calls=%fused_computation.1 | loop fusion | flops 7077888 | bytes 9437184 | tf_op jit(solution)/shard_map/stack | solution.py:61
  178.2 5.4 %gather_fusion = bf16[4,8,48,1536]{3,2,1,0:T(8,128)(2,1)} fusion(bf16[4,8,48,1536]{3,2,1,0:T(8,128)(2,1)} %pad_maximum_fusion, s32[1024]{0:T(1024)S(1)} %pad_clamp_fusion), kind=kCustom, calls=%fused_computation | custom fusion | bytes 9437200 | tf_op jit(solution)/shard_map/jit(_take)/gather | solution.py:61
  183.5 2.9 %select_bitcast_fusion = bf16[4,4,2,48,1536]{4,3,2,0,1:T(8,128)(2,1)S(1)} fusion(bf16[4,4,2,48,1536]{4,3,2,1,0:T(8,128)(2,1)} %bitcast.48, pred[4]{0:T(512)(128)(4,1)S(1)} %compare_and_fusion.1), kind=kLoop, calls=%fused_computation.2 | loop fusion | flops 2359296 | bytes 9437188 | tf_op jit(solution)/shard_map/transpose | solution.py:64
  186.4 0.0 copy-start.2
  186.4 0.5 copy.52
  186.9 1.2 copy-done.2
  188.1 2.6 %fusion = f32[768,1024]{1,0:T(8,128)S(1)} fusion(bf16[768,1536]{1,0:T(8,128)(2,1)S(1)} %bitcast.52, bf16[1536,1536]{1,0:T(8,128)(2,1)S(1)} %bitcast.50), kind=kOutput, calls=%fused_computation.5 | convolution fusion | flops 2415919104 | bytes 8650752 | tf_op jit(solution)/shard_map/dot_general | solution.py:68
  190.7 2.9 %convolution_convert_fusion = bf16[768,1536]{1,0:T(8,128)(2,1)} fusion(bf16[1536,1536]{1,0:T(8,128)(2,1)S(1)} %bitcast.51, f32[768,1024]{1,0:T(8,128)S(1)} %fusion), kind=kOutput, calls=%fused_computation.3 | convolution fusion | flops 1211498496 | bytes 7077888 | tf_op jit(solution)/shard_map/dot_general | solution.py:72
  193.5 0.0 copy-start.4
  193.5 12.6 %all-to-all-start.2 = ((bf16[32,24,1536]{2,1,0:T(8,128)(2,1)}), bf16[32,24,1536]{2,1,0:T(8,128)(2,1)S(1)}, u32[]{:S(2)}, u32[]{:S(2)}) async-start(bf16[32,24,1536]{2,1,0:T(8,128)(2,1)} %bitcast.53), calls=%async_computation.2 | async-start | bytes 4718592 | tf_op jit(solution)/shard_map/all_to_all | solution.py:76
  206.1 0.0 copy-done.4
  206.2 0.3 select_reduce_fusion
  206.5 30.8 %all-to-all-done.2 = bf16[32,24,1536]{2,1,0:T(8,128)(2,1)S(1)} async-done(((bf16[32,24,1536]{2,1,0:T(8,128)(2,1)}), bf16[32,24,1536]{2,1,0:T(8,128)(2,1)S(1)}, u32[]{:S(2)}, u32[]{:S(2)}) %all-to-all-start.2) | async-done | bytes 2359328 | tf_op jit(solution)/shard_map/all_to_all | solution.py:76
  237.3 0.5 fusion.10
  237.8 1.2 fusion.2
  (9 shorter events, 0.1 us)
Async XLA Ops:
  6.5 8.6 %copy-start = (bf16[128,1536]{1,0:T(8,128)(2,1)S(1)}, bf16[128,1536]{1,0:T(8,128)(2,1)}, u32[]{:S(2)}) copy-start(bf16[128,1536]{1,0:T(8,128)(2,1)} %param.7) | copy-start | bytes 1179652
  6.5 8.1 %copy-start.3 = (s32[128,6]{0,1:T(8,128)S(1)}, s32[128,6]{0,1:T(8,128)}, u32[]{:S(2)}) copy-start(s32[128,6]{0,1:T(8,128)} %param.11) | copy-start | bytes 9220
  17.3 81.6 %all-to-all-start = ((bf16[32,24,1536]{2,1,0:T(8,128)(2,1)}), bf16[32,24,1536]{2,1,0:T(8,128)(2,1)S(1)}, u32[]{:S(2)}, u32[]{:S(2)}) async-start(bf16[32,24,1536]{2,1,0:T(8,128)(2,1)} %bitcast.2), calls=%async_computation | async-start | bytes 4718592 | tf_op jit(solution)/shard_map/all_to_all | solution.py:43
  27.9 71.0 %all-gather.3.cloned.1.call-start = ((), (), s32[]{:S(2)}) async-start(), calls=%async_computation.3 | async-start | bytes 1474560 | tf_op jit(solution)/shard_map/all_gather | solution.py:26
  98.9 1.4 copy-start.1
  100.3 22.6 %all-to-all-start.1 = ((bf16[8,48,1536]{2,1,0:T(8,128)(2,1)}), bf16[8,48,1536]{2,1,0:T(8,128)(2,1)S(1)}, u32[]{:S(2)}, u32[]{:S(2)}) async-start(bf16[8,48,1536]{2,1,0:T(8,128)(2,1)} %all-gather.3.cloned.1.call-done), calls=%async_computation.1 | async-start | bytes 2359296 | tf_op jit(solution)/shard_map/all_to_all | solution.py:46
  122.9 51.8 %collective-permute-start = (bf16[8,48,1536]{2,1,0:T(8,128)(2,1)S(1)}, bf16[8,48,1536]{2,1,0:T(8,128)(2,1)S(1)}, u32[]{:S(2)}, u32[]{:S(2)}) collective-permute-start(bf16[8,48,1536]{2,1,0:T(8,128)(2,1)S(1)} %all-to-all-done.1), channel_id=1, source_target_pairs={{0,32},{32,64},{64,96},{96,1},{1,33},{33,65},{65,97},{97,2},{2,34}... | collective-permute-start | bytes 3538952 | tf_op jit(solution)/shard_map/ppermute | solution.py:51
  124.8 49.9 %collective-permute-start.1 = (bf16[8,48,1536]{2,1,0:T(8,128)(2,1)S(1)}, bf16[8,48,1536]{2,1,0:T(8,128)(2,1)}, u32[]{:S(2)}, u32[]{:S(2)}) collective-permute-start(bf16[8,48,1536]{2,1,0:T(8,128)(2,1)S(1)} %all-to-all-done.1), channel_id=1, source_target_pairs={{0,99},{32,0},{64,32},{96,64},{1,96},{33,1},{65,33},{97,65},{2,97}... | collective-permute-start | bytes 3538952 | tf_op jit(solution)/shard_map/ppermute | solution.py:51
  130.5 43.0 %collective-permute-start.2 = (bf16[4,48,1536]{2,1,0:T(8,128)(2,1)}, bf16[4,48,1536]{2,1,0:T(8,128)(2,1)S(1)}, u32[]{:S(2)}, u32[]{:S(2)}) collective-permute-start(bf16[4,48,1536]{2,1,0:T(8,128)(2,1)} %get-tuple-element.21), channel_id=1, source_target_pairs={{0,64},{32,96},{64,1},{96,33},{1,65},{33,97},{65,2},{97,34},{2,66}... | collective-permute-start | bytes 1769480 | tf_op jit(solution)/shard_map/ppermute | solution.py:51
  132.4 41.1 %collective-permute-start.3 = (bf16[4,48,1536]{2,1,0:T(8,128)(2,1)}, bf16[4,48,1536]{2,1,0:T(8,128)(2,1)}, u32[]{:S(2)}, u32[]{:S(2)}) collective-permute-start(bf16[4,48,1536]{2,1,0:T(8,128)(2,1)} %get-tuple-element.22), channel_id=1, source_target_pairs={{0,67},{32,99},{64,0},{96,32},{1,64},{33,96},{65,1},{97,33},{2,65}... | collective-permute-start | bytes 1769480 | tf_op jit(solution)/shard_map/ppermute | solution.py:51
  186.4 1.7 copy-start.2
  193.5 12.6 %copy-start.4 = (f32[128,6]{0,1:T(8,128)S(1)}, f32[128,6]{0,1:T(8,128)}, u32[]{:S(2)}) copy-start(f32[128,6]{0,1:T(8,128)} %param.12) | copy-start | bytes 9220
  193.5 43.8 %all-to-all-start.2 = ((bf16[32,24,1536]{2,1,0:T(8,128)(2,1)}), bf16[32,24,1536]{2,1,0:T(8,128)(2,1)S(1)}, u32[]{:S(2)}, u32[]{:S(2)}) async-start(bf16[32,24,1536]{2,1,0:T(8,128)(2,1)} %bitcast.53), calls=%async_computation.2 | async-start | bytes 4718592 | tf_op jit(solution)/shard_map/all_to_all | solution.py:76
Sparse Core Ops, SparseCore 0:
  30.8 68.0 all-gather.2

commit v7 on v6

--- a/solution.py
+++ b/solution.py
@@ -17,14 +17,20 @@
     capacity = tok_dev * top_count // experts
     total_slots = experts * capacity
 
-    slab = jnp.concatenate(
-        [gate_train, up_train, jnp.swapaxes(down_train, 1, 2)], axis=2
-    ).astype(jnp.bfloat16)
-    slab, tokens, routes, route_scores, live = lax.optimization_barrier(
-        (slab, tokens, routes, route_scores, live)
+    parts = 2
+    part = hidden_width // parts
+    down_t = jnp.swapaxes(down_train, 1, 2)
+    slabs = tuple(
+        jnp.concatenate(
+            [w[:, :, h * part : (h + 1) * part] for w in (gate_train, up_train, down_t)], axis=2
+        ).astype(jnp.bfloat16)
+        for h in range(parts)
     )
-    slab = lax.all_gather(slab, "zh", axis=0, tiled=False)
-    n_pairs, local_experts, rows, width = slab.shape
+    slabs, tokens, routes, route_scores, live = lax.optimization_barrier(
+        (slabs, tokens, routes, route_scores, live)
+    )
+    slabs = tuple(lax.all_gather(w, "zh", axis=0, tiled=False) for w in slabs)
+    n_pairs, local_experts, rows, width = slabs[0].shape
     route_share = route_scores / jnp.sum(route_scores, axis=1, keepdims=True)
     flat_route = routes.reshape(-1)
     flat_live = jnp.repeat(live, top_count)
@@ -41,37 +47,40 @@
     dispatch = jnp.any(picks, axis=2).astype(jnp.bfloat16)
     outgoing = jnp.dot(dispatch, tokens, preferred_element_type=jnp.float32).astype(jnp.bfloat16)
     incoming = lax.all_to_all(outgoing, TOKEN_GROUP, split_axis=0, concat_axis=0, tiled=True)
-    incoming, slab = lax.optimization_barrier((incoming, slab))
-    slab = slab.reshape(n_pairs * local_experts, rows, width)
-    slab = lax.all_to_all(slab, ("y", "c"), split_axis=0, concat_axis=0, tiled=True)
+    incoming, slabs = lax.optimization_barrier((incoming, slabs))
     zl_size, zh_size = lax.axis_size("zl"), lax.axis_size("zh")
     ring = zl_size * zh_size
     index = lambda z: (z % zl_size) * zh_size + z // zl_size
     pairs = lambda k: [(index(z), index((z + k) % ring)) for z in range(ring)]
     shift = lambda v, k: lax.ppermute(v, ("zl", "zh"), pairs(k))
-    half = slab.shape[0] // 2
-    quarters = [
-        slab,
-        shift(slab, 1),
-        shift(slab, -1),
-        jnp.concatenate([shift(slab[:half], 2), shift(slab[half:], -2)]),
-    ]
     zl_at = lax.axis_index("zl")
-    places = jnp.stack([zl_at, zl_at - 1, zl_at + 1, zl_at + 2]) % zl_size
-    slab = jnp.take(jnp.stack(quarters), jnp.argsort(places), axis=0)
-    y_size = slab.shape[1] // local_experts
-    slab = slab.reshape(zl_size, y_size, local_experts, rows, width)
-    weights = jnp.swapaxes(slab, 0, 1).reshape(model_width, width)
-    gate_up_w = weights[:, : 2 * hidden_width]
-    down_t = weights[:, 2 * hidden_width :]
+    places = [zl_at % zl_size, (zl_at - 1) % zl_size, (zl_at + 1) % zl_size, (zl_at + 2) % zl_size]
+    weights = []
+    for slab in slabs:
+        slab = slab.reshape(n_pairs * local_experts, rows, width)
+        slab = lax.all_to_all(slab, ("y", "c"), split_axis=0, concat_axis=0, tiled=True)
+        half = slab.shape[0] // 2
+        quarters = [
+            slab,
+            shift(slab, 1),
+            shift(slab, -1),
+            jnp.concatenate([shift(slab[:half], 2), shift(slab[half:], -2)]),
+        ]
+        y_size = slab.shape[0] // local_experts
+        full = jnp.zeros((y_size, zl_size, local_experts, rows, width), jnp.bfloat16)
+        for quarter, place in zip(quarters, places):
+            quarter = quarter.reshape(y_size, 1, local_experts, rows, width)
+            full = lax.dynamic_update_index_in_dim(full, quarter, place, axis=1)
+        weights.append(full.reshape(model_width, width))
 
-    gate_up = jnp.dot(incoming, gate_up_w, preferred_element_type=jnp.float32)
-    hidden = (jax.nn.silu(gate_up[:, :hidden_width]) * gate_up[:, hidden_width:]).astype(
-        jnp.bfloat16
-    )
-    expert_out = lax.dot_general(
-        hidden, down_t, (((1,), (1,)), ((), ())), preferred_element_type=jnp.float32
-    )
+    expert_out = None
+    for w in weights:
+        gate_up = jnp.dot(incoming, w[:, : 2 * part], preferred_element_type=jnp.float32)
+        hidden = (jax.nn.silu(gate_up[:, :part]) * gate_up[:, part:]).astype(jnp.bfloat16)
+        term = lax.dot_general(
+            hidden, w[:, 2 * part :], (((1,), (1,)), ((), ())), preferred_element_type=jnp.float32
+        )
+        expert_out = term if expert_out is None else expert_out + term
     expert_rows = expert_out.astype(jnp.bfloat16)
     returned = lax.all_to_all(expert_rows, TOKEN_GROUP, split_axis=0, concat_axis=0, tiled=True)
     weight = jnp.where(kept_mask, route_share.reshape(-1), 0.0).reshape(tok_dev, top_count)

time: 247 us -> 208 us (0.84)
  waiting for transfers between devices: 153 us -> 57.4 us
  blocking collectives: 0 us -> 75.7 us
  between operations: 13.6 us -> 0.47 us
  starting transfers between devices: 43.3 us -> 53.2 us
  other arithmetic: 15.3 us -> 6.33 us
  local copies, waits for them, and re-layouts: 11.4 us -> 4.24 us
    all_gather x1 -> x0, waiting for transfers between devices: 70.3 us -> none  [local(): slab = lax.all_gather(slab, 'zh', axis=0, tiled=False)]
    all_gather x0 -> x2, blocking collectives: none -> 56.6 us  [local(): slabs = tuple((lax.all_gather(w, 'zh', axis=0, tiled=False) for w in slabs))]
    all_to_all x0 -> x1, blocking collectives: none -> 19.1 us  [local(): lax.all_to_all(slab, ('y', 'c'), split_axis=0, concat_axis=0, tiled=True)]
    all_to_all x1, waiting for transfers between devices: 16.4 us -> 0.01 us  [local(): lax.all_to_all(slab, ('y', 'c'), split_axis=0, concat_axis=0, tiled=True)]
    ppermute x4 -> x8, starting transfers between devices: 13.9 us -> 30 us  [local(): shift = lambda v, k: lax.ppermute(v, ('zl', 'zh'), pairs(k))]
    ppermute x4 -> x8, waiting for transfers between devices: 34.7 us -> 26.6 us  [local(): shift = lambda v, k: lax.ppermute(v, ('zl', 'zh'), pairs(k))]
    gather x1 -> x0, local copies, waits for them, and re-layouts: 5.35 us -> none  [local(): slab = jnp.take(jnp.stack(quarters), jnp.argsort(places), axis=0)]
    all_to_all x1, starting transfers between devices: 12.6 us -> 8.48 us  [local(): lax.all_to_all(expert_rows, TOKEN_GROUP, split_axis=0, concat_axis=0, til...]
  transfers between devices with their start and end apart: 8 -> 11, of which waited for: 4 -> 4; matrix products, arithmetic and copies ran while one was open for 1% -> 1% of each run, Pallas kernels for 0% -> 0%
where the time goes in v7:
time: 208 us; the launch traced here: 207 us
  blocking collectives  75.7 us (36%)
  waiting for transfers between devices  57.4 us (28%)
  starting transfers between devices  53.2 us (26%)
  matrix products  9.74 us (5%)
  other arithmetic  6.33 us (3%)
  local copies, waits for them, and re-layouts  4.24 us (2%)
    all_gather x2, blocking collectives, local(): slabs = tuple((lax.all_gather(w, 'zh', axis=0, tiled=False) for w in slabs))  56.6 us
    all_to_all x1, waiting for transfers between devices, local(): lax.all_to_all(expert_rows, TOKEN_GROUP, split_axis=0, concat_axis=0, til...  30.8 us
    ppermute x8, starting transfers between devices, local(): shift = lambda v, k: lax.ppermute(v, ('zl', 'zh'), pairs(k))  30 us
    ppermute x8, waiting for transfers between devices, local(): shift = lambda v, k: lax.ppermute(v, ('zl', 'zh'), pairs(k))  26.6 us
    all_to_all x1, blocking collectives, local(): lax.all_to_all(slab, ('y', 'c'), split_axis=0, concat_axis=0, tiled=True)  19.1 us
    all_to_all x1, starting transfers between devices, local(): lax.all_to_all(outgoing, TOKEN_GROUP, split_axis=0, concat_axis=0, tiled=...  10.6 us
    all_to_all x1, starting transfers between devices, local(): lax.all_to_all(expert_rows, TOKEN_GROUP, split_axis=0, concat_axis=0, til...  8.48 us
    another operation x5, other arithmetic  4.66 us
  transfers between devices with their start and end apart: 11, of which 4 were waited for; matrix products, arithmetic and copies ran while one was open for 1% of the time, Pallas kernels for 0%

profile of v7, /device:TPU:1, one launch (start us, length us, event | category | flops | bytes accessed | tf_op | source)
XLA Modules:
  0.0 207.1 jit_solution(4501158249962114290)
XLA Ops:
  0.0 0.0 copy-start
  0.0 0.0 copy-start.3
  0.0 1.0 convert.18
  1.0 0.9 convert.19
  2.0 0.9 convert_bitcast_fusion
  3.0 0.7 broadcast_compare_fusion
  3.7 0.1 broadcast_in_dim.26.clone
  3.7 0.2 gt.29
  3.9 0.1 gt.28
  4.0 0.8 copy.35
  4.8 0.1 eq.54
  5.0 0.1 eq.50
  5.1 1.7 reduce-window.6
  6.9 0.3 slice_reduce_fusion
  7.2 0.1 fusion.20
  7.3 0.1 reduce_sum.30
  7.4 0.1 copy.40
  7.5 0.0 copy-done.3
  7.5 0.4 fusion.1
  7.9 0.0 copy-done
  7.9 2.2 %convolution_convert_fusion = bf16[768,1536]{1,0:T(8,128)(2,1)} fusion(pred[768,128]{1,0:T(8,128)(4,1)S(1)} %fusion.1, bf16[128,1536]{1,0:T(8,128)(2,1)S(1)} %copy-done), kind=kOutput, calls=%fused_computation.1 | convolution fusion | flops 303169536 | bytes 2850816 | tf_op jit(solution)/shard_map/dot_general | solution.py:48
  10.1 10.6 %all-to-all-start = ((bf16[32,24,1536]{2,1,0:T(8,128)(2,1)}), bf16[32,24,1536]{2,1,0:T(8,128)(2,1)S(1)}, u32[]{:S(2)}, u32[]{:S(2)}) async-start(bf16[32,24,1536]{2,1,0:T(8,128)(2,1)} %bitcast.2), calls=%async_computation | async-start | bytes 4718592 | tf_op jit(solution)/shard_map/all_to_all | solution.py:49
  20.7 30.5 %all-gather = bf16[8,48,768]{2,1,0:T(8,128)(2,1)} all-gather(bf16[2,48,768]{2,1,0:T(8,128)(2,1)S(1)} %get-tuple-element.18), channel_id=2, replica_groups=mesh['y'=4,'zl'=4,'c'=2,'x'=4,'zh'=4] {'zh'}, dimensions={0}, use_global_device_ids=true | all-gather | bytes 737280 | tf_op jit(solution)/shard_map/all_gather | solution.py:32
  51.2 26.1 %all-gather.1 = bf16[8,48,768]{2,1,0:T(8,128)(2,1)S(1)} all-gather(bf16[2,48,768]{2,1,0:T(8,128)(2,1)S(1)} %get-tuple-element.19), channel_id=3, replica_groups=mesh['y'=4,'zl'=4,'c'=2,'x'=4,'zh'=4] {'zh'}, dimensions={0}, use_global_device_ids=true | all-gather | bytes 737280 | tf_op jit(solution)/shard_map/all_gather | solution.py:32
  77.3 0.0 all-to-all-done
  77.3 0.0 copy-start.1
  77.3 1.4 copy-done.1
  78.7 19.1 %all_to_all.34 = bf16[8,48,768]{2,1,0:T(8,128)(2,1)S(1)} all-to-all(bf16[8,48,768]{2,1,0:T(8,128)(2,1)S(1)} %all-gather.1), channel_id=1, replica_groups=mesh['y'=4,'zl'=4,'c'=2,'x'=4,'zh'=4] {'y','c'}, dimensions={0} | all-to-all | bytes 1179648 | tf_op jit(solution)/shard_map/all_to_all | solution.py:61
  97.8 4.2 %all-to-all-start.1 = ((bf16[8,48,768]{2,1,0:T(8,128)(2,1)}), bf16[8,48,768]{2,1,0:T(8,128)(2,1)S(1)}, u32[]{:S(2)}, u32[]{:S(2)}) async-start(bf16[8,48,768]{2,1,0:T(8,128)(2,1)} %bitcast.6), calls=%async_computation.1 | async-start | bytes 1179648 | tf_op jit(solution)/shard_map/all_to_all | solution.py:61
  102.0 1.9 collective-permute-start.6
  104.0 5.5 %collective-permute-start.7 = (bf16[4,48,768]{2,1,0:T(8,128)(2,1)S(1)}, bf16[4,48,768]{2,1,0:T(8,128)(2,1)S(1)}, u32[]{:S(2)}, u32[]{:S(2)}) collective-permute-start(bf16[4,48,768]{2,1,0:T(8,128)(2,1)S(1)} %get-tuple-element.24), channel_id=1, source_target_pairs={{0,67},{32,99},{64,0},{96,32},{1,64},{33,96},{65,1},{97,33},{2,65}... | collective-permute-start | bytes 884744 | tf_op jit(solution)/shard_map/ppermute | solution.py:55
  109.5 2.8 %collective-permute-start.4 = (bf16[8,48,768]{2,1,0:T(8,128)(2,1)S(1)}, bf16[8,48,768]{2,1,0:T(8,128)(2,1)S(1)}, u32[]{:S(2)}, u32[]{:S(2)}) collective-permute-start(bf16[8,48,768]{2,1,0:T(8,128)(2,1)S(1)} %all_to_all.34), channel_id=1, source_target_pairs={{0,32},{32,64},{64,96},{96,1},{1,33},{33,65},{65,97},{97,2},{2,34}... | collective-permute-start | bytes 1769480 | tf_op jit(solution)/shard_map/ppermute | solution.py:55
  112.3 0.0 all-to-all-done.1
  112.4 4.3 %collective-permute-start.2 = (bf16[4,48,768]{2,1,0:T(8,128)(2,1)S(1)}, bf16[4,48,768]{2,1,0:T(8,128)(2,1)S(1)}, u32[]{:S(2)}, u32[]{:S(2)}) collective-permute-start(bf16[4,48,768]{2,1,0:T(8,128)(2,1)S(1)} %get-tuple-element.25), channel_id=1, source_target_pairs={{0,64},{32,96},{64,1},{96,33},{1,65},{33,97},{65,2},{97,34},{2,66}... | collective-permute-start | bytes 884744 | tf_op jit(solution)/shard_map/ppermute | solution.py:55
  116.7 3.1 %collective-permute-start.3 = (bf16[4,48,768]{2,1,0:T(8,128)(2,1)S(1)}, bf16[4,48,768]{2,1,0:T(8,128)(2,1)S(1)}, u32[]{:S(2)}, u32[]{:S(2)}) collective-permute-start(bf16[4,48,768]{2,1,0:T(8,128)(2,1)S(1)} %get-tuple-element.26), channel_id=1, source_target_pairs={{0,67},{32,99},{64,0},{96,32},{1,64},{33,96},{65,1},{97,33},{2,65}... | collective-permute-start | bytes 884744 | tf_op jit(solution)/shard_map/ppermute | solution.py:55
  119.8 0.0 collective-permute-done.6
  119.8 3.7 %collective-permute-start = (bf16[8,48,768]{2,1,0:T(8,128)(2,1)S(1)}, bf16[8,48,768]{2,1,0:T(8,128)(2,1)S(1)}, u32[]{:S(2)}, u32[]{:S(2)}) collective-permute-start(bf16[8,48,768]{2,1,0:T(8,128)(2,1)S(1)} %all-to-all-done.1), channel_id=1, source_target_pairs={{0,32},{32,64},{64,96},{96,1},{1,33},{33,65},{65,97},{97,2},{2,34}... | collective-permute-start | bytes 1769480 | tf_op jit(solution)/shard_map/ppermute | solution.py:55
  123.5 0.2 broadcast.76.clone.1
  123.8 0.0 collective-permute-done.7
  123.8 4.1 %collective-permute-start.5 = (bf16[8,48,768]{2,1,0:T(8,128)(2,1)S(1)}, bf16[8,48,768]{2,1,0:T(8,128)(2,1)S(1)}, u32[]{:S(2)}, u32[]{:S(2)}) collective-permute-start(bf16[8,48,768]{2,1,0:T(8,128)(2,1)S(1)} %all_to_all.34), channel_id=1, source_target_pairs={{0,99},{32,0},{64,32},{96,64},{1,96},{33,1},{65,33},{97,65},{2,97}... | collective-permute-start | bytes 1769480 | tf_op jit(solution)/shard_map/ppermute | solution.py:55
  127.9 0.2 broadcast.76.clone
  128.2 0.1 pad_maximum_fusion.1
  128.3 16.1 %collective-permute-done.2 = bf16[4,48,768]{2,1,0:T(8,128)(2,1)S(1)} collective-permute-done((bf16[4,48,768]{2,1,0:T(8,128)(2,1)S(1)}, bf16[4,48,768]{2,1,0:T(8,128)(2,1)S(1)}, u32[]{:S(2)}, u32[]{:S(2)}) %collective-permute-start.2) | collective-permute-done | bytes 294944 | tf_op jit(solution)/shard_map/ppermute | solution.py:55
  144.4 4.6 %collective-permute-start.1 = (bf16[8,48,768]{2,1,0:T(8,128)(2,1)S(1)}, bf16[8,48,768]{2,1,0:T(8,128)(2,1)S(1)}, u32[]{:S(2)}, u32[]{:S(2)}) collective-permute-start(bf16[8,48,768]{2,1,0:T(8,128)(2,1)S(1)} %all-to-all-done.1), channel_id=1, source_target_pairs={{0,99},{32,0},{64,32},{96,64},{1,96},{33,1},{65,33},{97,65},{2,97}... | collective-permute-start | bytes 1769480 | tf_op jit(solution)/shard_map/ppermute | solution.py:55
  148.9 0.0 collective-permute-done.3
  149.0 0.1 pad_maximum_fusion
  149.0 0.0 collective-permute-done.4
  149.0 0.0 copy-start.2
  149.1 9.4 %collective-permute-done = bf16[8,48,768]{2,1,0:T(8,128)(2,1)S(1)} collective-permute-done((bf16[8,48,768]{2,1,0:T(8,128)(2,1)S(1)}, bf16[8,48,768]{2,1,0:T(8,128)(2,1)S(1)}, u32[]{:S(2)}, u32[]{:S(2)}) %collective-permute-start) | collective-permute-done | bytes 589856 | tf_op jit(solution)/shard_map/ppermute | solution.py:55
  158.6 0.0 collective-permute-done.5
  158.7 0.0 copy-done.2
  158.7 1.4 fusion.2
  160.1 1.0 collective-permute-done.1
  161.2 1.4 fusion.4
  162.6 0.8 fusion.8
  163.4 2.3 %add_convert_fusion = bf16[768,1536]{1,0:T(8,128)(2,1)} fusion(f32[768,1536]{1,0:T(8,128)S(1)} %fusion.8, bf16[1536,768]{1,0:T(8,128)(2,1)S(1)} %bitcast.54, f32[768,512]{1,0:T(8,128)S(1)} %fusion.2), kind=kOutput, calls=%fused_computation | convolution fusion | flops 607518720 | bytes 9437184 | tf_op jit(solution)/shard_map/dot_general | solution.py:80
  165.7 0.0 copy-start.4
  165.7 8.5 %all-to-all-start.3 = ((bf16[32,24,1536]{2,1,0:T(8,128)(2,1)}), bf16[32,24,1536]{2,1,0:T(8,128)(2,1)S(1)}, u32[]{:S(2)}, u32[]{:S(2)}) async-start(bf16[32,24,1536]{2,1,0:T(8,128)(2,1)} %bitcast.48), calls=%async_computation.3 | async-start | bytes 4718592 | tf_op jit(solution)/shard_map/all_to_all | solution.py:85
  174.2 0.0 copy-done.4
  174.2 0.3 select_reduce_fusion
  174.5 30.8 %all-to-all-done.3 = bf16[32,24,1536]{2,1,0:T(8,128)(2,1)S(1)} async-done(((bf16[32,24,1536]{2,1,0:T(8,128)(2,1)}), bf16[32,24,1536]{2,1,0:T(8,128)(2,1)S(1)}, u32[]{:S(2)}, u32[]{:S(2)}) %all-to-all-start.3) | async-done | bytes 2359328 | tf_op jit(solution)/shard_map/all_to_all | solution.py:85
  205.3 0.5 fusion.17
  205.8 1.2 fusion
  (19 shorter events, 0.6 us)
Async XLA Ops:
  0.0 7.9 %copy-start = (bf16[128,1536]{1,0:T(8,128)(2,1)S(1)}, bf16[128,1536]{1,0:T(8,128)(2,1)}, u32[]{:S(2)}) copy-start(bf16[128,1536]{1,0:T(8,128)(2,1)} %param.7) | copy-start | bytes 1179652
  0.0 7.5 %copy-start.3 = (s32[128,6]{0,1:T(8,128)S(1)}, s32[128,6]{0,1:T(8,128)}, u32[]{:S(2)}) copy-start(s32[128,6]{0,1:T(8,128)} %param.11) | copy-start | bytes 9220
  10.1 67.1 %all-to-all-start = ((bf16[32,24,1536]{2,1,0:T(8,128)(2,1)}), bf16[32,24,1536]{2,1,0:T(8,128)(2,1)S(1)}, u32[]{:S(2)}, u32[]{:S(2)}) async-start(bf16[32,24,1536]{2,1,0:T(8,128)(2,1)} %bitcast.2), calls=%async_computation | async-start | bytes 4718592 | tf_op jit(solution)/shard_map/all_to_all | solution.py:49
  77.3 1.4 copy-start.1
  97.8 14.5 %all-to-all-start.1 = ((bf16[8,48,768]{2,1,0:T(8,128)(2,1)}), bf16[8,48,768]{2,1,0:T(8,128)(2,1)S(1)}, u32[]{:S(2)}, u32[]{:S(2)}) async-start(bf16[8,48,768]{2,1,0:T(8,128)(2,1)} %bitcast.6), calls=%async_computation.1 | async-start | bytes 1179648 | tf_op jit(solution)/shard_map/all_to_all | solution.py:61
  102.0 17.8 %collective-permute-start.6 = (bf16[4,48,768]{2,1,0:T(8,128)(2,1)S(1)}, bf16[4,48,768]{2,1,0:T(8,128)(2,1)S(1)}, u32[]{:S(2)}, u32[]{:S(2)}) collective-permute-start(bf16[4,48,768]{2,1,0:T(8,128)(2,1)S(1)} %get-tuple-element.23), channel_id=1, source_target_pairs={{0,64},{32,96},{64,1},{96,33},{1,65},{33,97},{65,2},{97,34},{2,66}... | collective-permute-start | bytes 884744 | tf_op jit(solution)/shard_map/ppermute | solution.py:55
  104.0 19.8 %collective-permute-start.7 = (bf16[4,48,768]{2,1,0:T(8,128)(2,1)S(1)}, bf16[4,48,768]{2,1,0:T(8,128)(2,1)S(1)}, u32[]{:S(2)}, u32[]{:S(2)}) collective-permute-start(bf16[4,48,768]{2,1,0:T(8,128)(2,1)S(1)} %get-tuple-element.24), channel_id=1, source_target_pairs={{0,67},{32,99},{64,0},{96,32},{1,64},{33,96},{65,1},{97,33},{2,65}... | collective-permute-start | bytes 884744 | tf_op jit(solution)/shard_map/ppermute | solution.py:55
  109.5 39.5 %collective-permute-start.4 = (bf16[8,48,768]{2,1,0:T(8,128)(2,1)S(1)}, bf16[8,48,768]{2,1,0:T(8,128)(2,1)S(1)}, u32[]{:S(2)}, u32[]{:S(2)}) collective-permute-start(bf16[8,48,768]{2,1,0:T(8,128)(2,1)S(1)} %all_to_all.34), channel_id=1, source_target_pairs={{0,32},{32,64},{64,96},{96,1},{1,33},{33,65},{65,97},{97,2},{2,34}... | collective-permute-start | bytes 1769480 | tf_op jit(solution)/shard_map/ppermute | solution.py:55
  112.4 32.0 %collective-permute-start.2 = (bf16[4,48,768]{2,1,0:T(8,128)(2,1)S(1)}, bf16[4,48,768]{2,1,0:T(8,128)(2,1)S(1)}, u32[]{:S(2)}, u32[]{:S(2)}) collective-permute-start(bf16[4,48,768]{2,1,0:T(8,128)(2,1)S(1)} %get-tuple-element.25), channel_id=1, source_target_pairs={{0,64},{32,96},{64,1},{96,33},{1,65},{33,97},{65,2},{97,34},{2,66}... | collective-permute-start | bytes 884744 | tf_op jit(solution)/shard_map/ppermute | solution.py:55
  116.7 32.3 %collective-permute-start.3 = (bf16[4,48,768]{2,1,0:T(8,128)(2,1)S(1)}, bf16[4,48,768]{2,1,0:T(8,128)(2,1)S(1)}, u32[]{:S(2)}, u32[]{:S(2)}) collective-permute-start(bf16[4,48,768]{2,1,0:T(8,128)(2,1)S(1)} %get-tuple-element.26), channel_id=1, source_target_pairs={{0,67},{32,99},{64,0},{96,32},{1,64},{33,96},{65,1},{97,33},{2,65}... | collective-permute-start | bytes 884744 | tf_op jit(solution)/shard_map/ppermute | solution.py:55
  119.8 38.7 %collective-permute-start = (bf16[8,48,768]{2,1,0:T(8,128)(2,1)S(1)}, bf16[8,48,768]{2,1,0:T(8,128)(2,1)S(1)}, u32[]{:S(2)}, u32[]{:S(2)}) collective-permute-start(bf16[8,48,768]{2,1,0:T(8,128)(2,1)S(1)} %all-to-all-done.1), channel_id=1, source_target_pairs={{0,32},{32,64},{64,96},{96,1},{1,33},{33,65},{65,97},{97,2},{2,34}... | collective-permute-start | bytes 1769480 | tf_op jit(solution)/shard_map/ppermute | solution.py:55
  123.8 34.8 %collective-permute-start.5 = (bf16[8,48,768]{2,1,0:T(8,128)(2,1)S(1)}, bf16[8,48,768]{2,1,0:T(8,128)(2,1)S(1)}, u32[]{:S(2)}, u32[]{:S(2)}) collective-permute-start(bf16[8,48,768]{2,1,0:T(8,128)(2,1)S(1)} %all_to_all.34), channel_id=1, source_target_pairs={{0,99},{32,0},{64,32},{96,64},{1,96},{33,1},{65,33},{97,65},{2,97}... | collective-permute-start | bytes 1769480 | tf_op jit(solution)/shard_map/ppermute | solution.py:55
  144.4 16.7 %collective-permute-start.1 = (bf16[8,48,768]{2,1,0:T(8,128)(2,1)S(1)}, bf16[8,48,768]{2,1,0:T(8,128)(2,1)S(1)}, u32[]{:S(2)}, u32[]{:S(2)}) collective-permute-start(bf16[8,48,768]{2,1,0:T(8,128)(2,1)S(1)} %all-to-all-done.1), channel_id=1, source_target_pairs={{0,99},{32,0},{64,32},{96,64},{1,96},{33,1},{65,33},{97,65},{2,97}... | collective-permute-start | bytes 1769480 | tf_op jit(solution)/shard_map/ppermute | solution.py:55
  149.0 9.7 %copy-start.2 = (bf16[32,24,1536]{2,1,0:T(8,128)(2,1)S(1)}, bf16[32,24,1536]{2,1,0:T(8,128)(2,1)}, u32[]{:S(2)}) copy-start(bf16[32,24,1536]{2,1,0:T(8,128)(2,1)} %copy-done.1) | copy-start | bytes 7077892
  165.7 8.5 %copy-start.4 = (f32[128,6]{0,1:T(8,128)S(1)}, f32[128,6]{0,1:T(8,128)}, u32[]{:S(2)}) copy-start(f32[128,6]{0,1:T(8,128)} %param.12) | copy-start | bytes 9220
  165.7 39.7 %all-to-all-start.3 = ((bf16[32,24,1536]{2,1,0:T(8,128)(2,1)}), bf16[32,24,1536]{2,1,0:T(8,128)(2,1)S(1)}, u32[]{:S(2)}, u32[]{:S(2)}) async-start(bf16[32,24,1536]{2,1,0:T(8,128)(2,1)} %bitcast.48), calls=%async_computation.3 | async-start | bytes 4718592 | tf_op jit(solution)/shard_map/all_to_all | solution.py:85

commit v8 on v7

--- a/solution.py
+++ b/solution.py
@@ -29,8 +29,25 @@
     slabs, tokens, routes, route_scores, live = lax.optimization_barrier(
         (slabs, tokens, routes, route_scores, live)
     )
-    slabs = tuple(lax.all_gather(w, "zh", axis=0, tiled=False) for w in slabs)
-    n_pairs, local_experts, rows, width = slabs[0].shape
+    zh_size = lax.axis_size("zh")
+    zh_at = lax.axis_index("zh")
+    zshift = lambda v, k: lax.ppermute(v, "zh", [(i, (i + k) % zh_size) for i in range(zh_size)])
+    local_experts, rows, width = slabs[0].shape
+    gathered = []
+    for slab in slabs:
+        split = rows // 2
+        pieces = [
+            (0, slab),
+            (1, zshift(slab, 1)),
+            (-1, zshift(slab, -1)),
+            (2, jnp.concatenate([zshift(slab[:, :split], 2), zshift(slab[:, split:], -2)], axis=1)),
+        ]
+        stack = jnp.zeros((zh_size, local_experts, rows, width), jnp.bfloat16)
+        for step, piece in pieces:
+            stack = lax.dynamic_update_index_in_dim(stack, piece, (zh_at - step) % zh_size, axis=0)
+        gathered.append(stack)
+    slabs = tuple(gathered)
+    n_pairs = zh_size
     route_share = route_scores / jnp.sum(route_scores, axis=1, keepdims=True)
     flat_route = routes.reshape(-1)
     flat_live = jnp.repeat(live, top_count)
@@ -48,7 +65,7 @@
     outgoing = jnp.dot(dispatch, tokens, preferred_element_type=jnp.float32).astype(jnp.bfloat16)
     incoming = lax.all_to_all(outgoing, TOKEN_GROUP, split_axis=0, concat_axis=0, tiled=True)
     incoming, slabs = lax.optimization_barrier((incoming, slabs))
-    zl_size, zh_size = lax.axis_size("zl"), lax.axis_size("zh")
+    zl_size = lax.axis_size("zl")
     ring = zl_size * zh_size
     index = lambda z: (z % zl_size) * zh_size + z // zl_size
     pairs = lambda k: [(index(z), index((z + k) % ring)) for z in range(ring)]

time: 208 us -> 222 us (1.067)
  blocking collectives: 75.7 us -> 20 us
  starting transfers between devices: 53.2 us -> 102 us
  waiting for transfers between devices: 57.4 us -> 66.9 us
  local copies, waits for them, and re-layouts: 4.24 us -> 13.3 us
  other arithmetic: 6.33 us -> 8.55 us
    all_gather x2 -> x0, blocking collectives: 56.6 us -> none  [local(): slabs = tuple((lax.all_gather(w, 'zh', axis=0, tiled=False) for w in slabs))]
    ppermute x0 -> x8, starting transfers between devices: none -> 49.6 us  [local(): lax.ppermute(v, 'zh', [(i, (i + k) % zh_size) for i in range(zh_size)])]
    ppermute x0 -> x8, waiting for transfers between devices: none -> 7.82 us  [local(): lax.ppermute(v, 'zh', [(i, (i + k) % zh_size) for i in range(zh_size)])]
    dynamic_update_slice x0 -> x6, local copies, waits for them, and re-layouts: none -> 6.6 us  [local(): lax.dynamic_update_index_in_dim(stack, piece, (zh_at - step) % zh_size, a...]
  transfers between devices with their start and end apart: 11 -> 19, of which waited for: 4 -> 6; matrix products, arithmetic and copies ran while one was open for 1% -> 6% of each run, Pallas kernels for 0% -> 0%
where the time goes in v8:
time: 222 us; the launch traced here: 221 us
  starting transfers between devices  102 us (46%)
  waiting for transfers between devices  66.9 us (30%)
  blocking collectives  20 us (9%)
  local copies, waits for them, and re-layouts  13.3 us (6%)
  matrix products  9.76 us (4%)
  other arithmetic  8.55 us (4%)
    ppermute x8, starting transfers between devices, local(): lax.ppermute(v, 'zh', [(i, (i + k) % zh_size) for i in range(zh_size)])  49.6 us
    all_to_all x1, waiting for transfers between devices, local(): lax.all_to_all(expert_rows, TOKEN_GROUP, split_axis=0, concat_axis=0, til...  30.8 us
    ppermute x8, starting transfers between devices, local(): shift = lambda v, k: lax.ppermute(v, ('zl', 'zh'), pairs(k))  28.5 us
    ppermute x8, waiting for transfers between devices, local(): shift = lambda v, k: lax.ppermute(v, ('zl', 'zh'), pairs(k))  28.3 us
    all_to_all x1, blocking collectives, local(): lax.all_to_all(slab, ('y', 'c'), split_axis=0, concat_axis=0, tiled=True)  20 us
    all_to_all x1, starting transfers between devices, local(): lax.all_to_all(outgoing, TOKEN_GROUP, split_axis=0, concat_axis=0, tiled=...  10.5 us
    all_to_all x1, starting transfers between devices, local(): lax.all_to_all(expert_rows, TOKEN_GROUP, split_axis=0, concat_axis=0, til...  9.3 us
    ppermute x8, waiting for transfers between devices, local(): lax.ppermute(v, 'zh', [(i, (i + k) % zh_size) for i in range(zh_size)])  7.82 us
  transfers between devices with their start and end apart: 19, of which 6 were waited for; matrix products, arithmetic and copies ran while one was open for 6% of the time, Pallas kernels for 0%

profile of v8, /device:TPU:1, one launch (start us, length us, event | category | flops | bytes accessed | tf_op | source)
XLA Modules:
  0.0 221.3 jit_solution(11035012354759350071)
XLA Ops:
  0.0 1.0 convert.18
  1.0 0.9 convert.19
  2.0 0.9 convert_bitcast_fusion
  3.0 0.7 pad_maximum_fusion.2
  3.6 0.7 broadcast_compare_fusion
  4.3 0.1 broadcast_in_dim.51.clone
  4.4 0.2 gt.29
  4.5 0.1 gt.28
  4.7 0.8 copy.28
  5.5 0.1 eq.62
  5.6 0.1 eq.58
  5.8 1.7 reduce-window.6
  7.5 0.3 slice_reduce_fusion
  7.8 0.1 fusion.22
  7.9 0.1 reduce_sum.30
  8.1 0.1 copy.33
  8.2 0.4 fusion.1
  8.6 2.2 convolution_convert_fusion
  10.8 10.5 %all-to-all-start = ((bf16[32,24,1536]{2,1,0:T(8,128)(2,1)}), bf16[32,24,1536]{2,1,0:T(8,128)(2,1)S(1)}, u32[]{:S(2)}, u32[]{:S(2)}) async-start(bf16[32,24,1536]{2,1,0:T(8,128)(2,1)} %bitcast.2), calls=%async_computation | async-start | bytes 4718592 | tf_op jit(solution)/shard_map/all_to_all | solution.py:66
  21.3 6.8 %collective-permute-start.4 = (bf16[2,48,768]{2,1,0:T(8,128)(2,1)}, bf16[2,48,768]{2,1,0:T(8,128)(2,1)}, u32[]{:S(2)}, u32[]{:S(2)}) collective-permute-start(bf16[2,48,768]{2,1,0:T(8,128)(2,1)} %get-tuple-element.19), channel_id=1, source_target_pairs={{0,1},{1,2},{2,3},{3,0},{4,5},{5,6},{6,7},{7,4},{8,9},{9,10},{10,1... | collective-permute-start | bytes 442376 | tf_op jit(solution)/shard_map/ppermute | solution.py:34
  28.2 5.6 %collective-permute-start.5 = (bf16[2,48,768]{2,1,0:T(8,128)(2,1)}, bf16[2,48,768]{2,1,0:T(8,128)(2,1)}, u32[]{:S(2)}, u32[]{:S(2)}) collective-permute-start(bf16[2,48,768]{2,1,0:T(8,128)(2,1)} %get-tuple-element.19), channel_id=1, source_target_pairs={{0,3},{1,0},{2,1},{3,2},{4,7},{5,4},{6,5},{7,6},{8,11},{9,8},{10,9... | collective-permute-start | bytes 442376 | tf_op jit(solution)/shard_map/ppermute | solution.py:34
  33.8 5.2 %collective-permute-start = (bf16[2,48,768]{2,1,0:T(8,128)(2,1)S(1)}, bf16[2,48,768]{2,1,0:T(8,128)(2,1)}, u32[]{:S(2)}, u32[]{:S(2)}) collective-permute-start(bf16[2,48,768]{2,1,0:T(8,128)(2,1)S(1)} %get-tuple-element.18), channel_id=1, source_target_pairs={{0,1},{1,2},{2,3},{3,0},{4,5},{5,6},{6,7},{7,4},{8,9},{9,10},{10,1... | collective-permute-start | bytes 442376 | tf_op jit(solution)/shard_map/ppermute | solution.py:34
  38.9 4.0 %collective-permute-start.1 = (bf16[2,48,768]{2,1,0:T(8,128)(2,1)S(1)}, bf16[2,48,768]{2,1,0:T(8,128)(2,1)}, u32[]{:S(2)}, u32[]{:S(2)}) collective-permute-start(bf16[2,48,768]{2,1,0:T(8,128)(2,1)S(1)} %get-tuple-element.18), channel_id=1, source_target_pairs={{0,3},{1,0},{2,1},{3,2},{4,7},{5,4},{6,5},{7,6},{8,11},{9,8},{10,9... | collective-permute-start | bytes 442376 | tf_op jit(solution)/shard_map/ppermute | solution.py:34
  43.0 1.6 fusion.30
  44.6 10.2 %collective-permute-start.6 = (bf16[2,24,768]{2,1,0:T(8,128)(2,1)}, bf16[2,24,768]{2,1,0:T(8,128)(2,1)}, u32[]{:S(2)}, u32[]{:S(2)}) collective-permute-start(bf16[2,24,768]{2,1,0:T(8,128)(2,1)} %get-tuple-element.27), channel_id=1, source_target_pairs={{0,2},{1,3},{2,0},{3,1},{4,6},{5,7},{6,4},{7,5},{8,10},{9,11},{10,... | collective-permute-start | bytes 221192 | tf_op jit(solution)/shard_map/ppermute | solution.py:34
  54.9 0.9 bitcast_dynamic-update-slice_fusion.2
  55.8 0.9 broadcast.83.clone
  56.7 0.7 bitcast_dynamic-update-slice_fusion.5
  57.4 3.8 %collective-permute-start.7 = (bf16[2,24,768]{2,1,0:T(8,128)(2,1)}, bf16[2,24,768]{2,1,0:T(8,128)(2,1)S(1)}, u32[]{:S(2)}, u32[]{:S(2)}) collective-permute-start(bf16[2,24,768]{2,1,0:T(8,128)(2,1)} %get-tuple-element.28), channel_id=1, source_target_pairs={{0,2},{1,3},{2,0},{3,1},{4,6},{5,7},{6,4},{7,5},{8,10},{9,11},{10,... | collective-permute-start | bytes 221192 | tf_op jit(solution)/shard_map/ppermute | solution.py:34
  61.2 0.9 bitcast_dynamic-update-slice_fusion.1
  62.1 10.2 %collective-permute-start.2 = (bf16[2,24,768]{2,1,0:T(8,128)(2,1)S(1)}, bf16[2,24,768]{2,1,0:T(8,128)(2,1)S(1)}, u32[]{:S(2)}, u32[]{:S(2)}) collective-permute-start(bf16[2,24,768]{2,1,0:T(8,128)(2,1)S(1)} %get-tuple-element.29), channel_id=1, source_target_pairs={{0,2},{1,3},{2,0},{3,1},{4,6},{5,7},{6,4},{7,5},{8,10},{9,11},{10,... | collective-permute-start | bytes 221192 | tf_op jit(solution)/shard_map/ppermute | solution.py:34
  72.3 1.6 bitcast_dynamic-update-slice_fusion.4
  73.9 3.7 %collective-permute-start.3 = (bf16[2,24,768]{2,1,0:T(8,128)(2,1)S(1)}, bf16[2,24,768]{2,1,0:T(8,128)(2,1)S(1)}, u32[]{:S(2)}, u32[]{:S(2)}) collective-permute-start(bf16[2,24,768]{2,1,0:T(8,128)(2,1)S(1)} %get-tuple-element.30), channel_id=1, source_target_pairs={{0,2},{1,3},{2,0},{3,1},{4,6},{5,7},{6,4},{7,5},{8,10},{9,11},{10,... | collective-permute-start | bytes 221192 | tf_op jit(solution)/shard_map/ppermute | solution.py:34
  77.7 0.9 bitcast_dynamic-update-slice_fusion
  78.6 1.6 bitcast_dynamic-update-slice_fusion.3
  80.2 0.9 fusion.19
  81.1 0.1 collective-permute-done.2
  81.2 7.7 %collective-permute-done.3 = bf16[2,24,768]{2,1,0:T(8,128)(2,1)S(1)} collective-permute-done((bf16[2,24,768]{2,1,0:T(8,128)(2,1)S(1)}, bf16[2,24,768]{2,1,0:T(8,128)(2,1)S(1)}, u32[]{:S(2)}, u32[]{:S(2)}) %collective-permute-start.3) | collective-permute-done | bytes 73760 | tf_op jit(solution)/shard_map/ppermute | solution.py:34
  88.9 0.7 fusion.18
  89.6 1.4 copy-done.1
  91.0 20.0 %all_to_all.34 = bf16[8,48,768]{2,1,0:T(8,128)(2,1)S(1)} all-to-all(bf16[8,48,768]{2,1,0:T(8,128)(2,1)S(1)} %bitcast.77), channel_id=1, replica_groups=mesh['y'=4,'zl'=4,'c'=2,'x'=4,'zh'=4] {'y','c'}, dimensions={0} | all-to-all | bytes 1179648 | tf_op jit(solution)/shard_map/all_to_all | solution.py:78
  111.0 4.2 %all-to-all-start.1 = ((bf16[8,48,768]{2,1,0:T(8,128)(2,1)}), bf16[8,48,768]{2,1,0:T(8,128)(2,1)S(1)}, u32[]{:S(2)}, u32[]{:S(2)}) async-start(bf16[8,48,768]{2,1,0:T(8,128)(2,1)} %bitcast.12), calls=%async_computation.1 | async-start | bytes 1179648 | tf_op jit(solution)/shard_map/all_to_all | solution.py:78
  115.2 1.9 collective-permute-start.14
  117.2 5.5 %collective-permute-start.15 = (bf16[4,48,768]{2,1,0:T(8,128)(2,1)S(1)}, bf16[4,48,768]{2,1,0:T(8,128)(2,1)S(1)}, u32[]{:S(2)}, u32[]{:S(2)}) collective-permute-start(bf16[4,48,768]{2,1,0:T(8,128)(2,1)S(1)} %get-tuple-element.24), channel_id=1, source_target_pairs={{0,67},{32,99},{64,0},{96,32},{1,64},{33,96},{65,1},{97,33},{2,65}... | collective-permute-start | bytes 884744 | tf_op jit(solution)/shard_map/ppermute | solution.py:72
  122.7 5.3 %collective-permute-start.12 = (bf16[8,48,768]{2,1,0:T(8,128)(2,1)S(1)}, bf16[8,48,768]{2,1,0:T(8,128)(2,1)S(1)}, u32[]{:S(2)}, u32[]{:S(2)}) collective-permute-start(bf16[8,48,768]{2,1,0:T(8,128)(2,1)S(1)} %all_to_all.34), channel_id=1, source_target_pairs={{0,32},{32,64},{64,96},{96,1},{1,33},{33,65},{65,97},{97,2},{2,34}... | collective-permute-start | bytes 1769480 | tf_op jit(solution)/shard_map/ppermute | solution.py:72
  128.1 1.9 collective-permute-start.10
  130.0 5.5 %collective-permute-start.11 = (bf16[4,48,768]{2,1,0:T(8,128)(2,1)S(1)}, bf16[4,48,768]{2,1,0:T(8,128)(2,1)S(1)}, u32[]{:S(2)}, u32[]{:S(2)}) collective-permute-start(bf16[4,48,768]{2,1,0:T(8,128)(2,1)S(1)} %get-tuple-element.26), channel_id=1, source_target_pairs={{0,67},{32,99},{64,0},{96,32},{1,64},{33,96},{65,1},{97,33},{2,65}... | collective-permute-start | bytes 884744 | tf_op jit(solution)/shard_map/ppermute | solution.py:72
  135.5 2.5 %collective-permute-start.8 = (bf16[8,48,768]{2,1,0:T(8,128)(2,1)S(1)}, bf16[8,48,768]{2,1,0:T(8,128)(2,1)S(1)}, u32[]{:S(2)}, u32[]{:S(2)}) collective-permute-start(bf16[8,48,768]{2,1,0:T(8,128)(2,1)S(1)} %all-to-all-done.1), channel_id=1, source_target_pairs={{0,32},{32,64},{64,96},{96,1},{1,33},{33,65},{65,97},{97,2},{2,34}... | collective-permute-start | bytes 1769480 | tf_op jit(solution)/shard_map/ppermute | solution.py:72
  138.0 0.2 broadcast.84.clone.1
  138.3 3.9 %collective-permute-start.13 = (bf16[8,48,768]{2,1,0:T(8,128)(2,1)S(1)}, bf16[8,48,768]{2,1,0:T(8,128)(2,1)S(1)}, u32[]{:S(2)}, u32[]{:S(2)}) collective-permute-start(bf16[8,48,768]{2,1,0:T(8,128)(2,1)S(1)} %all_to_all.34), channel_id=1, source_target_pairs={{0,99},{32,0},{64,32},{96,64},{1,96},{33,1},{65,33},{97,65},{2,97}... | collective-permute-start | bytes 1769480 | tf_op jit(solution)/shard_map/ppermute | solution.py:72
  142.3 0.2 broadcast.84.clone
  142.6 16.7 %collective-permute-done.10 = bf16[4,48,768]{2,1,0:T(8,128)(2,1)S(1)} collective-permute-done((bf16[4,48,768]{2,1,0:T(8,128)(2,1)S(1)}, bf16[4,48,768]{2,1,0:T(8,128)(2,1)S(1)}, u32[]{:S(2)}, u32[]{:S(2)}) %collective-permute-start.10) | collective-permute-done | bytes 294944 | tf_op jit(solution)/shard_map/ppermute | solution.py:72
  159.3 1.9 collective-permute-start.9
  161.4 11.2 %collective-permute-done.8 = bf16[8,48,768]{2,1,0:T(8,128)(2,1)S(1)} collective-permute-done((bf16[8,48,768]{2,1,0:T(8,128)(2,1)S(1)}, bf16[8,48,768]{2,1,0:T(8,128)(2,1)S(1)}, u32[]{:S(2)}, u32[]{:S(2)}) %collective-permute-start.8) | collective-permute-done | bytes 589856 | tf_op jit(solution)/shard_map/ppermute | solution.py:72
  172.7 1.4 fusion.2
  174.1 0.4 collective-permute-done.9
  174.6 1.4 fusion.4
  176.0 0.8 fusion.8
  176.8 2.3 %add_convert_fusion = bf16[768,1536]{1,0:T(8,128)(2,1)} fusion(f32[768,1536]{1,0:T(8,128)S(1)} %fusion.8, bf16[1536,768]{1,0:T(8,128)(2,1)S(1)} %bitcast.72, f32[768,512]{1,0:T(8,128)S(1)} %fusion.2), kind=kOutput, calls=%fused_computation | convolution fusion | flops 607518720 | bytes 9437184 | tf_op jit(solution)/shard_map/dot_general | solution.py:97
  179.1 9.3 %all-to-all-start.3 = ((bf16[32,24,1536]{2,1,0:T(8,128)(2,1)}), bf16[32,24,1536]{2,1,0:T(8,128)(2,1)S(1)}, u32[]{:S(2)}, u32[]{:S(2)}) async-start(bf16[32,24,1536]{2,1,0:T(8,128)(2,1)} %bitcast.66), calls=%async_computation.3 | async-start | bytes 4718592 | tf_op jit(solution)/shard_map/all_to_all | solution.py:102
  188.5 0.3 select_reduce_fusion
  188.8 30.8 %all-to-all-done.3 = bf16[32,24,1536]{2,1,0:T(8,128)(2,1)S(1)} async-done(((bf16[32,24,1536]{2,1,0:T(8,128)(2,1)}), bf16[32,24,1536]{2,1,0:T(8,128)(2,1)S(1)}, u32[]{:S(2)}, u32[]{:S(2)}) %all-to-all-start.3) | async-done | bytes 2359328 | tf_op jit(solution)/shard_map/all_to_all | solution.py:102
  219.6 0.5 fusion.17
  220.1 1.2 fusion
  (44 shorter events, 0.8 us)
Async XLA Ops:
  0.0 8.6 %copy-start = (bf16[128,1536]{1,0:T(8,128)(2,1)S(1)}, bf16[128,1536]{1,0:T(8,128)(2,1)}, u32[]{:S(2)}) copy-start(bf16[128,1536]{1,0:T(8,128)(2,1)} %param.7) | copy-start | bytes 1179652
  0.0 8.1 %copy-start.3 = (s32[128,6]{0,1:T(8,128)S(1)}, s32[128,6]{0,1:T(8,128)}, u32[]{:S(2)}) copy-start(s32[128,6]{0,1:T(8,128)} %param.11) | copy-start | bytes 9220
  10.8 78.8 %all-to-all-start = ((bf16[32,24,1536]{2,1,0:T(8,128)(2,1)}), bf16[32,24,1536]{2,1,0:T(8,128)(2,1)S(1)}, u32[]{:S(2)}, u32[]{:S(2)}) async-start(bf16[32,24,1536]{2,1,0:T(8,128)(2,1)} %bitcast.2), calls=%async_computation | async-start | bytes 4718592 | tf_op jit(solution)/shard_map/all_to_all | solution.py:66
  21.3 36.0 %collective-permute-start.4 = (bf16[2,48,768]{2,1,0:T(8,128)(2,1)}, bf16[2,48,768]{2,1,0:T(8,128)(2,1)}, u32[]{:S(2)}, u32[]{:S(2)}) collective-permute-start(bf16[2,48,768]{2,1,0:T(8,128)(2,1)} %get-tuple-element.19), channel_id=1, source_target_pairs={{0,1},{1,2},{2,3},{3,0},{4,5},{5,6},{6,7},{7,4},{8,9},{9,10},{10,1... | collective-permute-start | bytes 442376 | tf_op jit(solution)/shard_map/ppermute | solution.py:34
  28.2 45.7 %collective-permute-start.5 = (bf16[2,48,768]{2,1,0:T(8,128)(2,1)}, bf16[2,48,768]{2,1,0:T(8,128)(2,1)}, u32[]{:S(2)}, u32[]{:S(2)}) collective-permute-start(bf16[2,48,768]{2,1,0:T(8,128)(2,1)} %get-tuple-element.19), channel_id=1, source_target_pairs={{0,3},{1,0},{2,1},{3,2},{4,7},{5,4},{6,5},{7,6},{8,11},{9,8},{10,9... | collective-permute-start | bytes 442376 | tf_op jit(solution)/shard_map/ppermute | solution.py:34
  33.8 28.3 %collective-permute-start = (bf16[2,48,768]{2,1,0:T(8,128)(2,1)S(1)}, bf16[2,48,768]{2,1,0:T(8,128)(2,1)}, u32[]{:S(2)}, u32[]{:S(2)}) collective-permute-start(bf16[2,48,768]{2,1,0:T(8,128)(2,1)S(1)} %get-tuple-element.18), channel_id=1, source_target_pairs={{0,1},{1,2},{2,3},{3,0},{4,5},{5,6},{6,7},{7,4},{8,9},{9,10},{10,1... | collective-permute-start | bytes 442376 | tf_op jit(solution)/shard_map/ppermute | solution.py:34
  38.9 39.7 %collective-permute-start.1 = (bf16[2,48,768]{2,1,0:T(8,128)(2,1)S(1)}, bf16[2,48,768]{2,1,0:T(8,128)(2,1)}, u32[]{:S(2)}, u32[]{:S(2)}) collective-permute-start(bf16[2,48,768]{2,1,0:T(8,128)(2,1)S(1)} %get-tuple-element.18), channel_id=1, source_target_pairs={{0,3},{1,0},{2,1},{3,2},{4,7},{5,4},{6,5},{7,6},{8,11},{9,8},{10,9... | collective-permute-start | bytes 442376 | tf_op jit(solution)/shard_map/ppermute | solution.py:34
  44.6 35.7 %collective-permute-start.6 = (bf16[2,24,768]{2,1,0:T(8,128)(2,1)}, bf16[2,24,768]{2,1,0:T(8,128)(2,1)}, u32[]{:S(2)}, u32[]{:S(2)}) collective-permute-start(bf16[2,24,768]{2,1,0:T(8,128)(2,1)} %get-tuple-element.27), channel_id=1, source_target_pairs={{0,2},{1,3},{2,0},{3,1},{4,6},{5,7},{6,4},{7,5},{8,10},{9,11},{10,... | collective-permute-start | bytes 221192 | tf_op jit(solution)/shard_map/ppermute | solution.py:34
  57.4 22.8 %collective-permute-start.7 = (bf16[2,24,768]{2,1,0:T(8,128)(2,1)}, bf16[2,24,768]{2,1,0:T(8,128)(2,1)S(1)}, u32[]{:S(2)}, u32[]{:S(2)}) collective-permute-start(bf16[2,24,768]{2,1,0:T(8,128)(2,1)} %get-tuple-element.28), channel_id=1, source_target_pairs={{0,2},{1,3},{2,0},{3,1},{4,6},{5,7},{6,4},{7,5},{8,10},{9,11},{10,... | collective-permute-start | bytes 221192 | tf_op jit(solution)/shard_map/ppermute | solution.py:34
  62.1 19.1 %collective-permute-start.2 = (bf16[2,24,768]{2,1,0:T(8,128)(2,1)S(1)}, bf16[2,24,768]{2,1,0:T(8,128)(2,1)S(1)}, u32[]{:S(2)}, u32[]{:S(2)}) collective-permute-start(bf16[2,24,768]{2,1,0:T(8,128)(2,1)S(1)} %get-tuple-element.29), channel_id=1, source_target_pairs={{0,2},{1,3},{2,0},{3,1},{4,6},{5,7},{6,4},{7,5},{8,10},{9,11},{10,... | collective-permute-start | bytes 221192 | tf_op jit(solution)/shard_map/ppermute | solution.py:34
  73.9 15.0 %collective-permute-start.3 = (bf16[2,24,768]{2,1,0:T(8,128)(2,1)S(1)}, bf16[2,24,768]{2,1,0:T(8,128)(2,1)S(1)}, u32[]{:S(2)}, u32[]{:S(2)}) collective-permute-start(bf16[2,24,768]{2,1,0:T(8,128)(2,1)S(1)} %get-tuple-element.30), channel_id=1, source_target_pairs={{0,2},{1,3},{2,0},{3,1},{4,6},{5,7},{6,4},{7,5},{8,10},{9,11},{10,... | collective-permute-start | bytes 221192 | tf_op jit(solution)/shard_map/ppermute | solution.py:34
  89.6 1.4 copy-start.1
  111.0 17.0 %all-to-all-start.1 = ((bf16[8,48,768]{2,1,0:T(8,128)(2,1)}), bf16[8,48,768]{2,1,0:T(8,128)(2,1)S(1)}, u32[]{:S(2)}, u32[]{:S(2)}) async-start(bf16[8,48,768]{2,1,0:T(8,128)(2,1)} %bitcast.12), calls=%async_computation.1 | async-start | bytes 1179648 | tf_op jit(solution)/shard_map/all_to_all | solution.py:78
  115.2 20.2 %collective-permute-start.14 = (bf16[4,48,768]{2,1,0:T(8,128)(2,1)S(1)}, bf16[4,48,768]{2,1,0:T(8,128)(2,1)S(1)}, u32[]{:S(2)}, u32[]{:S(2)}) collective-permute-start(bf16[4,48,768]{2,1,0:T(8,128)(2,1)S(1)} %get-tuple-element.23), channel_id=1, source_target_pairs={{0,64},{32,96},{64,1},{96,33},{1,65},{33,97},{65,2},{97,34},{2,66}... | collective-permute-start | bytes 884744 | tf_op jit(solution)/shard_map/ppermute | solution.py:72
  117.2 21.1 %collective-permute-start.15 = (bf16[4,48,768]{2,1,0:T(8,128)(2,1)S(1)}, bf16[4,48,768]{2,1,0:T(8,128)(2,1)S(1)}, u32[]{:S(2)}, u32[]{:S(2)}) collective-permute-start(bf16[4,48,768]{2,1,0:T(8,128)(2,1)S(1)} %get-tuple-element.24), channel_id=1, source_target_pairs={{0,67},{32,99},{64,0},{96,32},{1,64},{33,96},{65,1},{97,33},{2,65}... | collective-permute-start | bytes 884744 | tf_op jit(solution)/shard_map/ppermute | solution.py:72
  122.7 38.6 %collective-permute-start.12 = (bf16[8,48,768]{2,1,0:T(8,128)(2,1)S(1)}, bf16[8,48,768]{2,1,0:T(8,128)(2,1)S(1)}, u32[]{:S(2)}, u32[]{:S(2)}) collective-permute-start(bf16[8,48,768]{2,1,0:T(8,128)(2,1)S(1)} %all_to_all.34), channel_id=1, source_target_pairs={{0,32},{32,64},{64,96},{96,1},{1,33},{33,65},{65,97},{97,2},{2,34}... | collective-permute-start | bytes 1769480 | tf_op jit(solution)/shard_map/ppermute | solution.py:72
  128.1 31.2 %collective-permute-start.10 = (bf16[4,48,768]{2,1,0:T(8,128)(2,1)S(1)}, bf16[4,48,768]{2,1,0:T(8,128)(2,1)S(1)}, u32[]{:S(2)}, u32[]{:S(2)}) collective-permute-start(bf16[4,48,768]{2,1,0:T(8,128)(2,1)S(1)} %get-tuple-element.25), channel_id=1, source_target_pairs={{0,64},{32,96},{64,1},{96,33},{1,65},{33,97},{65,2},{97,34},{2,66}... | collective-permute-start | bytes 884744 | tf_op jit(solution)/shard_map/ppermute | solution.py:72
  130.0 31.2 %collective-permute-start.11 = (bf16[4,48,768]{2,1,0:T(8,128)(2,1)S(1)}, bf16[4,48,768]{2,1,0:T(8,128)(2,1)S(1)}, u32[]{:S(2)}, u32[]{:S(2)}) collective-permute-start(bf16[4,48,768]{2,1,0:T(8,128)(2,1)S(1)} %get-tuple-element.26), channel_id=1, source_target_pairs={{0,67},{32,99},{64,0},{96,32},{1,64},{33,96},{65,1},{97,33},{2,65}... | collective-permute-start | bytes 884744 | tf_op jit(solution)/shard_map/ppermute | solution.py:72
  135.5 37.1 %collective-permute-start.8 = (bf16[8,48,768]{2,1,0:T(8,128)(2,1)S(1)}, bf16[8,48,768]{2,1,0:T(8,128)(2,1)S(1)}, u32[]{:S(2)}, u32[]{:S(2)}) collective-permute-start(bf16[8,48,768]{2,1,0:T(8,128)(2,1)S(1)} %all-to-all-done.1), channel_id=1, source_target_pairs={{0,32},{32,64},{64,96},{96,1},{1,33},{33,65},{65,97},{97,2},{2,34}... | collective-permute-start | bytes 1769480 | tf_op jit(solution)/shard_map/ppermute | solution.py:72
  138.3 34.3 %collective-permute-start.13 = (bf16[8,48,768]{2,1,0:T(8,128)(2,1)S(1)}, bf16[8,48,768]{2,1,0:T(8,128)(2,1)S(1)}, u32[]{:S(2)}, u32[]{:S(2)}) collective-permute-start(bf16[8,48,768]{2,1,0:T(8,128)(2,1)S(1)} %all_to_all.34), channel_id=1, source_target_pairs={{0,99},{32,0},{64,32},{96,64},{1,96},{33,1},{65,33},{97,65},{2,97}... | collective-permute-start | bytes 1769480 | tf_op jit(solution)/shard_map/ppermute | solution.py:72
  159.3 15.2 %collective-permute-start.9 = (bf16[8,48,768]{2,1,0:T(8,128)(2,1)S(1)}, bf16[8,48,768]{2,1,0:T(8,128)(2,1)S(1)}, u32[]{:S(2)}, u32[]{:S(2)}) collective-permute-start(bf16[8,48,768]{2,1,0:T(8,128)(2,1)S(1)} %all-to-all-done.1), channel_id=1, source_target_pairs={{0,99},{32,0},{64,32},{96,64},{1,96},{33,1},{65,33},{97,65},{2,97}... | collective-permute-start | bytes 1769480 | tf_op jit(solution)/shard_map/ppermute | solution.py:72
  161.3 11.4 %copy-start.2 = (bf16[32,24,1536]{2,1,0:T(8,128)(2,1)S(1)}, bf16[32,24,1536]{2,1,0:T(8,128)(2,1)}, u32[]{:S(2)}) copy-start(bf16[32,24,1536]{2,1,0:T(8,128)(2,1)} %copy-done.1) | copy-start | bytes 7077892
  179.1 9.3 %copy-start.4 = (f32[128,6]{0,1:T(8,128)S(1)}, f32[128,6]{0,1:T(8,128)}, u32[]{:S(2)}) copy-start(f32[128,6]{0,1:T(8,128)} %param.12) | copy-start | bytes 9220
  179.1 40.5 %all-to-all-start.3 = ((bf16[32,24,1536]{2,1,0:T(8,128)(2,1)}), bf16[32,24,1536]{2,1,0:T(8,128)(2,1)S(1)}, u32[]{:S(2)}, u32[]{:S(2)}) async-start(bf16[32,24,1536]{2,1,0:T(8,128)(2,1)} %bitcast.66), calls=%async_computation.3 | async-start | bytes 4718592 | tf_op jit(solution)/shard_map/all_to_all | solution.py:102

commit v9 on v7

--- a/solution.py
+++ b/solution.py
@@ -31,6 +31,9 @@
     )
     slabs = tuple(lax.all_gather(w, "zh", axis=0, tiled=False) for w in slabs)
     n_pairs, local_experts, rows, width = slabs[0].shape
+    slabs, tokens, routes, route_scores, live = lax.optimization_barrier(
+        (slabs, tokens, routes, route_scores, live)
+    )
     route_share = route_scores / jnp.sum(route_scores, axis=1, keepdims=True)
     flat_route = routes.reshape(-1)
     flat_live = jnp.repeat(live, top_count)
@@ -47,7 +50,6 @@
     dispatch = jnp.any(picks, axis=2).astype(jnp.bfloat16)
     outgoing = jnp.dot(dispatch, tokens, preferred_element_type=jnp.float32).astype(jnp.bfloat16)
     incoming = lax.all_to_all(outgoing, TOKEN_GROUP, split_axis=0, concat_axis=0, tiled=True)
-    incoming, slabs = lax.optimization_barrier((incoming, slabs))
     zl_size, zh_size = lax.axis_size("zl"), lax.axis_size("zh")
     ring = zl_size * zh_size
     index = lambda z: (z % zl_size) * zh_size + z // zl_size

time: 208 us -> 220 us (1.058)
  blocking collectives: 75.7 us -> 59.7 us
  waiting for transfers between devices: 57.4 us -> 66.4 us
  local copies, waits for them, and re-layouts: 4.24 us -> 13.2 us
  matrix products: 9.74 us -> 16.2 us
  starting transfers between devices: 53.2 us -> 57.3 us
    all_to_all x1 -> x0, blocking collectives: 19.1 us -> none  [local(): lax.all_to_all(slab, ('y', 'c'), split_axis=0, concat_axis=0, tiled=True)]
    all_to_all x1 -> x2, waiting for transfers between devices: 0.01 us -> 14.4 us  [local(): lax.all_to_all(slab, ('y', 'c'), split_axis=0, concat_axis=0, tiled=True)]
    all_to_all x1 -> x2, starting transfers between devices: 4.19 us -> 15.2 us  [local(): lax.all_to_all(slab, ('y', 'c'), split_axis=0, concat_axis=0, tiled=True)]
    dynamic_update_slice x8, local copies, waits for them, and re-layouts: 0.36 us -> 6.99 us  [local(): full = lax.dynamic_update_index_in_dim(full, quarter, place, axis=1)]
    ppermute x8, waiting for transfers between devices: 26.6 us -> 21.2 us  [local(): shift = lambda v, k: lax.ppermute(v, ('zl', 'zh'), pairs(k))]
    all_to_all x1, starting transfers between devices: 10.6 us -> 6.06 us  [local(): lax.all_to_all(outgoing, TOKEN_GROUP, split_axis=0, concat_axis=0, tiled=...]
    dot_general x2, matrix products: 2.75 us -> 6.98 us  [local(): jnp.dot(incoming, w[:, :2 * part], preferred_element_type=jnp.float32)]
    ppermute x8, starting transfers between devices: 30 us -> 26.8 us  [local(): shift = lambda v, k: lax.ppermute(v, ('zl', 'zh'), pairs(k))]
  transfers between devices with their start and end apart: 11 -> 12, of which waited for: 4 -> 6; matrix products, arithmetic and copies ran while one was open for 1% -> 8% of each run, Pallas kernels for 0% -> 0%
where the time goes in v9:
time: 220 us; the launch traced here: 219 us
  waiting for transfers between devices  66.4 us (30%)
  blocking collectives  59.7 us (27%)
  starting transfers between devices  57.3 us (26%)
  matrix products  16.2 us (7%)
  local copies, waits for them, and re-layouts  13.2 us (6%)
  other arithmetic  5.66 us (3%)
    all_gather x2, blocking collectives, local(): slabs = tuple((lax.all_gather(w, 'zh', axis=0, tiled=False) for w in slabs))  59.7 us
    all_to_all x1, waiting for transfers between devices, local(): lax.all_to_all(expert_rows, TOKEN_GROUP, split_axis=0, concat_axis=0, til...  30.8 us
    ppermute x8, starting transfers between devices, local(): shift = lambda v, k: lax.ppermute(v, ('zl', 'zh'), pairs(k))  26.8 us
    ppermute x8, waiting for transfers between devices, local(): shift = lambda v, k: lax.ppermute(v, ('zl', 'zh'), pairs(k))  21.2 us
    all_to_all x2, starting transfers between devices, local(): lax.all_to_all(slab, ('y', 'c'), split_axis=0, concat_axis=0, tiled=True)  15.2 us
    all_to_all x2, waiting for transfers between devices, local(): lax.all_to_all(slab, ('y', 'c'), split_axis=0, concat_axis=0, tiled=True)  14.4 us
    all_to_all x1, starting transfers between devices, local(): lax.all_to_all(expert_rows, TOKEN_GROUP, split_axis=0, concat_axis=0, til...  9.18 us
    dynamic_update_slice x8, local copies, waits for them, and re-layouts, local(): full = lax.dynamic_update_index_in_dim(full, quarter, place, axis=1)  6.99 us
  transfers between devices with their start and end apart: 12, of which 6 were waited for; matrix products, arithmetic and copies ran while one was open for 8% of the time, Pallas kernels for 0%

profile of v9, /device:TPU:1, one launch (start us, length us, event | category | flops | bytes accessed | tf_op | source)
XLA Modules:
  0.0 218.9 jit_solution(11979175386395438862)
XLA Ops:
  0.0 0.0 copy-start
  0.0 1.0 convert.18
  1.0 0.9 convert.19
  2.0 0.9 convert_bitcast_fusion
  3.0 33.8 %all-gather = bf16[8,48,768]{2,1,0:T(8,128)(2,1)} all-gather(bf16[2,48,768]{2,1,0:T(8,128)(2,1)S(1)} %get-tuple-element.17), channel_id=2, replica_groups=mesh['y'=4,'zl'=4,'c'=2,'x'=4,'zh'=4] {'zh'}, dimensions={0}, use_global_device_ids=true | all-gather | bytes 737280 | tf_op jit(solution)/shard_map/all_gather | solution.py:32
  36.8 26.0 %all-gather.1 = bf16[8,48,768]{2,1,0:T(8,128)(2,1)} all-gather(bf16[2,48,768]{2,1,0:T(8,128)(2,1)S(1)} %get-tuple-element.18), channel_id=3, replica_groups=mesh['y'=4,'zl'=4,'c'=2,'x'=4,'zh'=4] {'zh'}, dimensions={0}, use_global_device_ids=true | all-gather | bytes 737280 | tf_op jit(solution)/shard_map/all_gather | solution.py:32
  62.7 10.8 %all-to-all-start.2 = ((bf16[8,48,768]{2,1,0:T(8,128)(2,1)}), bf16[8,48,768]{2,1,0:T(8,128)(2,1)S(1)}, u32[]{:S(2)}, u32[]{:S(2)}) async-start(bf16[8,48,768]{2,1,0:T(8,128)(2,1)} %bitcast.12), calls=%async_computation.2 | async-start | bytes 1179648 | tf_op jit(solution)/shard_map/all_to_all | solution.py:63
  73.6 0.1 broadcast_in_dim.26.clone
  73.7 0.2 gt.29
  73.8 0.1 gt.28
  74.0 0.1 copy.35
  74.1 0.1 eq.54
  74.2 0.1 eq.50
  74.4 1.7 reduce-window.6
  76.1 0.3 slice_reduce_fusion
  76.4 0.1 fusion.20
  76.5 0.1 reduce_sum.30
  76.7 0.1 copy.40
  76.7 6.9 %all-to-all-done.2 = bf16[8,48,768]{2,1,0:T(8,128)(2,1)S(1)} async-done(((bf16[8,48,768]{2,1,0:T(8,128)(2,1)}), bf16[8,48,768]{2,1,0:T(8,128)(2,1)S(1)}, u32[]{:S(2)}, u32[]{:S(2)}) %all-to-all-start.2) | async-done | bytes 589856 | tf_op jit(solution)/shard_map/all_to_all | solution.py:63
  83.6 4.4 %all-to-all-start.1 = ((bf16[8,48,768]{2,1,0:T(8,128)(2,1)}), bf16[8,48,768]{2,1,0:T(8,128)(2,1)S(1)}, u32[]{:S(2)}, u32[]{:S(2)}) async-start(bf16[8,48,768]{2,1,0:T(8,128)(2,1)} %bitcast.6), calls=%async_computation.1 | async-start | bytes 1179648 | tf_op jit(solution)/shard_map/all_to_all | solution.py:63
  88.0 0.4 fusion.1
  88.4 2.2 convolution_convert_fusion
  90.6 7.5 %all-to-all-done.1 = bf16[8,48,768]{2,1,0:T(8,128)(2,1)S(1)} async-done(((bf16[8,48,768]{2,1,0:T(8,128)(2,1)}), bf16[8,48,768]{2,1,0:T(8,128)(2,1)S(1)}, u32[]{:S(2)}, u32[]{:S(2)}) %all-to-all-start.1) | async-done | bytes 589856 | tf_op jit(solution)/shard_map/all_to_all | solution.py:63
  98.1 6.1 %all-to-all-start = ((bf16[32,24,1536]{2,1,0:T(8,128)(2,1)}), bf16[32,24,1536]{2,1,0:T(8,128)(2,1)}, u32[]{:S(2)}, u32[]{:S(2)}) async-start(bf16[32,24,1536]{2,1,0:T(8,128)(2,1)} %bitcast.4), calls=%async_computation | async-start | bytes 4718592 | tf_op jit(solution)/shard_map/all_to_all | solution.py:52
  104.2 0.9 fusion.26
  105.0 1.9 collective-permute-start.6
  106.9 5.5 %collective-permute-start.7 = (bf16[4,48,768]{2,1,0:T(8,128)(2,1)}, bf16[4,48,768]{2,1,0:T(8,128)(2,1)S(1)}, u32[]{:S(2)}, u32[]{:S(2)}) collective-permute-start(bf16[4,48,768]{2,1,0:T(8,128)(2,1)} %get-tuple-element.30), channel_id=1, source_target_pairs={{0,67},{32,99},{64,0},{96,32},{1,64},{33,96},{65,1},{97,33},{2,65}... | collective-permute-start | bytes 884744 | tf_op jit(solution)/shard_map/ppermute | solution.py:57
  112.4 1.9 collective-permute-start.4
  114.4 0.8 fusion.27
  115.1 1.9 collective-permute-start.2
  117.1 5.5 %collective-permute-start.3 = (bf16[4,48,768]{2,1,0:T(8,128)(2,1)S(1)}, bf16[4,48,768]{2,1,0:T(8,128)(2,1)S(1)}, u32[]{:S(2)}, u32[]{:S(2)}) collective-permute-start(bf16[4,48,768]{2,1,0:T(8,128)(2,1)S(1)} %get-tuple-element.32), channel_id=1, source_target_pairs={{0,67},{32,99},{64,0},{96,32},{1,64},{33,96},{65,1},{97,33},{2,65}... | collective-permute-start | bytes 884744 | tf_op jit(solution)/shard_map/ppermute | solution.py:57
  122.6 0.0 collective-permute-done.6
  122.6 2.2 %collective-permute-start = (bf16[8,48,768]{2,1,0:T(8,128)(2,1)S(1)}, bf16[8,48,768]{2,1,0:T(8,128)(2,1)S(1)}, u32[]{:S(2)}, u32[]{:S(2)}) collective-permute-start(bf16[8,48,768]{2,1,0:T(8,128)(2,1)S(1)} %all-to-all-done.1), channel_id=1, source_target_pairs={{0,32},{32,64},{64,96},{96,1},{1,33},{33,65},{65,97},{97,2},{2,34}... | collective-permute-start | bytes 1769480 | tf_op jit(solution)/shard_map/ppermute | solution.py:57
  124.8 1.7 broadcast.76.clone.1
  126.5 0.9 constant_dynamic-update-slice_fusion.3
  127.3 0.0 collective-permute-done.7
  127.3 6.0 %collective-permute-start.5 = (bf16[8,48,768]{2,1,0:T(8,128)(2,1)S(1)}, bf16[8,48,768]{2,1,0:T(8,128)(2,1)S(1)}, u32[]{:S(2)}, u32[]{:S(2)}) collective-permute-start(bf16[8,48,768]{2,1,0:T(8,128)(2,1)S(1)} %all-to-all-done.2), channel_id=1, source_target_pairs={{0,99},{32,0},{64,32},{96,64},{1,96},{33,1},{65,33},{97,65},{2,97}... | collective-permute-start | bytes 1769480 | tf_op jit(solution)/shard_map/ppermute | solution.py:57
  133.4 1.7 broadcast.76.clone
  135.1 0.9 constant_dynamic-update-slice_fusion.7
  135.9 9.9 %collective-permute-done.2 = bf16[4,48,768]{2,1,0:T(8,128)(2,1)S(1)} collective-permute-done((bf16[4,48,768]{2,1,0:T(8,128)(2,1)}, bf16[4,48,768]{2,1,0:T(8,128)(2,1)S(1)}, u32[]{:S(2)}, u32[]{:S(2)}) %collective-permute-start.2) | collective-permute-done | bytes 294944 | tf_op jit(solution)/shard_map/ppermute | solution.py:57
  145.8 1.9 collective-permute-start.1
  147.7 0.1 pad_maximum_fusion.1
  147.8 0.0 collective-permute-done.3
  147.8 0.1 pad_maximum_fusion
  147.9 0.0 collective-permute-done.4
  147.9 0.9 constant_dynamic-update-slice_fusion.2
  148.8 10.4 %collective-permute-done = bf16[8,48,768]{2,1,0:T(8,128)(2,1)S(1)} collective-permute-done((bf16[8,48,768]{2,1,0:T(8,128)(2,1)S(1)}, bf16[8,48,768]{2,1,0:T(8,128)(2,1)S(1)}, u32[]{:S(2)}, u32[]{:S(2)}) %collective-permute-start) | collective-permute-done | bytes 589856 | tf_op jit(solution)/shard_map/ppermute | solution.py:57
  159.2 0.9 constant_dynamic-update-slice_fusion.6
  160.1 0.0 collective-permute-done.5
  160.1 0.9 constant_dynamic-update-slice_fusion.1
  160.9 0.9 collective-permute-done.1
  161.8 0.9 constant_dynamic-update-slice_fusion.5
  162.7 0.9 constant_dynamic-update-slice_fusion
  163.6 0.9 constant_dynamic-update-slice_fusion.4
  164.5 0.0 all-to-all-done
  164.5 3.5 %fusion.2 = f32[768,512]{1,0:T(8,128)S(1)} fusion(bf16[768,1536]{1,0:T(8,128)(2,1)} %bitcast.5, bf16[1536,768]{1,0:T(8,128)(2,1)} %bitcast.17), kind=kOutput, calls=%fused_computation.8 | convolution fusion | flops 1207959552 | bytes 5505024 | tf_op jit(solution)/shard_map/dot_general | solution.py:80
  168.0 3.5 %fusion.4 = f32[768,512]{1,0:T(8,128)S(1)} fusion(bf16[768,1536]{1,0:T(8,128)(2,1)} %bitcast.5, bf16[1536,768]{1,0:T(8,128)(2,1)} %bitcast.11), kind=kOutput, calls=%fused_computation.10 | convolution fusion | flops 1207959552 | bytes 5505024 | tf_op jit(solution)/shard_map/dot_general | solution.py:80
  171.4 2.0 fusion.8
  173.4 3.4 %add_convert_fusion = bf16[768,1536]{1,0:T(8,128)(2,1)} fusion(f32[768,1536]{1,0:T(8,128)S(1)} %fusion.8, bf16[1536,768]{1,0:T(8,128)(2,1)} %bitcast.17, f32[768,512]{1,0:T(8,128)S(1)} %fusion.2), kind=kOutput, calls=%fused_computation | convolution fusion | flops 607518720 | bytes 9437184 | tf_op jit(solution)/shard_map/dot_general | solution.py:82
  176.8 9.2 %all-to-all-start.3 = ((bf16[32,24,1536]{2,1,0:T(8,128)(2,1)}), bf16[32,24,1536]{2,1,0:T(8,128)(2,1)S(1)}, u32[]{:S(2)}, u32[]{:S(2)}) async-start(bf16[32,24,1536]{2,1,0:T(8,128)(2,1)} %bitcast.48), calls=%async_computation.3 | async-start | bytes 4718592 | tf_op jit(solution)/shard_map/all_to_all | solution.py:87
  186.0 0.3 select_reduce_fusion
  186.3 30.8 %all-to-all-done.3 = bf16[32,24,1536]{2,1,0:T(8,128)(2,1)S(1)} async-done(((bf16[32,24,1536]{2,1,0:T(8,128)(2,1)}), bf16[32,24,1536]{2,1,0:T(8,128)(2,1)S(1)}, u32[]{:S(2)}, u32[]{:S(2)}) %all-to-all-start.3) | async-done | bytes 2359328 | tf_op jit(solution)/shard_map/all_to_all | solution.py:87
  217.1 0.5 fusion.17
  217.6 1.2 fusion
  (17 shorter events, 0.1 us)
Async XLA Ops:
  0.0 88.4 %copy-start = (bf16[128,1536]{1,0:T(8,128)(2,1)S(1)}, bf16[128,1536]{1,0:T(8,128)(2,1)}, u32[]{:S(2)}) copy-start(bf16[128,1536]{1,0:T(8,128)(2,1)} %param.7) | copy-start | bytes 1179652
  0.0 74.0 %copy-start.1 = (s32[128,6]{0,1:T(8,128)S(1)}, s32[128,6]{0,1:T(8,128)}, u32[]{:S(2)}) copy-start(s32[128,6]{0,1:T(8,128)} %param.11) | copy-start | bytes 9220
  0.0 73.5 %copy-start.3 = (s32[128]{0:T(128)S(1)}, s32[128]{0:T(128)}, u32[]{:S(2)}) copy-start(s32[128]{0:T(128)} %param.13) | copy-start | bytes 1540
  62.7 20.9 %all-to-all-start.2 = ((bf16[8,48,768]{2,1,0:T(8,128)(2,1)}), bf16[8,48,768]{2,1,0:T(8,128)(2,1)S(1)}, u32[]{:S(2)}, u32[]{:S(2)}) async-start(bf16[8,48,768]{2,1,0:T(8,128)(2,1)} %bitcast.12), calls=%async_computation.2 | async-start | bytes 1179648 | tf_op jit(solution)/shard_map/all_to_all | solution.py:63
  83.6 14.5 %all-to-all-start.1 = ((bf16[8,48,768]{2,1,0:T(8,128)(2,1)}), bf16[8,48,768]{2,1,0:T(8,128)(2,1)S(1)}, u32[]{:S(2)}, u32[]{:S(2)}) async-start(bf16[8,48,768]{2,1,0:T(8,128)(2,1)} %bitcast.6), calls=%async_computation.1 | async-start | bytes 1179648 | tf_op jit(solution)/shard_map/all_to_all | solution.py:63
  98.1 66.4 %all-to-all-start = ((bf16[32,24,1536]{2,1,0:T(8,128)(2,1)}), bf16[32,24,1536]{2,1,0:T(8,128)(2,1)}, u32[]{:S(2)}, u32[]{:S(2)}) async-start(bf16[32,24,1536]{2,1,0:T(8,128)(2,1)} %bitcast.4), calls=%async_computation | async-start | bytes 4718592 | tf_op jit(solution)/shard_map/all_to_all | solution.py:52
  105.0 17.5 %collective-permute-start.6 = (bf16[4,48,768]{2,1,0:T(8,128)(2,1)}, bf16[4,48,768]{2,1,0:T(8,128)(2,1)S(1)}, u32[]{:S(2)}, u32[]{:S(2)}) collective-permute-start(bf16[4,48,768]{2,1,0:T(8,128)(2,1)} %get-tuple-element.29), channel_id=1, source_target_pairs={{0,64},{32,96},{64,1},{96,33},{1,65},{33,97},{65,2},{97,34},{2,66}... | collective-permute-start | bytes 884744 | tf_op jit(solution)/shard_map/ppermute | solution.py:57
  106.9 20.4 %collective-permute-start.7 = (bf16[4,48,768]{2,1,0:T(8,128)(2,1)}, bf16[4,48,768]{2,1,0:T(8,128)(2,1)S(1)}, u32[]{:S(2)}, u32[]{:S(2)}) collective-permute-start(bf16[4,48,768]{2,1,0:T(8,128)(2,1)} %get-tuple-element.30), channel_id=1, source_target_pairs={{0,67},{32,99},{64,0},{96,32},{1,64},{33,96},{65,1},{97,33},{2,65}... | collective-permute-start | bytes 884744 | tf_op jit(solution)/shard_map/ppermute | solution.py:57
  112.4 35.5 %collective-permute-start.4 = (bf16[8,48,768]{2,1,0:T(8,128)(2,1)S(1)}, bf16[8,48,768]{2,1,0:T(8,128)(2,1)S(1)}, u32[]{:S(2)}, u32[]{:S(2)}) collective-permute-start(bf16[8,48,768]{2,1,0:T(8,128)(2,1)S(1)} %all-to-all-done.2), channel_id=1, source_target_pairs={{0,32},{32,64},{64,96},{96,1},{1,33},{33,65},{65,97},{97,2},{2,34}... | collective-permute-start | bytes 1769480 | tf_op jit(solution)/shard_map/ppermute | solution.py:57
  115.1 30.7 %collective-permute-start.2 = (bf16[4,48,768]{2,1,0:T(8,128)(2,1)}, bf16[4,48,768]{2,1,0:T(8,128)(2,1)S(1)}, u32[]{:S(2)}, u32[]{:S(2)}) collective-permute-start(bf16[4,48,768]{2,1,0:T(8,128)(2,1)} %get-tuple-element.31), channel_id=1, source_target_pairs={{0,64},{32,96},{64,1},{96,33},{1,65},{33,97},{65,2},{97,34},{2,66}... | collective-permute-start | bytes 884744 | tf_op jit(solution)/shard_map/ppermute | solution.py:57
  117.1 30.7 %collective-permute-start.3 = (bf16[4,48,768]{2,1,0:T(8,128)(2,1)S(1)}, bf16[4,48,768]{2,1,0:T(8,128)(2,1)S(1)}, u32[]{:S(2)}, u32[]{:S(2)}) collective-permute-start(bf16[4,48,768]{2,1,0:T(8,128)(2,1)S(1)} %get-tuple-element.32), channel_id=1, source_target_pairs={{0,67},{32,99},{64,0},{96,32},{1,64},{33,96},{65,1},{97,33},{2,65}... | collective-permute-start | bytes 884744 | tf_op jit(solution)/shard_map/ppermute | solution.py:57
  122.6 36.6 %collective-permute-start = (bf16[8,48,768]{2,1,0:T(8,128)(2,1)S(1)}, bf16[8,48,768]{2,1,0:T(8,128)(2,1)S(1)}, u32[]{:S(2)}, u32[]{:S(2)}) collective-permute-start(bf16[8,48,768]{2,1,0:T(8,128)(2,1)S(1)} %all-to-all-done.1), channel_id=1, source_target_pairs={{0,32},{32,64},{64,96},{96,1},{1,33},{33,65},{65,97},{97,2},{2,34}... | collective-permute-start | bytes 1769480 | tf_op jit(solution)/shard_map/ppermute | solution.py:57
  127.3 32.7 %collective-permute-start.5 = (bf16[8,48,768]{2,1,0:T(8,128)(2,1)S(1)}, bf16[8,48,768]{2,1,0:T(8,128)(2,1)S(1)}, u32[]{:S(2)}, u32[]{:S(2)}) collective-permute-start(bf16[8,48,768]{2,1,0:T(8,128)(2,1)S(1)} %all-to-all-done.2), channel_id=1, source_target_pairs={{0,99},{32,0},{64,32},{96,64},{1,96},{33,1},{65,33},{97,65},{2,97}... | collective-permute-start | bytes 1769480 | tf_op jit(solution)/shard_map/ppermute | solution.py:57
  145.8 16.0 %collective-permute-start.1 = (bf16[8,48,768]{2,1,0:T(8,128)(2,1)S(1)}, bf16[8,48,768]{2,1,0:T(8,128)(2,1)S(1)}, u32[]{:S(2)}, u32[]{:S(2)}) collective-permute-start(bf16[8,48,768]{2,1,0:T(8,128)(2,1)S(1)} %all-to-all-done.1), channel_id=1, source_target_pairs={{0,99},{32,0},{64,32},{96,64},{1,96},{33,1},{65,33},{97,65},{2,97}... | collective-permute-start | bytes 1769480 | tf_op jit(solution)/shard_map/ppermute | solution.py:57
  176.8 9.2 %copy-start.2 = (f32[128,6]{0,1:T(8,128)S(1)}, f32[128,6]{0,1:T(8,128)}, u32[]{:S(2)}) copy-start(f32[128,6]{0,1:T(8,128)} %param.12) | copy-start | bytes 9220
  176.8 40.3 %all-to-all-start.3 = ((bf16[32,24,1536]{2,1,0:T(8,128)(2,1)}), bf16[32,24,1536]{2,1,0:T(8,128)(2,1)S(1)}, u32[]{:S(2)}, u32[]{:S(2)}) async-start(bf16[32,24,1536]{2,1,0:T(8,128)(2,1)} %bitcast.48), calls=%async_computation.3 | async-start | bytes 4718592 | tf_op jit(solution)/shard_map/all_to_all | solution.py:87

commit v10 on v7

--- a/solution.py
+++ b/solution.py
@@ -17,7 +17,7 @@
     capacity = tok_dev * top_count // experts
     total_slots = experts * capacity
 
-    parts = 2
+    parts = 4
     part = hidden_width // parts
     down_t = jnp.swapaxes(down_train, 1, 2)
     slabs = tuple(

time: 208 us -> 264 us (1.27)
  starting transfers between devices: 53.2 us -> 90.4 us
  blocking collectives: 75.7 us -> 101 us
  waiting for transfers between devices: 57.4 us -> 39.7 us
  local copies, waits for them, and re-layouts: 4.24 us -> 10.7 us
  matrix products: 9.74 us -> 13.8 us
    ppermute x8 -> x16, waiting for transfers between devices: 26.6 us -> 0.04 us  [local(): shift = lambda v, k: lax.ppermute(v, ('zl', 'zh'), pairs(k))]
    ppermute x8 -> x16, starting transfers between devices: 30 us -> 53.7 us  [local(): shift = lambda v, k: lax.ppermute(v, ('zl', 'zh'), pairs(k))]
    all_gather x2 -> x4, blocking collectives: 56.6 us -> 76.5 us  [local(): slabs = tuple((lax.all_gather(w, 'zh', axis=0, tiled=False) for w in slabs))]
    all_to_all x1 -> x3, starting transfers between devices: 4.19 us -> 14.3 us  [local(): lax.all_to_all(slab, ('y', 'c'), split_axis=0, concat_axis=0, tiled=True)]
    all_to_all x1 -> x3, waiting for transfers between devices: 0.01 us -> 8.85 us  [local(): lax.all_to_all(slab, ('y', 'c'), split_axis=0, concat_axis=0, tiled=True)]
    all_to_all x1, blocking collectives: 19.1 us -> 24.3 us  [local(): lax.all_to_all(slab, ('y', 'c'), split_axis=0, concat_axis=0, tiled=True)]
    all_to_all x1, starting transfers between devices: 8.48 us -> 11.8 us  [local(): lax.all_to_all(expert_rows, TOKEN_GROUP, split_axis=0, concat_axis=0, til...]
    dynamic_update_slice x8 -> x16, local copies, waits for them, and re-layouts: 0.36 us -> 3.65 us  [local(): full = lax.dynamic_update_index_in_dim(full, quarter, place, axis=1)]
  transfers between devices with their start and end apart: 11 -> 21, of which waited for: 4 -> 3; matrix products, arithmetic and copies ran while one was open for 1% -> 6% of each run, Pallas kernels for 0% -> 0%
where the time goes in v10:
time: 264 us; the launch traced here: 263 us
  blocking collectives  101 us (38%)
  starting transfers between devices  90.4 us (34%)
  waiting for transfers between devices  39.7 us (15%)
  matrix products  13.8 us (5%)
  local copies, waits for them, and re-layouts  10.7 us (4%)
  other arithmetic  6.66 us (3%)
    all_gather x4, blocking collectives, local(): slabs = tuple((lax.all_gather(w, 'zh', axis=0, tiled=False) for w in slabs))  76.5 us
    ppermute x16, starting transfers between devices, local(): shift = lambda v, k: lax.ppermute(v, ('zl', 'zh'), pairs(k))  53.7 us
    all_to_all x1, waiting for transfers between devices, local(): lax.all_to_all(expert_rows, TOKEN_GROUP, split_axis=0, concat_axis=0, til...  30.8 us
    all_to_all x1, blocking collectives, local(): lax.all_to_all(slab, ('y', 'c'), split_axis=0, concat_axis=0, tiled=True)  24.3 us
    all_to_all x3, starting transfers between devices, local(): lax.all_to_all(slab, ('y', 'c'), split_axis=0, concat_axis=0, tiled=True)  14.3 us
    all_to_all x1, starting transfers between devices, local(): lax.all_to_all(expert_rows, TOKEN_GROUP, split_axis=0, concat_axis=0, til...  11.8 us
    all_to_all x1, starting transfers between devices, local(): lax.all_to_all(outgoing, TOKEN_GROUP, split_axis=0, concat_axis=0, tiled=...  10.5 us
    all_to_all x3, waiting for transfers between devices, local(): lax.all_to_all(slab, ('y', 'c'), split_axis=0, concat_axis=0, tiled=True)  8.85 us
  transfers between devices with their start and end apart: 21, of which 3 were waited for; matrix products, arithmetic and copies ran while one was open for 6% of the time, Pallas kernels for 0%

profile of v10, /device:TPU:1, one launch (start us, length us, event | category | flops | bytes accessed | tf_op | source)
XLA Modules:
  0.0 262.7 jit_solution(8547667503947006429)
XLA Ops:
  0.0 1.0 convert.30
  1.1 0.9 convert.31
  2.0 0.9 convert_bitcast_fusion
  3.2 0.2 gt.29
  3.3 0.1 gt.28
  3.5 0.1 copy.35
  3.6 0.1 eq.54
  3.7 0.1 eq.50
  3.9 1.7 reduce-window.6
  5.7 0.3 slice_reduce_fusion
  6.1 0.1 reduce_sum.30
  6.3 0.4 fusion.1
  6.7 2.2 convolution_convert_fusion
  8.9 10.5 %all-to-all-start = ((bf16[32,24,1536]{2,1,0:T(8,128)(2,1)}), bf16[32,24,1536]{2,1,0:T(8,128)(2,1)S(1)}, u32[]{:S(2)}, u32[]{:S(2)}) async-start(bf16[32,24,1536]{2,1,0:T(8,128)(2,1)} %bitcast.2), calls=%async_computation | async-start | bytes 4718592 | tf_op jit(solution)/shard_map/all_to_all | solution.py:49
  19.5 23.4 %all-gather = bf16[8,48,384]{2,1,0:T(8,128)(2,1)} all-gather(bf16[2,48,384]{2,1,0:T(8,128)(2,1)S(1)} %get-tuple-element.22), channel_id=2, replica_groups=mesh['y'=4,'zl'=4,'c'=2,'x'=4,'zh'=4] {'zh'}, dimensions={0}, use_global_device_ids=true | all-gather | bytes 368640 | tf_op jit(solution)/shard_map/all_gather | solution.py:32
  42.9 19.1 %all-gather.1 = bf16[8,48,384]{2,1,0:T(8,128)(2,1)} all-gather(bf16[2,48,384]{2,1,0:T(8,128)(2,1)S(1)} %get-tuple-element.23), channel_id=3, replica_groups=mesh['y'=4,'zl'=4,'c'=2,'x'=4,'zh'=4] {'zh'}, dimensions={0}, use_global_device_ids=true | all-gather | bytes 368640 | tf_op jit(solution)/shard_map/all_gather | solution.py:32
  62.0 16.5 %all-gather.2 = bf16[8,48,384]{2,1,0:T(8,128)(2,1)} all-gather(bf16[2,48,384]{2,1,0:T(8,128)(2,1)S(1)} %get-tuple-element.24), channel_id=4, replica_groups=mesh['y'=4,'zl'=4,'c'=2,'x'=4,'zh'=4] {'zh'}, dimensions={0}, use_global_device_ids=true | all-gather | bytes 368640 | tf_op jit(solution)/shard_map/all_gather | solution.py:32
  78.4 17.5 %all-gather.3 = bf16[8,48,384]{2,1,0:T(8,128)(2,1)S(1)} all-gather(bf16[2,48,384]{2,1,0:T(8,128)(2,1)S(1)} %get-tuple-element.25), channel_id=5, replica_groups=mesh['y'=4,'zl'=4,'c'=2,'x'=4,'zh'=4] {'zh'}, dimensions={0}, use_global_device_ids=true | all-gather | bytes 368640 | tf_op jit(solution)/shard_map/all_gather | solution.py:32
  96.0 1.4 copy-done.1
  97.4 24.3 %all_to_all.44 = bf16[8,48,384]{2,1,0:T(8,128)(2,1)S(1)} all-to-all(bf16[8,48,384]{2,1,0:T(8,128)(2,1)S(1)} %all-gather.3), channel_id=1, replica_groups=mesh['y'=4,'zl'=4,'c'=2,'x'=4,'zh'=4] {'y','c'}, dimensions={0} | all-to-all | bytes 589824 | tf_op jit(solution)/shard_map/all_to_all | solution.py:61
  121.7 3.9 %all-to-all-start.2 = ((bf16[8,48,384]{2,1,0:T(8,128)(2,1)}), bf16[8,48,384]{2,1,0:T(8,128)(2,1)S(1)}, u32[]{:S(2)}, u32[]{:S(2)}) async-start(bf16[8,48,384]{2,1,0:T(8,128)(2,1)} %bitcast.14), calls=%async_computation.2 | async-start | bytes 589824 | tf_op jit(solution)/shard_map/all_to_all | solution.py:61
  125.6 6.8 %all-to-all-done.2 = bf16[8,48,384]{2,1,0:T(8,128)(2,1)S(1)} async-done(((bf16[8,48,384]{2,1,0:T(8,128)(2,1)}), bf16[8,48,384]{2,1,0:T(8,128)(2,1)S(1)}, u32[]{:S(2)}, u32[]{:S(2)}) %all-to-all-start.2) | async-done | bytes 294944 | tf_op jit(solution)/shard_map/all_to_all | solution.py:61
  132.4 4.4 %all-to-all-start.1 = ((bf16[8,48,384]{2,1,0:T(8,128)(2,1)}), bf16[8,48,384]{2,1,0:T(8,128)(2,1)S(1)}, u32[]{:S(2)}, u32[]{:S(2)}) async-start(bf16[8,48,384]{2,1,0:T(8,128)(2,1)} %bitcast.8), calls=%async_computation.1 | async-start | bytes 589824 | tf_op jit(solution)/shard_map/all_to_all | solution.py:61
  136.8 0.8 fusion.42
  137.6 1.9 collective-permute-start.14
  139.5 5.5 %collective-permute-start.15 = (bf16[4,48,384]{2,1,0:T(8,128)(2,1)}, bf16[4,48,384]{2,1,0:T(8,128)(2,1)}, u32[]{:S(2)}, u32[]{:S(2)}) collective-permute-start(bf16[4,48,384]{2,1,0:T(8,128)(2,1)} %get-tuple-element.32), channel_id=1, source_target_pairs={{0,67},{32,99},{64,0},{96,32},{1,64},{33,96},{65,1},{97,33},{2,65}... | collective-permute-start | bytes 442376 | tf_op jit(solution)/shard_map/ppermute | solution.py:55
  145.0 0.7 fusion.43
  145.7 1.9 collective-permute-start.6
  147.6 5.5 %collective-permute-start.7 = (bf16[4,48,384]{2,1,0:T(8,128)(2,1)S(1)}, bf16[4,48,384]{2,1,0:T(8,128)(2,1)S(1)}, u32[]{:S(2)}, u32[]{:S(2)}) collective-permute-start(bf16[4,48,384]{2,1,0:T(8,128)(2,1)S(1)} %get-tuple-element.34), channel_id=1, source_target_pairs={{0,67},{32,99},{64,0},{96,32},{1,64},{33,96},{65,1},{97,33},{2,65}... | collective-permute-start | bytes 442376 | tf_op jit(solution)/shard_map/ppermute | solution.py:55
  153.1 6.0 %all-to-all-start.3 = ((bf16[8,48,384]{2,1,0:T(8,128)(2,1)}), bf16[8,48,384]{2,1,0:T(8,128)(2,1)S(1)}, u32[]{:S(2)}, u32[]{:S(2)}) async-start(bf16[8,48,384]{2,1,0:T(8,128)(2,1)} %bitcast.20), calls=%async_computation.3 | async-start | bytes 589824 | tf_op jit(solution)/shard_map/all_to_all | solution.py:61
  159.0 0.7 fusion.44
  159.8 1.9 collective-permute-start.2
  161.8 1.2 broadcast.78.clone.2
  163.0 0.8 constant_dynamic-update-slice_fusion.11
  163.8 2.0 all-to-all-done.3
  166.2 0.7 copy-done.3
  166.9 3.4 %collective-permute-start.3 = (bf16[4,48,384]{2,1,0:T(8,128)(2,1)S(1)}, bf16[4,48,384]{2,1,0:T(8,128)(2,1)S(1)}, u32[]{:S(2)}, u32[]{:S(2)}) collective-permute-start(bf16[4,48,384]{2,1,0:T(8,128)(2,1)S(1)} %copy-done.3), channel_id=1, source_target_pairs={{0,67},{32,99},{64,0},{96,32},{1,64},{33,96},{65,1},{97,33},{2,65}... | collective-permute-start | bytes 442376 | tf_op jit(solution)/shard_map/ppermute | solution.py:55
  170.3 2.8 %collective-permute-start.10 = (bf16[4,48,384]{2,1,0:T(8,128)(2,1)S(1)}, bf16[4,48,384]{2,1,0:T(8,128)(2,1)S(1)}, u32[]{:S(2)}, u32[]{:S(2)}) collective-permute-start(bf16[4,48,384]{2,1,0:T(8,128)(2,1)S(1)} %get-tuple-element.37), channel_id=1, source_target_pairs={{0,64},{32,96},{64,1},{96,33},{1,65},{33,97},{65,2},{97,34},{2,66}... | collective-permute-start | bytes 442376 | tf_op jit(solution)/shard_map/ppermute | solution.py:55
  173.1 0.9 pad_maximum_fusion.3
  174.0 4.6 %collective-permute-start.11 = (bf16[4,48,384]{2,1,0:T(8,128)(2,1)S(1)}, bf16[4,48,384]{2,1,0:T(8,128)(2,1)S(1)}, u32[]{:S(2)}, u32[]{:S(2)}) collective-permute-start(bf16[4,48,384]{2,1,0:T(8,128)(2,1)S(1)} %get-tuple-element.38), channel_id=1, source_target_pairs={{0,67},{32,99},{64,0},{96,32},{1,64},{33,96},{65,1},{97,33},{2,65}... | collective-permute-start | bytes 442376 | tf_op jit(solution)/shard_map/ppermute | solution.py:55
  178.7 1.9 collective-permute-start.12
  180.7 4.6 %collective-permute-start.13 = (bf16[8,48,384]{2,1,0:T(8,128)(2,1)S(1)}, bf16[8,48,384]{2,1,0:T(8,128)(2,1)S(1)}, u32[]{:S(2)}, u32[]{:S(2)}) collective-permute-start(bf16[8,48,384]{2,1,0:T(8,128)(2,1)S(1)} %all_to_all.44), channel_id=1, source_target_pairs={{0,99},{32,0},{64,32},{96,64},{1,96},{33,1},{65,33},{97,65},{2,97}... | collective-permute-start | bytes 884744 | tf_op jit(solution)/shard_map/ppermute | solution.py:55
  185.2 1.9 collective-permute-start.4
  187.2 4.6 %collective-permute-start.5 = (bf16[8,48,384]{2,1,0:T(8,128)(2,1)S(1)}, bf16[8,48,384]{2,1,0:T(8,128)(2,1)S(1)}, u32[]{:S(2)}, u32[]{:S(2)}) collective-permute-start(bf16[8,48,384]{2,1,0:T(8,128)(2,1)S(1)} %all-to-all-done.2), channel_id=1, source_target_pairs={{0,99},{32,0},{64,32},{96,64},{1,96},{33,1},{65,33},{97,65},{2,97}... | collective-permute-start | bytes 884744 | tf_op jit(solution)/shard_map/ppermute | solution.py:55
  191.8 1.9 collective-permute-start
  193.8 4.6 %collective-permute-start.1 = (bf16[8,48,384]{2,1,0:T(8,128)(2,1)S(1)}, bf16[8,48,384]{2,1,0:T(8,128)(2,1)S(1)}, u32[]{:S(2)}, u32[]{:S(2)}) collective-permute-start(bf16[8,48,384]{2,1,0:T(8,128)(2,1)S(1)} %all-to-all-done.1), channel_id=1, source_target_pairs={{0,99},{32,0},{64,32},{96,64},{1,96},{33,1},{65,33},{97,65},{2,97}... | collective-permute-start | bytes 884744 | tf_op jit(solution)/shard_map/ppermute | solution.py:55
  198.5 2.1 collective-permute-start.8
  200.5 0.8 constant_dynamic-update-slice_fusion.10
  201.3 4.7 %collective-permute-start.9 = (bf16[8,48,384]{2,1,0:T(8,128)(2,1)S(1)}, bf16[8,48,384]{2,1,0:T(8,128)(2,1)S(1)}, u32[]{:S(2)}, u32[]{:S(2)}) collective-permute-start(bf16[8,48,384]{2,1,0:T(8,128)(2,1)S(1)} %all-to-all-done.3), channel_id=1, source_target_pairs={{0,99},{32,0},{64,32},{96,64},{1,96},{33,1},{65,33},{97,65},{2,97}... | collective-permute-start | bytes 884744 | tf_op jit(solution)/shard_map/ppermute | solution.py:55
  206.0 0.8 constant_dynamic-update-slice_fusion.9
  206.8 0.7 constant_dynamic-update-slice_fusion.8
  207.5 1.9 fusion.6
  209.5 1.8 fusion.16
  211.4 0.8 fusion.8
  212.4 0.8 fusion.19
  213.2 0.8 fusion.2
  214.1 0.8 fusion.4
  214.9 0.8 fusion.13
  215.7 2.3 add_convert_fusion
  218.0 11.8 %all-to-all-start.5 = ((bf16[32,24,1536]{2,1,0:T(8,128)(2,1)}), bf16[32,24,1536]{2,1,0:T(8,128)(2,1)S(1)}, u32[]{:S(2)}, u32[]{:S(2)}) async-start(bf16[32,24,1536]{2,1,0:T(8,128)(2,1)} %bitcast.64), calls=%async_computation.5 | async-start | bytes 4718592 | tf_op jit(solution)/shard_map/all_to_all | solution.py:85
  229.9 0.3 select_reduce_fusion
  230.2 30.8 %all-to-all-done.5 = bf16[32,24,1536]{2,1,0:T(8,128)(2,1)S(1)} async-done(((bf16[32,24,1536]{2,1,0:T(8,128)(2,1)}), bf16[32,24,1536]{2,1,0:T(8,128)(2,1)S(1)}, u32[]{:S(2)}, u32[]{:S(2)}) %all-to-all-start.5) | async-done | bytes 2359328 | tf_op jit(solution)/shard_map/all_to_all | solution.py:85
  261.0 0.5 fusion.27
  261.5 1.2 fusion
  (63 shorter events, 1.6 us)
Async XLA Ops:
  0.0 6.7 %copy-start = (bf16[128,1536]{1,0:T(8,128)(2,1)S(1)}, bf16[128,1536]{1,0:T(8,128)(2,1)}, u32[]{:S(2)}) copy-start(bf16[128,1536]{1,0:T(8,128)(2,1)} %param.7) | copy-start | bytes 1179652
  0.0 3.5 %copy-start.4 = (s32[128,6]{0,1:T(8,128)S(1)}, s32[128,6]{0,1:T(8,128)}, u32[]{:S(2)}) copy-start(s32[128,6]{0,1:T(8,128)} %param.11) | copy-start | bytes 9220
  0.0 3.1 %copy-start.6 = (s32[128]{0:T(128)S(1)}, s32[128]{0:T(128)}, u32[]{:S(2)}) copy-start(s32[128]{0:T(128)} %param.13) | copy-start | bytes 1540
  8.9 87.1 %all-to-all-start = ((bf16[32,24,1536]{2,1,0:T(8,128)(2,1)}), bf16[32,24,1536]{2,1,0:T(8,128)(2,1)S(1)}, u32[]{:S(2)}, u32[]{:S(2)}) async-start(bf16[32,24,1536]{2,1,0:T(8,128)(2,1)} %bitcast.2), calls=%async_computation | async-start | bytes 4718592 | tf_op jit(solution)/shard_map/all_to_all | solution.py:49
  96.0 1.4 copy-start.1
  121.7 10.7 %all-to-all-start.2 = ((bf16[8,48,384]{2,1,0:T(8,128)(2,1)}), bf16[8,48,384]{2,1,0:T(8,128)(2,1)S(1)}, u32[]{:S(2)}, u32[]{:S(2)}) async-start(bf16[8,48,384]{2,1,0:T(8,128)(2,1)} %bitcast.14), calls=%async_computation.2 | async-start | bytes 589824 | tf_op jit(solution)/shard_map/all_to_all | solution.py:61
  132.4 20.7 %all-to-all-start.1 = ((bf16[8,48,384]{2,1,0:T(8,128)(2,1)}), bf16[8,48,384]{2,1,0:T(8,128)(2,1)S(1)}, u32[]{:S(2)}, u32[]{:S(2)}) async-start(bf16[8,48,384]{2,1,0:T(8,128)(2,1)} %bitcast.8), calls=%async_computation.1 | async-start | bytes 589824 | tf_op jit(solution)/shard_map/all_to_all | solution.py:61
  137.6 28.6 %collective-permute-start.14 = (bf16[4,48,384]{2,1,0:T(8,128)(2,1)}, bf16[4,48,384]{2,1,0:T(8,128)(2,1)S(1)}, u32[]{:S(2)}, u32[]{:S(2)}) collective-permute-start(bf16[4,48,384]{2,1,0:T(8,128)(2,1)} %get-tuple-element.31), channel_id=1, source_target_pairs={{0,64},{32,96},{64,1},{96,33},{1,65},{33,97},{65,2},{97,34},{2,66}... | collective-permute-start | bytes 442376 | tf_op jit(solution)/shard_map/ppermute | solution.py:55
  139.5 30.8 %collective-permute-start.15 = (bf16[4,48,384]{2,1,0:T(8,128)(2,1)}, bf16[4,48,384]{2,1,0:T(8,128)(2,1)}, u32[]{:S(2)}, u32[]{:S(2)}) collective-permute-start(bf16[4,48,384]{2,1,0:T(8,128)(2,1)} %get-tuple-element.32), channel_id=1, source_target_pairs={{0,67},{32,99},{64,0},{96,32},{1,64},{33,96},{65,1},{97,33},{2,65}... | collective-permute-start | bytes 442376 | tf_op jit(solution)/shard_map/ppermute | solution.py:55
  145.7 28.3 %collective-permute-start.6 = (bf16[4,48,384]{2,1,0:T(8,128)(2,1)}, bf16[4,48,384]{2,1,0:T(8,128)(2,1)S(1)}, u32[]{:S(2)}, u32[]{:S(2)}) collective-permute-start(bf16[4,48,384]{2,1,0:T(8,128)(2,1)} %get-tuple-element.33), channel_id=1, source_target_pairs={{0,64},{32,96},{64,1},{96,33},{1,65},{33,97},{65,2},{97,34},{2,66}... | collective-permute-start | bytes 442376 | tf_op jit(solution)/shard_map/ppermute | solution.py:55
  147.6 31.1 %collective-permute-start.7 = (bf16[4,48,384]{2,1,0:T(8,128)(2,1)S(1)}, bf16[4,48,384]{2,1,0:T(8,128)(2,1)S(1)}, u32[]{:S(2)}, u32[]{:S(2)}) collective-permute-start(bf16[4,48,384]{2,1,0:T(8,128)(2,1)S(1)} %get-tuple-element.34), channel_id=1, source_target_pairs={{0,67},{32,99},{64,0},{96,32},{1,64},{33,96},{65,1},{97,33},{2,65}... | collective-permute-start | bytes 442376 | tf_op jit(solution)/shard_map/ppermute | solution.py:55
  153.1 12.7 %all-to-all-start.3 = ((bf16[8,48,384]{2,1,0:T(8,128)(2,1)}), bf16[8,48,384]{2,1,0:T(8,128)(2,1)S(1)}, u32[]{:S(2)}, u32[]{:S(2)}) async-start(bf16[8,48,384]{2,1,0:T(8,128)(2,1)} %bitcast.20), calls=%async_computation.3 | async-start | bytes 589824 | tf_op jit(solution)/shard_map/all_to_all | solution.py:61
  159.8 20.9 %collective-permute-start.2 = (bf16[4,48,384]{2,1,0:T(8,128)(2,1)}, bf16[4,48,384]{2,1,0:T(8,128)(2,1)S(1)}, u32[]{:S(2)}, u32[]{:S(2)}) collective-permute-start(bf16[4,48,384]{2,1,0:T(8,128)(2,1)} %get-tuple-element.35), channel_id=1, source_target_pairs={{0,64},{32,96},{64,1},{96,33},{1,65},{33,97},{65,2},{97,34},{2,66}... | collective-permute-start | bytes 442376 | tf_op jit(solution)/shard_map/ppermute | solution.py:55
  166.0 0.9 copy-start.3
  166.9 18.4 %collective-permute-start.3 = (bf16[4,48,384]{2,1,0:T(8,128)(2,1)S(1)}, bf16[4,48,384]{2,1,0:T(8,128)(2,1)S(1)}, u32[]{:S(2)}, u32[]{:S(2)}) collective-permute-start(bf16[4,48,384]{2,1,0:T(8,128)(2,1)S(1)} %copy-done.3), channel_id=1, source_target_pairs={{0,67},{32,99},{64,0},{96,32},{1,64},{33,96},{65,1},{97,33},{2,65}... | collective-permute-start | bytes 442376 | tf_op jit(solution)/shard_map/ppermute | solution.py:55
  170.3 16.9 %collective-permute-start.10 = (bf16[4,48,384]{2,1,0:T(8,128)(2,1)S(1)}, bf16[4,48,384]{2,1,0:T(8,128)(2,1)S(1)}, u32[]{:S(2)}, u32[]{:S(2)}) collective-permute-start(bf16[4,48,384]{2,1,0:T(8,128)(2,1)S(1)} %get-tuple-element.37), channel_id=1, source_target_pairs={{0,64},{32,96},{64,1},{96,33},{1,65},{33,97},{65,2},{97,34},{2,66}... | collective-permute-start | bytes 442376 | tf_op jit(solution)/shard_map/ppermute | solution.py:55
  174.0 17.8 %collective-permute-start.11 = (bf16[4,48,384]{2,1,0:T(8,128)(2,1)S(1)}, bf16[4,48,384]{2,1,0:T(8,128)(2,1)S(1)}, u32[]{:S(2)}, u32[]{:S(2)}) collective-permute-start(bf16[4,48,384]{2,1,0:T(8,128)(2,1)S(1)} %get-tuple-element.38), channel_id=1, source_target_pairs={{0,67},{32,99},{64,0},{96,32},{1,64},{33,96},{65,1},{97,33},{2,65}... | collective-permute-start | bytes 442376 | tf_op jit(solution)/shard_map/ppermute | solution.py:55
  178.7 15.1 %collective-permute-start.12 = (bf16[8,48,384]{2,1,0:T(8,128)(2,1)S(1)}, bf16[8,48,384]{2,1,0:T(8,128)(2,1)S(1)}, u32[]{:S(2)}, u32[]{:S(2)}) collective-permute-start(bf16[8,48,384]{2,1,0:T(8,128)(2,1)S(1)} %all_to_all.44), channel_id=1, source_target_pairs={{0,32},{32,64},{64,96},{96,1},{1,33},{33,65},{65,97},{97,2},{2,34}... | collective-permute-start | bytes 884744 | tf_op jit(solution)/shard_map/ppermute | solution.py:55
  180.7 31.6 %collective-permute-start.13 = (bf16[8,48,384]{2,1,0:T(8,128)(2,1)S(1)}, bf16[8,48,384]{2,1,0:T(8,128)(2,1)S(1)}, u32[]{:S(2)}, u32[]{:S(2)}) collective-permute-start(bf16[8,48,384]{2,1,0:T(8,128)(2,1)S(1)} %all_to_all.44), channel_id=1, source_target_pairs={{0,99},{32,0},{64,32},{96,64},{1,96},{33,1},{65,33},{97,65},{2,97}... | collective-permute-start | bytes 884744 | tf_op jit(solution)/shard_map/ppermute | solution.py:55
  185.2 13.2 %collective-permute-start.4 = (bf16[8,48,384]{2,1,0:T(8,128)(2,1)S(1)}, bf16[8,48,384]{2,1,0:T(8,128)(2,1)S(1)}, u32[]{:S(2)}, u32[]{:S(2)}) collective-permute-start(bf16[8,48,384]{2,1,0:T(8,128)(2,1)S(1)} %all-to-all-done.2), channel_id=1, source_target_pairs={{0,32},{32,64},{64,96},{96,1},{1,33},{33,65},{65,97},{97,2},{2,34}... | collective-permute-start | bytes 884744 | tf_op jit(solution)/shard_map/ppermute | solution.py:55
  187.2 14.1 %collective-permute-start.5 = (bf16[8,48,384]{2,1,0:T(8,128)(2,1)S(1)}, bf16[8,48,384]{2,1,0:T(8,128)(2,1)S(1)}, u32[]{:S(2)}, u32[]{:S(2)}) collective-permute-start(bf16[8,48,384]{2,1,0:T(8,128)(2,1)S(1)} %all-to-all-done.2), channel_id=1, source_target_pairs={{0,99},{32,0},{64,32},{96,64},{1,96},{33,1},{65,33},{97,65},{2,97}... | collective-permute-start | bytes 884744 | tf_op jit(solution)/shard_map/ppermute | solution.py:55
  191.8 17.6 %collective-permute-start = (bf16[8,48,384]{2,1,0:T(8,128)(2,1)S(1)}, bf16[8,48,384]{2,1,0:T(8,128)(2,1)S(1)}, u32[]{:S(2)}, u32[]{:S(2)}) collective-permute-start(bf16[8,48,384]{2,1,0:T(8,128)(2,1)S(1)} %all-to-all-done.1), channel_id=1, source_target_pairs={{0,32},{32,64},{64,96},{96,1},{1,33},{33,65},{65,97},{97,2},{2,34}... | collective-permute-start | bytes 884744 | tf_op jit(solution)/shard_map/ppermute | solution.py:55
  193.8 17.5 %collective-permute-start.1 = (bf16[8,48,384]{2,1,0:T(8,128)(2,1)S(1)}, bf16[8,48,384]{2,1,0:T(8,128)(2,1)S(1)}, u32[]{:S(2)}, u32[]{:S(2)}) collective-permute-start(bf16[8,48,384]{2,1,0:T(8,128)(2,1)S(1)} %all-to-all-done.1), channel_id=1, source_target_pairs={{0,99},{32,0},{64,32},{96,64},{1,96},{33,1},{65,33},{97,65},{2,97}... | collective-permute-start | bytes 884744 | tf_op jit(solution)/shard_map/ppermute | solution.py:55
  198.4 9.2 %copy-start.2 = (bf16[32,24,1536]{2,1,0:T(8,128)(2,1)S(1)}, bf16[32,24,1536]{2,1,0:T(8,128)(2,1)}, u32[]{:S(2)}) copy-start(bf16[32,24,1536]{2,1,0:T(8,128)(2,1)} %copy-done.1) | copy-start | bytes 7077892
  198.5 14.7 %collective-permute-start.8 = (bf16[8,48,384]{2,1,0:T(8,128)(2,1)S(1)}, bf16[8,48,384]{2,1,0:T(8,128)(2,1)S(1)}, u32[]{:S(2)}, u32[]{:S(2)}) collective-permute-start(bf16[8,48,384]{2,1,0:T(8,128)(2,1)S(1)} %all-to-all-done.3), channel_id=1, source_target_pairs={{0,32},{32,64},{64,96},{96,1},{1,33},{33,65},{65,97},{97,2},{2,34}... | collective-permute-start | bytes 884744 | tf_op jit(solution)/shard_map/ppermute | solution.py:55
  201.3 12.7 %collective-permute-start.9 = (bf16[8,48,384]{2,1,0:T(8,128)(2,1)S(1)}, bf16[8,48,384]{2,1,0:T(8,128)(2,1)S(1)}, u32[]{:S(2)}, u32[]{:S(2)}) collective-permute-start(bf16[8,48,384]{2,1,0:T(8,128)(2,1)S(1)} %all-to-all-done.3), channel_id=1, source_target_pairs={{0,99},{32,0},{64,32},{96,64},{1,96},{33,1},{65,33},{97,65},{2,97}... | collective-permute-start | bytes 884744 | tf_op jit(solution)/shard_map/ppermute | solution.py:55
  218.0 11.8 %copy-start.5 = (f32[128,6]{0,1:T(8,128)S(1)}, f32[128,6]{0,1:T(8,128)}, u32[]{:S(2)}) copy-start(f32[128,6]{0,1:T(8,128)} %param.12) | copy-start | bytes 9220
  218.0 43.0 %all-to-all-start.5 = ((bf16[32,24,1536]{2,1,0:T(8,128)(2,1)}), bf16[32,24,1536]{2,1,0:T(8,128)(2,1)S(1)}, u32[]{:S(2)}, u32[]{:S(2)}) async-start(bf16[32,24,1536]{2,1,0:T(8,128)(2,1)} %bitcast.64), calls=%async_computation.5 | async-start | bytes 4718592 | tf_op jit(solution)/shard_map/all_to_all | solution.py:85

commit v11 on v7

--- a/solution.py
+++ b/solution.py
@@ -35,11 +35,13 @@
     flat_route = routes.reshape(-1)
     flat_live = jnp.repeat(live, top_count)
     expert_ids = jnp.arange(experts, dtype=jnp.int32)
-    onehot = ((flat_route[:, None] == expert_ids[None, :]) & (flat_live[:, None] > 0)).astype(
-        jnp.int32
+    onehot = (flat_route[:, None] == expert_ids[None, :]) & (flat_live[:, None] > 0)
+    requests = flat_route.shape[0]
+    before = jnp.arange(requests)[None, :] < jnp.arange(requests)[:, None]
+    earlier = jnp.dot(
+        before.astype(jnp.bfloat16), onehot.astype(jnp.bfloat16), preferred_element_type=jnp.float32
     )
-    earlier = jnp.cumsum(onehot, axis=0) - onehot
-    slot_index = jnp.sum(earlier * onehot, axis=1)
+    slot_index = jnp.sum(jnp.where(onehot, earlier, 0.0), axis=1).astype(jnp.int32)
     kept_mask = (flat_live > 0) & (slot_index < capacity)
     target = jnp.where(kept_mask, flat_route * capacity + slot_index, total_slots)
     slot_ids = jnp.arange(total_slots, dtype=jnp.int32)

time: 208 us -> 206 us (level)
    another operation x5 -> x3, other arithmetic: 4.66 us -> 2.89 us
  transfers between devices with their start and end apart: 11 -> 11, of which waited for: 4 -> 5; matrix products, arithmetic and copies ran while one was open for 1% -> 1% of each run, Pallas kernels for 0% -> 0%
where the time goes in v11:
time: 206 us; the launch traced here: 205 us
  blocking collectives  76.5 us (37%)
  waiting for transfers between devices  57.2 us (28%)
  starting transfers between devices  52.9 us (26%)
  matrix products  10.1 us (5%)
  other arithmetic  4.44 us (2%)
  local copies, waits for them, and re-layouts  3.7 us (2%)
    all_gather x2, blocking collectives, local(): slabs = tuple((lax.all_gather(w, 'zh', axis=0, tiled=False) for w in slabs))  56.3 us
    all_to_all x1, waiting for transfers between devices, local(): lax.all_to_all(expert_rows, TOKEN_GROUP, split_axis=0, concat_axis=0, til...  30.8 us
    ppermute x8, starting transfers between devices, local(): shift = lambda v, k: lax.ppermute(v, ('zl', 'zh'), pairs(k))  29 us
    ppermute x8, waiting for transfers between devices, local(): shift = lambda v, k: lax.ppermute(v, ('zl', 'zh'), pairs(k))  26.2 us
    all_to_all x1, blocking collectives, local(): lax.all_to_all(slab, ('y', 'c'), split_axis=0, concat_axis=0, tiled=True)  20.2 us
    all_to_all x1, starting transfers between devices, local(): lax.all_to_all(outgoing, TOKEN_GROUP, split_axis=0, concat_axis=0, tiled=...  10.6 us
    all_to_all x1, starting transfers between devices, local(): lax.all_to_all(expert_rows, TOKEN_GROUP, split_axis=0, concat_axis=0, til...  9.12 us
    all_to_all x1, starting transfers between devices, local(): lax.all_to_all(slab, ('y', 'c'), split_axis=0, concat_axis=0, tiled=True)  4.19 us
  transfers between devices with their start and end apart: 11, of which 5 were waited for; matrix products, arithmetic and copies ran while one was open for 1% of the time, Pallas kernels for 0%

profile of v11, /device:TPU:1, one launch (start us, length us, event | category | flops | bytes accessed | tf_op | source)
XLA Modules:
  0.0 205.3 jit_solution(17975842432536201888)
XLA Ops:
  0.0 0.0 copy-start
  0.0 0.0 copy-start.3
  0.0 1.0 convert.18
  1.0 0.9 convert.19
  2.0 0.9 convert_bitcast_fusion
  3.0 0.7 broadcast_compare_fusion
  3.7 0.1 broadcast_in_dim.32.clone
  3.7 0.2 gt.23
  3.9 0.8 copy.29
  4.7 0.1 eq.40
  4.8 0.4 fusion.8
  5.2 0.1 convert_element_type.37
  5.3 0.1 copy.31
  5.4 0.0 copy-done.3
  5.4 0.4 fusion.1
  5.8 0.0 copy-done
  5.8 2.2 %convolution_convert_fusion = bf16[768,1536]{1,0:T(8,128)(2,1)} fusion(pred[768,128]{1,0:T(8,128)(4,1)S(1)} %fusion.1, bf16[128,1536]{1,0:T(8,128)(2,1)S(1)} %copy-done), kind=kOutput, calls=%fused_computation.1 | convolution fusion | flops 303169536 | bytes 2850816 | tf_op jit(solution)/shard_map/dot_general | solution.py:50
  8.0 10.6 %all-to-all-start = ((bf16[32,24,1536]{2,1,0:T(8,128)(2,1)}), bf16[32,24,1536]{2,1,0:T(8,128)(2,1)S(1)}, u32[]{:S(2)}, u32[]{:S(2)}) async-start(bf16[32,24,1536]{2,1,0:T(8,128)(2,1)} %bitcast.1), calls=%async_computation | async-start | bytes 4718592 | tf_op jit(solution)/shard_map/all_to_all | solution.py:51
  18.6 30.5 %all-gather = bf16[8,48,768]{2,1,0:T(8,128)(2,1)} all-gather(bf16[2,48,768]{2,1,0:T(8,128)(2,1)S(1)} %get-tuple-element.18), channel_id=2, replica_groups=mesh['y'=4,'zl'=4,'c'=2,'x'=4,'zh'=4] {'zh'}, dimensions={0}, use_global_device_ids=true | all-gather | bytes 737280 | tf_op jit(solution)/shard_map/all_gather | solution.py:32
  49.1 25.8 %all-gather.1 = bf16[8,48,768]{2,1,0:T(8,128)(2,1)S(1)} all-gather(bf16[2,48,768]{2,1,0:T(8,128)(2,1)S(1)} %get-tuple-element.19), channel_id=3, replica_groups=mesh['y'=4,'zl'=4,'c'=2,'x'=4,'zh'=4] {'zh'}, dimensions={0}, use_global_device_ids=true | all-gather | bytes 737280 | tf_op jit(solution)/shard_map/all_gather | solution.py:32
  74.9 0.0 all-to-all-done
  74.9 0.0 copy-start.1
  74.9 1.4 copy-done.1
  76.3 20.2 %all_to_all.34 = bf16[8,48,768]{2,1,0:T(8,128)(2,1)S(1)} all-to-all(bf16[8,48,768]{2,1,0:T(8,128)(2,1)S(1)} %all-gather.1), channel_id=1, replica_groups=mesh['y'=4,'zl'=4,'c'=2,'x'=4,'zh'=4] {'y','c'}, dimensions={0} | all-to-all | bytes 1179648 | tf_op jit(solution)/shard_map/all_to_all | solution.py:63
  96.5 4.2 %all-to-all-start.1 = ((bf16[8,48,768]{2,1,0:T(8,128)(2,1)}), bf16[8,48,768]{2,1,0:T(8,128)(2,1)S(1)}, u32[]{:S(2)}, u32[]{:S(2)}) async-start(bf16[8,48,768]{2,1,0:T(8,128)(2,1)} %bitcast.5), calls=%async_computation.1 | async-start | bytes 1179648 | tf_op jit(solution)/shard_map/all_to_all | solution.py:63
  100.7 1.9 collective-permute-start.6
  102.7 5.5 %collective-permute-start.7 = (bf16[4,48,768]{2,1,0:T(8,128)(2,1)S(1)}, bf16[4,48,768]{2,1,0:T(8,128)(2,1)S(1)}, u32[]{:S(2)}, u32[]{:S(2)}) collective-permute-start(bf16[4,48,768]{2,1,0:T(8,128)(2,1)S(1)} %get-tuple-element.24), channel_id=1, source_target_pairs={{0,67},{32,99},{64,0},{96,32},{1,64},{33,96},{65,1},{97,33},{2,65}... | collective-permute-start | bytes 884744 | tf_op jit(solution)/shard_map/ppermute | solution.py:57
  108.2 2.3 %collective-permute-start.4 = (bf16[8,48,768]{2,1,0:T(8,128)(2,1)S(1)}, bf16[8,48,768]{2,1,0:T(8,128)(2,1)S(1)}, u32[]{:S(2)}, u32[]{:S(2)}) collective-permute-start(bf16[8,48,768]{2,1,0:T(8,128)(2,1)S(1)} %all_to_all.34), channel_id=1, source_target_pairs={{0,32},{32,64},{64,96},{96,1},{1,33},{33,65},{65,97},{97,2},{2,34}... | collective-permute-start | bytes 1769480 | tf_op jit(solution)/shard_map/ppermute | solution.py:57
  110.5 0.2 all-to-all-done.1
  110.8 3.2 %collective-permute-start.2 = (bf16[4,48,768]{2,1,0:T(8,128)(2,1)S(1)}, bf16[4,48,768]{2,1,0:T(8,128)(2,1)S(1)}, u32[]{:S(2)}, u32[]{:S(2)}) collective-permute-start(bf16[4,48,768]{2,1,0:T(8,128)(2,1)S(1)} %get-tuple-element.25), channel_id=1, source_target_pairs={{0,64},{32,96},{64,1},{96,33},{1,65},{33,97},{65,2},{97,34},{2,66}... | collective-permute-start | bytes 884744 | tf_op jit(solution)/shard_map/ppermute | solution.py:57
  114.1 4.2 %collective-permute-start.3 = (bf16[4,48,768]{2,1,0:T(8,128)(2,1)S(1)}, bf16[4,48,768]{2,1,0:T(8,128)(2,1)S(1)}, u32[]{:S(2)}, u32[]{:S(2)}) collective-permute-start(bf16[4,48,768]{2,1,0:T(8,128)(2,1)S(1)} %get-tuple-element.26), channel_id=1, source_target_pairs={{0,67},{32,99},{64,0},{96,32},{1,64},{33,96},{65,1},{97,33},{2,65}... | collective-permute-start | bytes 884744 | tf_op jit(solution)/shard_map/ppermute | solution.py:57
  118.2 0.0 collective-permute-done.6
  118.2 3.4 %collective-permute-start = (bf16[8,48,768]{2,1,0:T(8,128)(2,1)S(1)}, bf16[8,48,768]{2,1,0:T(8,128)(2,1)S(1)}, u32[]{:S(2)}, u32[]{:S(2)}) collective-permute-start(bf16[8,48,768]{2,1,0:T(8,128)(2,1)S(1)} %all-to-all-done.1), channel_id=1, source_target_pairs={{0,32},{32,64},{64,96},{96,1},{1,33},{33,65},{65,97},{97,2},{2,34}... | collective-permute-start | bytes 1769480 | tf_op jit(solution)/shard_map/ppermute | solution.py:57
  121.6 0.2 broadcast.52.clone.1
  121.9 0.0 collective-permute-done.7
  121.9 4.2 %collective-permute-start.5 = (bf16[8,48,768]{2,1,0:T(8,128)(2,1)S(1)}, bf16[8,48,768]{2,1,0:T(8,128)(2,1)S(1)}, u32[]{:S(2)}, u32[]{:S(2)}) collective-permute-start(bf16[8,48,768]{2,1,0:T(8,128)(2,1)S(1)} %all_to_all.34), channel_id=1, source_target_pairs={{0,99},{32,0},{64,32},{96,64},{1,96},{33,1},{65,33},{97,65},{2,97}... | collective-permute-start | bytes 1769480 | tf_op jit(solution)/shard_map/ppermute | solution.py:57
  126.1 0.2 broadcast.52.clone
  126.4 0.1 pad_maximum_fusion.1
  126.5 16.2 %collective-permute-done.2 = bf16[4,48,768]{2,1,0:T(8,128)(2,1)S(1)} collective-permute-done((bf16[4,48,768]{2,1,0:T(8,128)(2,1)S(1)}, bf16[4,48,768]{2,1,0:T(8,128)(2,1)S(1)}, u32[]{:S(2)}, u32[]{:S(2)}) %collective-permute-start.2) | collective-permute-done | bytes 294944 | tf_op jit(solution)/shard_map/ppermute | solution.py:57
  142.7 4.4 %collective-permute-start.1 = (bf16[8,48,768]{2,1,0:T(8,128)(2,1)S(1)}, bf16[8,48,768]{2,1,0:T(8,128)(2,1)S(1)}, u32[]{:S(2)}, u32[]{:S(2)}) collective-permute-start(bf16[8,48,768]{2,1,0:T(8,128)(2,1)S(1)} %all-to-all-done.1), channel_id=1, source_target_pairs={{0,99},{32,0},{64,32},{96,64},{1,96},{33,1},{65,33},{97,65},{2,97}... | collective-permute-start | bytes 1769480 | tf_op jit(solution)/shard_map/ppermute | solution.py:57
  147.1 0.0 collective-permute-done.3
  147.1 0.1 pad_maximum_fusion
  147.1 0.0 collective-permute-done.4
  147.1 0.0 copy-start.2
  147.2 9.7 %collective-permute-done = bf16[8,48,768]{2,1,0:T(8,128)(2,1)S(1)} collective-permute-done((bf16[8,48,768]{2,1,0:T(8,128)(2,1)S(1)}, bf16[8,48,768]{2,1,0:T(8,128)(2,1)S(1)}, u32[]{:S(2)}, u32[]{:S(2)}) %collective-permute-start) | collective-permute-done | bytes 589856 | tf_op jit(solution)/shard_map/ppermute | solution.py:57
  157.0 0.0 collective-permute-done.5
  157.1 0.0 copy-done.2
  157.1 1.4 fusion.3
  158.5 0.2 collective-permute-done.1
  158.8 1.4 fusion.5
  160.2 0.8 fusion.11
  161.0 2.3 %add_convert_fusion = bf16[768,1536]{1,0:T(8,128)(2,1)} fusion(f32[768,1536]{1,0:T(8,128)S(1)} %fusion.11, bf16[1536,768]{1,0:T(8,128)(2,1)S(1)} %bitcast.34, f32[768,512]{1,0:T(8,128)S(1)} %fusion.3), kind=kOutput, calls=%fused_computation | convolution fusion | flops 607518720 | bytes 9437184 | tf_op jit(solution)/shard_map/dot_general | solution.py:82
  163.3 0.0 copy-start.4
  163.3 9.1 %all-to-all-start.3 = ((bf16[32,24,1536]{2,1,0:T(8,128)(2,1)}), bf16[32,24,1536]{2,1,0:T(8,128)(2,1)S(1)}, u32[]{:S(2)}, u32[]{:S(2)}) async-start(bf16[32,24,1536]{2,1,0:T(8,128)(2,1)} %bitcast.28), calls=%async_computation.3 | async-start | bytes 4718592 | tf_op jit(solution)/shard_map/all_to_all | solution.py:87
  172.4 0.0 copy-done.4
  172.5 0.3 select_reduce_fusion
  172.8 30.8 %all-to-all-done.3 = bf16[32,24,1536]{2,1,0:T(8,128)(2,1)S(1)} async-done(((bf16[32,24,1536]{2,1,0:T(8,128)(2,1)}), bf16[32,24,1536]{2,1,0:T(8,128)(2,1)S(1)}, u32[]{:S(2)}, u32[]{:S(2)}) %all-to-all-start.3) | async-done | bytes 2359328 | tf_op jit(solution)/shard_map/all_to_all | solution.py:87
  203.6 0.5 fusion.20
  204.1 1.2 fusion
  (18 shorter events, 0.5 us)
Async XLA Ops:
  0.0 5.8 %copy-start = (bf16[128,1536]{1,0:T(8,128)(2,1)S(1)}, bf16[128,1536]{1,0:T(8,128)(2,1)}, u32[]{:S(2)}) copy-start(bf16[128,1536]{1,0:T(8,128)(2,1)} %param.7) | copy-start | bytes 1179652
  0.0 5.4 %copy-start.3 = (s32[128,6]{0,1:T(8,128)S(1)}, s32[128,6]{0,1:T(8,128)}, u32[]{:S(2)}) copy-start(s32[128,6]{0,1:T(8,128)} %param.11) | copy-start | bytes 9220
  8.0 66.9 %all-to-all-start = ((bf16[32,24,1536]{2,1,0:T(8,128)(2,1)}), bf16[32,24,1536]{2,1,0:T(8,128)(2,1)S(1)}, u32[]{:S(2)}, u32[]{:S(2)}) async-start(bf16[32,24,1536]{2,1,0:T(8,128)(2,1)} %bitcast.1), calls=%async_computation | async-start | bytes 4718592 | tf_op jit(solution)/shard_map/all_to_all | solution.py:51
  74.9 1.4 copy-start.1
  96.5 14.3 %all-to-all-start.1 = ((bf16[8,48,768]{2,1,0:T(8,128)(2,1)}), bf16[8,48,768]{2,1,0:T(8,128)(2,1)S(1)}, u32[]{:S(2)}, u32[]{:S(2)}) async-start(bf16[8,48,768]{2,1,0:T(8,128)(2,1)} %bitcast.5), calls=%async_computation.1 | async-start | bytes 1179648 | tf_op jit(solution)/shard_map/all_to_all | solution.py:63
  100.7 17.5 %collective-permute-start.6 = (bf16[4,48,768]{2,1,0:T(8,128)(2,1)S(1)}, bf16[4,48,768]{2,1,0:T(8,128)(2,1)S(1)}, u32[]{:S(2)}, u32[]{:S(2)}) collective-permute-start(bf16[4,48,768]{2,1,0:T(8,128)(2,1)S(1)} %get-tuple-element.23), channel_id=1, source_target_pairs={{0,64},{32,96},{64,1},{96,33},{1,65},{33,97},{65,2},{97,34},{2,66}... | collective-permute-start | bytes 884744 | tf_op jit(solution)/shard_map/ppermute | solution.py:57
  102.7 19.2 %collective-permute-start.7 = (bf16[4,48,768]{2,1,0:T(8,128)(2,1)S(1)}, bf16[4,48,768]{2,1,0:T(8,128)(2,1)S(1)}, u32[]{:S(2)}, u32[]{:S(2)}) collective-permute-start(bf16[4,48,768]{2,1,0:T(8,128)(2,1)S(1)} %get-tuple-element.24), channel_id=1, source_target_pairs={{0,67},{32,99},{64,0},{96,32},{1,64},{33,96},{65,1},{97,33},{2,65}... | collective-permute-start | bytes 884744 | tf_op jit(solution)/shard_map/ppermute | solution.py:57
  108.2 38.9 %collective-permute-start.4 = (bf16[8,48,768]{2,1,0:T(8,128)(2,1)S(1)}, bf16[8,48,768]{2,1,0:T(8,128)(2,1)S(1)}, u32[]{:S(2)}, u32[]{:S(2)}) collective-permute-start(bf16[8,48,768]{2,1,0:T(8,128)(2,1)S(1)} %all_to_all.34), channel_id=1, source_target_pairs={{0,32},{32,64},{64,96},{96,1},{1,33},{33,65},{65,97},{97,2},{2,34}... | collective-permute-start | bytes 1769480 | tf_op jit(solution)/shard_map/ppermute | solution.py:57
  110.8 31.9 %collective-permute-start.2 = (bf16[4,48,768]{2,1,0:T(8,128)(2,1)S(1)}, bf16[4,48,768]{2,1,0:T(8,128)(2,1)S(1)}, u32[]{:S(2)}, u32[]{:S(2)}) collective-permute-start(bf16[4,48,768]{2,1,0:T(8,128)(2,1)S(1)} %get-tuple-element.25), channel_id=1, source_target_pairs={{0,64},{32,96},{64,1},{96,33},{1,65},{33,97},{65,2},{97,34},{2,66}... | collective-permute-start | bytes 884744 | tf_op jit(solution)/shard_map/ppermute | solution.py:57
  114.1 33.0 %collective-permute-start.3 = (bf16[4,48,768]{2,1,0:T(8,128)(2,1)S(1)}, bf16[4,48,768]{2,1,0:T(8,128)(2,1)S(1)}, u32[]{:S(2)}, u32[]{:S(2)}) collective-permute-start(bf16[4,48,768]{2,1,0:T(8,128)(2,1)S(1)} %get-tuple-element.26), channel_id=1, source_target_pairs={{0,67},{32,99},{64,0},{96,32},{1,64},{33,96},{65,1},{97,33},{2,65}... | collective-permute-start | bytes 884744 | tf_op jit(solution)/shard_map/ppermute | solution.py:57
  118.2 38.7 %collective-permute-start = (bf16[8,48,768]{2,1,0:T(8,128)(2,1)S(1)}, bf16[8,48,768]{2,1,0:T(8,128)(2,1)S(1)}, u32[]{:S(2)}, u32[]{:S(2)}) collective-permute-start(bf16[8,48,768]{2,1,0:T(8,128)(2,1)S(1)} %all-to-all-done.1), channel_id=1, source_target_pairs={{0,32},{32,64},{64,96},{96,1},{1,33},{33,65},{65,97},{97,2},{2,34}... | collective-permute-start | bytes 1769480 | tf_op jit(solution)/shard_map/ppermute | solution.py:57
  121.9 35.1 %collective-permute-start.5 = (bf16[8,48,768]{2,1,0:T(8,128)(2,1)S(1)}, bf16[8,48,768]{2,1,0:T(8,128)(2,1)S(1)}, u32[]{:S(2)}, u32[]{:S(2)}) collective-permute-start(bf16[8,48,768]{2,1,0:T(8,128)(2,1)S(1)} %all_to_all.34), channel_id=1, source_target_pairs={{0,99},{32,0},{64,32},{96,64},{1,96},{33,1},{65,33},{97,65},{2,97}... | collective-permute-start | bytes 1769480 | tf_op jit(solution)/shard_map/ppermute | solution.py:57
  142.7 16.0 %collective-permute-start.1 = (bf16[8,48,768]{2,1,0:T(8,128)(2,1)S(1)}, bf16[8,48,768]{2,1,0:T(8,128)(2,1)S(1)}, u32[]{:S(2)}, u32[]{:S(2)}) collective-permute-start(bf16[8,48,768]{2,1,0:T(8,128)(2,1)S(1)} %all-to-all-done.1), channel_id=1, source_target_pairs={{0,99},{32,0},{64,32},{96,64},{1,96},{33,1},{65,33},{97,65},{2,97}... | collective-permute-start | bytes 1769480 | tf_op jit(solution)/shard_map/ppermute | solution.py:57
  147.1 10.0 %copy-start.2 = (bf16[32,24,1536]{2,1,0:T(8,128)(2,1)S(1)}, bf16[32,24,1536]{2,1,0:T(8,128)(2,1)}, u32[]{:S(2)}) copy-start(bf16[32,24,1536]{2,1,0:T(8,128)(2,1)} %copy-done.1) | copy-start | bytes 7077892
  163.3 9.1 %copy-start.4 = (f32[128,6]{0,1:T(8,128)S(1)}, f32[128,6]{0,1:T(8,128)}, u32[]{:S(2)}) copy-start(f32[128,6]{0,1:T(8,128)} %param.12) | copy-start | bytes 9220
  163.3 40.3 %all-to-all-start.3 = ((bf16[32,24,1536]{2,1,0:T(8,128)(2,1)}), bf16[32,24,1536]{2,1,0:T(8,128)(2,1)S(1)}, u32[]{:S(2)}, u32[]{:S(2)}) async-start(bf16[32,24,1536]{2,1,0:T(8,128)(2,1)} %bitcast.28), calls=%async_computation.3 | async-start | bytes 4718592 | tf_op jit(solution)/shard_map/all_to_all | solution.py:87

commit v12 on v11

--- a/solution.py
+++ b/solution.py
@@ -17,20 +17,19 @@
     capacity = tok_dev * top_count // experts
     total_slots = experts * capacity
 
-    parts = 2
-    part = hidden_width // parts
+    cuts = (0, hidden_width // 4, hidden_width)
     down_t = jnp.swapaxes(down_train, 1, 2)
     slabs = tuple(
-        jnp.concatenate(
-            [w[:, :, h * part : (h + 1) * part] for w in (gate_train, up_train, down_t)], axis=2
-        ).astype(jnp.bfloat16)
-        for h in range(parts)
+        jnp.concatenate([w[:, :, lo:hi] for w in (gate_train, up_train, down_t)], axis=2).astype(
+            jnp.bfloat16
+        )
+        for lo, hi in zip(cuts[:-1], cuts[1:])
     )
     slabs, tokens, routes, route_scores, live = lax.optimization_barrier(
         (slabs, tokens, routes, route_scores, live)
     )
     slabs = tuple(lax.all_gather(w, "zh", axis=0, tiled=False) for w in slabs)
-    n_pairs, local_experts, rows, width = slabs[0].shape
+    n_pairs, local_experts, rows = slabs[0].shape[:3]
     route_share = route_scores / jnp.sum(route_scores, axis=1, keepdims=True)
     flat_route = routes.reshape(-1)
     flat_live = jnp.repeat(live, top_count)
@@ -59,6 +58,7 @@
     places = [zl_at % zl_size, (zl_at - 1) % zl_size, (zl_at + 1) % zl_size, (zl_at + 2) % zl_size]
     weights = []
     for slab in slabs:
+        width = slab.shape[-1]
         slab = slab.reshape(n_pairs * local_experts, rows, width)
         slab = lax.all_to_all(slab, ("y", "c"), split_axis=0, concat_axis=0, tiled=True)
         half = slab.shape[0] // 2
@@ -77,6 +77,7 @@
 
     expert_out = None
     for w in weights:
+        part = w.shape[1] // 3
         gate_up = jnp.dot(incoming, w[:, : 2 * part], preferred_element_type=jnp.float32)
         hidden = (jax.nn.silu(gate_up[:, :part]) * gate_up[:, part:]).astype(jnp.bfloat16)
         term = lax.dot_general(

time: 206 us -> 219 us (1.063)
  waiting for transfers between devices: 57.2 us -> 72.4 us
  matrix products: 10.1 us -> 14 us
  blocking collectives: 76.5 us -> 73.7 us
  starting transfers between devices: 52.9 us -> 50.2 us
    ppermute x8, waiting for transfers between devices: 26.2 us -> 41.5 us  [local(): shift = lambda v, k: lax.ppermute(v, ('zl', 'zh'), pairs(k))]
    all_to_all x1, blocking collectives: 20.2 us -> 15.3 us  [local(): lax.all_to_all(slab, ('y', 'c'), split_axis=0, concat_axis=0, tiled=True)]
    dot_general x2, matrix products: 2.75 us -> 6.12 us  [local(): jnp.dot(incoming, w[:, :2 * part], preferred_element_type=jnp.float32)]
    ppermute x8, starting transfers between devices: 29 us -> 26.1 us  [local(): shift = lambda v, k: lax.ppermute(v, ('zl', 'zh'), pairs(k))]
  transfers between devices with their start and end apart: 11 -> 11, of which waited for: 5 -> 6; matrix products, arithmetic and copies ran while one was open for 1% -> 2% of each run, Pallas kernels for 0% -> 0%
where the time goes in v12:
time: 219 us
  blocking collectives  73.7 us (34%)
  waiting for transfers between devices  72.4 us (33%)
  starting transfers between devices  50.2 us (23%)
  matrix products  14 us (6%)
  other arithmetic  5.38 us (2%)
  local copies, waits for them, and re-layouts  2.6 us (1%)
    all_gather x2, blocking collectives, local(): slabs = tuple((lax.all_gather(w, 'zh', axis=0, tiled=False) for w in slabs))  58.4 us
    ppermute x8, waiting for transfers between devices, local(): shift = lambda v, k: lax.ppermute(v, ('zl', 'zh'), pairs(k))  41.5 us
    all_to_all x1, waiting for transfers between devices, local(): lax.all_to_all(expert_rows, TOKEN_GROUP, split_axis=0, concat_axis=0, til...  30.8 us
    ppermute x8, starting transfers between devices, local(): shift = lambda v, k: lax.ppermute(v, ('zl', 'zh'), pairs(k))  26.1 us
    all_to_all x1, blocking collectives, local(): lax.all_to_all(slab, ('y', 'c'), split_axis=0, concat_axis=0, tiled=True)  15.3 us
    all_to_all x1, starting transfers between devices, local(): lax.all_to_all(outgoing, TOKEN_GROUP, split_axis=0, concat_axis=0, tiled=...  11.2 us
    all_to_all x1, starting transfers between devices, local(): lax.all_to_all(expert_rows, TOKEN_GROUP, split_axis=0, concat_axis=0, til...  8.91 us
    dot_general x2, matrix products, local(): jnp.dot(incoming, w[:, :2 * part], preferred_element_type=jnp.float32)  6.12 us
  transfers between devices with their start and end apart: 11, of which 6 were waited for; matrix products, arithmetic and copies ran while one was open for 2% of the time, Pallas kernels for 0%

profile of v12, /device:TPU:1, one launch (start us, length us, event | category | flops | bytes accessed | tf_op | source)
XLA Modules:
  0.0 218.7 jit_solution(17768777056270206131)
XLA Ops:
  0.0 0.0 copy-start
  0.0 0.0 copy-start.1
  0.0 1.0 convert.18
  1.0 0.9 convert.19
  2.0 0.9 convert_bitcast_fusion
  3.0 0.7 broadcast_compare_fusion
  3.7 0.1 broadcast_in_dim.38.clone
  3.8 0.2 gt.23
  4.0 0.8 copy.29
  4.7 0.1 eq.40
  4.9 0.4 fusion.9
  5.3 0.1 convert_element_type.37
  5.4 0.1 copy.31
  5.5 0.0 copy-done.1
  5.5 0.4 fusion.3
  5.9 0.0 copy-done
  5.9 2.2 convolution_convert_fusion
  8.1 11.2 %all-to-all-start = ((bf16[32,24,1536]{2,1,0:T(8,128)(2,1)}), bf16[32,24,1536]{2,1,0:T(8,128)(2,1)}, u32[]{:S(2)}, u32[]{:S(2)}) async-start(bf16[32,24,1536]{2,1,0:T(8,128)(2,1)} %bitcast.1), calls=%async_computation | async-start | bytes 4718592 | tf_op jit(solution)/shard_map/all_to_all | solution.py:50
  19.3 22.2 %all-gather = bf16[8,48,384]{2,1,0:T(8,128)(2,1)S(1)} all-gather(bf16[2,48,384]{2,1,0:T(8,128)(2,1)S(1)} %pad_maximum_fusion.3), channel_id=2, replica_groups=mesh['y'=4,'zl'=4,'c'=2,'x'=4,'zh'=4] {'zh'}, dimensions={0}, use_global_device_ids=true | all-gather | bytes 368640 | tf_op jit(solution)/shard_map/all_gather | solution.py:31
  41.5 36.2 %all-gather.1 = bf16[8,48,1152]{2,1,0:T(8,128)(2,1)} all-gather(bf16[2,48,1152]{2,1,0:T(8,128)(2,1)S(1)} %pad_maximum_fusion.2), channel_id=3, replica_groups=mesh['y'=4,'zl'=4,'c'=2,'x'=4,'zh'=4] {'zh'}, dimensions={0}, use_global_device_ids=true | all-gather | bytes 1105920 | tf_op jit(solution)/shard_map/all_gather | solution.py:31
  77.7 0.0 all-to-all-done
  77.7 15.3 %all_to_all.34 = bf16[8,48,384]{2,1,0:T(8,128)(2,1)S(1)} all-to-all(bf16[8,48,384]{2,1,0:T(8,128)(2,1)S(1)} %all-gather), channel_id=1, replica_groups=mesh['y'=4,'zl'=4,'c'=2,'x'=4,'zh'=4] {'y','c'}, dimensions={0} | all-to-all | bytes 589824 | tf_op jit(solution)/shard_map/all_to_all | solution.py:63
  93.0 4.0 %all-to-all-start.2 = ((bf16[8,48,1152]{2,1,0:T(8,128)(2,1)}), bf16[8,48,1152]{2,1,0:T(8,128)(2,1)S(1)}, u32[]{:S(2)}, u32[]{:S(2)}) async-start(bf16[8,48,1152]{2,1,0:T(8,128)(2,1)} %bitcast.11), calls=%async_computation.2 | async-start | bytes 1769472 | tf_op jit(solution)/shard_map/all_to_all | solution.py:63
  97.0 1.9 collective-permute-start
  99.0 4.8 %collective-permute-start.2 = (bf16[4,48,384]{2,1,0:T(8,128)(2,1)S(1)}, bf16[4,48,384]{2,1,0:T(8,128)(2,1)S(1)}, u32[]{:S(2)}, u32[]{:S(2)}) collective-permute-start(bf16[4,48,384]{2,1,0:T(8,128)(2,1)S(1)} %get-tuple-element.25), channel_id=1, source_target_pairs={{0,64},{32,96},{64,1},{96,33},{1,65},{33,97},{65,2},{97,34},{2,66}... | collective-permute-start | bytes 442376 | tf_op jit(solution)/shard_map/ppermute | solution.py:56
  103.8 2.6 %collective-permute-start.3 = (bf16[4,48,384]{2,1,0:T(8,128)(2,1)S(1)}, bf16[4,48,384]{2,1,0:T(8,128)(2,1)}, u32[]{:S(2)}, u32[]{:S(2)}) collective-permute-start(bf16[4,48,384]{2,1,0:T(8,128)(2,1)S(1)} %get-tuple-element.26), channel_id=1, source_target_pairs={{0,67},{32,99},{64,0},{96,32},{1,64},{33,96},{65,1},{97,33},{2,65}... | collective-permute-start | bytes 442376 | tf_op jit(solution)/shard_map/ppermute | solution.py:56
  106.4 3.4 %collective-permute-start.1 = (bf16[8,48,384]{2,1,0:T(8,128)(2,1)S(1)}, bf16[8,48,384]{2,1,0:T(8,128)(2,1)S(1)}, u32[]{:S(2)}, u32[]{:S(2)}) collective-permute-start(bf16[8,48,384]{2,1,0:T(8,128)(2,1)S(1)} %all_to_all.34), channel_id=1, source_target_pairs={{0,99},{32,0},{64,32},{96,64},{1,96},{33,1},{65,33},{97,65},{2,97}... | collective-permute-start | bytes 884744 | tf_op jit(solution)/shard_map/ppermute | solution.py:56
  109.8 0.1 broadcast_in_dim.44
  109.9 0.1 constant_dynamic-update-slice_fusion.7
  110.0 4.3 %collective-permute-done.2 = bf16[4,48,384]{2,1,0:T(8,128)(2,1)S(1)} collective-permute-done((bf16[4,48,384]{2,1,0:T(8,128)(2,1)S(1)}, bf16[4,48,384]{2,1,0:T(8,128)(2,1)S(1)}, u32[]{:S(2)}, u32[]{:S(2)}) %collective-permute-start.2) | collective-permute-done | bytes 147488 | tf_op jit(solution)/shard_map/ppermute | solution.py:56
  114.3 1.2 collective-permute-done.3
  115.5 0.9 pad_maximum_fusion.1
  116.4 0.0 collective-permute-done
  116.4 0.1 constant_dynamic-update-slice_fusion.6
  116.5 3.5 %collective-permute-done.1 = bf16[8,48,384]{2,1,0:T(8,128)(2,1)S(1)} collective-permute-done((bf16[8,48,384]{2,1,0:T(8,128)(2,1)S(1)}, bf16[8,48,384]{2,1,0:T(8,128)(2,1)S(1)}, u32[]{:S(2)}, u32[]{:S(2)}) %collective-permute-start.1) | collective-permute-done | bytes 294944 | tf_op jit(solution)/shard_map/ppermute | solution.py:56
  120.0 0.1 constant_dynamic-update-slice_fusion.4
  120.1 0.0 all-to-all-done.2
  120.1 4.1 %collective-permute-start.4 = (bf16[8,48,1152]{2,1,0:T(8,128)(2,1)S(1)}, bf16[8,48,1152]{2,1,0:T(8,128)(2,1)S(1)}, u32[]{:S(2)}, u32[]{:S(2)}) collective-permute-start(bf16[8,48,1152]{2,1,0:T(8,128)(2,1)S(1)} %all-to-all-done.2), channel_id=1, source_target_pairs={{0,32},{32,64},{64,96},{96,1},{1,33},{33,65},{65,97},{97,2},{2,34}... | collective-permute-start | bytes 2654216 | tf_op jit(solution)/shard_map/ppermute | solution.py:56
  124.2 0.1 fusion.27
  124.2 2.5 %collective-permute-start.6 = (bf16[4,48,1152]{2,1,0:T(8,128)(2,1)S(1)}, bf16[4,48,1152]{2,1,0:T(8,128)(2,1)S(1)}, u32[]{:S(2)}, u32[]{:S(2)}) collective-permute-start(bf16[4,48,1152]{2,1,0:T(8,128)(2,1)S(1)} %get-tuple-element.23), channel_id=1, source_target_pairs={{0,64},{32,96},{64,1},{96,33},{1,65},{33,97},{65,2},{97,34},{2,66}... | collective-permute-start | bytes 1327112 | tf_op jit(solution)/shard_map/ppermute | solution.py:56
  126.7 4.9 %collective-permute-start.7 = (bf16[4,48,1152]{2,1,0:T(8,128)(2,1)S(1)}, bf16[4,48,1152]{2,1,0:T(8,128)(2,1)S(1)}, u32[]{:S(2)}, u32[]{:S(2)}) collective-permute-start(bf16[4,48,1152]{2,1,0:T(8,128)(2,1)S(1)} %get-tuple-element.24), channel_id=1, source_target_pairs={{0,67},{32,99},{64,0},{96,32},{1,64},{33,96},{65,1},{97,33},{2,65}... | collective-permute-start | bytes 1327112 | tf_op jit(solution)/shard_map/ppermute | solution.py:56
  131.6 1.9 collective-permute-start.5
  133.6 2.4 %fusion.10 = f32[768,256]{1,0:T(8,128)S(1)} fusion(bf16[768,1536]{1,0:T(8,128)(2,1)} %bitcast.2, bf16[1536,384]{1,0:T(8,128)(2,1)S(1)} %bitcast.34), kind=kOutput, calls=%fused_computation.19 | convolution fusion | flops 603979776 | bytes 3932160 | tf_op jit(solution)/shard_map/dot_general | solution.py:81
  136.0 0.3 broadcast_in_dim.45
  136.3 0.1 constant_dynamic-update-slice_fusion.3
  136.4 27.6 %collective-permute-done.6 = bf16[4,48,1152]{2,1,0:T(8,128)(2,1)S(1)} collective-permute-done((bf16[4,48,1152]{2,1,0:T(8,128)(2,1)S(1)}, bf16[4,48,1152]{2,1,0:T(8,128)(2,1)S(1)}, u32[]{:S(2)}, u32[]{:S(2)}) %collective-permute-start.6) | collective-permute-done | bytes 442400 | tf_op jit(solution)/shard_map/ppermute | solution.py:56
  164.1 0.0 collective-permute-done.7
  164.1 0.1 pad_maximum_fusion
  164.2 0.0 collective-permute-done.4
  164.2 0.1 constant_dynamic-update-slice_fusion.2
  164.3 5.0 %collective-permute-done.5 = bf16[8,48,1152]{2,1,0:T(8,128)(2,1)S(1)} collective-permute-done((bf16[8,48,1152]{2,1,0:T(8,128)(2,1)S(1)}, bf16[8,48,1152]{2,1,0:T(8,128)(2,1)S(1)}, u32[]{:S(2)}, u32[]{:S(2)}) %collective-permute-start.5) | collective-permute-done | bytes 884768 | tf_op jit(solution)/shard_map/ppermute | solution.py:56
  169.3 0.1 constant_dynamic-update-slice_fusion.1
  169.4 0.1 constant_dynamic-update-slice_fusion
  169.5 3.7 %fusion.1 = f32[768,768]{1,0:T(8,128)S(1)} fusion(bf16[768,1536]{1,0:T(8,128)(2,1)} %bitcast.2, bf16[1536,1152]{1,0:T(8,128)(2,1)S(1)} %bitcast.31), kind=kOutput, calls=%fused_computation.4 | convolution fusion | flops 1811939328 | bytes 7077888 | tf_op jit(solution)/shard_map/dot_general | solution.py:81
  173.2 1.4 fusion.5
  174.7 2.2 %add_convert_fusion = bf16[768,1536]{1,0:T(8,128)(2,1)} fusion(f32[768,1536]{1,0:T(8,128)S(1)} %fusion.5, bf16[1536,384]{1,0:T(8,128)(2,1)S(1)} %bitcast.35, f32[768,256]{1,0:T(8,128)S(1)} %fusion.10), kind=kOutput, calls=%fused_computation | convolution fusion | flops 304939008 | bytes 8257536 | tf_op jit(solution)/shard_map/dot_general | solution.py:83
  176.9 0.0 copy-start.2
  176.9 8.9 %all-to-all-start.3 = ((bf16[32,24,1536]{2,1,0:T(8,128)(2,1)}), bf16[32,24,1536]{2,1,0:T(8,128)(2,1)S(1)}, u32[]{:S(2)}, u32[]{:S(2)}) async-start(bf16[32,24,1536]{2,1,0:T(8,128)(2,1)} %bitcast.28), calls=%async_computation.3 | async-start | bytes 4718592 | tf_op jit(solution)/shard_map/all_to_all | solution.py:88
  185.8 0.0 copy-done.2
  185.8 0.3 select_reduce_fusion
  186.1 30.8 %all-to-all-done.3 = bf16[32,24,1536]{2,1,0:T(8,128)(2,1)S(1)} async-done(((bf16[32,24,1536]{2,1,0:T(8,128)(2,1)}), bf16[32,24,1536]{2,1,0:T(8,128)(2,1)S(1)}, u32[]{:S(2)}, u32[]{:S(2)}) %all-to-all-start.3) | async-done | bytes 2359328 | tf_op jit(solution)/shard_map/all_to_all | solution.py:88
  216.9 0.5 fusion.19
  217.4 1.2 fusion
  (14 shorter events, 0.2 us)
Async XLA Ops:
  0.0 5.9 %copy-start = (bf16[128,1536]{1,0:T(8,128)(2,1)S(1)}, bf16[128,1536]{1,0:T(8,128)(2,1)}, u32[]{:S(2)}) copy-start(bf16[128,1536]{1,0:T(8,128)(2,1)} %param.7) | copy-start | bytes 1179652
  0.0 5.5 %copy-start.1 = (s32[128,6]{0,1:T(8,128)S(1)}, s32[128,6]{0,1:T(8,128)}, u32[]{:S(2)}) copy-start(s32[128,6]{0,1:T(8,128)} %param.11) | copy-start | bytes 9220
  8.1 69.6 %all-to-all-start = ((bf16[32,24,1536]{2,1,0:T(8,128)(2,1)}), bf16[32,24,1536]{2,1,0:T(8,128)(2,1)}, u32[]{:S(2)}, u32[]{:S(2)}) async-start(bf16[32,24,1536]{2,1,0:T(8,128)(2,1)} %bitcast.1), calls=%async_computation | async-start | bytes 4718592 | tf_op jit(solution)/shard_map/all_to_all | solution.py:50
  93.0 27.1 %all-to-all-start.2 = ((bf16[8,48,1152]{2,1,0:T(8,128)(2,1)}), bf16[8,48,1152]{2,1,0:T(8,128)(2,1)S(1)}, u32[]{:S(2)}, u32[]{:S(2)}) async-start(bf16[8,48,1152]{2,1,0:T(8,128)(2,1)} %bitcast.11), calls=%async_computation.2 | async-start | bytes 1769472 | tf_op jit(solution)/shard_map/all_to_all | solution.py:63
  97.0 19.4 %collective-permute-start = (bf16[8,48,384]{2,1,0:T(8,128)(2,1)S(1)}, bf16[8,48,384]{2,1,0:T(8,128)(2,1)S(1)}, u32[]{:S(2)}, u32[]{:S(2)}) collective-permute-start(bf16[8,48,384]{2,1,0:T(8,128)(2,1)S(1)} %all_to_all.34), channel_id=1, source_target_pairs={{0,32},{32,64},{64,96},{96,1},{1,33},{33,65},{65,97},{97,2},{2,34}... | collective-permute-start | bytes 884744 | tf_op jit(solution)/shard_map/ppermute | solution.py:56
  99.0 15.3 %collective-permute-start.2 = (bf16[4,48,384]{2,1,0:T(8,128)(2,1)S(1)}, bf16[4,48,384]{2,1,0:T(8,128)(2,1)S(1)}, u32[]{:S(2)}, u32[]{:S(2)}) collective-permute-start(bf16[4,48,384]{2,1,0:T(8,128)(2,1)S(1)} %get-tuple-element.25), channel_id=1, source_target_pairs={{0,64},{32,96},{64,1},{96,33},{1,65},{33,97},{65,2},{97,34},{2,66}... | collective-permute-start | bytes 442376 | tf_op jit(solution)/shard_map/ppermute | solution.py:56
  103.8 11.6 %collective-permute-start.3 = (bf16[4,48,384]{2,1,0:T(8,128)(2,1)S(1)}, bf16[4,48,384]{2,1,0:T(8,128)(2,1)}, u32[]{:S(2)}, u32[]{:S(2)}) collective-permute-start(bf16[4,48,384]{2,1,0:T(8,128)(2,1)S(1)} %get-tuple-element.26), channel_id=1, source_target_pairs={{0,67},{32,99},{64,0},{96,32},{1,64},{33,96},{65,1},{97,33},{2,65}... | collective-permute-start | bytes 442376 | tf_op jit(solution)/shard_map/ppermute | solution.py:56
  106.4 13.5 %collective-permute-start.1 = (bf16[8,48,384]{2,1,0:T(8,128)(2,1)S(1)}, bf16[8,48,384]{2,1,0:T(8,128)(2,1)S(1)}, u32[]{:S(2)}, u32[]{:S(2)}) collective-permute-start(bf16[8,48,384]{2,1,0:T(8,128)(2,1)S(1)} %all_to_all.34), channel_id=1, source_target_pairs={{0,99},{32,0},{64,32},{96,64},{1,96},{33,1},{65,33},{97,65},{2,97}... | collective-permute-start | bytes 884744 | tf_op jit(solution)/shard_map/ppermute | solution.py:56
  120.1 44.1 %collective-permute-start.4 = (bf16[8,48,1152]{2,1,0:T(8,128)(2,1)S(1)}, bf16[8,48,1152]{2,1,0:T(8,128)(2,1)S(1)}, u32[]{:S(2)}, u32[]{:S(2)}) collective-permute-start(bf16[8,48,1152]{2,1,0:T(8,128)(2,1)S(1)} %all-to-all-done.2), channel_id=1, source_target_pairs={{0,32},{32,64},{64,96},{96,1},{1,33},{33,65},{65,97},{97,2},{2,34}... | collective-permute-start | bytes 2654216 | tf_op jit(solution)/shard_map/ppermute | solution.py:56
  124.2 39.8 %collective-permute-start.6 = (bf16[4,48,1152]{2,1,0:T(8,128)(2,1)S(1)}, bf16[4,48,1152]{2,1,0:T(8,128)(2,1)S(1)}, u32[]{:S(2)}, u32[]{:S(2)}) collective-permute-start(bf16[4,48,1152]{2,1,0:T(8,128)(2,1)S(1)} %get-tuple-element.23), channel_id=1, source_target_pairs={{0,64},{32,96},{64,1},{96,33},{1,65},{33,97},{65,2},{97,34},{2,66}... | collective-permute-start | bytes 1327112 | tf_op jit(solution)/shard_map/ppermute | solution.py:56
  126.7 37.3 %collective-permute-start.7 = (bf16[4,48,1152]{2,1,0:T(8,128)(2,1)S(1)}, bf16[4,48,1152]{2,1,0:T(8,128)(2,1)S(1)}, u32[]{:S(2)}, u32[]{:S(2)}) collective-permute-start(bf16[4,48,1152]{2,1,0:T(8,128)(2,1)S(1)} %get-tuple-element.24), channel_id=1, source_target_pairs={{0,67},{32,99},{64,0},{96,32},{1,64},{33,96},{65,1},{97,33},{2,65}... | collective-permute-start | bytes 1327112 | tf_op jit(solution)/shard_map/ppermute | solution.py:56
  131.6 37.6 %collective-permute-start.5 = (bf16[8,48,1152]{2,1,0:T(8,128)(2,1)S(1)}, bf16[8,48,1152]{2,1,0:T(8,128)(2,1)S(1)}, u32[]{:S(2)}, u32[]{:S(2)}) collective-permute-start(bf16[8,48,1152]{2,1,0:T(8,128)(2,1)S(1)} %all-to-all-done.2), channel_id=1, source_target_pairs={{0,99},{32,0},{64,32},{96,64},{1,96},{33,1},{65,33},{97,65},{2,97}... | collective-permute-start | bytes 2654216 | tf_op jit(solution)/shard_map/ppermute | solution.py:56
  176.9 8.9 %copy-start.2 = (f32[128,6]{0,1:T(8,128)S(1)}, f32[128,6]{0,1:T(8,128)}, u32[]{:S(2)}) copy-start(f32[128,6]{0,1:T(8,128)} %param.12) | copy-start | bytes 9220
  176.9 40.1 %all-to-all-start.3 = ((bf16[32,24,1536]{2,1,0:T(8,128)(2,1)}), bf16[32,24,1536]{2,1,0:T(8,128)(2,1)S(1)}, u32[]{:S(2)}, u32[]{:S(2)}) async-start(bf16[32,24,1536]{2,1,0:T(8,128)(2,1)} %bitcast.28), calls=%async_computation.3 | async-start | bytes 4718592 | tf_op jit(solution)/shard_map/all_to_all | solution.py:88

commit v13 on v11

--- a/solution.py
+++ b/solution.py
@@ -29,8 +29,8 @@
     slabs, tokens, routes, route_scores, live = lax.optimization_barrier(
         (slabs, tokens, routes, route_scores, live)
     )
-    slabs = tuple(lax.all_gather(w, "zh", axis=0, tiled=False) for w in slabs)
-    n_pairs, local_experts, rows, width = slabs[0].shape
+    first = lax.all_gather(slabs[0], "zh", axis=0, tiled=False)
+    n_pairs, local_experts, rows, width = first.shape
     route_share = route_scores / jnp.sum(route_scores, axis=1, keepdims=True)
     flat_route = routes.reshape(-1)
     flat_live = jnp.repeat(live, top_count)
@@ -49,7 +49,6 @@
     dispatch = jnp.any(picks, axis=2).astype(jnp.bfloat16)
     outgoing = jnp.dot(dispatch, tokens, preferred_element_type=jnp.float32).astype(jnp.bfloat16)
     incoming = lax.all_to_all(outgoing, TOKEN_GROUP, split_axis=0, concat_axis=0, tiled=True)
-    incoming, slabs = lax.optimization_barrier((incoming, slabs))
     zl_size, zh_size = lax.axis_size("zl"), lax.axis_size("zh")
     ring = zl_size * zh_size
     index = lambda z: (z % zl_size) * zh_size + z // zl_size
@@ -58,9 +57,15 @@
     zl_at = lax.axis_index("zl")
     places = [zl_at % zl_size, (zl_at - 1) % zl_size, (zl_at + 1) % zl_size, (zl_at + 2) % zl_size]
     weights = []
-    for slab in slabs:
+    slab = first
+    for h in range(len(slabs)):
+        if h == len(slabs) - 1:
+            incoming, slab = lax.optimization_barrier((incoming, slab))
         slab = slab.reshape(n_pairs * local_experts, rows, width)
         slab = lax.all_to_all(slab, ("y", "c"), split_axis=0, concat_axis=0, tiled=True)
+        if h + 1 < len(slabs):
+            _, upcoming = lax.optimization_barrier((slab, slabs[h + 1]))
+            upcoming = lax.all_gather(upcoming, "zh", axis=0, tiled=False)
         half = slab.shape[0] // 2
         quarters = [
             slab,
@@ -74,6 +79,8 @@
             quarter = quarter.reshape(y_size, 1, local_experts, rows, width)
             full = lax.dynamic_update_index_in_dim(full, quarter, place, axis=1)
         weights.append(full.reshape(model_width, width))
+        if h + 1 < len(slabs):
+            slab = upcoming
 
     expert_out = None
     for w in weights:

time: 206 us -> 215 us (1.044)
  matrix products: 10.1 us -> 15.9 us
  blocking collectives: 76.5 us -> 80.7 us
    all_gather x2, blocking collectives: 56.3 us -> 80.7 us  [the longest x1 47 us: local(): upcoming = lax.all_gather(upcoming, 'zh', axis=0, tiled=False)]
    all_to_all x1 -> x0, blocking collectives: 20.2 us -> none  [local(): lax.all_to_all(slab, ('y', 'c'), split_axis=0, concat_axis=0, tiled=True)]
    ppermute x8, waiting for transfers between devices: 26.2 us -> 14.4 us  [local(): shift = lambda v, k: lax.ppermute(v, ('zl', 'zh'), pairs(k))]
    all_to_all x1 -> x2, starting transfers between devices: 4.19 us -> 15.3 us  [local(): lax.all_to_all(slab, ('y', 'c'), split_axis=0, concat_axis=0, tiled=True)]
    all_to_all x1 -> x2, waiting for transfers between devices: 0.25 us -> 11.1 us  [local(): lax.all_to_all(slab, ('y', 'c'), split_axis=0, concat_axis=0, tiled=True)]
    all_to_all x1, starting transfers between devices: 10.6 us -> 6.08 us  [local(): lax.all_to_all(outgoing, TOKEN_GROUP, split_axis=0, concat_axis=0, tiled=...]
    dot_general x2, matrix products: 2.75 us -> 7.22 us  [local(): jnp.dot(incoming, w[:, :2 * part], preferred_element_type=jnp.float32)]
    all_to_all x1, starting transfers between devices: 9.12 us -> 5.85 us  [local(): lax.all_to_all(expert_rows, TOKEN_GROUP, split_axis=0, concat_axis=0, til...]
  transfers between devices with their start and end apart: 11 -> 12, of which waited for: 5 -> 6; matrix products, arithmetic and copies ran while one was open for 1% -> 6% of each run, Pallas kernels for 0% -> 0%
where the time goes in v13:
time: 215 us; the launch traced here: 214 us
  blocking collectives  80.7 us (38%)
  waiting for transfers between devices  56.3 us (26%)
  starting transfers between devices  53.8 us (25%)
  matrix products  15.9 us (7%)
  other arithmetic  4.63 us (2%)
  local copies, waits for them, and re-layouts  2.65 us (1%)
    all_gather x1, blocking collectives, local(): upcoming = lax.all_gather(upcoming, 'zh', axis=0, tiled=False)  47 us
    all_gather x1, blocking collectives, local(): first = lax.all_gather(slabs[0], 'zh', axis=0, tiled=False)  33.8 us
    all_to_all x1, waiting for transfers between devices, local(): lax.all_to_all(expert_rows, TOKEN_GROUP, split_axis=0, concat_axis=0, til...  30.8 us
    ppermute x8, starting transfers between devices, local(): shift = lambda v, k: lax.ppermute(v, ('zl', 'zh'), pairs(k))  26.6 us
    all_to_all x2, starting transfers between devices, local(): lax.all_to_all(slab, ('y', 'c'), split_axis=0, concat_axis=0, tiled=True)  15.3 us
    ppermute x8, waiting for transfers between devices, local(): shift = lambda v, k: lax.ppermute(v, ('zl', 'zh'), pairs(k))  14.4 us
    all_to_all x2, waiting for transfers between devices, local(): lax.all_to_all(slab, ('y', 'c'), split_axis=0, concat_axis=0, tiled=True)  11.1 us
    dot_general x2, matrix products, local(): jnp.dot(incoming, w[:, :2 * part], preferred_element_type=jnp.float32)  7.22 us
  transfers between devices with their start and end apart: 12, of which 6 were waited for; matrix products, arithmetic and copies ran while one was open for 6% of the time, Pallas kernels for 0%

profile of v13, /device:TPU:1, one launch (start us, length us, event | category | flops | bytes accessed | tf_op | source)
XLA Modules:
  0.0 214.5 jit_solution(14014034175964900223)
XLA Ops:
  0.0 0.0 copy-start
  0.0 0.0 copy-start.1
  0.0 0.0 copy-start.3
  0.0 1.0 convert.18
  1.0 0.9 convert.19
  2.0 0.9 convert_bitcast_fusion
  3.0 33.8 %all-gather = bf16[8,48,768]{2,1,0:T(8,128)(2,1)} all-gather(bf16[2,48,768]{2,1,0:T(8,128)(2,1)S(1)} %get-tuple-element.18), channel_id=2, replica_groups=mesh['y'=4,'zl'=4,'c'=2,'x'=4,'zh'=4] {'zh'}, dimensions={0}, use_global_device_ids=true | all-gather | bytes 737280 | tf_op jit(solution)/shard_map/all_gather | solution.py:32
  36.8 9.4 %all-to-all-start.1 = ((bf16[8,48,768]{2,1,0:T(8,128)(2,1)}), bf16[8,48,768]{2,1,0:T(8,128)(2,1)S(1)}, u32[]{:S(2)}, u32[]{:S(2)}) async-start(bf16[8,48,768]{2,1,0:T(8,128)(2,1)} %all-gather), calls=%async_computation.1 | async-start | bytes 1179648 | tf_op jit(solution)/shard_map/all_to_all | solution.py:65
  46.2 0.0 copy-done.3
  46.2 0.1 broadcast_in_dim.32.clone
  46.3 0.2 gt.23
  46.4 0.0 copy-done.1
  46.4 0.1 copy.29
  46.6 0.1 eq.40
  46.7 0.4 fusion.8
  47.1 0.1 convert_element_type.37
  47.2 0.1 copy.31
  47.3 0.4 fusion.1
  47.7 0.0 copy-done
  47.7 2.2 %convolution_convert_fusion = bf16[768,1536]{1,0:T(8,128)(2,1)} fusion(pred[768,128]{1,0:T(8,128)(4,1)S(1)} %fusion.1, bf16[128,1536]{1,0:T(8,128)(2,1)S(1)} %copy-done), kind=kOutput, calls=%fused_computation.1 | convolution fusion | flops 303169536 | bytes 2850816 | tf_op jit(solution)/shard_map/dot_general | solution.py:50
  49.9 6.4 %all-to-all-done.1 = bf16[8,48,768]{2,1,0:T(8,128)(2,1)S(1)} async-done(((bf16[8,48,768]{2,1,0:T(8,128)(2,1)}), bf16[8,48,768]{2,1,0:T(8,128)(2,1)S(1)}, u32[]{:S(2)}, u32[]{:S(2)}) %all-to-all-start.1) | async-done | bytes 589856 | tf_op jit(solution)/shard_map/all_to_all | solution.py:65
  56.2 6.1 %all-to-all-start = ((bf16[32,24,1536]{2,1,0:T(8,128)(2,1)}), bf16[32,24,1536]{2,1,0:T(8,128)(2,1)}, u32[]{:S(2)}, u32[]{:S(2)}) async-start(bf16[32,24,1536]{2,1,0:T(8,128)(2,1)} %bitcast.1), calls=%async_computation | async-start | bytes 4718592 | tf_op jit(solution)/shard_map/all_to_all | solution.py:51
  62.4 1.9 collective-permute-start
  64.4 2.2 %collective-permute-start.2 = (bf16[4,48,768]{2,1,0:T(8,128)(2,1)S(1)}, bf16[4,48,768]{2,1,0:T(8,128)(2,1)S(1)}, u32[]{:S(2)}, u32[]{:S(2)}) collective-permute-start(bf16[4,48,768]{2,1,0:T(8,128)(2,1)S(1)} %get-tuple-element.25), channel_id=1, source_target_pairs={{0,64},{32,96},{64,1},{96,33},{1,65},{33,97},{65,2},{97,34},{2,66}... | collective-permute-start | bytes 884744 | tf_op jit(solution)/shard_map/ppermute | solution.py:56
  66.6 5.2 %collective-permute-start.3 = (bf16[4,48,768]{2,1,0:T(8,128)(2,1)S(1)}, bf16[4,48,768]{2,1,0:T(8,128)(2,1)S(1)}, u32[]{:S(2)}, u32[]{:S(2)}) collective-permute-start(bf16[4,48,768]{2,1,0:T(8,128)(2,1)S(1)} %get-tuple-element.26), channel_id=1, source_target_pairs={{0,67},{32,99},{64,0},{96,32},{1,64},{33,96},{65,1},{97,33},{2,65}... | collective-permute-start | bytes 884744 | tf_op jit(solution)/shard_map/ppermute | solution.py:56
  71.8 3.4 %collective-permute-start.1 = (bf16[8,48,768]{2,1,0:T(8,128)(2,1)S(1)}, bf16[8,48,768]{2,1,0:T(8,128)(2,1)S(1)}, u32[]{:S(2)}, u32[]{:S(2)}) collective-permute-start(bf16[8,48,768]{2,1,0:T(8,128)(2,1)S(1)} %all-to-all-done.1), channel_id=1, source_target_pairs={{0,99},{32,0},{64,32},{96,64},{1,96},{33,1},{65,33},{97,65},{2,97}... | collective-permute-start | bytes 1769480 | tf_op jit(solution)/shard_map/ppermute | solution.py:56
  75.1 0.2 broadcast.52.clone
  75.4 47.0 %all-gather.1 = bf16[8,48,768]{2,1,0:T(8,128)(2,1)} all-gather(bf16[2,48,768]{2,1,0:T(8,128)(2,1)S(1)} %get-tuple-element.20), channel_id=3, replica_groups=mesh['y'=4,'zl'=4,'c'=2,'x'=4,'zh'=4] {'zh'}, dimensions={0}, use_global_device_ids=true | all-gather | bytes 737280 | tf_op jit(solution)/shard_map/all_gather | solution.py:68
  122.4 0.0 collective-permute-done.2
  122.4 0.0 collective-permute-done.3
  122.4 0.9 pad_maximum_fusion
  123.3 0.0 collective-permute-done
  123.4 0.0 collective-permute-done.1
  123.4 0.0 all-to-all-done
  123.4 5.9 %all-to-all-start.2 = ((bf16[8,48,768]{2,1,0:T(8,128)(2,1)}), bf16[8,48,768]{2,1,0:T(8,128)(2,1)S(1)}, u32[]{:S(2)}, u32[]{:S(2)}) async-start(bf16[8,48,768]{2,1,0:T(8,128)(2,1)} %all-gather.1), calls=%async_computation.2 | async-start | bytes 1179648 | tf_op jit(solution)/shard_map/all_to_all | solution.py:65
  129.3 1.1 constant_dynamic-update-slice_fusion.4
  130.4 4.2 %fusion.5 = f32[768,512]{1,0:T(8,128)} fusion(bf16[768,1536]{1,0:T(8,128)(2,1)} %bitcast.2, bf16[1536,768]{1,0:T(8,128)(2,1)S(1)} %bitcast.31), kind=kOutput, calls=%fused_computation.12 | convolution fusion | flops 1207959552 | bytes 5505024 | tf_op jit(solution)/shard_map/dot_general | solution.py:87
  134.6 4.8 %all-to-all-done.2 = bf16[8,48,768]{2,1,0:T(8,128)(2,1)S(1)} async-done(((bf16[8,48,768]{2,1,0:T(8,128)(2,1)}), bf16[8,48,768]{2,1,0:T(8,128)(2,1)S(1)}, u32[]{:S(2)}, u32[]{:S(2)}) %all-to-all-start.2) | async-done | bytes 589856 | tf_op jit(solution)/shard_map/all_to_all | solution.py:65
  139.4 1.9 collective-permute-start.6
  141.3 5.5 %collective-permute-start.7 = (bf16[4,48,768]{2,1,0:T(8,128)(2,1)S(1)}, bf16[4,48,768]{2,1,0:T(8,128)(2,1)S(1)}, u32[]{:S(2)}, u32[]{:S(2)}) collective-permute-start(bf16[4,48,768]{2,1,0:T(8,128)(2,1)S(1)} %get-tuple-element.24), channel_id=1, source_target_pairs={{0,67},{32,99},{64,0},{96,32},{1,64},{33,96},{65,1},{97,33},{2,65}... | collective-permute-start | bytes 884744 | tf_op jit(solution)/shard_map/ppermute | solution.py:56
  146.8 1.9 collective-permute-start.4
  148.7 4.6 %collective-permute-start.5 = (bf16[8,48,768]{2,1,0:T(8,128)(2,1)S(1)}, bf16[8,48,768]{2,1,0:T(8,128)(2,1)S(1)}, u32[]{:S(2)}, u32[]{:S(2)}) collective-permute-start(bf16[8,48,768]{2,1,0:T(8,128)(2,1)S(1)} %all-to-all-done.2), channel_id=1, source_target_pairs={{0,99},{32,0},{64,32},{96,64},{1,96},{33,1},{65,33},{97,65},{2,97}... | collective-permute-start | bytes 1769480 | tf_op jit(solution)/shard_map/ppermute | solution.py:56
  153.3 2.2 %fusion.11 = f32[768,1536]{1,0:T(8,128)S(1)} fusion(bf16[1536,768]{1,0:T(8,128)(2,1)S(1)} %bitcast.32, f32[768,512]{1,0:T(8,128)} %fusion.5), kind=kOutput, calls=%fused_computation.19 | convolution fusion | flops 605159424 | bytes 7077888 | tf_op jit(solution)/shard_map/dot_general | solution.py:89
  155.5 0.2 broadcast.52.clone.1
  155.8 0.0 collective-permute-done.6
  155.8 1.9 collective-permute-done.7
  157.7 0.1 pad_maximum_fusion.1
  157.7 7.9 %collective-permute-done.4 = bf16[8,48,768]{2,1,0:T(8,128)(2,1)S(1)} collective-permute-done((bf16[8,48,768]{2,1,0:T(8,128)(2,1)S(1)}, bf16[8,48,768]{2,1,0:T(8,128)(2,1)S(1)}, u32[]{:S(2)}, u32[]{:S(2)}) %collective-permute-start.4) | collective-permute-done | bytes 589856 | tf_op jit(solution)/shard_map/ppermute | solution.py:56
  165.7 4.6 %collective-permute-done.5 = bf16[8,48,768]{2,1,0:T(8,128)(2,1)S(1)} collective-permute-done((bf16[8,48,768]{2,1,0:T(8,128)(2,1)S(1)}, bf16[8,48,768]{2,1,0:T(8,128)(2,1)S(1)}, u32[]{:S(2)}, u32[]{:S(2)}) %collective-permute-start.5) | collective-permute-done | bytes 589856 | tf_op jit(solution)/shard_map/ppermute | solution.py:56
  170.4 3.0 %fusion.3 = f32[768,512]{1,0:T(8,128)S(1)} fusion(bf16[768,1536]{1,0:T(8,128)(2,1)} %bitcast.2, bf16[1536,768]{1,0:T(8,128)(2,1)S(1)} %bitcast.29), kind=kOutput, calls=%fused_computation.10 | convolution fusion | flops 1207959552 | bytes 5505024 | tf_op jit(solution)/shard_map/dot_general | solution.py:87
  173.4 2.3 %add_convert_fusion = bf16[768,1536]{1,0:T(8,128)(2,1)} fusion(f32[768,1536]{1,0:T(8,128)S(1)} %fusion.11, bf16[1536,768]{1,0:T(8,128)(2,1)S(1)} %bitcast.30, f32[768,512]{1,0:T(8,128)S(1)} %fusion.3), kind=kOutput, calls=%fused_computation | convolution fusion | flops 607518720 | bytes 9437184 | tf_op jit(solution)/shard_map/dot_general | solution.py:89
  175.7 0.0 copy-start.2
  175.7 5.9 %all-to-all-start.3 = ((bf16[32,24,1536]{2,1,0:T(8,128)(2,1)}), bf16[32,24,1536]{2,1,0:T(8,128)(2,1)S(1)}, u32[]{:S(2)}, u32[]{:S(2)}) async-start(bf16[32,24,1536]{2,1,0:T(8,128)(2,1)} %bitcast.26), calls=%async_computation.3 | async-start | bytes 4718592 | tf_op jit(solution)/shard_map/all_to_all | solution.py:94
  181.6 0.0 copy-done.2
  181.6 0.3 select_reduce_fusion
  181.9 30.8 %all-to-all-done.3 = bf16[32,24,1536]{2,1,0:T(8,128)(2,1)S(1)} async-done(((bf16[32,24,1536]{2,1,0:T(8,128)(2,1)}), bf16[32,24,1536]{2,1,0:T(8,128)(2,1)S(1)}, u32[]{:S(2)}, u32[]{:S(2)}) %all-to-all-start.3) | async-done | bytes 2359328 | tf_op jit(solution)/shard_map/all_to_all | solution.py:94
  212.7 0.5 fusion.20
  213.2 1.2 fusion
  (18 shorter events, 0.5 us)
Async XLA Ops:
  0.0 47.7 %copy-start = (bf16[128,1536]{1,0:T(8,128)(2,1)S(1)}, bf16[128,1536]{1,0:T(8,128)(2,1)}, u32[]{:S(2)}) copy-start(bf16[128,1536]{1,0:T(8,128)(2,1)} %param.7) | copy-start | bytes 1179652
  0.0 46.4 %copy-start.1 = (s32[128,6]{0,1:T(8,128)S(1)}, s32[128,6]{0,1:T(8,128)}, u32[]{:S(2)}) copy-start(s32[128,6]{0,1:T(8,128)} %param.11) | copy-start | bytes 9220
  0.0 46.2 %copy-start.3 = (s32[128]{0:T(128)S(1)}, s32[128]{0:T(128)}, u32[]{:S(2)}) copy-start(s32[128]{0:T(128)} %param.13) | copy-start | bytes 1540
  36.8 19.5 %all-to-all-start.1 = ((bf16[8,48,768]{2,1,0:T(8,128)(2,1)}), bf16[8,48,768]{2,1,0:T(8,128)(2,1)S(1)}, u32[]{:S(2)}, u32[]{:S(2)}) async-start(bf16[8,48,768]{2,1,0:T(8,128)(2,1)} %all-gather), calls=%async_computation.1 | async-start | bytes 1179648 | tf_op jit(solution)/shard_map/all_to_all | solution.py:65
  56.2 67.2 %all-to-all-start = ((bf16[32,24,1536]{2,1,0:T(8,128)(2,1)}), bf16[32,24,1536]{2,1,0:T(8,128)(2,1)}, u32[]{:S(2)}, u32[]{:S(2)}) async-start(bf16[32,24,1536]{2,1,0:T(8,128)(2,1)} %bitcast.1), calls=%async_computation | async-start | bytes 4718592 | tf_op jit(solution)/shard_map/all_to_all | solution.py:51
  62.4 60.9 %collective-permute-start = (bf16[8,48,768]{2,1,0:T(8,128)(2,1)S(1)}, bf16[8,48,768]{2,1,0:T(8,128)(2,1)S(1)}, u32[]{:S(2)}, u32[]{:S(2)}) collective-permute-start(bf16[8,48,768]{2,1,0:T(8,128)(2,1)S(1)} %all-to-all-done.1), channel_id=1, source_target_pairs={{0,32},{32,64},{64,96},{96,1},{1,33},{33,65},{65,97},{97,2},{2,34}... | collective-permute-start | bytes 1769480 | tf_op jit(solution)/shard_map/ppermute | solution.py:56
  64.4 58.0 %collective-permute-start.2 = (bf16[4,48,768]{2,1,0:T(8,128)(2,1)S(1)}, bf16[4,48,768]{2,1,0:T(8,128)(2,1)S(1)}, u32[]{:S(2)}, u32[]{:S(2)}) collective-permute-start(bf16[4,48,768]{2,1,0:T(8,128)(2,1)S(1)} %get-tuple-element.25), channel_id=1, source_target_pairs={{0,64},{32,96},{64,1},{96,33},{1,65},{33,97},{65,2},{97,34},{2,66}... | collective-permute-start | bytes 884744 | tf_op jit(solution)/shard_map/ppermute | solution.py:56
  66.6 55.8 %collective-permute-start.3 = (bf16[4,48,768]{2,1,0:T(8,128)(2,1)S(1)}, bf16[4,48,768]{2,1,0:T(8,128)(2,1)S(1)}, u32[]{:S(2)}, u32[]{:S(2)}) collective-permute-start(bf16[4,48,768]{2,1,0:T(8,128)(2,1)S(1)} %get-tuple-element.26), channel_id=1, source_target_pairs={{0,67},{32,99},{64,0},{96,32},{1,64},{33,96},{65,1},{97,33},{2,65}... | collective-permute-start | bytes 884744 | tf_op jit(solution)/shard_map/ppermute | solution.py:56
  71.8 51.6 %collective-permute-start.1 = (bf16[8,48,768]{2,1,0:T(8,128)(2,1)S(1)}, bf16[8,48,768]{2,1,0:T(8,128)(2,1)S(1)}, u32[]{:S(2)}, u32[]{:S(2)}) collective-permute-start(bf16[8,48,768]{2,1,0:T(8,128)(2,1)S(1)} %all-to-all-done.1), channel_id=1, source_target_pairs={{0,99},{32,0},{64,32},{96,64},{1,96},{33,1},{65,33},{97,65},{2,97}... | collective-permute-start | bytes 1769480 | tf_op jit(solution)/shard_map/ppermute | solution.py:56
  123.4 15.9 %all-to-all-start.2 = ((bf16[8,48,768]{2,1,0:T(8,128)(2,1)}), bf16[8,48,768]{2,1,0:T(8,128)(2,1)S(1)}, u32[]{:S(2)}, u32[]{:S(2)}) async-start(bf16[8,48,768]{2,1,0:T(8,128)(2,1)} %all-gather.1), calls=%async_computation.2 | async-start | bytes 1179648 | tf_op jit(solution)/shard_map/all_to_all | solution.py:65
  139.4 16.4 %collective-permute-start.6 = (bf16[4,48,768]{2,1,0:T(8,128)(2,1)S(1)}, bf16[4,48,768]{2,1,0:T(8,128)(2,1)S(1)}, u32[]{:S(2)}, u32[]{:S(2)}) collective-permute-start(bf16[4,48,768]{2,1,0:T(8,128)(2,1)S(1)} %get-tuple-element.23), channel_id=1, source_target_pairs={{0,64},{32,96},{64,1},{96,33},{1,65},{33,97},{65,2},{97,34},{2,66}... | collective-permute-start | bytes 884744 | tf_op jit(solution)/shard_map/ppermute | solution.py:56
  141.3 16.4 %collective-permute-start.7 = (bf16[4,48,768]{2,1,0:T(8,128)(2,1)S(1)}, bf16[4,48,768]{2,1,0:T(8,128)(2,1)S(1)}, u32[]{:S(2)}, u32[]{:S(2)}) collective-permute-start(bf16[4,48,768]{2,1,0:T(8,128)(2,1)S(1)} %get-tuple-element.24), channel_id=1, source_target_pairs={{0,67},{32,99},{64,0},{96,32},{1,64},{33,96},{65,1},{97,33},{2,65}... | collective-permute-start | bytes 884744 | tf_op jit(solution)/shard_map/ppermute | solution.py:56
  146.8 18.9 %collective-permute-start.4 = (bf16[8,48,768]{2,1,0:T(8,128)(2,1)S(1)}, bf16[8,48,768]{2,1,0:T(8,128)(2,1)S(1)}, u32[]{:S(2)}, u32[]{:S(2)}) collective-permute-start(bf16[8,48,768]{2,1,0:T(8,128)(2,1)S(1)} %all-to-all-done.2), channel_id=1, source_target_pairs={{0,32},{32,64},{64,96},{96,1},{1,33},{33,65},{65,97},{97,2},{2,34}... | collective-permute-start | bytes 1769480 | tf_op jit(solution)/shard_map/ppermute | solution.py:56
  148.7 21.6 %collective-permute-start.5 = (bf16[8,48,768]{2,1,0:T(8,128)(2,1)S(1)}, bf16[8,48,768]{2,1,0:T(8,128)(2,1)S(1)}, u32[]{:S(2)}, u32[]{:S(2)}) collective-permute-start(bf16[8,48,768]{2,1,0:T(8,128)(2,1)S(1)} %all-to-all-done.2), channel_id=1, source_target_pairs={{0,99},{32,0},{64,32},{96,64},{1,96},{33,1},{65,33},{97,65},{2,97}... | collective-permute-start | bytes 1769480 | tf_op jit(solution)/shard_map/ppermute | solution.py:56
  175.7 5.9 %copy-start.2 = (f32[128,6]{0,1:T(8,128)S(1)}, f32[128,6]{0,1:T(8,128)}, u32[]{:S(2)}) copy-start(f32[128,6]{0,1:T(8,128)} %param.12) | copy-start | bytes 9220
  175.7 37.0 %all-to-all-start.3 = ((bf16[32,24,1536]{2,1,0:T(8,128)(2,1)}), bf16[32,24,1536]{2,1,0:T(8,128)(2,1)S(1)}, u32[]{:S(2)}, u32[]{:S(2)}) async-start(bf16[32,24,1536]{2,1,0:T(8,128)(2,1)} %bitcast.26), calls=%async_computation.3 | async-start | bytes 4718592 | tf_op jit(solution)/shard_map/all_to_all | solution.py:94

commit v14 on v11

--- a/solution.py
+++ b/solution.py
@@ -6,7 +6,7 @@
 
 AXES = ("y", "zl", "c", "x", "zh")
 ROWS = ("y", "zl", "c", "x", "zh")
-TOKEN_GROUP = ("x", "y", "c")
+TOKEN_GROUP = ("y", "x", "c")
 
 
 def local(tokens, gate_train, up_train, down_train, routes, route_scores, live):
@@ -33,6 +33,10 @@
     n_pairs, local_experts, rows, width = slabs[0].shape
     route_share = route_scores / jnp.sum(route_scores, axis=1, keepdims=True)
     flat_route = routes.reshape(-1)
+    pair, core = flat_route // 2, flat_route % 2
+    x_size = lax.axis_size("x")
+    y_size = experts // (2 * x_size)
+    flat_route = ((pair % y_size) * x_size + pair // y_size) * 2 + core
     flat_live = jnp.repeat(live, top_count)
     expert_ids = jnp.arange(experts, dtype=jnp.int32)
     onehot = (flat_route[:, None] == expert_ids[None, :]) & (flat_live[:, None] > 0)

time: 206 us -> 207 us (level)
  no operation moved by 1% of the time
where the time goes in v14:
time: 207 us; the launch traced here: 206 us
  blocking collectives  77.2 us (37%)
  waiting for transfers between devices  56.5 us (27%)
  starting transfers between devices  53.2 us (26%)
  matrix products  10.1 us (5%)
  other arithmetic  4.48 us (2%)
  local copies, waits for them, and re-layouts  3.7 us (2%)
    all_gather x2, blocking collectives, local(): slabs = tuple((lax.all_gather(w, 'zh', axis=0, tiled=False) for w in slabs))  57.9 us
    all_to_all x1, waiting for transfers between devices, local(): lax.all_to_all(expert_rows, TOKEN_GROUP, split_axis=0, concat_axis=0, til...  31.2 us
    ppermute x8, starting transfers between devices, local(): shift = lambda v, k: lax.ppermute(v, ('zl', 'zh'), pairs(k))  30.2 us
    ppermute x8, waiting for transfers between devices, local(): shift = lambda v, k: lax.ppermute(v, ('zl', 'zh'), pairs(k))  24.7 us
    all_to_all x1, blocking collectives, local(): lax.all_to_all(slab, ('y', 'c'), split_axis=0, concat_axis=0, tiled=True)  19.4 us
    all_to_all x1, starting transfers between devices, local(): lax.all_to_all(outgoing, TOKEN_GROUP, split_axis=0, concat_axis=0, tiled=...  10.5 us
    all_to_all x1, starting transfers between devices, local(): lax.all_to_all(expert_rows, TOKEN_GROUP, split_axis=0, concat_axis=0, til...  8.24 us
    all_to_all x1, starting transfers between devices, local(): lax.all_to_all(slab, ('y', 'c'), split_axis=0, concat_axis=0, tiled=True)  4.19 us
  transfers between devices with their start and end apart: 11, of which 5 were waited for; matrix products, arithmetic and copies ran while one was open for 1% of the time, Pallas kernels for 0%

profile of v14, /device:TPU:1, one launch (start us, length us, event | category | flops | bytes accessed | tf_op | source)
XLA Modules:
  0.0 205.6 jit_solution(17041458647933475709)
XLA Ops:
  0.0 0.0 copy-start
  0.0 0.0 copy-start.3
  0.0 1.0 convert.18
  1.0 0.9 convert.19
  2.0 0.9 convert_bitcast_fusion
  3.0 0.7 broadcast_compare_fusion
  3.7 0.1 broadcast_in_dim.33.clone
  3.7 0.2 gt.23
  3.9 0.8 copy.35
  4.7 0.1 reshape.214
  4.9 0.4 fusion.8
  5.2 0.1 convert_element_type.37
  5.4 0.1 copy.37
  5.4 0.0 copy-done.3
  5.5 0.4 fusion.1
  5.9 0.0 copy-done
  5.9 2.2 %convolution_convert_fusion = bf16[768,1536]{1,0:T(8,128)(2,1)} fusion(pred[768,128]{1,0:T(8,128)(4,1)S(1)} %fusion.1, bf16[128,1536]{1,0:T(8,128)(2,1)S(1)} %copy-done), kind=kOutput, calls=%fused_computation.1 | convolution fusion | flops 303169536 | bytes 2850816 | tf_op jit(solution)/shard_map/dot_general | solution.py:54
  8.1 10.5 %all-to-all-start = ((bf16[32,24,1536]{2,1,0:T(8,128)(2,1)}), bf16[32,24,1536]{2,1,0:T(8,128)(2,1)S(1)}, u32[]{:S(2)}, u32[]{:S(2)}) async-start(bf16[32,24,1536]{2,1,0:T(8,128)(2,1)} %bitcast.1), calls=%async_computation | async-start | bytes 4718592 | tf_op jit(solution)/shard_map/all_to_all | solution.py:55
  18.6 30.5 %all-gather = bf16[8,48,768]{2,1,0:T(8,128)(2,1)} all-gather(bf16[2,48,768]{2,1,0:T(8,128)(2,1)S(1)} %get-tuple-element.18), channel_id=2, replica_groups=mesh['y'=4,'zl'=4,'c'=2,'x'=4,'zh'=4] {'zh'}, dimensions={0}, use_global_device_ids=true | all-gather | bytes 737280 | tf_op jit(solution)/shard_map/all_gather | solution.py:32
  49.1 27.4 %all-gather.1 = bf16[8,48,768]{2,1,0:T(8,128)(2,1)S(1)} all-gather(bf16[2,48,768]{2,1,0:T(8,128)(2,1)S(1)} %get-tuple-element.19), channel_id=3, replica_groups=mesh['y'=4,'zl'=4,'c'=2,'x'=4,'zh'=4] {'zh'}, dimensions={0}, use_global_device_ids=true | all-gather | bytes 737280 | tf_op jit(solution)/shard_map/all_gather | solution.py:32
  76.5 0.0 all-to-all-done
  76.5 0.0 copy-start.1
  76.5 1.4 copy-done.1
  77.9 19.4 %all_to_all.34 = bf16[8,48,768]{2,1,0:T(8,128)(2,1)S(1)} all-to-all(bf16[8,48,768]{2,1,0:T(8,128)(2,1)S(1)} %all-gather.1), channel_id=1, replica_groups=mesh['y'=4,'zl'=4,'c'=2,'x'=4,'zh'=4] {'y','c'}, dimensions={0} | all-to-all | bytes 1179648 | tf_op jit(solution)/shard_map/all_to_all | solution.py:67
  97.3 4.2 %all-to-all-start.1 = ((bf16[8,48,768]{2,1,0:T(8,128)(2,1)}), bf16[8,48,768]{2,1,0:T(8,128)(2,1)S(1)}, u32[]{:S(2)}, u32[]{:S(2)}) async-start(bf16[8,48,768]{2,1,0:T(8,128)(2,1)} %bitcast.5), calls=%async_computation.1 | async-start | bytes 1179648 | tf_op jit(solution)/shard_map/all_to_all | solution.py:67
  101.5 1.9 collective-permute-start.6
  103.5 5.5 %collective-permute-start.7 = (bf16[4,48,768]{2,1,0:T(8,128)(2,1)S(1)}, bf16[4,48,768]{2,1,0:T(8,128)(2,1)S(1)}, u32[]{:S(2)}, u32[]{:S(2)}) collective-permute-start(bf16[4,48,768]{2,1,0:T(8,128)(2,1)S(1)} %get-tuple-element.24), channel_id=1, source_target_pairs={{0,67},{32,99},{64,0},{96,32},{1,64},{33,96},{65,1},{97,33},{2,65}... | collective-permute-start | bytes 884744 | tf_op jit(solution)/shard_map/ppermute | solution.py:61
  109.0 1.9 collective-permute-start.4
  110.9 0.6 all-to-all-done.1
  111.6 1.9 collective-permute-start.2
  113.5 5.5 %collective-permute-start.3 = (bf16[4,48,768]{2,1,0:T(8,128)(2,1)S(1)}, bf16[4,48,768]{2,1,0:T(8,128)(2,1)S(1)}, u32[]{:S(2)}, u32[]{:S(2)}) collective-permute-start(bf16[4,48,768]{2,1,0:T(8,128)(2,1)S(1)} %get-tuple-element.26), channel_id=1, source_target_pairs={{0,67},{32,99},{64,0},{96,32},{1,64},{33,96},{65,1},{97,33},{2,65}... | collective-permute-start | bytes 884744 | tf_op jit(solution)/shard_map/ppermute | solution.py:61
  119.0 0.0 collective-permute-done.6
  119.0 1.9 collective-permute-start
  121.0 0.2 broadcast.229.clone.1
  121.2 0.0 collective-permute-done.7
  121.3 4.6 %collective-permute-start.5 = (bf16[8,48,768]{2,1,0:T(8,128)(2,1)S(1)}, bf16[8,48,768]{2,1,0:T(8,128)(2,1)S(1)}, u32[]{:S(2)}, u32[]{:S(2)}) collective-permute-start(bf16[8,48,768]{2,1,0:T(8,128)(2,1)S(1)} %all_to_all.34), channel_id=1, source_target_pairs={{0,99},{32,0},{64,32},{96,64},{1,96},{33,1},{65,33},{97,65},{2,97}... | collective-permute-start | bytes 1769480 | tf_op jit(solution)/shard_map/ppermute | solution.py:61
  125.8 0.2 broadcast.229.clone
  126.1 0.1 pad_maximum_fusion.1
  126.2 13.0 %collective-permute-done.2 = bf16[4,48,768]{2,1,0:T(8,128)(2,1)S(1)} collective-permute-done((bf16[4,48,768]{2,1,0:T(8,128)(2,1)S(1)}, bf16[4,48,768]{2,1,0:T(8,128)(2,1)S(1)}, u32[]{:S(2)}, u32[]{:S(2)}) %collective-permute-start.2) | collective-permute-done | bytes 294944 | tf_op jit(solution)/shard_map/ppermute | solution.py:61
  139.2 7.0 %collective-permute-start.1 = (bf16[8,48,768]{2,1,0:T(8,128)(2,1)S(1)}, bf16[8,48,768]{2,1,0:T(8,128)(2,1)S(1)}, u32[]{:S(2)}, u32[]{:S(2)}) collective-permute-start(bf16[8,48,768]{2,1,0:T(8,128)(2,1)S(1)} %all-to-all-done.1), channel_id=1, source_target_pairs={{0,99},{32,0},{64,32},{96,64},{1,96},{33,1},{65,33},{97,65},{2,97}... | collective-permute-start | bytes 1769480 | tf_op jit(solution)/shard_map/ppermute | solution.py:61
  146.2 0.0 collective-permute-done.3
  146.2 0.1 pad_maximum_fusion
  146.2 0.0 collective-permute-done.4
  146.3 0.0 copy-start.2
  146.3 9.7 %collective-permute-done = bf16[8,48,768]{2,1,0:T(8,128)(2,1)S(1)} collective-permute-done((bf16[8,48,768]{2,1,0:T(8,128)(2,1)S(1)}, bf16[8,48,768]{2,1,0:T(8,128)(2,1)S(1)}, u32[]{:S(2)}, u32[]{:S(2)}) %collective-permute-start) | collective-permute-done | bytes 589856 | tf_op jit(solution)/shard_map/ppermute | solution.py:61
  156.1 0.0 collective-permute-done.5
  156.2 0.0 copy-done.2
  156.2 1.4 fusion.3
  157.6 2.0 collective-permute-done.1
  159.7 1.4 fusion.5
  161.0 0.8 fusion.11
  161.9 2.3 %add_convert_fusion = bf16[768,1536]{1,0:T(8,128)(2,1)} fusion(f32[768,1536]{1,0:T(8,128)S(1)} %fusion.11, bf16[1536,768]{1,0:T(8,128)(2,1)S(1)} %bitcast.34, f32[768,512]{1,0:T(8,128)S(1)} %fusion.3), kind=kOutput, calls=%fused_computation | convolution fusion | flops 607518720 | bytes 9437184 | tf_op jit(solution)/shard_map/dot_general | solution.py:86
  164.1 0.0 copy-start.4
  164.1 8.2 %all-to-all-start.3 = ((bf16[32,24,1536]{2,1,0:T(8,128)(2,1)}), bf16[32,24,1536]{2,1,0:T(8,128)(2,1)S(1)}, u32[]{:S(2)}, u32[]{:S(2)}) async-start(bf16[32,24,1536]{2,1,0:T(8,128)(2,1)} %bitcast.28), calls=%async_computation.3 | async-start | bytes 4718592 | tf_op jit(solution)/shard_map/all_to_all | solution.py:91
  172.4 0.0 copy-done.4
  172.4 0.3 select_reduce_fusion
  172.7 31.2 %all-to-all-done.3 = bf16[32,24,1536]{2,1,0:T(8,128)(2,1)S(1)} async-done(((bf16[32,24,1536]{2,1,0:T(8,128)(2,1)}), bf16[32,24,1536]{2,1,0:T(8,128)(2,1)S(1)}, u32[]{:S(2)}, u32[]{:S(2)}) %all-to-all-start.3) | async-done | bytes 2359328 | tf_op jit(solution)/shard_map/all_to_all | solution.py:91
  203.9 0.5 fusion.20
  204.4 1.2 fusion
  (19 shorter events, 0.6 us)
Async XLA Ops:
  0.0 5.9 %copy-start = (bf16[128,1536]{1,0:T(8,128)(2,1)S(1)}, bf16[128,1536]{1,0:T(8,128)(2,1)}, u32[]{:S(2)}) copy-start(bf16[128,1536]{1,0:T(8,128)(2,1)} %param.7) | copy-start | bytes 1179652
  0.0 5.4 %copy-start.3 = (s32[128,6]{0,1:T(8,128)S(1)}, s32[128,6]{0,1:T(8,128)}, u32[]{:S(2)}) copy-start(s32[128,6]{0,1:T(8,128)} %param.11) | copy-start | bytes 9220
  8.1 68.4 %all-to-all-start = ((bf16[32,24,1536]{2,1,0:T(8,128)(2,1)}), bf16[32,24,1536]{2,1,0:T(8,128)(2,1)S(1)}, u32[]{:S(2)}, u32[]{:S(2)}) async-start(bf16[32,24,1536]{2,1,0:T(8,128)(2,1)} %bitcast.1), calls=%async_computation | async-start | bytes 4718592 | tf_op jit(solution)/shard_map/all_to_all | solution.py:55
  76.5 1.4 copy-start.1
  97.3 14.3 %all-to-all-start.1 = ((bf16[8,48,768]{2,1,0:T(8,128)(2,1)}), bf16[8,48,768]{2,1,0:T(8,128)(2,1)S(1)}, u32[]{:S(2)}, u32[]{:S(2)}) async-start(bf16[8,48,768]{2,1,0:T(8,128)(2,1)} %bitcast.5), calls=%async_computation.1 | async-start | bytes 1179648 | tf_op jit(solution)/shard_map/all_to_all | solution.py:67
  101.5 17.5 %collective-permute-start.6 = (bf16[4,48,768]{2,1,0:T(8,128)(2,1)S(1)}, bf16[4,48,768]{2,1,0:T(8,128)(2,1)S(1)}, u32[]{:S(2)}, u32[]{:S(2)}) collective-permute-start(bf16[4,48,768]{2,1,0:T(8,128)(2,1)S(1)} %get-tuple-element.23), channel_id=1, source_target_pairs={{0,64},{32,96},{64,1},{96,33},{1,65},{33,97},{65,2},{97,34},{2,66}... | collective-permute-start | bytes 884744 | tf_op jit(solution)/shard_map/ppermute | solution.py:61
  103.5 17.7 %collective-permute-start.7 = (bf16[4,48,768]{2,1,0:T(8,128)(2,1)S(1)}, bf16[4,48,768]{2,1,0:T(8,128)(2,1)S(1)}, u32[]{:S(2)}, u32[]{:S(2)}) collective-permute-start(bf16[4,48,768]{2,1,0:T(8,128)(2,1)S(1)} %get-tuple-element.24), channel_id=1, source_target_pairs={{0,67},{32,99},{64,0},{96,32},{1,64},{33,96},{65,1},{97,33},{2,65}... | collective-permute-start | bytes 884744 | tf_op jit(solution)/shard_map/ppermute | solution.py:61
  109.0 37.3 %collective-permute-start.4 = (bf16[8,48,768]{2,1,0:T(8,128)(2,1)S(1)}, bf16[8,48,768]{2,1,0:T(8,128)(2,1)S(1)}, u32[]{:S(2)}, u32[]{:S(2)}) collective-permute-start(bf16[8,48,768]{2,1,0:T(8,128)(2,1)S(1)} %all_to_all.34), channel_id=1, source_target_pairs={{0,32},{32,64},{64,96},{96,1},{1,33},{33,65},{65,97},{97,2},{2,34}... | collective-permute-start | bytes 1769480 | tf_op jit(solution)/shard_map/ppermute | solution.py:61
  111.6 27.6 %collective-permute-start.2 = (bf16[4,48,768]{2,1,0:T(8,128)(2,1)S(1)}, bf16[4,48,768]{2,1,0:T(8,128)(2,1)S(1)}, u32[]{:S(2)}, u32[]{:S(2)}) collective-permute-start(bf16[4,48,768]{2,1,0:T(8,128)(2,1)S(1)} %get-tuple-element.25), channel_id=1, source_target_pairs={{0,64},{32,96},{64,1},{96,33},{1,65},{33,97},{65,2},{97,34},{2,66}... | collective-permute-start | bytes 884744 | tf_op jit(solution)/shard_map/ppermute | solution.py:61
  113.5 32.6 %collective-permute-start.3 = (bf16[4,48,768]{2,1,0:T(8,128)(2,1)S(1)}, bf16[4,48,768]{2,1,0:T(8,128)(2,1)S(1)}, u32[]{:S(2)}, u32[]{:S(2)}) collective-permute-start(bf16[4,48,768]{2,1,0:T(8,128)(2,1)S(1)} %get-tuple-element.26), channel_id=1, source_target_pairs={{0,67},{32,99},{64,0},{96,32},{1,64},{33,96},{65,1},{97,33},{2,65}... | collective-permute-start | bytes 884744 | tf_op jit(solution)/shard_map/ppermute | solution.py:61
  119.0 37.0 %collective-permute-start = (bf16[8,48,768]{2,1,0:T(8,128)(2,1)S(1)}, bf16[8,48,768]{2,1,0:T(8,128)(2,1)S(1)}, u32[]{:S(2)}, u32[]{:S(2)}) collective-permute-start(bf16[8,48,768]{2,1,0:T(8,128)(2,1)S(1)} %all-to-all-done.1), channel_id=1, source_target_pairs={{0,32},{32,64},{64,96},{96,1},{1,33},{33,65},{65,97},{97,2},{2,34}... | collective-permute-start | bytes 1769480 | tf_op jit(solution)/shard_map/ppermute | solution.py:61
  121.3 34.8 %collective-permute-start.5 = (bf16[8,48,768]{2,1,0:T(8,128)(2,1)S(1)}, bf16[8,48,768]{2,1,0:T(8,128)(2,1)S(1)}, u32[]{:S(2)}, u32[]{:S(2)}) collective-permute-start(bf16[8,48,768]{2,1,0:T(8,128)(2,1)S(1)} %all_to_all.34), channel_id=1, source_target_pairs={{0,99},{32,0},{64,32},{96,64},{1,96},{33,1},{65,33},{97,65},{2,97}... | collective-permute-start | bytes 1769480 | tf_op jit(solution)/shard_map/ppermute | solution.py:61
  139.2 20.4 %collective-permute-start.1 = (bf16[8,48,768]{2,1,0:T(8,128)(2,1)S(1)}, bf16[8,48,768]{2,1,0:T(8,128)(2,1)S(1)}, u32[]{:S(2)}, u32[]{:S(2)}) collective-permute-start(bf16[8,48,768]{2,1,0:T(8,128)(2,1)S(1)} %all-to-all-done.1), channel_id=1, source_target_pairs={{0,99},{32,0},{64,32},{96,64},{1,96},{33,1},{65,33},{97,65},{2,97}... | collective-permute-start | bytes 1769480 | tf_op jit(solution)/shard_map/ppermute | solution.py:61
  146.3 9.9 %copy-start.2 = (bf16[32,24,1536]{2,1,0:T(8,128)(2,1)S(1)}, bf16[32,24,1536]{2,1,0:T(8,128)(2,1)}, u32[]{:S(2)}) copy-start(bf16[32,24,1536]{2,1,0:T(8,128)(2,1)} %copy-done.1) | copy-start | bytes 7077892
  164.1 8.3 %copy-start.4 = (f32[128,6]{0,1:T(8,128)S(1)}, f32[128,6]{0,1:T(8,128)}, u32[]{:S(2)}) copy-start(f32[128,6]{0,1:T(8,128)} %param.12) | copy-start | bytes 9220
  164.1 39.8 %all-to-all-start.3 = ((bf16[32,24,1536]{2,1,0:T(8,128)(2,1)}), bf16[32,24,1536]{2,1,0:T(8,128)(2,1)S(1)}, u32[]{:S(2)}, u32[]{:S(2)}) async-start(bf16[32,24,1536]{2,1,0:T(8,128)(2,1)} %bitcast.28), calls=%async_computation.3 | async-start | bytes 4718592 | tf_op jit(solution)/shard_map/all_to_all | solution.py:91

commit v15 on v11

--- a/solution.py
+++ b/solution.py
@@ -62,11 +62,12 @@
         slab = slab.reshape(n_pairs * local_experts, rows, width)
         slab = lax.all_to_all(slab, ("y", "c"), split_axis=0, concat_axis=0, tiled=True)
         half = slab.shape[0] // 2
+        plus, minus = shift(slab, 1), shift(slab, -1)
         quarters = [
             slab,
-            shift(slab, 1),
-            shift(slab, -1),
-            jnp.concatenate([shift(slab[:half], 2), shift(slab[half:], -2)]),
+            plus,
+            minus,
+            jnp.concatenate([shift(plus[:half], 1), shift(minus[half:], -1)]),
         ]
         y_size = slab.shape[0] // local_experts
         full = jnp.zeros((y_size, zl_size, local_experts, rows, width), jnp.bfloat16)

time: 206 us -> 194 us (0.942)
  waiting for transfers between devices: 57.2 us -> 42.7 us
  starting transfers between devices: 52.9 us -> 44.9 us
  local copies, waits for them, and re-layouts: 3.7 us -> 11.2 us
    ppermute x8, waiting for transfers between devices: 26.2 us -> 7.12 us  [local(): shift = lambda v, k: lax.ppermute(v, ('zl', 'zh'), pairs(k))]
    ppermute x8, starting transfers between devices: 29 us -> 21.2 us  [local(): shift = lambda v, k: lax.ppermute(v, ('zl', 'zh'), pairs(k))]
    all_to_all x1, waiting for transfers between devices: 0.25 us -> 4.79 us  [local(): lax.all_to_all(slab, ('y', 'c'), split_axis=0, concat_axis=0, tiled=True)]
    dynamic_update_slice x8, local copies, waits for them, and re-layouts: 0.36 us -> 4.62 us  [local(): full = lax.dynamic_update_index_in_dim(full, quarter, place, axis=1)]
    slice x2 -> x4, local copies, waits for them, and re-layouts: 0.08 us -> 3.93 us  [the longest x2 1.96 us: local(): plus[:half]]
  transfers between devices with their start and end apart: 11 -> 11, of which waited for: 5 -> 5; matrix products, arithmetic and copies ran while one was open for 1% -> 6% of each run, Pallas kernels for 0% -> 0%
where the time goes in v15:
time: 194 us; the launch traced here: 193 us
  blocking collectives  78.5 us (40%)
  starting transfers between devices  44.9 us (23%)
  waiting for transfers between devices  42.7 us (22%)
  local copies, waits for them, and re-layouts  11.2 us (6%)
  matrix products  10.1 us (5%)
  other arithmetic  5.1 us (3%)
    all_gather x2, blocking collectives, local(): slabs = tuple((lax.all_gather(w, 'zh', axis=0, tiled=False) for w in slabs))  58.1 us
    all_to_all x1, waiting for transfers between devices, local(): lax.all_to_all(expert_rows, TOKEN_GROUP, split_axis=0, concat_axis=0, til...  30.8 us
    ppermute x8, starting transfers between devices, local(): shift = lambda v, k: lax.ppermute(v, ('zl', 'zh'), pairs(k))  21.2 us
    all_to_all x1, blocking collectives, local(): lax.all_to_all(slab, ('y', 'c'), split_axis=0, concat_axis=0, tiled=True)  20.4 us
    all_to_all x1, starting transfers between devices, local(): lax.all_to_all(outgoing, TOKEN_GROUP, split_axis=0, concat_axis=0, tiled=...  10.5 us
    all_to_all x1, starting transfers between devices, local(): lax.all_to_all(expert_rows, TOKEN_GROUP, split_axis=0, concat_axis=0, til...  9.01 us
    ppermute x8, waiting for transfers between devices, local(): shift = lambda v, k: lax.ppermute(v, ('zl', 'zh'), pairs(k))  7.12 us
    all_to_all x1, waiting for transfers between devices, local(): lax.all_to_all(slab, ('y', 'c'), split_axis=0, concat_axis=0, tiled=True)  4.79 us
  transfers between devices with their start and end apart: 11, of which 5 were waited for; matrix products, arithmetic and copies ran while one was open for 6% of the time, Pallas kernels for 0%

profile of v15, /device:TPU:1, one launch (start us, length us, event | category | flops | bytes accessed | tf_op | source)
XLA Modules:
  0.0 193.0 jit_solution(10587585678331851917)
XLA Ops:
  0.0 0.0 copy-start
  0.0 1.0 convert_bitcast_fusion
  1.0 0.9 convert.19
  2.0 0.9 convert.18
  3.0 0.7 pad_maximum_fusion.2
  3.6 0.8 copy.29
  4.4 0.1 eq.40
  4.6 0.7 broadcast_compare_fusion
  5.2 0.1 broadcast_in_dim.32.clone
  5.3 0.2 gt.23
  5.5 0.4 fusion.8
  5.9 0.1 convert_element_type.37
  6.0 0.1 copy.31
  6.0 0.0 copy-done.2
  6.1 0.4 fusion.1
  6.5 0.0 copy-done
  6.5 2.2 %convolution_convert_fusion = bf16[768,1536]{1,0:T(8,128)(2,1)} fusion(pred[768,128]{1,0:T(8,128)(4,1)S(1)} %fusion.1, bf16[128,1536]{1,0:T(8,128)(2,1)S(1)} %copy-done), kind=kOutput, calls=%fused_computation.1 | convolution fusion | flops 303169536 | bytes 2850816 | tf_op jit(solution)/shard_map/dot_general | solution.py:50
  8.7 10.5 %all-to-all-start = ((bf16[32,24,1536]{2,1,0:T(8,128)(2,1)}), bf16[32,24,1536]{2,1,0:T(8,128)(2,1)S(1)}, u32[]{:S(2)}, u32[]{:S(2)}) async-start(bf16[32,24,1536]{2,1,0:T(8,128)(2,1)} %bitcast.1), calls=%async_computation | async-start | bytes 4718592 | tf_op jit(solution)/shard_map/all_to_all | solution.py:51
  19.2 31.1 %all-gather = bf16[8,48,768]{2,1,0:T(8,128)(2,1)S(1)} all-gather(bf16[2,48,768]{2,1,0:T(8,128)(2,1)} %get-tuple-element.18), channel_id=2, replica_groups=mesh['y'=4,'zl'=4,'c'=2,'x'=4,'zh'=4] {'zh'}, dimensions={0}, use_global_device_ids=true | all-gather | bytes 737280 | tf_op jit(solution)/shard_map/all_gather | solution.py:32
  50.3 27.0 %all-gather.1 = bf16[8,48,768]{2,1,0:T(8,128)(2,1)} all-gather(bf16[2,48,768]{2,1,0:T(8,128)(2,1)S(1)} %get-tuple-element.19), channel_id=3, replica_groups=mesh['y'=4,'zl'=4,'c'=2,'x'=4,'zh'=4] {'zh'}, dimensions={0}, use_global_device_ids=true | all-gather | bytes 737280 | tf_op jit(solution)/shard_map/all_gather | solution.py:32
  77.3 0.0 all-to-all-done
  77.3 20.4 %all_to_all.34 = bf16[8,48,768]{2,1,0:T(8,128)(2,1)} all-to-all(bf16[8,48,768]{2,1,0:T(8,128)(2,1)S(1)} %all-gather), channel_id=1, replica_groups=mesh['y'=4,'zl'=4,'c'=2,'x'=4,'zh'=4] {'y','c'}, dimensions={0} | all-to-all | bytes 1179648 | tf_op jit(solution)/shard_map/all_to_all | solution.py:63
  97.7 4.2 %all-to-all-start.2 = ((bf16[8,48,768]{2,1,0:T(8,128)(2,1)}), bf16[8,48,768]{2,1,0:T(8,128)(2,1)S(1)}, u32[]{:S(2)}, u32[]{:S(2)}) async-start(bf16[8,48,768]{2,1,0:T(8,128)(2,1)} %all-gather.1), calls=%async_computation.2 | async-start | bytes 1179648 | tf_op jit(solution)/shard_map/all_to_all | solution.py:63
  101.9 1.9 collective-permute-start.1
  103.8 3.4 %collective-permute-start = (bf16[8,48,768]{2,1,0:T(8,128)(2,1)}, bf16[8,48,768]{2,1,0:T(8,128)(2,1)}, u32[]{:S(2)}, u32[]{:S(2)}) collective-permute-start(bf16[8,48,768]{2,1,0:T(8,128)(2,1)} %all_to_all.34), channel_id=1, source_target_pairs={{0,32},{32,64},{64,96},{96,1},{1,33},{33,65},{65,97},{97,2},{2,34}... | collective-permute-start | bytes 1769480 | tf_op jit(solution)/shard_map/ppermute | solution.py:57
  107.2 4.8 %all-to-all-done.2 = bf16[8,48,768]{2,1,0:T(8,128)(2,1)S(1)} async-done(((bf16[8,48,768]{2,1,0:T(8,128)(2,1)}), bf16[8,48,768]{2,1,0:T(8,128)(2,1)S(1)}, u32[]{:S(2)}, u32[]{:S(2)}) %all-to-all-start.2) | async-done | bytes 589856 | tf_op jit(solution)/shard_map/all_to_all | solution.py:63
  112.0 1.9 collective-permute-start.5
  113.9 3.4 %collective-permute-start.4 = (bf16[8,48,768]{2,1,0:T(8,128)(2,1)S(1)}, bf16[8,48,768]{2,1,0:T(8,128)(2,1)}, u32[]{:S(2)}, u32[]{:S(2)}) collective-permute-start(bf16[8,48,768]{2,1,0:T(8,128)(2,1)S(1)} %all-to-all-done.2), channel_id=1, source_target_pairs={{0,32},{32,64},{64,96},{96,1},{1,33},{33,65},{65,97},{97,2},{2,34}... | collective-permute-start | bytes 1769480 | tf_op jit(solution)/shard_map/ppermute | solution.py:57
  117.3 0.0 copy-start.1
  117.4 0.2 broadcast.52.clone
  117.6 0.8 copy-done.1
  118.5 0.2 broadcast.52.clone.1
  118.7 0.1 collective-permute-done.1
  118.9 1.0 slice.85
  119.9 3.4 %collective-permute-start.3 = (bf16[4,48,768]{2,1,0:T(8,128)(2,1)S(1)}, bf16[4,48,768]{2,1,0:T(8,128)(2,1)S(1)}, u32[]{:S(2)}, u32[]{:S(2)}) collective-permute-start(bf16[4,48,768]{2,1,0:T(8,128)(2,1)S(1)} %slice.85), channel_id=1, source_target_pairs={{0,99},{32,0},{64,32},{96,64},{1,96},{33,1},{65,33},{97,65},{2,97}... | collective-permute-start | bytes 884744 | tf_op jit(solution)/shard_map/ppermute | solution.py:57
  123.3 0.0 collective-permute-done
  123.3 1.0 slice.84
  124.3 1.9 collective-permute-start.2
  126.2 5.3 %collective-permute-done.5 = bf16[8,48,768]{2,1,0:T(8,128)(2,1)} collective-permute-done((bf16[8,48,768]{2,1,0:T(8,128)(2,1)S(1)}, bf16[8,48,768]{2,1,0:T(8,128)(2,1)}, u32[]{:S(2)}, u32[]{:S(2)}) %collective-permute-start.5) | collective-permute-done | bytes 589856 | tf_op jit(solution)/shard_map/ppermute | solution.py:57
  131.5 1.0 slice.91
  132.5 3.4 %collective-permute-start.7 = (bf16[4,48,768]{2,1,0:T(8,128)(2,1)S(1)}, bf16[4,48,768]{2,1,0:T(8,128)(2,1)S(1)}, u32[]{:S(2)}, u32[]{:S(2)}) collective-permute-start(bf16[4,48,768]{2,1,0:T(8,128)(2,1)S(1)} %slice.91), channel_id=1, source_target_pairs={{0,99},{32,0},{64,32},{96,64},{1,96},{33,1},{65,33},{97,65},{2,97}... | collective-permute-start | bytes 884744 | tf_op jit(solution)/shard_map/ppermute | solution.py:57
  135.9 0.0 collective-permute-done.4
  135.9 1.0 slice.90
  136.9 1.9 collective-permute-start.6
  138.8 1.1 constant_dynamic-update-slice_fusion.6
  140.0 1.1 constant_dynamic-update-slice_fusion.2
  141.1 1.1 constant_dynamic-update-slice_fusion.5
  142.2 1.1 constant_dynamic-update-slice_fusion.1
  143.3 0.0 collective-permute-done.3
  143.3 0.0 collective-permute-done.2
  143.3 0.1 pad_maximum_fusion
  143.4 1.4 fusion.5
  144.8 0.8 fusion.11
  145.6 0.0 collective-permute-done.7
  145.7 1.7 collective-permute-done.6
  147.3 0.1 pad_maximum_fusion.1
  147.4 1.4 fusion.3
  148.8 2.2 %add_convert_fusion = bf16[768,1536]{1,0:T(8,128)(2,1)} fusion(f32[768,1536]{1,0:T(8,128)S(1)} %fusion.11, bf16[1536,768]{1,0:T(8,128)(2,1)S(1)} %bitcast.30, f32[768,512]{1,0:T(8,128)S(1)} %fusion.3), kind=kOutput, calls=%fused_computation | convolution fusion | flops 607518720 | bytes 9437184 | tf_op jit(solution)/shard_map/dot_general | solution.py:83
  151.1 9.0 %all-to-all-start.3 = ((bf16[32,24,1536]{2,1,0:T(8,128)(2,1)}), bf16[32,24,1536]{2,1,0:T(8,128)(2,1)S(1)}, u32[]{:S(2)}, u32[]{:S(2)}) async-start(bf16[32,24,1536]{2,1,0:T(8,128)(2,1)} %bitcast.28), calls=%async_computation.3 | async-start | bytes 4718592 | tf_op jit(solution)/shard_map/all_to_all | solution.py:88
  160.1 0.0 copy-done.3
  160.1 0.3 select_reduce_fusion
  160.4 30.8 %all-to-all-done.3 = bf16[32,24,1536]{2,1,0:T(8,128)(2,1)S(1)} async-done(((bf16[32,24,1536]{2,1,0:T(8,128)(2,1)}), bf16[32,24,1536]{2,1,0:T(8,128)(2,1)S(1)}, u32[]{:S(2)}, u32[]{:S(2)}) %all-to-all-start.3) | async-done | bytes 2359328 | tf_op jit(solution)/shard_map/all_to_all | solution.py:88
  191.2 0.5 fusion.20
  191.7 1.2 fusion
  (13 shorter events, 0.3 us)
Async XLA Ops:
  0.0 6.5 %copy-start = (bf16[128,1536]{1,0:T(8,128)(2,1)S(1)}, bf16[128,1536]{1,0:T(8,128)(2,1)}, u32[]{:S(2)}) copy-start(bf16[128,1536]{1,0:T(8,128)(2,1)} %param.7) | copy-start | bytes 1179652
  0.0 6.0 %copy-start.2 = (s32[128,6]{0,1:T(8,128)S(1)}, s32[128,6]{0,1:T(8,128)}, u32[]{:S(2)}) copy-start(s32[128,6]{0,1:T(8,128)} %param.11) | copy-start | bytes 9220
  8.7 68.6 %all-to-all-start = ((bf16[32,24,1536]{2,1,0:T(8,128)(2,1)}), bf16[32,24,1536]{2,1,0:T(8,128)(2,1)S(1)}, u32[]{:S(2)}, u32[]{:S(2)}) async-start(bf16[32,24,1536]{2,1,0:T(8,128)(2,1)} %bitcast.1), calls=%async_computation | async-start | bytes 4718592 | tf_op jit(solution)/shard_map/all_to_all | solution.py:51
  97.7 14.3 %all-to-all-start.2 = ((bf16[8,48,768]{2,1,0:T(8,128)(2,1)}), bf16[8,48,768]{2,1,0:T(8,128)(2,1)S(1)}, u32[]{:S(2)}, u32[]{:S(2)}) async-start(bf16[8,48,768]{2,1,0:T(8,128)(2,1)} %all-gather.1), calls=%async_computation.2 | async-start | bytes 1179648 | tf_op jit(solution)/shard_map/all_to_all | solution.py:63
  101.9 17.0 %collective-permute-start.1 = (bf16[8,48,768]{2,1,0:T(8,128)(2,1)}, bf16[8,48,768]{2,1,0:T(8,128)(2,1)}, u32[]{:S(2)}, u32[]{:S(2)}) collective-permute-start(bf16[8,48,768]{2,1,0:T(8,128)(2,1)} %all_to_all.34), channel_id=1, source_target_pairs={{0,99},{32,0},{64,32},{96,64},{1,96},{33,1},{65,33},{97,65},{2,97}... | collective-permute-start | bytes 1769480 | tf_op jit(solution)/shard_map/ppermute | solution.py:57
  103.8 19.5 %collective-permute-start = (bf16[8,48,768]{2,1,0:T(8,128)(2,1)}, bf16[8,48,768]{2,1,0:T(8,128)(2,1)}, u32[]{:S(2)}, u32[]{:S(2)}) collective-permute-start(bf16[8,48,768]{2,1,0:T(8,128)(2,1)} %all_to_all.34), channel_id=1, source_target_pairs={{0,32},{32,64},{64,96},{96,1},{1,33},{33,65},{65,97},{97,2},{2,34}... | collective-permute-start | bytes 1769480 | tf_op jit(solution)/shard_map/ppermute | solution.py:57
  112.0 19.5 %collective-permute-start.5 = (bf16[8,48,768]{2,1,0:T(8,128)(2,1)S(1)}, bf16[8,48,768]{2,1,0:T(8,128)(2,1)}, u32[]{:S(2)}, u32[]{:S(2)}) collective-permute-start(bf16[8,48,768]{2,1,0:T(8,128)(2,1)S(1)} %all-to-all-done.2), channel_id=1, source_target_pairs={{0,99},{32,0},{64,32},{96,64},{1,96},{33,1},{65,33},{97,65},{2,97}... | collective-permute-start | bytes 1769480 | tf_op jit(solution)/shard_map/ppermute | solution.py:57
  113.9 22.0 %collective-permute-start.4 = (bf16[8,48,768]{2,1,0:T(8,128)(2,1)S(1)}, bf16[8,48,768]{2,1,0:T(8,128)(2,1)}, u32[]{:S(2)}, u32[]{:S(2)}) collective-permute-start(bf16[8,48,768]{2,1,0:T(8,128)(2,1)S(1)} %all-to-all-done.2), channel_id=1, source_target_pairs={{0,32},{32,64},{64,96},{96,1},{1,33},{33,65},{65,97},{97,2},{2,34}... | collective-permute-start | bytes 1769480 | tf_op jit(solution)/shard_map/ppermute | solution.py:57
  117.3 1.1 copy-start.1
  119.9 23.4 %collective-permute-start.3 = (bf16[4,48,768]{2,1,0:T(8,128)(2,1)S(1)}, bf16[4,48,768]{2,1,0:T(8,128)(2,1)S(1)}, u32[]{:S(2)}, u32[]{:S(2)}) collective-permute-start(bf16[4,48,768]{2,1,0:T(8,128)(2,1)S(1)} %slice.85), channel_id=1, source_target_pairs={{0,99},{32,0},{64,32},{96,64},{1,96},{33,1},{65,33},{97,65},{2,97}... | collective-permute-start | bytes 884744 | tf_op jit(solution)/shard_map/ppermute | solution.py:57
  124.3 19.0 %collective-permute-start.2 = (bf16[4,48,768]{2,1,0:T(8,128)(2,1)S(1)}, bf16[4,48,768]{2,1,0:T(8,128)(2,1)S(1)}, u32[]{:S(2)}, u32[]{:S(2)}) collective-permute-start(bf16[4,48,768]{2,1,0:T(8,128)(2,1)S(1)} %slice.84), channel_id=1, source_target_pairs={{0,32},{32,64},{64,96},{96,1},{1,33},{33,65},{65,97},{97,2},{2,34}... | collective-permute-start | bytes 884744 | tf_op jit(solution)/shard_map/ppermute | solution.py:57
  132.5 13.1 %collective-permute-start.7 = (bf16[4,48,768]{2,1,0:T(8,128)(2,1)S(1)}, bf16[4,48,768]{2,1,0:T(8,128)(2,1)S(1)}, u32[]{:S(2)}, u32[]{:S(2)}) collective-permute-start(bf16[4,48,768]{2,1,0:T(8,128)(2,1)S(1)} %slice.91), channel_id=1, source_target_pairs={{0,99},{32,0},{64,32},{96,64},{1,96},{33,1},{65,33},{97,65},{2,97}... | collective-permute-start | bytes 884744 | tf_op jit(solution)/shard_map/ppermute | solution.py:57
  136.9 10.4 %collective-permute-start.6 = (bf16[4,48,768]{2,1,0:T(8,128)(2,1)S(1)}, bf16[4,48,768]{2,1,0:T(8,128)(2,1)S(1)}, u32[]{:S(2)}, u32[]{:S(2)}) collective-permute-start(bf16[4,48,768]{2,1,0:T(8,128)(2,1)S(1)} %slice.90), channel_id=1, source_target_pairs={{0,32},{32,64},{64,96},{96,1},{1,33},{33,65},{65,97},{97,2},{2,34}... | collective-permute-start | bytes 884744 | tf_op jit(solution)/shard_map/ppermute | solution.py:57
  151.1 9.0 %copy-start.3 = (f32[128,6]{0,1:T(8,128)S(1)}, f32[128,6]{0,1:T(8,128)}, u32[]{:S(2)}) copy-start(f32[128,6]{0,1:T(8,128)} %param.12) | copy-start | bytes 9220
  151.1 40.2 %all-to-all-start.3 = ((bf16[32,24,1536]{2,1,0:T(8,128)(2,1)}), bf16[32,24,1536]{2,1,0:T(8,128)(2,1)S(1)}, u32[]{:S(2)}, u32[]{:S(2)}) async-start(bf16[32,24,1536]{2,1,0:T(8,128)(2,1)} %bitcast.28), calls=%async_computation.3 | async-start | bytes 4718592 | tf_op jit(solution)/shard_map/all_to_all | solution.py:88

commit v16 on v11

--- a/solution.py
+++ b/solution.py
@@ -57,23 +57,32 @@
     shift = lambda v, k: lax.ppermute(v, ("zl", "zh"), pairs(k))
     zl_at = lax.axis_index("zl")
     places = [zl_at % zl_size, (zl_at - 1) % zl_size, (zl_at + 1) % zl_size, (zl_at + 2) % zl_size]
-    weights = []
-    for slab in slabs:
-        slab = slab.reshape(n_pairs * local_experts, rows, width)
-        slab = lax.all_to_all(slab, ("y", "c"), split_axis=0, concat_axis=0, tiled=True)
-        half = slab.shape[0] // 2
-        quarters = [
-            slab,
-            shift(slab, 1),
-            shift(slab, -1),
-            jnp.concatenate([shift(slab[:half], 2), shift(slab[half:], -2)]),
-        ]
-        y_size = slab.shape[0] // local_experts
+    y_size = experts // (2 * lax.axis_size("x"))
+
+    def assemble(quarters):
         full = jnp.zeros((y_size, zl_size, local_experts, rows, width), jnp.bfloat16)
         for quarter, place in zip(quarters, places):
             quarter = quarter.reshape(y_size, 1, local_experts, rows, width)
             full = lax.dynamic_update_index_in_dim(full, quarter, place, axis=1)
-        weights.append(full.reshape(model_width, width))
+        return full.reshape(model_width, width)
+
+    weights, last = [], None
+    for slab in slabs:
+        slab = slab.reshape(n_pairs * local_experts, rows, width)
+        slab = lax.all_to_all(slab, ("y", "c"), split_axis=0, concat_axis=0, tiled=True)
+        count, half = slab.shape[0], slab.shape[0] // 2
+        if last is None:
+            plus, minus = shift(slab, 1), shift(slab, -1)
+        else:
+            own, left, right = last
+            ahead = shift(jnp.concatenate([slab, left[:half]]), 1)
+            behind = shift(jnp.concatenate([slab, right[half:]]), -1)
+            plus, minus = ahead[:count], behind[:count]
+            weights.append(assemble([own, left, right, jnp.concatenate([ahead[count:], behind[count:]])]))
+        last = (slab, plus, minus)
+    own, left, right = last
+    far = jnp.concatenate([shift(left[:half], 1), shift(right[half:], -1)])
+    weights.append(assemble([own, left, right, far]))
 
     expert_out = None
     for w in weights:

time: 206 us -> 202 us (0.981)
  starting transfers between devices: 52.9 us -> 42.8 us
  local copies, waits for them, and re-layouts: 3.7 us -> 13.2 us
  waiting for transfers between devices: 57.2 us -> 50.2 us
  other arithmetic: 4.44 us -> 7.5 us
    ppermute x8 -> x6, starting transfers between devices: 29 us -> 19.5 us  [local(): shift = lambda v, k: lax.ppermute(v, ('zl', 'zh'), pairs(k))]
    slice x2 -> x6, local copies, waits for them, and re-layouts: 0.08 us -> 7.78 us  [the longest x2 2.21 us: local(): plus, minus = (ahead[:count], behind[:count])]
    ppermute x8 -> x6, waiting for transfers between devices: 26.2 us -> 19.3 us  [local(): shift = lambda v, k: lax.ppermute(v, ('zl', 'zh'), pairs(k))]
    dynamic_update_slice x8, local copies, waits for them, and re-layouts: 0.36 us -> 3.56 us  [assemble(): full = lax.dynamic_update_index_in_dim(full, quarter, place, axis=1)]
    concatenate x2 -> x3, other arithmetic: 0.11 us -> 2.51 us  [the longest x1 2.4 us: local(): ahead = shift(jnp.concatenate([slab, left[:half]]), 1)]
  transfers between devices with their start and end apart: 11 -> 9, of which waited for: 5 -> 5; matrix products, arithmetic and copies ran while one was open for 1% -> 7% of each run, Pallas kernels for 0% -> 0%
where the time goes in v16:
time: 202 us; the launch traced here: 201 us
  blocking collectives  76.8 us (38%)
  waiting for transfers between devices  50.2 us (25%)
  starting transfers between devices  42.8 us (21%)
  local copies, waits for them, and re-layouts  13.2 us (7%)
  matrix products  10.1 us (5%)
  other arithmetic  7.5 us (4%)
    all_gather x2, blocking collectives, local(): slabs = tuple((lax.all_gather(w, 'zh', axis=0, tiled=False) for w in slabs))  57.5 us
    all_to_all x1, waiting for transfers between devices, local(): lax.all_to_all(expert_rows, TOKEN_GROUP, split_axis=0, concat_axis=0, til...  30.8 us
    ppermute x6, starting transfers between devices, local(): shift = lambda v, k: lax.ppermute(v, ('zl', 'zh'), pairs(k))  19.5 us
    all_to_all x1, blocking collectives, local(): lax.all_to_all(slab, ('y', 'c'), split_axis=0, concat_axis=0, tiled=True)  19.4 us
    ppermute x6, waiting for transfers between devices, local(): shift = lambda v, k: lax.ppermute(v, ('zl', 'zh'), pairs(k))  19.3 us
    all_to_all x1, starting transfers between devices, local(): lax.all_to_all(outgoing, TOKEN_GROUP, split_axis=0, concat_axis=0, tiled=...  10.5 us
    all_to_all x1, starting transfers between devices, local(): lax.all_to_all(expert_rows, TOKEN_GROUP, split_axis=0, concat_axis=0, til...  8.01 us
    all_to_all x1, starting transfers between devices, local(): lax.all_to_all(slab, ('y', 'c'), split_axis=0, concat_axis=0, tiled=True)  4.76 us
  transfers between devices with their start and end apart: 9, of which 5 were waited for; matrix products, arithmetic and copies ran while one was open for 7% of the time, Pallas kernels for 0%

profile of v16, /device:TPU:1, one launch (start us, length us, event | category | flops | bytes accessed | tf_op | source)
XLA Modules:
  0.0 200.9 jit_solution(1768693919604053830)
XLA Ops:
  0.0 0.0 copy-start
  0.0 0.0 copy-start.1
  0.0 1.0 convert.18
  1.0 0.9 convert.19
  2.0 0.9 convert_bitcast_fusion
  3.0 0.7 pad_maximum_fusion.4
  3.6 0.7 broadcast_compare_fusion
  4.3 0.1 broadcast_in_dim.32.clone
  4.4 0.2 gt.23
  4.5 0.8 copy.29
  5.3 0.1 eq.40
  5.5 0.4 fusion.8
  5.8 0.1 convert_element_type.37
  6.0 0.1 copy.31
  6.0 0.0 copy-done.1
  6.1 0.4 fusion.1
  6.5 0.0 copy-done
  6.5 2.2 %convolution_convert_fusion = bf16[768,1536]{1,0:T(8,128)(2,1)} fusion(pred[768,128]{1,0:T(8,128)(4,1)S(1)} %fusion.1, bf16[128,1536]{1,0:T(8,128)(2,1)S(1)} %copy-done), kind=kOutput, calls=%fused_computation.1 | convolution fusion | flops 303169536 | bytes 2850816 | tf_op jit(solution)/shard_map/dot_general | solution.py:50
  8.7 10.5 %all-to-all-start = ((bf16[32,24,1536]{2,1,0:T(8,128)(2,1)}), bf16[32,24,1536]{2,1,0:T(8,128)(2,1)S(1)}, u32[]{:S(2)}, u32[]{:S(2)}) async-start(bf16[32,24,1536]{2,1,0:T(8,128)(2,1)} %bitcast.1), calls=%async_computation | async-start | bytes 4718592 | tf_op jit(solution)/shard_map/all_to_all | solution.py:51
  19.2 30.7 %all-gather = bf16[8,48,768]{2,1,0:T(8,128)(2,1)S(1)} all-gather(bf16[2,48,768]{2,1,0:T(8,128)(2,1)} %get-tuple-element.18), channel_id=2, replica_groups=mesh['y'=4,'zl'=4,'c'=2,'x'=4,'zh'=4] {'zh'}, dimensions={0}, use_global_device_ids=true | all-gather | bytes 737280 | tf_op jit(solution)/shard_map/all_gather | solution.py:32
  49.9 26.8 %all-gather.1 = bf16[8,48,768]{2,1,0:T(8,128)(2,1)} all-gather(bf16[2,48,768]{2,1,0:T(8,128)(2,1)S(1)} %get-tuple-element.19), channel_id=3, replica_groups=mesh['y'=4,'zl'=4,'c'=2,'x'=4,'zh'=4] {'zh'}, dimensions={0}, use_global_device_ids=true | all-gather | bytes 737280 | tf_op jit(solution)/shard_map/all_gather | solution.py:32
  76.7 0.0 all-to-all-done
  76.7 19.4 %all_to_all.34 = bf16[8,48,768]{2,1,0:T(8,128)(2,1)} all-to-all(bf16[8,48,768]{2,1,0:T(8,128)(2,1)S(1)} %all-gather), channel_id=1, replica_groups=mesh['y'=4,'zl'=4,'c'=2,'x'=4,'zh'=4] {'y','c'}, dimensions={0} | all-to-all | bytes 1179648 | tf_op jit(solution)/shard_map/all_to_all | solution.py:72
  96.1 1.9 collective-permute-start
  98.0 4.6 %collective-permute-start.1 = (bf16[8,48,768]{2,1,0:T(8,128)(2,1)}, bf16[8,48,768]{2,1,0:T(8,128)(2,1)}, u32[]{:S(2)}, u32[]{:S(2)}) collective-permute-start(bf16[8,48,768]{2,1,0:T(8,128)(2,1)} %all_to_all.34), channel_id=1, source_target_pairs={{0,99},{32,0},{64,32},{96,64},{1,96},{33,1},{65,33},{97,65},{2,97}... | collective-permute-start | bytes 1769480 | tf_op jit(solution)/shard_map/ppermute | solution.py:57
  102.6 4.8 %all-to-all-start.2 = ((bf16[8,48,768]{2,1,0:T(8,128)(2,1)}), bf16[8,48,768]{2,1,0:T(8,128)(2,1)S(1)}, u32[]{:S(2)}, u32[]{:S(2)}) async-start(bf16[8,48,768]{2,1,0:T(8,128)(2,1)} %all-gather.1), calls=%async_computation.2 | async-start | bytes 1179648 | tf_op jit(solution)/shard_map/all_to_all | solution.py:72
  107.3 6.3 %collective-permute-done = bf16[8,48,768]{2,1,0:T(8,128)(2,1)} collective-permute-done((bf16[8,48,768]{2,1,0:T(8,128)(2,1)}, bf16[8,48,768]{2,1,0:T(8,128)(2,1)}, u32[]{:S(2)}, u32[]{:S(2)}) %collective-permute-start) | collective-permute-done | bytes 589856 | tf_op jit(solution)/shard_map/ppermute | solution.py:57
  113.6 1.7 slice.102
  115.3 0.3 collective-permute-done.1
  115.6 1.7 slice.104
  117.3 0.1 all-to-all-done.2
  117.4 2.4 %pad_maximum_fusion.1 = (bf16[12,48,768]{2,1,0:T(8,128)(2,1)}, bf16[12,48,768]{2,1,0:T(8,128)(2,1)}) fusion(bf16[8,48,768]{2,1,0:T(8,128)(2,1)S(1)} %all-to-all-done.2, bf16[4,48,768]{2,1,0:T(8,128)(2,1)} %slice.102, bf16[4,48,768]{2,1,0:T(8,128)(2,1)} %slice.104), kind=kLoop, calls=%fused_computation.17 | loop fusion | flops 884736 | bytes 2949120 | tf_op jit(solution)/shard_map/concatenate | solution.py:78
  119.8 3.0 %collective-permute-start.2 = (bf16[12,48,768]{2,1,0:T(8,128)(2,1)}, bf16[12,48,768]{2,1,0:T(8,128)(2,1)}, u32[]{:S(2)}, u32[]{:S(2)}) collective-permute-start(bf16[12,48,768]{2,1,0:T(8,128)(2,1)} %get-tuple-element.27), channel_id=1, source_target_pairs={{0,32},{32,64},{64,96},{96,1},{1,33},{33,65},{65,97},{97,2},{2,34}... | collective-permute-start | bytes 2654216 | tf_op jit(solution)/shard_map/ppermute | solution.py:57
  122.8 3.5 %collective-permute-start.3 = (bf16[12,48,768]{2,1,0:T(8,128)(2,1)}, bf16[12,48,768]{2,1,0:T(8,128)(2,1)}, u32[]{:S(2)}, u32[]{:S(2)}) collective-permute-start(bf16[12,48,768]{2,1,0:T(8,128)(2,1)} %get-tuple-element.28), channel_id=1, source_target_pairs={{0,99},{32,0},{64,32},{96,64},{1,96},{33,1},{65,33},{97,65},{2,97}... | collective-permute-start | bytes 2654216 | tf_op jit(solution)/shard_map/ppermute | solution.py:57
  126.4 0.2 broadcast.52.clone.1
  126.7 0.2 broadcast.52.clone
  126.9 1.1 constant_dynamic-update-slice_fusion.7
  128.0 1.1 constant_dynamic-update-slice_fusion.6
  129.1 1.1 constant_dynamic-update-slice_fusion.5
  130.2 12.7 %collective-permute-done.2 = bf16[12,48,768]{2,1,0:T(8,128)(2,1)} collective-permute-done((bf16[12,48,768]{2,1,0:T(8,128)(2,1)}, bf16[12,48,768]{2,1,0:T(8,128)(2,1)}, u32[]{:S(2)}, u32[]{:S(2)}) %collective-permute-start.2) | collective-permute-done | bytes 884768 | tf_op jit(solution)/shard_map/ppermute | solution.py:57
  142.9 1.1 fusion.27
  144.0 1.9 collective-permute-start.4
  145.9 0.0 collective-permute-done.3
  145.9 1.1 fusion.28
  147.0 4.6 %collective-permute-start.5 = (bf16[4,48,768]{2,1,0:T(8,128)(2,1)S(1)}, bf16[4,48,768]{2,1,0:T(8,128)(2,1)S(1)}, u32[]{:S(2)}, u32[]{:S(2)}) collective-permute-start(bf16[4,48,768]{2,1,0:T(8,128)(2,1)S(1)} %get-tuple-element.25), channel_id=1, source_target_pairs={{0,99},{32,0},{64,32},{96,64},{1,96},{33,1},{65,33},{97,65},{2,97}... | collective-permute-start | bytes 884744 | tf_op jit(solution)/shard_map/ppermute | solution.py:57
  151.6 1.1 slice.110
  152.8 1.1 slice.111
  153.9 0.1 pad_maximum_fusion.2
  154.1 1.4 fusion.5
  155.4 0.8 fusion.11
  156.3 0.0 collective-permute-done.4
  156.3 0.0 collective-permute-done.5
  156.3 0.1 pad_maximum_fusion.3
  156.4 1.4 fusion.3
  157.8 2.2 %add_convert_fusion = bf16[768,1536]{1,0:T(8,128)(2,1)} fusion(f32[768,1536]{1,0:T(8,128)S(1)} %fusion.11, bf16[1536,768]{1,0:T(8,128)(2,1)S(1)} %bitcast.33, f32[768,512]{1,0:T(8,128)S(1)} %fusion.3), kind=kOutput, calls=%fused_computation | convolution fusion | flops 607518720 | bytes 9437184 | tf_op jit(solution)/shard_map/dot_general | solution.py:91
  160.0 0.0 copy-start.2
  160.0 8.0 %all-to-all-start.3 = ((bf16[32,24,1536]{2,1,0:T(8,128)(2,1)}), bf16[32,24,1536]{2,1,0:T(8,128)(2,1)S(1)}, u32[]{:S(2)}, u32[]{:S(2)}) async-start(bf16[32,24,1536]{2,1,0:T(8,128)(2,1)} %bitcast.28), calls=%async_computation.3 | async-start | bytes 4718592 | tf_op jit(solution)/shard_map/all_to_all | solution.py:96
  168.0 0.0 copy-done.2
  168.1 0.3 select_reduce_fusion
  168.4 30.8 %all-to-all-done.3 = bf16[32,24,1536]{2,1,0:T(8,128)(2,1)S(1)} async-done(((bf16[32,24,1536]{2,1,0:T(8,128)(2,1)}), bf16[32,24,1536]{2,1,0:T(8,128)(2,1)S(1)}, u32[]{:S(2)}, u32[]{:S(2)}) %all-to-all-start.3) | async-done | bytes 2359328 | tf_op jit(solution)/shard_map/all_to_all | solution.py:96
  199.2 0.5 fusion.20
  199.7 1.2 fusion
  (12 shorter events, 0.3 us)
Async XLA Ops:
  0.0 6.5 %copy-start = (bf16[128,1536]{1,0:T(8,128)(2,1)S(1)}, bf16[128,1536]{1,0:T(8,128)(2,1)}, u32[]{:S(2)}) copy-start(bf16[128,1536]{1,0:T(8,128)(2,1)} %param.7) | copy-start | bytes 1179652
  0.0 6.0 %copy-start.1 = (s32[128,6]{0,1:T(8,128)S(1)}, s32[128,6]{0,1:T(8,128)}, u32[]{:S(2)}) copy-start(s32[128,6]{0,1:T(8,128)} %param.11) | copy-start | bytes 9220
  8.7 68.1 %all-to-all-start = ((bf16[32,24,1536]{2,1,0:T(8,128)(2,1)}), bf16[32,24,1536]{2,1,0:T(8,128)(2,1)S(1)}, u32[]{:S(2)}, u32[]{:S(2)}) async-start(bf16[32,24,1536]{2,1,0:T(8,128)(2,1)} %bitcast.1), calls=%async_computation | async-start | bytes 4718592 | tf_op jit(solution)/shard_map/all_to_all | solution.py:51
  96.1 17.6 %collective-permute-start = (bf16[8,48,768]{2,1,0:T(8,128)(2,1)}, bf16[8,48,768]{2,1,0:T(8,128)(2,1)}, u32[]{:S(2)}, u32[]{:S(2)}) collective-permute-start(bf16[8,48,768]{2,1,0:T(8,128)(2,1)} %all_to_all.34), channel_id=1, source_target_pairs={{0,32},{32,64},{64,96},{96,1},{1,33},{33,65},{65,97},{97,2},{2,34}... | collective-permute-start | bytes 1769480 | tf_op jit(solution)/shard_map/ppermute | solution.py:57
  98.0 17.6 %collective-permute-start.1 = (bf16[8,48,768]{2,1,0:T(8,128)(2,1)}, bf16[8,48,768]{2,1,0:T(8,128)(2,1)}, u32[]{:S(2)}, u32[]{:S(2)}) collective-permute-start(bf16[8,48,768]{2,1,0:T(8,128)(2,1)} %all_to_all.34), channel_id=1, source_target_pairs={{0,99},{32,0},{64,32},{96,64},{1,96},{33,1},{65,33},{97,65},{2,97}... | collective-permute-start | bytes 1769480 | tf_op jit(solution)/shard_map/ppermute | solution.py:57
  102.6 14.8 %all-to-all-start.2 = ((bf16[8,48,768]{2,1,0:T(8,128)(2,1)}), bf16[8,48,768]{2,1,0:T(8,128)(2,1)S(1)}, u32[]{:S(2)}, u32[]{:S(2)}) async-start(bf16[8,48,768]{2,1,0:T(8,128)(2,1)} %all-gather.1), calls=%async_computation.2 | async-start | bytes 1179648 | tf_op jit(solution)/shard_map/all_to_all | solution.py:72
  119.8 23.1 %collective-permute-start.2 = (bf16[12,48,768]{2,1,0:T(8,128)(2,1)}, bf16[12,48,768]{2,1,0:T(8,128)(2,1)}, u32[]{:S(2)}, u32[]{:S(2)}) collective-permute-start(bf16[12,48,768]{2,1,0:T(8,128)(2,1)} %get-tuple-element.27), channel_id=1, source_target_pairs={{0,32},{32,64},{64,96},{96,1},{1,33},{33,65},{65,97},{97,2},{2,34}... | collective-permute-start | bytes 2654216 | tf_op jit(solution)/shard_map/ppermute | solution.py:57
  122.8 23.1 %collective-permute-start.3 = (bf16[12,48,768]{2,1,0:T(8,128)(2,1)}, bf16[12,48,768]{2,1,0:T(8,128)(2,1)}, u32[]{:S(2)}, u32[]{:S(2)}) collective-permute-start(bf16[12,48,768]{2,1,0:T(8,128)(2,1)} %get-tuple-element.28), channel_id=1, source_target_pairs={{0,99},{32,0},{64,32},{96,64},{1,96},{33,1},{65,33},{97,65},{2,97}... | collective-permute-start | bytes 2654216 | tf_op jit(solution)/shard_map/ppermute | solution.py:57
  144.0 12.3 %collective-permute-start.4 = (bf16[4,48,768]{2,1,0:T(8,128)(2,1)S(1)}, bf16[4,48,768]{2,1,0:T(8,128)(2,1)S(1)}, u32[]{:S(2)}, u32[]{:S(2)}) collective-permute-start(bf16[4,48,768]{2,1,0:T(8,128)(2,1)S(1)} %get-tuple-element.23), channel_id=1, source_target_pairs={{0,32},{32,64},{64,96},{96,1},{1,33},{33,65},{65,97},{97,2},{2,34}... | collective-permute-start | bytes 884744 | tf_op jit(solution)/shard_map/ppermute | solution.py:57
  147.0 9.2 %collective-permute-start.5 = (bf16[4,48,768]{2,1,0:T(8,128)(2,1)S(1)}, bf16[4,48,768]{2,1,0:T(8,128)(2,1)S(1)}, u32[]{:S(2)}, u32[]{:S(2)}) collective-permute-start(bf16[4,48,768]{2,1,0:T(8,128)(2,1)S(1)} %get-tuple-element.25), channel_id=1, source_target_pairs={{0,99},{32,0},{64,32},{96,64},{1,96},{33,1},{65,33},{97,65},{2,97}... | collective-permute-start | bytes 884744 | tf_op jit(solution)/shard_map/ppermute | solution.py:57
  160.0 8.0 %copy-start.2 = (f32[128,6]{0,1:T(8,128)S(1)}, f32[128,6]{0,1:T(8,128)}, u32[]{:S(2)}) copy-start(f32[128,6]{0,1:T(8,128)} %param.12) | copy-start | bytes 9220
  160.0 39.2 %all-to-all-start.3 = ((bf16[32,24,1536]{2,1,0:T(8,128)(2,1)}), bf16[32,24,1536]{2,1,0:T(8,128)(2,1)S(1)}, u32[]{:S(2)}, u32[]{:S(2)}) async-start(bf16[32,24,1536]{2,1,0:T(8,128)(2,1)} %bitcast.28), calls=%async_computation.3 | async-start | bytes 4718592 | tf_op jit(solution)/shard_map/all_to_all | solution.py:96

commit v17 on v15

--- a/solution.py
+++ b/solution.py
@@ -70,11 +70,14 @@
             jnp.concatenate([shift(plus[:half], 1), shift(minus[half:], -1)]),
         ]
         y_size = slab.shape[0] // local_experts
-        full = jnp.zeros((y_size, zl_size, local_experts, rows, width), jnp.bfloat16)
-        for quarter, place in zip(quarters, places):
-            quarter = quarter.reshape(y_size, 1, local_experts, rows, width)
-            full = lax.dynamic_update_index_in_dim(full, quarter, place, axis=1)
-        weights.append(full.reshape(model_width, width))
+        quarters = [q.reshape(y_size, local_experts, rows, width) for q in quarters]
+        picked = []
+        for q in range(zl_size):
+            chosen = quarters[0]
+            for quarter, place in zip(quarters[1:], places[1:]):
+                chosen = jnp.where(place == q, quarter, chosen)
+            picked.append(chosen)
+        weights.append(jnp.stack(picked, axis=1).reshape(model_width, width))
 
     expert_out = None
     for w in weights:

time: 194 us -> 194 us (level)
  starting transfers between devices: 44.9 us -> 49 us
  waiting for transfers between devices: 42.7 us -> 39.4 us
  local copies, waits for them, and re-layouts: 11.2 us -> 8.63 us
  other arithmetic: 5.1 us -> 7.2 us
    ppermute x8, starting transfers between devices: 21.2 us -> 25.9 us  [local(): shift = lambda v, k: lax.ppermute(v, ('zl', 'zh'), pairs(k))]
    dynamic_update_slice x8 -> x0, local copies, waits for them, and re-layouts: 4.62 us -> none  [local(): full = lax.dynamic_update_index_in_dim(full, quarter, place, axis=1)]
    unnamed x8 -> x12, local copies, waits for them, and re-layouts: 0.83 us -> 3.79 us
    ppermute x8, waiting for transfers between devices: 7.12 us -> 4.95 us  [local(): shift = lambda v, k: lax.ppermute(v, ('zl', 'zh'), pairs(k))]
  transfers between devices with their start and end apart: 11 -> 11, of which waited for: 5 -> 4; matrix products, arithmetic and copies ran while one was open for 6% -> 4% of each run, Pallas kernels for 0% -> 0%
where the time goes in v17:
time: 194 us; the launch traced here: 193 us
  blocking collectives  78 us (40%)
  starting transfers between devices  49 us (25%)
  waiting for transfers between devices  39.4 us (20%)
  matrix products  10.1 us (5%)
  local copies, waits for them, and re-layouts  8.63 us (4%)
  other arithmetic  7.2 us (4%)
    all_gather x2, blocking collectives, local(): slabs = tuple((lax.all_gather(w, 'zh', axis=0, tiled=False) for w in slabs))  57.9 us
    all_to_all x1, waiting for transfers between devices, local(): lax.all_to_all(expert_rows, TOKEN_GROUP, split_axis=0, concat_axis=0, til...  30.8 us
    ppermute x8, starting transfers between devices, local(): shift = lambda v, k: lax.ppermute(v, ('zl', 'zh'), pairs(k))  25.9 us
    all_to_all x1, blocking collectives, local(): lax.all_to_all(slab, ('y', 'c'), split_axis=0, concat_axis=0, tiled=True)  20.2 us
    all_to_all x1, starting transfers between devices, local(): lax.all_to_all(outgoing, TOKEN_GROUP, split_axis=0, concat_axis=0, tiled=...  10.5 us
    all_to_all x1, starting transfers between devices, local(): lax.all_to_all(expert_rows, TOKEN_GROUP, split_axis=0, concat_axis=0, til...  8.32 us
    ppermute x8, waiting for transfers between devices, local(): shift = lambda v, k: lax.ppermute(v, ('zl', 'zh'), pairs(k))  4.95 us
    all_to_all x1, starting transfers between devices, local(): lax.all_to_all(slab, ('y', 'c'), split_axis=0, concat_axis=0, tiled=True)  4.19 us
  transfers between devices with their start and end apart: 11, of which 4 were waited for; matrix products, arithmetic and copies ran while one was open for 4% of the time, Pallas kernels for 0%

profile of v17, /device:TPU:1, one launch (start us, length us, event | category | flops | bytes accessed | tf_op | source)
XLA Modules:
  0.0 192.7 jit_solution(17966598587099076746)
XLA Ops:
  0.0 0.0 copy-start
  0.0 0.0 copy-start.3
  0.0 1.0 convert_bitcast_fusion
  1.0 0.9 convert.19
  2.0 0.9 convert.18
  3.0 0.7 pad_maximum_fusion.2
  3.6 0.8 copy.29
  4.4 0.1 eq.87
  4.6 0.7 broadcast_compare_fusion
  5.2 0.1 broadcast_in_dim.32.clone
  5.3 0.2 gt.23
  5.5 0.4 fusion.8
  5.9 0.1 convert_element_type.37
  6.0 0.1 copy.31
  6.0 0.0 copy-done.3
  6.1 0.4 fusion.1
  6.5 0.0 copy-done
  6.5 2.2 %convolution_convert_fusion = bf16[768,1536]{1,0:T(8,128)(2,1)} fusion(pred[768,128]{1,0:T(8,128)(4,1)S(1)} %fusion.1, bf16[128,1536]{1,0:T(8,128)(2,1)S(1)} %copy-done), kind=kOutput, calls=%fused_computation.1 | convolution fusion | flops 303169536 | bytes 2850816 | tf_op jit(solution)/shard_map/dot_general | solution.py:50
  8.7 10.5 %all-to-all-start = ((bf16[32,24,1536]{2,1,0:T(8,128)(2,1)}), bf16[32,24,1536]{2,1,0:T(8,128)(2,1)S(1)}, u32[]{:S(2)}, u32[]{:S(2)}) async-start(bf16[32,24,1536]{2,1,0:T(8,128)(2,1)} %bitcast.1), calls=%async_computation | async-start | bytes 4718592 | tf_op jit(solution)/shard_map/all_to_all | solution.py:51
  19.2 30.8 %all-gather = bf16[8,48,768]{2,1,0:T(8,128)(2,1)S(1)} all-gather(bf16[2,48,768]{2,1,0:T(8,128)(2,1)} %get-tuple-element.18), channel_id=2, replica_groups=mesh['y'=4,'zl'=4,'c'=2,'x'=4,'zh'=4] {'zh'}, dimensions={0}, use_global_device_ids=true | all-gather | bytes 737280 | tf_op jit(solution)/shard_map/all_gather | solution.py:32
  50.1 27.0 %all-gather.1 = bf16[8,48,768]{2,1,0:T(8,128)(2,1)} all-gather(bf16[2,48,768]{2,1,0:T(8,128)(2,1)S(1)} %get-tuple-element.19), channel_id=3, replica_groups=mesh['y'=4,'zl'=4,'c'=2,'x'=4,'zh'=4] {'zh'}, dimensions={0}, use_global_device_ids=true | all-gather | bytes 737280 | tf_op jit(solution)/shard_map/all_gather | solution.py:32
  77.1 0.0 all-to-all-done
  77.1 0.0 copy-start.1
  77.1 1.4 copy-done.1
  78.5 20.2 %all_to_all.34 = bf16[8,48,768]{2,1,0:T(8,128)(2,1)S(1)} all-to-all(bf16[8,48,768]{2,1,0:T(8,128)(2,1)S(1)} %all-gather), channel_id=1, replica_groups=mesh['y'=4,'zl'=4,'c'=2,'x'=4,'zh'=4] {'y','c'}, dimensions={0} | all-to-all | bytes 1179648 | tf_op jit(solution)/shard_map/all_to_all | solution.py:63
  98.7 4.2 %all-to-all-start.2 = ((bf16[8,48,768]{2,1,0:T(8,128)(2,1)}), bf16[8,48,768]{2,1,0:T(8,128)(2,1)S(1)}, u32[]{:S(2)}, u32[]{:S(2)}) async-start(bf16[8,48,768]{2,1,0:T(8,128)(2,1)} %bitcast.11), calls=%async_computation.2 | async-start | bytes 1179648 | tf_op jit(solution)/shard_map/all_to_all | solution.py:63
  102.9 1.9 collective-permute-start
  104.8 4.6 %collective-permute-start.2 = (bf16[8,48,768]{2,1,0:T(8,128)(2,1)S(1)}, bf16[8,48,768]{2,1,0:T(8,128)(2,1)}, u32[]{:S(2)}, u32[]{:S(2)}) collective-permute-start(bf16[8,48,768]{2,1,0:T(8,128)(2,1)S(1)} %all_to_all.34), channel_id=1, source_target_pairs={{0,99},{32,0},{64,32},{96,64},{1,96},{33,1},{65,33},{97,65},{2,97}... | collective-permute-start | bytes 1769480 | tf_op jit(solution)/shard_map/ppermute | solution.py:57
  109.4 3.6 %all-to-all-done.2 = bf16[8,48,768]{2,1,0:T(8,128)(2,1)S(1)} async-done(((bf16[8,48,768]{2,1,0:T(8,128)(2,1)}), bf16[8,48,768]{2,1,0:T(8,128)(2,1)S(1)}, u32[]{:S(2)}, u32[]{:S(2)}) %all-to-all-start.2) | async-done | bytes 589856 | tf_op jit(solution)/shard_map/all_to_all | solution.py:63
  113.0 1.9 collective-permute-start.4
  114.9 4.6 %collective-permute-start.6 = (bf16[8,48,768]{2,1,0:T(8,128)(2,1)S(1)}, bf16[8,48,768]{2,1,0:T(8,128)(2,1)S(1)}, u32[]{:S(2)}, u32[]{:S(2)}) collective-permute-start(bf16[8,48,768]{2,1,0:T(8,128)(2,1)S(1)} %all-to-all-done.2), channel_id=1, source_target_pairs={{0,99},{32,0},{64,32},{96,64},{1,96},{33,1},{65,33},{97,65},{2,97}... | collective-permute-start | bytes 1769480 | tf_op jit(solution)/shard_map/ppermute | solution.py:57
  119.4 1.3 collective-permute-done
  120.7 0.7 slice.84
  121.5 1.9 collective-permute-start.1
  123.4 0.0 collective-permute-done.2
  123.4 1.7 slice.85
  125.1 4.6 %collective-permute-start.3 = (bf16[4,48,768]{2,1,0:T(8,128)(2,1)}, bf16[4,48,768]{2,1,0:T(8,128)(2,1)}, u32[]{:S(2)}, u32[]{:S(2)}) collective-permute-start(bf16[4,48,768]{2,1,0:T(8,128)(2,1)} %slice.85), channel_id=1, source_target_pairs={{0,99},{32,0},{64,32},{96,64},{1,96},{33,1},{65,33},{97,65},{2,97}... | collective-permute-start | bytes 884744 | tf_op jit(solution)/shard_map/ppermute | solution.py:57
  129.7 3.7 %collective-permute-done.4 = bf16[8,48,768]{2,1,0:T(8,128)(2,1)S(1)} collective-permute-done((bf16[8,48,768]{2,1,0:T(8,128)(2,1)S(1)}, bf16[8,48,768]{2,1,0:T(8,128)(2,1)S(1)}, u32[]{:S(2)}, u32[]{:S(2)}) %collective-permute-start.4) | collective-permute-done | bytes 589856 | tf_op jit(solution)/shard_map/ppermute | solution.py:57
  133.4 1.9 collective-permute-start.5
  135.3 0.0 collective-permute-done.6
  135.4 4.6 %collective-permute-start.7 = (bf16[4,48,768]{2,1,0:T(8,128)(2,1)S(1)}, bf16[4,48,768]{2,1,0:T(8,128)(2,1)S(1)}, u32[]{:S(2)}, u32[]{:S(2)}) collective-permute-start(bf16[4,48,768]{2,1,0:T(8,128)(2,1)S(1)} %slice.91), channel_id=1, source_target_pairs={{0,99},{32,0},{64,32},{96,64},{1,96},{33,1},{65,33},{97,65},{2,97}... | collective-permute-start | bytes 884744 | tf_op jit(solution)/shard_map/ppermute | solution.py:57
  139.9 0.0 collective-permute-done.1
  140.0 1.0 constant_dynamic-update-slice_fusion.1
  140.9 0.0 collective-permute-done.3
  140.9 1.0 constant_dynamic-update-slice_fusion
  141.9 1.3 select_select_fusion.7
  143.3 0.0 copy-start.2
  143.3 0.3 pad_maximum_fusion
  143.6 1.4 copy-done.2
  144.9 1.4 fusion.5
  146.3 0.0 collective-permute-done.5
  146.4 0.8 fusion.11
  147.2 0.0 collective-permute-done.7
  147.2 0.3 select_select_fusion.3
  147.5 0.3 pad_maximum_fusion.1
  147.8 1.4 fusion.3
  149.2 2.3 %add_convert_fusion = bf16[768,1536]{1,0:T(8,128)(2,1)} fusion(f32[768,1536]{1,0:T(8,128)S(1)} %fusion.11, bf16[1536,768]{1,0:T(8,128)(2,1)S(1)} %bitcast.32, f32[768,512]{1,0:T(8,128)S(1)} %fusion.3), kind=kOutput, calls=%fused_computation | convolution fusion | flops 607518720 | bytes 9437184 | tf_op jit(solution)/shard_map/dot_general | solution.py:86
  151.5 0.0 copy-start.4
  151.5 8.3 %all-to-all-start.3 = ((bf16[32,24,1536]{2,1,0:T(8,128)(2,1)}), bf16[32,24,1536]{2,1,0:T(8,128)(2,1)S(1)}, u32[]{:S(2)}, u32[]{:S(2)}) async-start(bf16[32,24,1536]{2,1,0:T(8,128)(2,1)} %bitcast.28), calls=%async_computation.3 | async-start | bytes 4718592 | tf_op jit(solution)/shard_map/all_to_all | solution.py:91
  159.8 0.0 copy-done.4
  159.8 0.3 select_reduce_fusion
  160.1 30.8 %all-to-all-done.3 = bf16[32,24,1536]{2,1,0:T(8,128)(2,1)S(1)} async-done(((bf16[32,24,1536]{2,1,0:T(8,128)(2,1)}), bf16[32,24,1536]{2,1,0:T(8,128)(2,1)S(1)}, u32[]{:S(2)}, u32[]{:S(2)}) %all-to-all-start.3) | async-done | bytes 2359328 | tf_op jit(solution)/shard_map/all_to_all | solution.py:91
  191.0 0.5 fusion.20
  191.4 1.2 fusion
  (11 shorter events, 0.2 us)
Async XLA Ops:
  0.0 6.5 %copy-start = (bf16[128,1536]{1,0:T(8,128)(2,1)S(1)}, bf16[128,1536]{1,0:T(8,128)(2,1)}, u32[]{:S(2)}) copy-start(bf16[128,1536]{1,0:T(8,128)(2,1)} %param.7) | copy-start | bytes 1179652
  0.0 6.0 %copy-start.3 = (s32[128,6]{0,1:T(8,128)S(1)}, s32[128,6]{0,1:T(8,128)}, u32[]{:S(2)}) copy-start(s32[128,6]{0,1:T(8,128)} %param.11) | copy-start | bytes 9220
  8.7 68.4 %all-to-all-start = ((bf16[32,24,1536]{2,1,0:T(8,128)(2,1)}), bf16[32,24,1536]{2,1,0:T(8,128)(2,1)S(1)}, u32[]{:S(2)}, u32[]{:S(2)}) async-start(bf16[32,24,1536]{2,1,0:T(8,128)(2,1)} %bitcast.1), calls=%async_computation | async-start | bytes 4718592 | tf_op jit(solution)/shard_map/all_to_all | solution.py:51
  77.1 1.4 copy-start.1
  98.7 14.3 %all-to-all-start.2 = ((bf16[8,48,768]{2,1,0:T(8,128)(2,1)}), bf16[8,48,768]{2,1,0:T(8,128)(2,1)S(1)}, u32[]{:S(2)}, u32[]{:S(2)}) async-start(bf16[8,48,768]{2,1,0:T(8,128)(2,1)} %bitcast.11), calls=%async_computation.2 | async-start | bytes 1179648 | tf_op jit(solution)/shard_map/all_to_all | solution.py:63
  102.9 17.9 %collective-permute-start = (bf16[8,48,768]{2,1,0:T(8,128)(2,1)S(1)}, bf16[8,48,768]{2,1,0:T(8,128)(2,1)S(1)}, u32[]{:S(2)}, u32[]{:S(2)}) collective-permute-start(bf16[8,48,768]{2,1,0:T(8,128)(2,1)S(1)} %all_to_all.34), channel_id=1, source_target_pairs={{0,32},{32,64},{64,96},{96,1},{1,33},{33,65},{65,97},{97,2},{2,34}... | collective-permute-start | bytes 1769480 | tf_op jit(solution)/shard_map/ppermute | solution.py:57
  104.8 18.6 %collective-permute-start.2 = (bf16[8,48,768]{2,1,0:T(8,128)(2,1)S(1)}, bf16[8,48,768]{2,1,0:T(8,128)(2,1)}, u32[]{:S(2)}, u32[]{:S(2)}) collective-permute-start(bf16[8,48,768]{2,1,0:T(8,128)(2,1)S(1)} %all_to_all.34), channel_id=1, source_target_pairs={{0,99},{32,0},{64,32},{96,64},{1,96},{33,1},{65,33},{97,65},{2,97}... | collective-permute-start | bytes 1769480 | tf_op jit(solution)/shard_map/ppermute | solution.py:57
  113.0 20.4 %collective-permute-start.4 = (bf16[8,48,768]{2,1,0:T(8,128)(2,1)S(1)}, bf16[8,48,768]{2,1,0:T(8,128)(2,1)S(1)}, u32[]{:S(2)}, u32[]{:S(2)}) collective-permute-start(bf16[8,48,768]{2,1,0:T(8,128)(2,1)S(1)} %all-to-all-done.2), channel_id=1, source_target_pairs={{0,32},{32,64},{64,96},{96,1},{1,33},{33,65},{65,97},{97,2},{2,34}... | collective-permute-start | bytes 1769480 | tf_op jit(solution)/shard_map/ppermute | solution.py:57
  114.9 20.5 %collective-permute-start.6 = (bf16[8,48,768]{2,1,0:T(8,128)(2,1)S(1)}, bf16[8,48,768]{2,1,0:T(8,128)(2,1)S(1)}, u32[]{:S(2)}, u32[]{:S(2)}) collective-permute-start(bf16[8,48,768]{2,1,0:T(8,128)(2,1)S(1)} %all-to-all-done.2), channel_id=1, source_target_pairs={{0,99},{32,0},{64,32},{96,64},{1,96},{33,1},{65,33},{97,65},{2,97}... | collective-permute-start | bytes 1769480 | tf_op jit(solution)/shard_map/ppermute | solution.py:57
  121.5 18.5 %collective-permute-start.1 = (bf16[4,48,768]{2,1,0:T(8,128)(2,1)}, bf16[4,48,768]{2,1,0:T(8,128)(2,1)}, u32[]{:S(2)}, u32[]{:S(2)}) collective-permute-start(bf16[4,48,768]{2,1,0:T(8,128)(2,1)} %slice.84), channel_id=1, source_target_pairs={{0,32},{32,64},{64,96},{96,1},{1,33},{33,65},{65,97},{97,2},{2,34}... | collective-permute-start | bytes 884744 | tf_op jit(solution)/shard_map/ppermute | solution.py:57
  125.1 15.9 %collective-permute-start.3 = (bf16[4,48,768]{2,1,0:T(8,128)(2,1)}, bf16[4,48,768]{2,1,0:T(8,128)(2,1)}, u32[]{:S(2)}, u32[]{:S(2)}) collective-permute-start(bf16[4,48,768]{2,1,0:T(8,128)(2,1)} %slice.85), channel_id=1, source_target_pairs={{0,99},{32,0},{64,32},{96,64},{1,96},{33,1},{65,33},{97,65},{2,97}... | collective-permute-start | bytes 884744 | tf_op jit(solution)/shard_map/ppermute | solution.py:57
  133.4 12.9 %collective-permute-start.5 = (bf16[4,48,768]{2,1,0:T(8,128)(2,1)S(1)}, bf16[4,48,768]{2,1,0:T(8,128)(2,1)S(1)}, u32[]{:S(2)}, u32[]{:S(2)}) collective-permute-start(bf16[4,48,768]{2,1,0:T(8,128)(2,1)S(1)} %slice.90), channel_id=1, source_target_pairs={{0,32},{32,64},{64,96},{96,1},{1,33},{33,65},{65,97},{97,2},{2,34}... | collective-permute-start | bytes 884744 | tf_op jit(solution)/shard_map/ppermute | solution.py:57
  135.4 11.8 %collective-permute-start.7 = (bf16[4,48,768]{2,1,0:T(8,128)(2,1)S(1)}, bf16[4,48,768]{2,1,0:T(8,128)(2,1)S(1)}, u32[]{:S(2)}, u32[]{:S(2)}) collective-permute-start(bf16[4,48,768]{2,1,0:T(8,128)(2,1)S(1)} %slice.91), channel_id=1, source_target_pairs={{0,99},{32,0},{64,32},{96,64},{1,96},{33,1},{65,33},{97,65},{2,97}... | collective-permute-start | bytes 884744 | tf_op jit(solution)/shard_map/ppermute | solution.py:57
  143.3 1.7 copy-start.2
  151.5 8.3 %copy-start.4 = (f32[128,6]{0,1:T(8,128)S(1)}, f32[128,6]{0,1:T(8,128)}, u32[]{:S(2)}) copy-start(f32[128,6]{0,1:T(8,128)} %param.12) | copy-start | bytes 9220
  151.5 39.5 %all-to-all-start.3 = ((bf16[32,24,1536]{2,1,0:T(8,128)(2,1)}), bf16[32,24,1536]{2,1,0:T(8,128)(2,1)S(1)}, u32[]{:S(2)}, u32[]{:S(2)}) async-start(bf16[32,24,1536]{2,1,0:T(8,128)(2,1)} %bitcast.28), calls=%async_computation.3 | async-start | bytes 4718592 | tf_op jit(solution)/shard_map/all_to_all | solution.py:91

commit v18 on v17

--- a/solution.py
+++ b/solution.py
@@ -29,8 +29,8 @@
     slabs, tokens, routes, route_scores, live = lax.optimization_barrier(
         (slabs, tokens, routes, route_scores, live)
     )
-    slabs = tuple(lax.all_gather(w, "zh", axis=0, tiled=False) for w in slabs)
-    n_pairs, local_experts, rows, width = slabs[0].shape
+    first = lax.all_gather(slabs[0], "zh", axis=0, tiled=False)
+    n_pairs, local_experts, rows, width = first.shape
     route_share = route_scores / jnp.sum(route_scores, axis=1, keepdims=True)
     flat_route = routes.reshape(-1)
     flat_live = jnp.repeat(live, top_count)
@@ -49,7 +49,6 @@
     dispatch = jnp.any(picks, axis=2).astype(jnp.bfloat16)
     outgoing = jnp.dot(dispatch, tokens, preferred_element_type=jnp.float32).astype(jnp.bfloat16)
     incoming = lax.all_to_all(outgoing, TOKEN_GROUP, split_axis=0, concat_axis=0, tiled=True)
-    incoming, slabs = lax.optimization_barrier((incoming, slabs))
     zl_size, zh_size = lax.axis_size("zl"), lax.axis_size("zh")
     ring = zl_size * zh_size
     index = lambda z: (z % zl_size) * zh_size + z // zl_size
@@ -58,9 +57,16 @@
     zl_at = lax.axis_index("zl")
     places = [zl_at % zl_size, (zl_at - 1) % zl_size, (zl_at + 1) % zl_size, (zl_at + 2) % zl_size]
     weights = []
-    for slab in slabs:
+    slab = first
+    for h in range(len(slabs)):
+        if h == len(slabs) - 1:
+            incoming, slab = lax.optimization_barrier((incoming, slab))
         slab = slab.reshape(n_pairs * local_experts, rows, width)
         slab = lax.all_to_all(slab, ("y", "c"), split_axis=0, concat_axis=0, tiled=True)
+        if h + 1 < len(slabs):
+            _, upcoming = lax.optimization_barrier((slab, slabs[h + 1]))
+            upcoming = lax.all_gather(upcoming, "zh", axis=0, tiled=False)
+            slab, upcoming = lax.optimization_barrier((slab, upcoming))
         half = slab.shape[0] // 2
         plus, minus = shift(slab, 1), shift(slab, -1)
         quarters = [
@@ -78,6 +84,8 @@
                 chosen = jnp.where(place == q, quarter, chosen)
             picked.append(chosen)
         weights.append(jnp.stack(picked, axis=1).reshape(model_width, width))
+        if h + 1 < len(slabs):
+            slab = upcoming
 
     expert_out = None
     for w in weights:

time: 194 us -> 211 us (1.088)
  waiting for transfers between devices: 39.4 us -> 65.9 us
  blocking collectives: 78 us -> 64.6 us
  starting transfers between devices: 49 us -> 55.8 us
  local copies, waits for them, and re-layouts: 8.63 us -> 5.8 us
    all_to_all x1 -> x0, blocking collectives: 20.2 us -> none  [local(): lax.all_to_all(slab, ('y', 'c'), split_axis=0, concat_axis=0, tiled=True)]
    ppermute x8, waiting for transfers between devices: 4.95 us -> 22.1 us  [local(): shift = lambda v, k: lax.ppermute(v, ('zl', 'zh'), pairs(k))]
    all_to_all x1 -> x2, starting transfers between devices: 4.19 us -> 15.7 us  [local(): lax.all_to_all(slab, ('y', 'c'), split_axis=0, concat_axis=0, tiled=True)]
    all_to_all x1 -> x2, waiting for transfers between devices: 3.58 us -> 13 us  [local(): lax.all_to_all(slab, ('y', 'c'), split_axis=0, concat_axis=0, tiled=True)]
    all_gather x2, blocking collectives: 57.9 us -> 64.6 us  [the longest x1 33.8 us: local(): first = lax.all_gather(slabs[0], 'zh', axis=0, tiled=False)]
    all_to_all x1, starting transfers between devices: 10.5 us -> 6.03 us  [local(): lax.all_to_all(outgoing, TOKEN_GROUP, split_axis=0, concat_axis=0, tiled=...]
  transfers between devices with their start and end apart: 11 -> 12, of which waited for: 4 -> 7; matrix products, arithmetic and copies ran while one was open for 4% -> 6% of each run, Pallas kernels for 0% -> 0%
where the time goes in v18:
time: 211 us; the launch traced here: 210 us
  waiting for transfers between devices  65.9 us (31%)
  blocking collectives  64.6 us (31%)
  starting transfers between devices  55.8 us (26%)
  matrix products  10.1 us (5%)
  other arithmetic  7.11 us (3%)
  local copies, waits for them, and re-layouts  5.8 us (3%)
    all_gather x1, blocking collectives, local(): first = lax.all_gather(slabs[0], 'zh', axis=0, tiled=False)  33.8 us
    all_gather x1, blocking collectives, local(): upcoming = lax.all_gather(upcoming, 'zh', axis=0, tiled=False)  30.8 us
    all_to_all x1, waiting for transfers between devices, local(): lax.all_to_all(expert_rows, TOKEN_GROUP, split_axis=0, concat_axis=0, til...  30.8 us
    ppermute x8, starting transfers between devices, local(): shift = lambda v, k: lax.ppermute(v, ('zl', 'zh'), pairs(k))  25.9 us
    ppermute x8, waiting for transfers between devices, local(): shift = lambda v, k: lax.ppermute(v, ('zl', 'zh'), pairs(k))  22.1 us
    all_to_all x2, starting transfers between devices, local(): lax.all_to_all(slab, ('y', 'c'), split_axis=0, concat_axis=0, tiled=True)  15.7 us
    all_to_all x2, waiting for transfers between devices, local(): lax.all_to_all(slab, ('y', 'c'), split_axis=0, concat_axis=0, tiled=True)  13 us
    all_to_all x1, starting transfers between devices, local(): lax.all_to_all(expert_rows, TOKEN_GROUP, split_axis=0, concat_axis=0, til...  8.12 us
  transfers between devices with their start and end apart: 12, of which 7 were waited for; matrix products, arithmetic and copies ran while one was open for 6% of the time, Pallas kernels for 0%

profile of v18, /device:TPU:1, one launch (start us, length us, event | category | flops | bytes accessed | tf_op | source)
XLA Modules:
  0.0 209.7 jit_solution(9951800379749595768)
XLA Ops:
  0.0 0.0 copy-start
  0.0 1.0 convert_bitcast_fusion
  1.0 0.9 convert.19
  2.0 0.9 convert.18
  3.0 33.8 %all-gather = bf16[8,48,768]{2,1,0:T(8,128)(2,1)} all-gather(bf16[2,48,768]{2,1,0:T(8,128)(2,1)S(1)} %get-tuple-element.20), channel_id=2, replica_groups=mesh['y'=4,'zl'=4,'c'=2,'x'=4,'zh'=4] {'zh'}, dimensions={0}, use_global_device_ids=true | all-gather | bytes 737280 | tf_op jit(solution)/shard_map/all_gather | solution.py:32
  36.7 9.4 %all-to-all-start.1 = ((bf16[8,48,768]{2,1,0:T(8,128)(2,1)}), bf16[8,48,768]{2,1,0:T(8,128)(2,1)S(1)}, u32[]{:S(2)}, u32[]{:S(2)}) async-start(bf16[8,48,768]{2,1,0:T(8,128)(2,1)} %all-gather), calls=%async_computation.1 | async-start | bytes 1179648 | tf_op jit(solution)/shard_map/all_to_all | solution.py:65
  46.2 0.0 copy-done.5
  46.2 0.1 copy.29
  46.3 0.1 eq.87
  46.4 0.0 copy-done.7
  46.4 0.1 broadcast_in_dim.32.clone
  46.5 0.2 gt.23
  46.7 0.4 fusion.8
  47.0 0.1 convert_element_type.37
  47.2 0.1 copy.31
  47.3 0.4 fusion.1
  47.7 0.0 copy-done
  47.7 2.2 %convolution_convert_fusion = bf16[768,1536]{1,0:T(8,128)(2,1)} fusion(pred[768,128]{1,0:T(8,128)(4,1)S(1)} %fusion.1, bf16[128,1536]{1,0:T(8,128)(2,1)S(1)} %copy-done), kind=kOutput, calls=%fused_computation.1 | convolution fusion | flops 303169536 | bytes 2850816 | tf_op jit(solution)/shard_map/dot_general | solution.py:50
  49.9 6.3 %all-to-all-done.1 = bf16[8,48,768]{2,1,0:T(8,128)(2,1)S(1)} async-done(((bf16[8,48,768]{2,1,0:T(8,128)(2,1)}), bf16[8,48,768]{2,1,0:T(8,128)(2,1)S(1)}, u32[]{:S(2)}, u32[]{:S(2)}) %all-to-all-start.1) | async-done | bytes 589856 | tf_op jit(solution)/shard_map/all_to_all | solution.py:65
  56.2 6.0 %all-to-all-start = ((bf16[32,24,1536]{2,1,0:T(8,128)(2,1)}), bf16[32,24,1536]{2,1,0:T(8,128)(2,1)S(1)}, u32[]{:S(2)}, u32[]{:S(2)}) async-start(bf16[32,24,1536]{2,1,0:T(8,128)(2,1)} %bitcast.1), calls=%async_computation | async-start | bytes 4718592 | tf_op jit(solution)/shard_map/all_to_all | solution.py:51
  62.2 30.8 %all-gather.1 = bf16[8,48,768]{2,1,0:T(8,128)(2,1)} all-gather(bf16[2,48,768]{2,1,0:T(8,128)(2,1)S(1)} %get-tuple-element.22), channel_id=3, replica_groups=mesh['y'=4,'zl'=4,'c'=2,'x'=4,'zh'=4] {'zh'}, dimensions={0}, use_global_device_ids=true | all-gather | bytes 737280 | tf_op jit(solution)/shard_map/all_gather | solution.py:68
  93.1 1.9 collective-permute-start
  95.0 4.6 %collective-permute-start.2 = (bf16[8,48,768]{2,1,0:T(8,128)(2,1)S(1)}, bf16[8,48,768]{2,1,0:T(8,128)(2,1)S(1)}, u32[]{:S(2)}, u32[]{:S(2)}) collective-permute-start(bf16[8,48,768]{2,1,0:T(8,128)(2,1)S(1)} %all-to-all-done.1), channel_id=1, source_target_pairs={{0,99},{32,0},{64,32},{96,64},{1,96},{33,1},{65,33},{97,65},{2,97}... | collective-permute-start | bytes 1769480 | tf_op jit(solution)/shard_map/ppermute | solution.py:56
  99.6 11.0 %collective-permute-done = bf16[8,48,768]{2,1,0:T(8,128)(2,1)S(1)} collective-permute-done((bf16[8,48,768]{2,1,0:T(8,128)(2,1)S(1)}, bf16[8,48,768]{2,1,0:T(8,128)(2,1)S(1)}, u32[]{:S(2)}, u32[]{:S(2)}) %collective-permute-start) | collective-permute-done | bytes 589856 | tf_op jit(solution)/shard_map/ppermute | solution.py:56
  110.6 0.8 slice.84
  111.4 1.9 collective-permute-start.1
  113.3 0.0 collective-permute-done.2
  113.3 0.0 copy-done.3
  113.3 0.0 copy-start.4
  113.3 0.8 slice.85
  114.1 0.1 copy-done.4
  114.2 4.6 %collective-permute-start.3 = (bf16[4,48,768]{2,1,0:T(8,128)(2,1)}, bf16[4,48,768]{2,1,0:T(8,128)(2,1)}, u32[]{:S(2)}, u32[]{:S(2)}) collective-permute-start(bf16[4,48,768]{2,1,0:T(8,128)(2,1)} %slice.85), channel_id=1, source_target_pairs={{0,99},{32,0},{64,32},{96,64},{1,96},{33,1},{65,33},{97,65},{2,97}... | collective-permute-start | bytes 884744 | tf_op jit(solution)/shard_map/ppermute | solution.py:56
  118.9 0.0 all-to-all-done
  118.9 0.0 copy-start.1
  118.9 6.3 %all-to-all-start.2 = ((bf16[8,48,768]{2,1,0:T(8,128)(2,1)}), bf16[8,48,768]{2,1,0:T(8,128)(2,1)}, u32[]{:S(2)}, u32[]{:S(2)}) async-start(bf16[8,48,768]{2,1,0:T(8,128)(2,1)} %all-gather.1), calls=%async_computation.2 | async-start | bytes 1179648 | tf_op jit(solution)/shard_map/all_to_all | solution.py:65
  125.2 0.0 collective-permute-done.1
  125.2 1.0 constant_dynamic-update-slice_fusion.1
  126.2 0.0 collective-permute-done.3
  126.2 0.0 copy-done.1
  126.2 1.0 constant_dynamic-update-slice_fusion
  127.2 1.5 select_select_fusion.7
  128.7 6.6 %all-to-all-done.2 = bf16[8,48,768]{2,1,0:T(8,128)(2,1)} async-done(((bf16[8,48,768]{2,1,0:T(8,128)(2,1)}), bf16[8,48,768]{2,1,0:T(8,128)(2,1)}, u32[]{:S(2)}, u32[]{:S(2)}) %all-to-all-start.2) | async-done | bytes 589856 | tf_op jit(solution)/shard_map/all_to_all | solution.py:65
  135.3 1.9 collective-permute-start.4
  137.2 4.6 %collective-permute-start.6 = (bf16[8,48,768]{2,1,0:T(8,128)(2,1)}, bf16[8,48,768]{2,1,0:T(8,128)(2,1)S(1)}, u32[]{:S(2)}, u32[]{:S(2)}) collective-permute-start(bf16[8,48,768]{2,1,0:T(8,128)(2,1)} %all-to-all-done.2), channel_id=1, source_target_pairs={{0,99},{32,0},{64,32},{96,64},{1,96},{33,1},{65,33},{97,65},{2,97}... | collective-permute-start | bytes 1769480 | tf_op jit(solution)/shard_map/ppermute | solution.py:56
  141.8 0.0 copy-start.2
  141.8 0.3 pad_maximum_fusion
  142.1 1.4 copy-done.2
  143.5 1.4 fusion.5
  144.9 7.7 %collective-permute-done.4 = bf16[8,48,768]{2,1,0:T(8,128)(2,1)S(1)} collective-permute-done((bf16[8,48,768]{2,1,0:T(8,128)(2,1)}, bf16[8,48,768]{2,1,0:T(8,128)(2,1)S(1)}, u32[]{:S(2)}, u32[]{:S(2)}) %collective-permute-start.4) | collective-permute-done | bytes 589856 | tf_op jit(solution)/shard_map/ppermute | solution.py:56
  152.6 1.9 collective-permute-start.5
  154.5 0.0 collective-permute-done.6
  154.5 4.6 %collective-permute-start.7 = (bf16[4,48,768]{2,1,0:T(8,128)(2,1)S(1)}, bf16[4,48,768]{2,1,0:T(8,128)(2,1)S(1)}, u32[]{:S(2)}, u32[]{:S(2)}) collective-permute-start(bf16[4,48,768]{2,1,0:T(8,128)(2,1)S(1)} %slice.91), channel_id=1, source_target_pairs={{0,99},{32,0},{64,32},{96,64},{1,96},{33,1},{65,33},{97,65},{2,97}... | collective-permute-start | bytes 884744 | tf_op jit(solution)/shard_map/ppermute | solution.py:56
  159.1 0.8 fusion.11
  160.0 2.5 %collective-permute-done.5 = bf16[4,48,768]{2,1,0:T(8,128)(2,1)S(1)} collective-permute-done((bf16[4,48,768]{2,1,0:T(8,128)(2,1)S(1)}, bf16[4,48,768]{2,1,0:T(8,128)(2,1)S(1)}, u32[]{:S(2)}, u32[]{:S(2)}) %collective-permute-start.5) | collective-permute-done | bytes 294944 | tf_op jit(solution)/shard_map/ppermute | solution.py:56
  162.4 0.9 collective-permute-done.7
  163.4 1.3 select_select_fusion.3
  164.7 0.3 pad_maximum_fusion.1
  165.0 1.4 fusion.3
  166.4 2.3 %add_convert_fusion = bf16[768,1536]{1,0:T(8,128)(2,1)} fusion(f32[768,1536]{1,0:T(8,128)S(1)} %fusion.11, bf16[1536,768]{1,0:T(8,128)(2,1)S(1)} %bitcast.30, f32[768,512]{1,0:T(8,128)S(1)} %fusion.3), kind=kOutput, calls=%fused_computation | convolution fusion | flops 607518720 | bytes 9437184 | tf_op jit(solution)/shard_map/dot_general | solution.py:94
  168.7 8.1 %all-to-all-start.3 = ((bf16[32,24,1536]{2,1,0:T(8,128)(2,1)}), bf16[32,24,1536]{2,1,0:T(8,128)(2,1)S(1)}, u32[]{:S(2)}, u32[]{:S(2)}) async-start(bf16[32,24,1536]{2,1,0:T(8,128)(2,1)} %bitcast.26), calls=%async_computation.3 | async-start | bytes 4718592 | tf_op jit(solution)/shard_map/all_to_all | solution.py:99
  176.9 0.3 select_reduce_fusion
  177.2 30.8 %all-to-all-done.3 = bf16[32,24,1536]{2,1,0:T(8,128)(2,1)S(1)} async-done(((bf16[32,24,1536]{2,1,0:T(8,128)(2,1)}), bf16[32,24,1536]{2,1,0:T(8,128)(2,1)S(1)}, u32[]{:S(2)}, u32[]{:S(2)}) %all-to-all-start.3) | async-done | bytes 2359328 | tf_op jit(solution)/shard_map/all_to_all | solution.py:99
  208.0 0.5 fusion.20
  208.5 1.2 fusion
  (18 shorter events, 0.2 us)
Async XLA Ops:
  0.0 47.7 %copy-start = (bf16[128,1536]{1,0:T(8,128)(2,1)S(1)}, bf16[128,1536]{1,0:T(8,128)(2,1)}, u32[]{:S(2)}) copy-start(bf16[128,1536]{1,0:T(8,128)(2,1)} %param.7) | copy-start | bytes 1179652
  0.0 46.2 %copy-start.5 = (s32[128,6]{0,1:T(8,128)S(1)}, s32[128,6]{0,1:T(8,128)}, u32[]{:S(2)}) copy-start(s32[128,6]{0,1:T(8,128)} %param.11) | copy-start | bytes 9220
  0.0 46.4 %copy-start.7 = (s32[128]{0:T(128)S(1)}, s32[128]{0:T(128)}, u32[]{:S(2)}) copy-start(s32[128]{0:T(128)} %param.13) | copy-start | bytes 1540
  36.7 19.5 %all-to-all-start.1 = ((bf16[8,48,768]{2,1,0:T(8,128)(2,1)}), bf16[8,48,768]{2,1,0:T(8,128)(2,1)S(1)}, u32[]{:S(2)}, u32[]{:S(2)}) async-start(bf16[8,48,768]{2,1,0:T(8,128)(2,1)} %all-gather), calls=%async_computation.1 | async-start | bytes 1179648 | tf_op jit(solution)/shard_map/all_to_all | solution.py:65
  56.2 62.7 %all-to-all-start = ((bf16[32,24,1536]{2,1,0:T(8,128)(2,1)}), bf16[32,24,1536]{2,1,0:T(8,128)(2,1)S(1)}, u32[]{:S(2)}, u32[]{:S(2)}) async-start(bf16[32,24,1536]{2,1,0:T(8,128)(2,1)} %bitcast.1), calls=%async_computation | async-start | bytes 4718592 | tf_op jit(solution)/shard_map/all_to_all | solution.py:51
  93.1 17.5 %collective-permute-start = (bf16[8,48,768]{2,1,0:T(8,128)(2,1)S(1)}, bf16[8,48,768]{2,1,0:T(8,128)(2,1)S(1)}, u32[]{:S(2)}, u32[]{:S(2)}) collective-permute-start(bf16[8,48,768]{2,1,0:T(8,128)(2,1)S(1)} %all-to-all-done.1), channel_id=1, source_target_pairs={{0,32},{32,64},{64,96},{96,1},{1,33},{33,65},{65,97},{97,2},{2,34}... | collective-permute-start | bytes 1769480 | tf_op jit(solution)/shard_map/ppermute | solution.py:56
  95.0 18.3 %collective-permute-start.2 = (bf16[8,48,768]{2,1,0:T(8,128)(2,1)S(1)}, bf16[8,48,768]{2,1,0:T(8,128)(2,1)S(1)}, u32[]{:S(2)}, u32[]{:S(2)}) collective-permute-start(bf16[8,48,768]{2,1,0:T(8,128)(2,1)S(1)} %all-to-all-done.1), channel_id=1, source_target_pairs={{0,99},{32,0},{64,32},{96,64},{1,96},{33,1},{65,33},{97,65},{2,97}... | collective-permute-start | bytes 1769480 | tf_op jit(solution)/shard_map/ppermute | solution.py:56
  110.6 2.7 %copy-start.3 = (bf16[8,48,768]{2,1,0:T(8,128)(2,1)}, bf16[8,48,768]{2,1,0:T(8,128)(2,1)S(1)}, u32[]{:S(2)}) copy-start(bf16[8,48,768]{2,1,0:T(8,128)(2,1)S(1)} %collective-permute-done) | copy-start | bytes 1769476
  111.4 13.8 %collective-permute-start.1 = (bf16[4,48,768]{2,1,0:T(8,128)(2,1)}, bf16[4,48,768]{2,1,0:T(8,128)(2,1)}, u32[]{:S(2)}, u32[]{:S(2)}) collective-permute-start(bf16[4,48,768]{2,1,0:T(8,128)(2,1)} %slice.84), channel_id=1, source_target_pairs={{0,32},{32,64},{64,96},{96,1},{1,33},{33,65},{65,97},{97,2},{2,34}... | collective-permute-start | bytes 884744 | tf_op jit(solution)/shard_map/ppermute | solution.py:56
  113.3 0.9 copy-start.4
  114.2 11.9 %collective-permute-start.3 = (bf16[4,48,768]{2,1,0:T(8,128)(2,1)}, bf16[4,48,768]{2,1,0:T(8,128)(2,1)}, u32[]{:S(2)}, u32[]{:S(2)}) collective-permute-start(bf16[4,48,768]{2,1,0:T(8,128)(2,1)} %slice.85), channel_id=1, source_target_pairs={{0,99},{32,0},{64,32},{96,64},{1,96},{33,1},{65,33},{97,65},{2,97}... | collective-permute-start | bytes 884744 | tf_op jit(solution)/shard_map/ppermute | solution.py:56
  118.9 7.3 %copy-start.1 = (bf16[32,24,1536]{2,1,0:T(8,128)(2,1)}, bf16[32,24,1536]{2,1,0:T(8,128)(2,1)S(1)}, u32[]{:S(2)}) copy-start(bf16[32,24,1536]{2,1,0:T(8,128)(2,1)S(1)} %all-to-all-done) | copy-start | bytes 7077892
  118.9 16.4 %all-to-all-start.2 = ((bf16[8,48,768]{2,1,0:T(8,128)(2,1)}), bf16[8,48,768]{2,1,0:T(8,128)(2,1)}, u32[]{:S(2)}, u32[]{:S(2)}) async-start(bf16[8,48,768]{2,1,0:T(8,128)(2,1)} %all-gather.1), calls=%async_computation.2 | async-start | bytes 1179648 | tf_op jit(solution)/shard_map/all_to_all | solution.py:65
  135.3 17.2 %collective-permute-start.4 = (bf16[8,48,768]{2,1,0:T(8,128)(2,1)}, bf16[8,48,768]{2,1,0:T(8,128)(2,1)S(1)}, u32[]{:S(2)}, u32[]{:S(2)}) collective-permute-start(bf16[8,48,768]{2,1,0:T(8,128)(2,1)} %all-to-all-done.2), channel_id=1, source_target_pairs={{0,32},{32,64},{64,96},{96,1},{1,33},{33,65},{65,97},{97,2},{2,34}... | collective-permute-start | bytes 1769480 | tf_op jit(solution)/shard_map/ppermute | solution.py:56
  137.2 17.3 %collective-permute-start.6 = (bf16[8,48,768]{2,1,0:T(8,128)(2,1)}, bf16[8,48,768]{2,1,0:T(8,128)(2,1)S(1)}, u32[]{:S(2)}, u32[]{:S(2)}) collective-permute-start(bf16[8,48,768]{2,1,0:T(8,128)(2,1)} %all-to-all-done.2), channel_id=1, source_target_pairs={{0,99},{32,0},{64,32},{96,64},{1,96},{33,1},{65,33},{97,65},{2,97}... | collective-permute-start | bytes 1769480 | tf_op jit(solution)/shard_map/ppermute | solution.py:56
  141.8 1.7 copy-start.2
  152.6 9.8 %collective-permute-start.5 = (bf16[4,48,768]{2,1,0:T(8,128)(2,1)S(1)}, bf16[4,48,768]{2,1,0:T(8,128)(2,1)S(1)}, u32[]{:S(2)}, u32[]{:S(2)}) collective-permute-start(bf16[4,48,768]{2,1,0:T(8,128)(2,1)S(1)} %slice.90), channel_id=1, source_target_pairs={{0,32},{32,64},{64,96},{96,1},{1,33},{33,65},{65,97},{97,2},{2,34}... | collective-permute-start | bytes 884744 | tf_op jit(solution)/shard_map/ppermute | solution.py:56
  154.5 8.8 %collective-permute-start.7 = (bf16[4,48,768]{2,1,0:T(8,128)(2,1)S(1)}, bf16[4,48,768]{2,1,0:T(8,128)(2,1)S(1)}, u32[]{:S(2)}, u32[]{:S(2)}) collective-permute-start(bf16[4,48,768]{2,1,0:T(8,128)(2,1)S(1)} %slice.91), channel_id=1, source_target_pairs={{0,99},{32,0},{64,32},{96,64},{1,96},{33,1},{65,33},{97,65},{2,97}... | collective-permute-start | bytes 884744 | tf_op jit(solution)/shard_map/ppermute | solution.py:56
  168.7 8.1 %copy-start.6 = (f32[128,6]{0,1:T(8,128)S(1)}, f32[128,6]{0,1:T(8,128)}, u32[]{:S(2)}) copy-start(f32[128,6]{0,1:T(8,128)} %param.12) | copy-start | bytes 9220
  168.7 39.3 %all-to-all-start.3 = ((bf16[32,24,1536]{2,1,0:T(8,128)(2,1)}), bf16[32,24,1536]{2,1,0:T(8,128)(2,1)S(1)}, u32[]{:S(2)}, u32[]{:S(2)}) async-start(bf16[32,24,1536]{2,1,0:T(8,128)(2,1)} %bitcast.26), calls=%async_computation.3 | async-start | bytes 4718592 | tf_op jit(solution)/shard_map/all_to_all | solution.py:99

commit v19 on v17

--- a/solution.py
+++ b/solution.py
@@ -61,13 +61,13 @@
     for slab in slabs:
         slab = slab.reshape(n_pairs * local_experts, rows, width)
         slab = lax.all_to_all(slab, ("y", "c"), split_axis=0, concat_axis=0, tiled=True)
-        half = slab.shape[0] // 2
-        plus, minus = shift(slab, 1), shift(slab, -1)
+        halves = slab.reshape(2, slab.shape[0] // 2, rows, width)
+        plus, minus = shift(halves, 1), shift(halves, -1)
         quarters = [
             slab,
             plus,
             minus,
-            jnp.concatenate([shift(plus[:half], 1), shift(minus[half:], -1)]),
+            jnp.concatenate([shift(plus[0], 1), shift(minus[1], -1)]),
         ]
         y_size = slab.shape[0] // local_experts
         quarters = [q.reshape(y_size, local_experts, rows, width) for q in quarters]

time: 194 us -> 193 us (level)
  waiting for transfers between devices: 39.4 us -> 49.8 us
  starting transfers between devices: 49 us -> 43.3 us
  local copies, waits for them, and re-layouts: 8.63 us -> 4.24 us
    ppermute x8, waiting for transfers between devices: 4.95 us -> 14.2 us  [local(): shift = lambda v, k: lax.ppermute(v, ('zl', 'zh'), pairs(k))]
    ppermute x8, starting transfers between devices: 25.9 us -> 21.2 us  [local(): shift = lambda v, k: lax.ppermute(v, ('zl', 'zh'), pairs(k))]
    slice x4 -> x0, local copies, waits for them, and re-layouts: 2.46 us -> none  [the longest x2 1.71 us: local(): minus[half:]]
  transfers between devices with their start and end apart: 11 -> 11, of which waited for: 4 -> 7; matrix products, arithmetic and copies ran while one was open for 4% -> 2% of each run, Pallas kernels for 0% -> 0%
where the time goes in v19:
time: 193 us; the launch traced here: 192 us
  blocking collectives  78 us (40%)
  waiting for transfers between devices  49.8 us (26%)
  starting transfers between devices  43.3 us (22%)
  matrix products  10.1 us (5%)
  other arithmetic  6.28 us (3%)
  local copies, waits for them, and re-layouts  4.24 us (2%)
    all_gather x2, blocking collectives, local(): slabs = tuple((lax.all_gather(w, 'zh', axis=0, tiled=False) for w in slabs))  57.9 us
    all_to_all x1, waiting for transfers between devices, local(): lax.all_to_all(expert_rows, TOKEN_GROUP, split_axis=0, concat_axis=0, til...  30.8 us
    ppermute x8, starting transfers between devices, local(): shift = lambda v, k: lax.ppermute(v, ('zl', 'zh'), pairs(k))  21.2 us
    all_to_all x1, blocking collectives, local(): lax.all_to_all(slab, ('y', 'c'), split_axis=0, concat_axis=0, tiled=True)  20.2 us
    ppermute x8, waiting for transfers between devices, local(): shift = lambda v, k: lax.ppermute(v, ('zl', 'zh'), pairs(k))  14.2 us
    all_to_all x1, starting transfers between devices, local(): lax.all_to_all(outgoing, TOKEN_GROUP, split_axis=0, concat_axis=0, tiled=...  10.5 us
    all_to_all x1, starting transfers between devices, local(): lax.all_to_all(expert_rows, TOKEN_GROUP, split_axis=0, concat_axis=0, til...  7.33 us
    all_to_all x1, waiting for transfers between devices, local(): lax.all_to_all(slab, ('y', 'c'), split_axis=0, concat_axis=0, tiled=True)  4.8 us
  transfers between devices with their start and end apart: 11, of which 7 were waited for; matrix products, arithmetic and copies ran while one was open for 2% of the time, Pallas kernels for 0%

profile of v19, /device:TPU:1, one launch (start us, length us, event | category | flops | bytes accessed | tf_op | source)
XLA Modules:
  0.0 192.1 jit_solution(7913905539067158713)
XLA Ops:
  0.0 0.0 copy-start
  0.0 0.0 copy-start.3
  0.0 1.0 convert_bitcast_fusion
  1.0 0.9 convert.19
  2.0 0.9 convert.18
  3.0 0.7 pad_maximum_fusion.4
  3.6 0.8 copy.29
  4.4 0.1 eq.87
  4.6 0.7 broadcast_compare_fusion
  5.2 0.1 broadcast_in_dim.32.clone
  5.3 0.2 gt.23
  5.5 0.4 fusion.8
  5.9 0.1 convert_element_type.37
  6.0 0.1 copy.31
  6.0 0.0 copy-done.3
  6.1 0.4 fusion.1
  6.5 0.0 copy-done
  6.5 2.2 %convolution_convert_fusion = bf16[768,1536]{1,0:T(8,128)(2,1)} fusion(pred[768,128]{1,0:T(8,128)(4,1)S(1)} %fusion.1, bf16[128,1536]{1,0:T(8,128)(2,1)S(1)} %copy-done), kind=kOutput, calls=%fused_computation.1 | convolution fusion | flops 303169536 | bytes 2850816 | tf_op jit(solution)/shard_map/dot_general | solution.py:50
  8.7 10.5 %all-to-all-start = ((bf16[32,24,1536]{2,1,0:T(8,128)(2,1)}), bf16[32,24,1536]{2,1,0:T(8,128)(2,1)S(1)}, u32[]{:S(2)}, u32[]{:S(2)}) async-start(bf16[32,24,1536]{2,1,0:T(8,128)(2,1)} %bitcast.1), calls=%async_computation | async-start | bytes 4718592 | tf_op jit(solution)/shard_map/all_to_all | solution.py:51
  19.2 30.8 %all-gather = bf16[8,48,768]{2,1,0:T(8,128)(2,1)S(1)} all-gather(bf16[2,48,768]{2,1,0:T(8,128)(2,1)} %get-tuple-element.18), channel_id=2, replica_groups=mesh['y'=4,'zl'=4,'c'=2,'x'=4,'zh'=4] {'zh'}, dimensions={0}, use_global_device_ids=true | all-gather | bytes 737280 | tf_op jit(solution)/shard_map/all_gather | solution.py:32
  50.1 27.0 %all-gather.1 = bf16[8,48,768]{2,1,0:T(8,128)(2,1)} all-gather(bf16[2,48,768]{2,1,0:T(8,128)(2,1)S(1)} %get-tuple-element.19), channel_id=3, replica_groups=mesh['y'=4,'zl'=4,'c'=2,'x'=4,'zh'=4] {'zh'}, dimensions={0}, use_global_device_ids=true | all-gather | bytes 737280 | tf_op jit(solution)/shard_map/all_gather | solution.py:32
  77.1 0.0 all-to-all-done
  77.1 0.0 copy-start.1
  77.1 1.4 copy-done.1
  78.5 20.2 %all_to_all.34 = bf16[8,48,768]{2,1,0:T(8,128)(2,1)S(1)} all-to-all(bf16[8,48,768]{2,1,0:T(8,128)(2,1)S(1)} %all-gather), channel_id=1, replica_groups=mesh['y'=4,'zl'=4,'c'=2,'x'=4,'zh'=4] {'y','c'}, dimensions={0} | all-to-all | bytes 1179648 | tf_op jit(solution)/shard_map/all_to_all | solution.py:63
  98.7 4.2 %all-to-all-start.2 = ((bf16[8,48,768]{2,1,0:T(8,128)(2,1)}), bf16[8,48,768]{2,1,0:T(8,128)(2,1)S(1)}, u32[]{:S(2)}, u32[]{:S(2)}) async-start(bf16[8,48,768]{2,1,0:T(8,128)(2,1)} %bitcast.14), calls=%async_computation.2 | async-start | bytes 1179648 | tf_op jit(solution)/shard_map/all_to_all | solution.py:63
  102.9 1.9 collective-permute-start.2
  104.8 3.4 %collective-permute-start = (bf16[2,4,48,768]{3,2,1,0:T(8,128)(2,1)S(1)}, bf16[2,4,48,768]{3,2,1,0:T(8,128)(2,1)S(1)}, u32[]{:S(2)}, u32[]{:S(2)}) collective-permute-start(bf16[2,4,48,768]{3,2,1,0:T(8,128)(2,1)S(1)} %bitcast.47), channel_id=1, source_target_pairs={{0,32},{32,64},{64,96},{96,1},{1,33},{33,65},{65,97},{97,2},{2,34}... | collective-permute-start | bytes 1769480 | tf_op jit(solution)/shard_map/ppermute | solution.py:57
  108.2 4.8 %all-to-all-done.2 = bf16[8,48,768]{2,1,0:T(8,128)(2,1)S(1)} async-done(((bf16[8,48,768]{2,1,0:T(8,128)(2,1)}), bf16[8,48,768]{2,1,0:T(8,128)(2,1)S(1)}, u32[]{:S(2)}, u32[]{:S(2)}) %all-to-all-start.2) | async-done | bytes 589856 | tf_op jit(solution)/shard_map/all_to_all | solution.py:63
  113.0 1.9 collective-permute-start.6
  114.9 3.4 %collective-permute-start.4 = (bf16[2,4,48,768]{3,2,1,0:T(8,128)(2,1)S(1)}, bf16[2,4,48,768]{3,2,1,0:T(8,128)(2,1)S(1)}, u32[]{:S(2)}, u32[]{:S(2)}) collective-permute-start(bf16[2,4,48,768]{3,2,1,0:T(8,128)(2,1)S(1)} %bitcast.44), channel_id=1, source_target_pairs={{0,32},{32,64},{64,96},{96,1},{1,33},{33,65},{65,97},{97,2},{2,34}... | collective-permute-start | bytes 1769480 | tf_op jit(solution)/shard_map/ppermute | solution.py:57
  118.3 1.2 collective-permute-done.2
  119.5 3.4 %collective-permute-start.3 = (bf16[4,48,768]{2,1,0:T(8,128)(2,1)S(1)}, bf16[4,48,768]{2,1,0:T(8,128)(2,1)S(1)}, u32[]{:S(2)}, u32[]{:S(2)}) collective-permute-start(bf16[4,48,768]{2,1,0:T(8,128)(2,1)S(1)} %slice_bitcast_fusion.2), channel_id=1, source_target_pairs={{0,99},{32,0},{64,32},{96,64},{1,96},{33,1},{65,33},{97,65},{2,97}... | collective-permute-start | bytes 884744 | tf_op jit(solution)/shard_map/ppermute | solution.py:57
  123.0 0.0 collective-permute-done
  123.0 1.9 collective-permute-start.1
  124.9 7.2 %collective-permute-done.6 = bf16[2,4,48,768]{3,2,1,0:T(8,128)(2,1)S(1)} collective-permute-done((bf16[2,4,48,768]{3,2,1,0:T(8,128)(2,1)S(1)}, bf16[2,4,48,768]{3,2,1,0:T(8,128)(2,1)S(1)}, u32[]{:S(2)}, u32[]{:S(2)}) %collective-permute-start.6) | collective-permute-done | bytes 589856 | tf_op jit(solution)/shard_map/ppermute | solution.py:57
  132.2 3.4 %collective-permute-start.7 = (bf16[4,48,768]{2,1,0:T(8,128)(2,1)S(1)}, bf16[4,48,768]{2,1,0:T(8,128)(2,1)S(1)}, u32[]{:S(2)}, u32[]{:S(2)}) collective-permute-start(bf16[4,48,768]{2,1,0:T(8,128)(2,1)S(1)} %slice_bitcast_fusion), channel_id=1, source_target_pairs={{0,99},{32,0},{64,32},{96,64},{1,96},{33,1},{65,33},{97,65},{2,97}... | collective-permute-start | bytes 884744 | tf_op jit(solution)/shard_map/ppermute | solution.py:57
  135.6 0.0 collective-permute-done.4
  135.6 1.9 collective-permute-start.5
  137.6 0.9 collective-permute-done.3
  138.5 3.1 %collective-permute-done.1 = bf16[4,48,768]{2,1,0:T(8,128)(2,1)S(1)} collective-permute-done((bf16[4,48,768]{2,1,0:T(8,128)(2,1)S(1)}, bf16[4,48,768]{2,1,0:T(8,128)(2,1)S(1)}, u32[]{:S(2)}, u32[]{:S(2)}) %collective-permute-start.1) | collective-permute-done | bytes 294944 | tf_op jit(solution)/shard_map/ppermute | solution.py:57
  141.6 0.1 pad_maximum_fusion.2
  141.7 0.3 select_select_fusion.7
  142.0 0.0 copy-start.2
  142.0 0.3 pad_maximum_fusion
  142.3 1.4 copy-done.2
  143.6 1.4 fusion.5
  145.0 0.8 fusion.11
  145.8 0.0 collective-permute-done.7
  145.9 1.7 collective-permute-done.5
  147.5 0.1 pad_maximum_fusion.3
  147.6 0.3 select_select_fusion.3
  147.9 0.3 pad_maximum_fusion.1
  148.2 1.4 fusion.3
  149.6 2.3 %add_convert_fusion = bf16[768,1536]{1,0:T(8,128)(2,1)} fusion(f32[768,1536]{1,0:T(8,128)S(1)} %fusion.11, bf16[1536,768]{1,0:T(8,128)(2,1)S(1)} %bitcast.40, f32[768,512]{1,0:T(8,128)S(1)} %fusion.3), kind=kOutput, calls=%fused_computation | convolution fusion | flops 607518720 | bytes 9437184 | tf_op jit(solution)/shard_map/dot_general | solution.py:86
  151.8 0.0 copy-start.4
  151.8 7.3 %all-to-all-start.3 = ((bf16[32,24,1536]{2,1,0:T(8,128)(2,1)}), bf16[32,24,1536]{2,1,0:T(8,128)(2,1)S(1)}, u32[]{:S(2)}, u32[]{:S(2)}) async-start(bf16[32,24,1536]{2,1,0:T(8,128)(2,1)} %bitcast.38), calls=%async_computation.3 | async-start | bytes 4718592 | tf_op jit(solution)/shard_map/all_to_all | solution.py:91
  159.2 0.0 copy-done.4
  159.2 0.3 select_reduce_fusion
  159.5 30.8 %all-to-all-done.3 = bf16[32,24,1536]{2,1,0:T(8,128)(2,1)S(1)} async-done(((bf16[32,24,1536]{2,1,0:T(8,128)(2,1)}), bf16[32,24,1536]{2,1,0:T(8,128)(2,1)S(1)}, u32[]{:S(2)}, u32[]{:S(2)}) %all-to-all-start.3) | async-done | bytes 2359328 | tf_op jit(solution)/shard_map/all_to_all | solution.py:91
  190.3 0.5 fusion.20
  190.8 1.2 fusion
  (11 shorter events, 0.2 us)
Async XLA Ops:
  0.0 6.5 %copy-start = (bf16[128,1536]{1,0:T(8,128)(2,1)S(1)}, bf16[128,1536]{1,0:T(8,128)(2,1)}, u32[]{:S(2)}) copy-start(bf16[128,1536]{1,0:T(8,128)(2,1)} %param.7) | copy-start | bytes 1179652
  0.0 6.0 %copy-start.3 = (s32[128,6]{0,1:T(8,128)S(1)}, s32[128,6]{0,1:T(8,128)}, u32[]{:S(2)}) copy-start(s32[128,6]{0,1:T(8,128)} %param.11) | copy-start | bytes 9220
  8.7 68.4 %all-to-all-start = ((bf16[32,24,1536]{2,1,0:T(8,128)(2,1)}), bf16[32,24,1536]{2,1,0:T(8,128)(2,1)S(1)}, u32[]{:S(2)}, u32[]{:S(2)}) async-start(bf16[32,24,1536]{2,1,0:T(8,128)(2,1)} %bitcast.1), calls=%async_computation | async-start | bytes 4718592 | tf_op jit(solution)/shard_map/all_to_all | solution.py:51
  77.1 1.4 copy-start.1
  98.7 14.3 %all-to-all-start.2 = ((bf16[8,48,768]{2,1,0:T(8,128)(2,1)}), bf16[8,48,768]{2,1,0:T(8,128)(2,1)S(1)}, u32[]{:S(2)}, u32[]{:S(2)}) async-start(bf16[8,48,768]{2,1,0:T(8,128)(2,1)} %bitcast.14), calls=%async_computation.2 | async-start | bytes 1179648 | tf_op jit(solution)/shard_map/all_to_all | solution.py:63
  102.9 16.6 %collective-permute-start.2 = (bf16[2,4,48,768]{3,2,1,0:T(8,128)(2,1)S(1)}, bf16[2,4,48,768]{3,2,1,0:T(8,128)(2,1)S(1)}, u32[]{:S(2)}, u32[]{:S(2)}) collective-permute-start(bf16[2,4,48,768]{3,2,1,0:T(8,128)(2,1)S(1)} %bitcast.46), channel_id=1, source_target_pairs={{0,99},{32,0},{64,32},{96,64},{1,96},{33,1},{65,33},{97,65},{2,97}... | collective-permute-start | bytes 1769480 | tf_op jit(solution)/shard_map/ppermute | solution.py:57
  104.8 18.2 %collective-permute-start = (bf16[2,4,48,768]{3,2,1,0:T(8,128)(2,1)S(1)}, bf16[2,4,48,768]{3,2,1,0:T(8,128)(2,1)S(1)}, u32[]{:S(2)}, u32[]{:S(2)}) collective-permute-start(bf16[2,4,48,768]{3,2,1,0:T(8,128)(2,1)S(1)} %bitcast.47), channel_id=1, source_target_pairs={{0,32},{32,64},{64,96},{96,1},{1,33},{33,65},{65,97},{97,2},{2,34}... | collective-permute-start | bytes 1769480 | tf_op jit(solution)/shard_map/ppermute | solution.py:57
  113.0 19.2 %collective-permute-start.6 = (bf16[2,4,48,768]{3,2,1,0:T(8,128)(2,1)S(1)}, bf16[2,4,48,768]{3,2,1,0:T(8,128)(2,1)S(1)}, u32[]{:S(2)}, u32[]{:S(2)}) collective-permute-start(bf16[2,4,48,768]{3,2,1,0:T(8,128)(2,1)S(1)} %bitcast.43), channel_id=1, source_target_pairs={{0,99},{32,0},{64,32},{96,64},{1,96},{33,1},{65,33},{97,65},{2,97}... | collective-permute-start | bytes 1769480 | tf_op jit(solution)/shard_map/ppermute | solution.py:57
  114.9 20.7 %collective-permute-start.4 = (bf16[2,4,48,768]{3,2,1,0:T(8,128)(2,1)S(1)}, bf16[2,4,48,768]{3,2,1,0:T(8,128)(2,1)S(1)}, u32[]{:S(2)}, u32[]{:S(2)}) collective-permute-start(bf16[2,4,48,768]{3,2,1,0:T(8,128)(2,1)S(1)} %bitcast.44), channel_id=1, source_target_pairs={{0,32},{32,64},{64,96},{96,1},{1,33},{33,65},{65,97},{97,2},{2,34}... | collective-permute-start | bytes 1769480 | tf_op jit(solution)/shard_map/ppermute | solution.py:57
  119.5 18.9 %collective-permute-start.3 = (bf16[4,48,768]{2,1,0:T(8,128)(2,1)S(1)}, bf16[4,48,768]{2,1,0:T(8,128)(2,1)S(1)}, u32[]{:S(2)}, u32[]{:S(2)}) collective-permute-start(bf16[4,48,768]{2,1,0:T(8,128)(2,1)S(1)} %slice_bitcast_fusion.2), channel_id=1, source_target_pairs={{0,99},{32,0},{64,32},{96,64},{1,96},{33,1},{65,33},{97,65},{2,97}... | collective-permute-start | bytes 884744 | tf_op jit(solution)/shard_map/ppermute | solution.py:57
  123.0 18.6 %collective-permute-start.1 = (bf16[4,48,768]{2,1,0:T(8,128)(2,1)S(1)}, bf16[4,48,768]{2,1,0:T(8,128)(2,1)S(1)}, u32[]{:S(2)}, u32[]{:S(2)}) collective-permute-start(bf16[4,48,768]{2,1,0:T(8,128)(2,1)S(1)} %slice_bitcast_fusion.3), channel_id=1, source_target_pairs={{0,32},{32,64},{64,96},{96,1},{1,33},{33,65},{65,97},{97,2},{2,34}... | collective-permute-start | bytes 884744 | tf_op jit(solution)/shard_map/ppermute | solution.py:57
  132.2 13.7 %collective-permute-start.7 = (bf16[4,48,768]{2,1,0:T(8,128)(2,1)S(1)}, bf16[4,48,768]{2,1,0:T(8,128)(2,1)S(1)}, u32[]{:S(2)}, u32[]{:S(2)}) collective-permute-start(bf16[4,48,768]{2,1,0:T(8,128)(2,1)S(1)} %slice_bitcast_fusion), channel_id=1, source_target_pairs={{0,99},{32,0},{64,32},{96,64},{1,96},{33,1},{65,33},{97,65},{2,97}... | collective-permute-start | bytes 884744 | tf_op jit(solution)/shard_map/ppermute | solution.py:57
  135.6 11.9 %collective-permute-start.5 = (bf16[4,48,768]{2,1,0:T(8,128)(2,1)S(1)}, bf16[4,48,768]{2,1,0:T(8,128)(2,1)S(1)}, u32[]{:S(2)}, u32[]{:S(2)}) collective-permute-start(bf16[4,48,768]{2,1,0:T(8,128)(2,1)S(1)} %slice_bitcast_fusion.1), channel_id=1, source_target_pairs={{0,32},{32,64},{64,96},{96,1},{1,33},{33,65},{65,97},{97,2},{2,34}... | collective-permute-start | bytes 884744 | tf_op jit(solution)/shard_map/ppermute | solution.py:57
  142.0 1.7 copy-start.2
  151.8 7.3 %copy-start.4 = (f32[128,6]{0,1:T(8,128)S(1)}, f32[128,6]{0,1:T(8,128)}, u32[]{:S(2)}) copy-start(f32[128,6]{0,1:T(8,128)} %param.12) | copy-start | bytes 9220
  151.8 38.5 %all-to-all-start.3 = ((bf16[32,24,1536]{2,1,0:T(8,128)(2,1)}), bf16[32,24,1536]{2,1,0:T(8,128)(2,1)S(1)}, u32[]{:S(2)}, u32[]{:S(2)}) async-start(bf16[32,24,1536]{2,1,0:T(8,128)(2,1)} %bitcast.38), calls=%async_computation.3 | async-start | bytes 4718592 | tf_op jit(solution)/shard_map/all_to_all | solution.py:91

commit v20 on v19

--- a/solution.py
+++ b/solution.py
@@ -94,9 +94,10 @@
     combine_hi = lax.reduce_precision(combine, exponent_bits=8, mantissa_bits=7)
     combine_lo = (combine - combine_hi).astype(jnp.bfloat16)
     combine_hi = combine_hi.astype(jnp.bfloat16)
-    combined = jnp.dot(combine_hi, returned, preferred_element_type=jnp.float32) + jnp.dot(
-        combine_lo, returned, preferred_element_type=jnp.float32
+    both = jnp.dot(
+        jnp.concatenate([combine_hi, combine_lo]), returned, preferred_element_type=jnp.float32
     )
+    combined = both[:tok_dev] + both[tok_dev:]
     return combined.astype(jnp.bfloat16)
 
 

time: 193 us -> 193 us (level)
  no operation moved by 1% of the time
where the time goes in v20:
time: 193 us; the launch traced here: 192 us
  blocking collectives  78 us (40%)
  waiting for transfers between devices  49.7 us (26%)
  starting transfers between devices  43.3 us (22%)
  matrix products  9.17 us (5%)
  other arithmetic  7.15 us (4%)
  local copies, waits for them, and re-layouts  4.25 us (2%)
    all_gather x2, blocking collectives, local(): slabs = tuple((lax.all_gather(w, 'zh', axis=0, tiled=False) for w in slabs))  57.9 us
    all_to_all x1, waiting for transfers between devices, local(): lax.all_to_all(expert_rows, TOKEN_GROUP, split_axis=0, concat_axis=0, til...  30.8 us
    ppermute x8, starting transfers between devices, local(): shift = lambda v, k: lax.ppermute(v, ('zl', 'zh'), pairs(k))  21.2 us
    all_to_all x1, blocking collectives, local(): lax.all_to_all(slab, ('y', 'c'), split_axis=0, concat_axis=0, tiled=True)  20.2 us
    ppermute x8, waiting for transfers between devices, local(): shift = lambda v, k: lax.ppermute(v, ('zl', 'zh'), pairs(k))  14.2 us
    all_to_all x1, starting transfers between devices, local(): lax.all_to_all(outgoing, TOKEN_GROUP, split_axis=0, concat_axis=0, tiled=...  10.5 us
    all_to_all x1, starting transfers between devices, local(): lax.all_to_all(expert_rows, TOKEN_GROUP, split_axis=0, concat_axis=0, til...  7.33 us
    all_to_all x1, waiting for transfers between devices, local(): lax.all_to_all(slab, ('y', 'c'), split_axis=0, concat_axis=0, tiled=True)  4.8 us
  transfers between devices with their start and end apart: 11, of which 7 were waited for; matrix products, arithmetic and copies ran while one was open for 2% of the time, Pallas kernels for 0%

profile of v20, /device:TPU:1, one launch (start us, length us, event | category | flops | bytes accessed | tf_op | source)
XLA Modules:
  0.0 192.0 jit_solution(17237838846538343338)
XLA Ops:
  0.0 0.0 copy-start
  0.0 0.0 copy-start.3
  0.0 1.0 convert_bitcast_fusion
  1.0 0.9 convert.19
  2.0 0.9 convert.18
  3.0 0.7 pad_maximum_fusion.4
  3.6 0.8 copy.29
  4.4 0.1 eq.87
  4.6 0.7 broadcast_compare_fusion
  5.2 0.1 broadcast_in_dim.32.clone
  5.3 0.2 gt.23
  5.5 0.4 fusion.7
  5.9 0.1 convert_element_type.37
  6.0 0.1 copy.31
  6.0 0.0 copy-done.3
  6.1 0.4 fusion
  6.5 0.0 copy-done
  6.5 2.2 %convolution_convert_fusion = bf16[768,1536]{1,0:T(8,128)(2,1)} fusion(pred[768,128]{1,0:T(8,128)(4,1)S(1)} %fusion, bf16[128,1536]{1,0:T(8,128)(2,1)S(1)} %copy-done), kind=kOutput, calls=%fused_computation.1 | convolution fusion | flops 303169536 | bytes 2850816 | tf_op jit(solution)/shard_map/dot_general | solution.py:50
  8.7 10.5 %all-to-all-start = ((bf16[32,24,1536]{2,1,0:T(8,128)(2,1)}), bf16[32,24,1536]{2,1,0:T(8,128)(2,1)S(1)}, u32[]{:S(2)}, u32[]{:S(2)}) async-start(bf16[32,24,1536]{2,1,0:T(8,128)(2,1)} %bitcast.1), calls=%async_computation | async-start | bytes 4718592 | tf_op jit(solution)/shard_map/all_to_all | solution.py:51
  19.2 30.8 %all-gather = bf16[8,48,768]{2,1,0:T(8,128)(2,1)S(1)} all-gather(bf16[2,48,768]{2,1,0:T(8,128)(2,1)} %get-tuple-element.18), channel_id=2, replica_groups=mesh['y'=4,'zl'=4,'c'=2,'x'=4,'zh'=4] {'zh'}, dimensions={0}, use_global_device_ids=true | all-gather | bytes 737280 | tf_op jit(solution)/shard_map/all_gather | solution.py:32
  50.1 27.0 %all-gather.1 = bf16[8,48,768]{2,1,0:T(8,128)(2,1)} all-gather(bf16[2,48,768]{2,1,0:T(8,128)(2,1)S(1)} %get-tuple-element.19), channel_id=3, replica_groups=mesh['y'=4,'zl'=4,'c'=2,'x'=4,'zh'=4] {'zh'}, dimensions={0}, use_global_device_ids=true | all-gather | bytes 737280 | tf_op jit(solution)/shard_map/all_gather | solution.py:32
  77.1 0.0 all-to-all-done
  77.1 0.0 copy-start.1
  77.1 1.4 copy-done.1
  78.5 20.2 %all_to_all.34 = bf16[8,48,768]{2,1,0:T(8,128)(2,1)S(1)} all-to-all(bf16[8,48,768]{2,1,0:T(8,128)(2,1)S(1)} %all-gather), channel_id=1, replica_groups=mesh['y'=4,'zl'=4,'c'=2,'x'=4,'zh'=4] {'y','c'}, dimensions={0} | all-to-all | bytes 1179648 | tf_op jit(solution)/shard_map/all_to_all | solution.py:63
  98.7 4.2 %all-to-all-start.2 = ((bf16[8,48,768]{2,1,0:T(8,128)(2,1)}), bf16[8,48,768]{2,1,0:T(8,128)(2,1)S(1)}, u32[]{:S(2)}, u32[]{:S(2)}) async-start(bf16[8,48,768]{2,1,0:T(8,128)(2,1)} %bitcast.14), calls=%async_computation.2 | async-start | bytes 1179648 | tf_op jit(solution)/shard_map/all_to_all | solution.py:63
  102.9 1.9 collective-permute-start.2
  104.8 3.4 %collective-permute-start = (bf16[2,4,48,768]{3,2,1,0:T(8,128)(2,1)S(1)}, bf16[2,4,48,768]{3,2,1,0:T(8,128)(2,1)S(1)}, u32[]{:S(2)}, u32[]{:S(2)}) collective-permute-start(bf16[2,4,48,768]{3,2,1,0:T(8,128)(2,1)S(1)} %bitcast.45), channel_id=1, source_target_pairs={{0,32},{32,64},{64,96},{96,1},{1,33},{33,65},{65,97},{97,2},{2,34}... | collective-permute-start | bytes 1769480 | tf_op jit(solution)/shard_map/ppermute | solution.py:57
  108.2 4.8 %all-to-all-done.2 = bf16[8,48,768]{2,1,0:T(8,128)(2,1)S(1)} async-done(((bf16[8,48,768]{2,1,0:T(8,128)(2,1)}), bf16[8,48,768]{2,1,0:T(8,128)(2,1)S(1)}, u32[]{:S(2)}, u32[]{:S(2)}) %all-to-all-start.2) | async-done | bytes 589856 | tf_op jit(solution)/shard_map/all_to_all | solution.py:63
  113.0 1.9 collective-permute-start.6
  115.0 3.4 %collective-permute-start.4 = (bf16[2,4,48,768]{3,2,1,0:T(8,128)(2,1)S(1)}, bf16[2,4,48,768]{3,2,1,0:T(8,128)(2,1)S(1)}, u32[]{:S(2)}, u32[]{:S(2)}) collective-permute-start(bf16[2,4,48,768]{3,2,1,0:T(8,128)(2,1)S(1)} %bitcast.42), channel_id=1, source_target_pairs={{0,32},{32,64},{64,96},{96,1},{1,33},{33,65},{65,97},{97,2},{2,34}... | collective-permute-start | bytes 1769480 | tf_op jit(solution)/shard_map/ppermute | solution.py:57
  118.3 1.2 collective-permute-done.2
  119.6 3.4 %collective-permute-start.3 = (bf16[4,48,768]{2,1,0:T(8,128)(2,1)S(1)}, bf16[4,48,768]{2,1,0:T(8,128)(2,1)S(1)}, u32[]{:S(2)}, u32[]{:S(2)}) collective-permute-start(bf16[4,48,768]{2,1,0:T(8,128)(2,1)S(1)} %slice_bitcast_fusion.2), channel_id=1, source_target_pairs={{0,99},{32,0},{64,32},{96,64},{1,96},{33,1},{65,33},{97,65},{2,97}... | collective-permute-start | bytes 884744 | tf_op jit(solution)/shard_map/ppermute | solution.py:57
  123.0 0.0 collective-permute-done
  123.0 1.9 %collective-permute-start.1 = (bf16[4,48,768]{2,1,0:T(8,128)(2,1)S(1)}, bf16[4,48,768]{2,1,0:T(8,128)(2,1)S(1)}, u32[]{:S(2)}, u32[]{:S(2)}) collective-permute-start(bf16[4,48,768]{2,1,0:T(8,128)(2,1)S(1)} %slice_bitcast_fusion.3), channel_id=1, source_target_pairs={{0,32},{32,64},{64,96},{96,1},{1,33},{33,65},{65,97},{97,2},{2,34}... | collective-permute-start | bytes 884744 | tf_op jit(solution)/shard_map/ppermute | solution.py:57
  125.0 7.2 %collective-permute-done.6 = bf16[2,4,48,768]{3,2,1,0:T(8,128)(2,1)S(1)} collective-permute-done((bf16[2,4,48,768]{3,2,1,0:T(8,128)(2,1)S(1)}, bf16[2,4,48,768]{3,2,1,0:T(8,128)(2,1)S(1)}, u32[]{:S(2)}, u32[]{:S(2)}) %collective-permute-start.6) | collective-permute-done | bytes 589856 | tf_op jit(solution)/shard_map/ppermute | solution.py:57
  132.2 3.4 %collective-permute-start.7 = (bf16[4,48,768]{2,1,0:T(8,128)(2,1)S(1)}, bf16[4,48,768]{2,1,0:T(8,128)(2,1)S(1)}, u32[]{:S(2)}, u32[]{:S(2)}) collective-permute-start(bf16[4,48,768]{2,1,0:T(8,128)(2,1)S(1)} %slice_bitcast_fusion), channel_id=1, source_target_pairs={{0,99},{32,0},{64,32},{96,64},{1,96},{33,1},{65,33},{97,65},{2,97}... | collective-permute-start | bytes 884744 | tf_op jit(solution)/shard_map/ppermute | solution.py:57
  135.6 0.0 collective-permute-done.4
  135.7 1.9 %collective-permute-start.5 = (bf16[4,48,768]{2,1,0:T(8,128)(2,1)S(1)}, bf16[4,48,768]{2,1,0:T(8,128)(2,1)S(1)}, u32[]{:S(2)}, u32[]{:S(2)}) collective-permute-start(bf16[4,48,768]{2,1,0:T(8,128)(2,1)S(1)} %slice_bitcast_fusion.1), channel_id=1, source_target_pairs={{0,32},{32,64},{64,96},{96,1},{1,33},{33,65},{65,97},{97,2},{2,34}... | collective-permute-start | bytes 884744 | tf_op jit(solution)/shard_map/ppermute | solution.py:57
  137.6 0.9 collective-permute-done.3
  138.5 3.1 %collective-permute-done.1 = bf16[4,48,768]{2,1,0:T(8,128)(2,1)S(1)} collective-permute-done((bf16[4,48,768]{2,1,0:T(8,128)(2,1)S(1)}, bf16[4,48,768]{2,1,0:T(8,128)(2,1)S(1)}, u32[]{:S(2)}, u32[]{:S(2)}) %collective-permute-start.1) | collective-permute-done | bytes 294944 | tf_op jit(solution)/shard_map/ppermute | solution.py:57
  141.6 0.1 pad_maximum_fusion.2
  141.7 0.3 select_select_fusion.7
  142.0 0.0 copy-start.2
  142.0 0.3 pad_maximum_fusion
  142.3 1.4 copy-done.2
  143.7 1.4 fusion.4
  145.0 0.8 fusion.11
  145.9 0.0 collective-permute-done.7
  145.9 1.7 collective-permute-done.5
  147.6 0.1 pad_maximum_fusion.3
  147.6 0.3 select_select_fusion.3
  147.9 0.3 pad_maximum_fusion.1
  148.2 1.4 fusion.2
  149.6 2.3 %add_convert_fusion = bf16[768,1536]{1,0:T(8,128)(2,1)} fusion(f32[768,1536]{1,0:T(8,128)S(1)} %fusion.11, bf16[1536,768]{1,0:T(8,128)(2,1)S(1)} %bitcast.38, f32[768,512]{1,0:T(8,128)S(1)} %fusion.2), kind=kOutput, calls=%fused_computation | convolution fusion | flops 607518720 | bytes 9437184 | tf_op jit(solution)/shard_map/dot_general | solution.py:86
  151.9 0.0 copy-start.4
  151.9 7.3 %all-to-all-start.3 = ((bf16[32,24,1536]{2,1,0:T(8,128)(2,1)}), bf16[32,24,1536]{2,1,0:T(8,128)(2,1)S(1)}, u32[]{:S(2)}, u32[]{:S(2)}) async-start(bf16[32,24,1536]{2,1,0:T(8,128)(2,1)} %bitcast.36), calls=%async_computation.3 | async-start | bytes 4718592 | tf_op jit(solution)/shard_map/all_to_all | solution.py:91
  159.2 0.0 copy-done.4
  159.3 0.3 select_reduce_fusion
  159.6 30.8 %all-to-all-done.3 = bf16[32,24,1536]{2,1,0:T(8,128)(2,1)S(1)} async-done(((bf16[32,24,1536]{2,1,0:T(8,128)(2,1)}), bf16[32,24,1536]{2,1,0:T(8,128)(2,1)S(1)}, u32[]{:S(2)}, u32[]{:S(2)}) %all-to-all-start.3) | async-done | bytes 2359328 | tf_op jit(solution)/shard_map/all_to_all | solution.py:91
  190.4 0.8 fusion.17
  191.2 0.8 fusion.8
  (12 shorter events, 0.2 us)
Async XLA Ops:
  0.0 6.5 %copy-start = (bf16[128,1536]{1,0:T(8,128)(2,1)S(1)}, bf16[128,1536]{1,0:T(8,128)(2,1)}, u32[]{:S(2)}) copy-start(bf16[128,1536]{1,0:T(8,128)(2,1)} %param.7) | copy-start | bytes 1179652
  0.0 6.0 %copy-start.3 = (s32[128,6]{0,1:T(8,128)S(1)}, s32[128,6]{0,1:T(8,128)}, u32[]{:S(2)}) copy-start(s32[128,6]{0,1:T(8,128)} %param.11) | copy-start | bytes 9220
  8.7 68.4 %all-to-all-start = ((bf16[32,24,1536]{2,1,0:T(8,128)(2,1)}), bf16[32,24,1536]{2,1,0:T(8,128)(2,1)S(1)}, u32[]{:S(2)}, u32[]{:S(2)}) async-start(bf16[32,24,1536]{2,1,0:T(8,128)(2,1)} %bitcast.1), calls=%async_computation | async-start | bytes 4718592 | tf_op jit(solution)/shard_map/all_to_all | solution.py:51
  77.1 1.4 copy-start.1
  98.7 14.3 %all-to-all-start.2 = ((bf16[8,48,768]{2,1,0:T(8,128)(2,1)}), bf16[8,48,768]{2,1,0:T(8,128)(2,1)S(1)}, u32[]{:S(2)}, u32[]{:S(2)}) async-start(bf16[8,48,768]{2,1,0:T(8,128)(2,1)} %bitcast.14), calls=%async_computation.2 | async-start | bytes 1179648 | tf_op jit(solution)/shard_map/all_to_all | solution.py:63
  102.9 16.6 %collective-permute-start.2 = (bf16[2,4,48,768]{3,2,1,0:T(8,128)(2,1)S(1)}, bf16[2,4,48,768]{3,2,1,0:T(8,128)(2,1)S(1)}, u32[]{:S(2)}, u32[]{:S(2)}) collective-permute-start(bf16[2,4,48,768]{3,2,1,0:T(8,128)(2,1)S(1)} %bitcast.44), channel_id=1, source_target_pairs={{0,99},{32,0},{64,32},{96,64},{1,96},{33,1},{65,33},{97,65},{2,97}... | collective-permute-start | bytes 1769480 | tf_op jit(solution)/shard_map/ppermute | solution.py:57
  104.8 18.2 %collective-permute-start = (bf16[2,4,48,768]{3,2,1,0:T(8,128)(2,1)S(1)}, bf16[2,4,48,768]{3,2,1,0:T(8,128)(2,1)S(1)}, u32[]{:S(2)}, u32[]{:S(2)}) collective-permute-start(bf16[2,4,48,768]{3,2,1,0:T(8,128)(2,1)S(1)} %bitcast.45), channel_id=1, source_target_pairs={{0,32},{32,64},{64,96},{96,1},{1,33},{33,65},{65,97},{97,2},{2,34}... | collective-permute-start | bytes 1769480 | tf_op jit(solution)/shard_map/ppermute | solution.py:57
  113.0 19.2 %collective-permute-start.6 = (bf16[2,4,48,768]{3,2,1,0:T(8,128)(2,1)S(1)}, bf16[2,4,48,768]{3,2,1,0:T(8,128)(2,1)S(1)}, u32[]{:S(2)}, u32[]{:S(2)}) collective-permute-start(bf16[2,4,48,768]{3,2,1,0:T(8,128)(2,1)S(1)} %bitcast.41), channel_id=1, source_target_pairs={{0,99},{32,0},{64,32},{96,64},{1,96},{33,1},{65,33},{97,65},{2,97}... | collective-permute-start | bytes 1769480 | tf_op jit(solution)/shard_map/ppermute | solution.py:57
  115.0 20.7 %collective-permute-start.4 = (bf16[2,4,48,768]{3,2,1,0:T(8,128)(2,1)S(1)}, bf16[2,4,48,768]{3,2,1,0:T(8,128)(2,1)S(1)}, u32[]{:S(2)}, u32[]{:S(2)}) collective-permute-start(bf16[2,4,48,768]{3,2,1,0:T(8,128)(2,1)S(1)} %bitcast.42), channel_id=1, source_target_pairs={{0,32},{32,64},{64,96},{96,1},{1,33},{33,65},{65,97},{97,2},{2,34}... | collective-permute-start | bytes 1769480 | tf_op jit(solution)/shard_map/ppermute | solution.py:57
  119.6 18.9 %collective-permute-start.3 = (bf16[4,48,768]{2,1,0:T(8,128)(2,1)S(1)}, bf16[4,48,768]{2,1,0:T(8,128)(2,1)S(1)}, u32[]{:S(2)}, u32[]{:S(2)}) collective-permute-start(bf16[4,48,768]{2,1,0:T(8,128)(2,1)S(1)} %slice_bitcast_fusion.2), channel_id=1, source_target_pairs={{0,99},{32,0},{64,32},{96,64},{1,96},{33,1},{65,33},{97,65},{2,97}... | collective-permute-start | bytes 884744 | tf_op jit(solution)/shard_map/ppermute | solution.py:57
  123.0 18.6 %collective-permute-start.1 = (bf16[4,48,768]{2,1,0:T(8,128)(2,1)S(1)}, bf16[4,48,768]{2,1,0:T(8,128)(2,1)S(1)}, u32[]{:S(2)}, u32[]{:S(2)}) collective-permute-start(bf16[4,48,768]{2,1,0:T(8,128)(2,1)S(1)} %slice_bitcast_fusion.3), channel_id=1, source_target_pairs={{0,32},{32,64},{64,96},{96,1},{1,33},{33,65},{65,97},{97,2},{2,34}... | collective-permute-start | bytes 884744 | tf_op jit(solution)/shard_map/ppermute | solution.py:57
  132.2 13.7 %collective-permute-start.7 = (bf16[4,48,768]{2,1,0:T(8,128)(2,1)S(1)}, bf16[4,48,768]{2,1,0:T(8,128)(2,1)S(1)}, u32[]{:S(2)}, u32[]{:S(2)}) collective-permute-start(bf16[4,48,768]{2,1,0:T(8,128)(2,1)S(1)} %slice_bitcast_fusion), channel_id=1, source_target_pairs={{0,99},{32,0},{64,32},{96,64},{1,96},{33,1},{65,33},{97,65},{2,97}... | collective-permute-start | bytes 884744 | tf_op jit(solution)/shard_map/ppermute | solution.py:57
  135.7 11.9 %collective-permute-start.5 = (bf16[4,48,768]{2,1,0:T(8,128)(2,1)S(1)}, bf16[4,48,768]{2,1,0:T(8,128)(2,1)S(1)}, u32[]{:S(2)}, u32[]{:S(2)}) collective-permute-start(bf16[4,48,768]{2,1,0:T(8,128)(2,1)S(1)} %slice_bitcast_fusion.1), channel_id=1, source_target_pairs={{0,32},{32,64},{64,96},{96,1},{1,33},{33,65},{65,97},{97,2},{2,34}... | collective-permute-start | bytes 884744 | tf_op jit(solution)/shard_map/ppermute | solution.py:57
  142.0 1.7 copy-start.2
  151.9 7.3 %copy-start.4 = (f32[128,6]{0,1:T(8,128)S(1)}, f32[128,6]{0,1:T(8,128)}, u32[]{:S(2)}) copy-start(f32[128,6]{0,1:T(8,128)} %param.12) | copy-start | bytes 9220
  151.9 38.5 %all-to-all-start.3 = ((bf16[32,24,1536]{2,1,0:T(8,128)(2,1)}), bf16[32,24,1536]{2,1,0:T(8,128)(2,1)S(1)}, u32[]{:S(2)}, u32[]{:S(2)}) async-start(bf16[32,24,1536]{2,1,0:T(8,128)(2,1)} %bitcast.36), calls=%async_computation.3 | async-start | bytes 4718592 | tf_op jit(solution)/shard_map/all_to_all | solution.py:91
